TPU v7x, 32 devices: a whole 2x2x4 slice. The times are simulated.
32 devices in a mesh: grp: 2 (over y), seq: 4 (over z), kvh: 2 (over x), sub: 2 (over core).
Axes of the slice: x: 2, y: 2, z: 4, core: 2. Of those that a mesh axis runs over, the one named last changes fastest.
Arguments:
- tokens: bfloat16 [4096, 4096], P(('grp', 'seq'), ('kvh', 'sub')), parts along dimension 0, may hold values from -6 to 6
- norm_gain: float32 [4096], replicated, may hold values from 0.5 to 1.5
- w_query: bfloat16 [4096, 8, 512], P(None, 'kvh', 'sub')
- w_key: bfloat16 [4096, 8, 128], P('sub', 'kvh')
- w_value: bfloat16 [4096, 8, 128], P('sub', 'kvh'), may hold values from -0.09375 to 0.09375
- links: int32 [3, 8], replicated, may hold values from 0 to 7, as said below
Outputs:
- attended: bfloat16 [4096, 8, 512], P(('grp', 'seq'), 'kvh', 'sub'), parts along dimension 0
- gram: float32 [8192, 4096], P(('grp', 'seq'), ('kvh', 'sub')), parts along dimension 0
There are 2 independent parts, one for each index of `grp`. A program takes and returns all parts, laid end to end along the dimension named above; an argument that names none is the same for every part. Nothing has to cross between parts.
Inputs may be any that keep to these rules, and one draw needn't show every extreme that they name: links[b, i] is either i or i xor 2 ** b; the pattern is symmetric: block i names its section-b partner exactly when that partner names i; block 0 names its partner at every section.
All inputs are finite; a program needn't handle non-finite values.
Results may differ from a plain program's by a relative error of at most 0.0095.
Values may be sent and summed in bfloat16 or wider, within the bound.
No kernel may reach another device: no remote copies, remote signals or barrier semaphores. Data moves between devices by JAX's collectives and lax.ppermute only.
A program may use at most 128 MiB of HBM per device.

v0:
```python
import math

import jax
import jax.numpy as jnp
from jax import lax
from jax.sharding import PartitionSpec as P

rope_base = 500000.0


def from_partner(block, axis, bit):
    count = lax.axis_size(axis)
    route = []
    for low in range(count):
        high = low | 1 << bit
        if high != low and high < count:
            route += [(low, high), (high, low)]
    return lax.ppermute(block, axis, route)


def swap_halves(pieces, count, index):
    whole = [None] * count
    whole[0] = pieces
    for shift in range(1, count):
        route = [(j, (j + shift) % count) for j in range(count)]
        whole[shift] = lax.ppermute(pieces, "sub", route)
    return whole


def split_send(blocks, axis, bit):
    count = lax.axis_size("sub")
    index = lax.axis_index("sub")
    share = blocks[0].shape[0] // count
    mine = tuple(lax.dynamic_slice_in_dim(b, index * share, share, 0) for b in blocks)
    got = from_partner(mine, axis, bit)
    whole = swap_halves(got, count, index)
    out = []
    for n, b in enumerate(blocks):
        full = jnp.zeros_like(b)
        for shift in range(count):
            source = (index - shift) % count
            full = lax.dynamic_update_slice_in_dim(full, whole[shift][n], source * share, 0)
        out.append(full)
    return tuple(out)


def rotate(vectors, positions):
    width = vectors.shape[-1]
    half = width // 2
    inverse = jnp.exp(jnp.arange(half, dtype=jnp.float32) * (-2.0 * math.log(rope_base) / width))
    angles = positions.astype(jnp.float32)[:, None] * inverse[None, :]
    shape = (angles.shape[0],) + (1,) * (vectors.ndim - 2) + (half,)
    cosine = jnp.cos(angles).reshape(shape)
    sine = jnp.sin(angles).reshape(shape)
    first = vectors[..., :half]
    second = vectors[..., half:]
    return jnp.concatenate(
        [first * cosine - second * sine, second * cosine + first * sine], axis=-1
    )


def body(tokens, norm_gain, w_query, w_key, w_value, links):
    gathered = lax.all_gather(tokens, ("kvh", "sub"), axis=1, tiled=True)
    widened = gathered.astype(jnp.float32)
    mean_square = jnp.mean(widened * widened, axis=-1, keepdims=True)
    normed = (widened * lax.rsqrt(mean_square + 1e-05) * norm_gain).astype(jnp.bfloat16)
    row_count = normed.shape[0]
    block_len = row_count // 2
    width = normed.shape[1]
    seq_index = lax.axis_index("seq")
    local_rows = jnp.arange(row_count, dtype=jnp.int32)
    positions = seq_index * row_count + local_rows
    head_size = w_key.shape[2]
    local_groups = w_key.shape[1]
    per_group = w_query.shape[2] // head_size
    queries = jnp.einsum("td,dgc->tgc", normed, w_query, preferred_element_type=jnp.float32)
    queries = rotate(
        queries.reshape(row_count, local_groups, per_group, head_size), positions
    ).astype(jnp.bfloat16)
    sub_count = lax.axis_size("sub")
    sub_index = lax.axis_index("sub")
    row_share = w_key.shape[0]
    key_more = None
    value_more = None
    for shift in range(sub_count):
        if shift == 0:
            key_part, value_part = w_key, w_value
        else:
            route = [(j, (j + shift) % sub_count) for j in range(sub_count)]
            key_part, value_part = lax.ppermute((w_key, w_value), "sub", route)
        source = (sub_index - shift) % sub_count
        rows = lax.dynamic_slice_in_dim(normed, source * row_share, row_share, 1)
        key_step = jnp.einsum("td,dgh->tgh", rows, key_part, preferred_element_type=jnp.float32)
        value_step = jnp.einsum("td,dgh->tgh", rows, value_part, preferred_element_type=jnp.float32)
        key_more = key_step if key_more is None else key_more + key_step
        value_more = value_step if value_more is None else value_more + value_step
    keys = rotate(key_more, positions).astype(jnp.bfloat16)
    values = value_more.astype(jnp.bfloat16)
    block_ids = seq_index * 2 + jnp.arange(2, dtype=jnp.int32)
    query_block = local_rows // block_len
    scale = 1.0 / math.sqrt(head_size)
    scores = jnp.einsum("tgrh,ugh->grtu", queries, keys, preferred_element_type=jnp.float32) * scale
    near_linked = lax.dynamic_slice_in_dim(links[0], seq_index * 2, 2) != block_ids
    same_block = query_block[:, None] == query_block[None, :]
    causal = same_block & (local_rows[None, :] <= local_rows[:, None])
    across = ~same_block & near_linked[query_block][:, None]
    allowed = causal | across
    scores = jnp.where(allowed[None, None], scores, -jnp.inf)
    running_max = jnp.max(scores, axis=-1)
    weights = jnp.exp(scores - running_max[..., None])
    total = jnp.sum(weights, axis=-1)
    accum = jnp.einsum(
        "grtu,ugh->tgrh", weights.astype(jnp.bfloat16), values, preferred_element_type=jnp.float32
    )
    query_pairs = queries.reshape(2, block_len, local_groups, per_group, head_size)
    for section in range(1, lax.axis_size("seq").bit_length()):
        far_keys, far_values = split_send((keys, values), "seq", section - 1)
        far_keys = far_keys.reshape(2, block_len, local_groups, head_size)
        far_values = far_values.reshape(2, block_len, local_groups, head_size)
        linked = lax.dynamic_slice_in_dim(links[section], seq_index * 2, 2) != block_ids
        offset = jnp.where(linked, 0.0, -1e30).astype(jnp.float32)[query_block]
        far_scores = jnp.einsum(
            "jtgrh,jugh->grjtu", query_pairs, far_keys, preferred_element_type=jnp.float32
        )
        far_scores = (
            far_scores.reshape(local_groups, per_group, row_count, block_len) * scale
            + offset[None, None, :, None]
        )
        new_max = jnp.maximum(running_max, jnp.max(far_scores, axis=-1))
        shrink = jnp.exp(running_max - new_max)
        far_weights = jnp.exp(far_scores - new_max[..., None])
        total = total * shrink + jnp.sum(far_weights, axis=-1)
        paired = far_weights.astype(jnp.bfloat16).reshape(
            local_groups, per_group, 2, block_len, block_len
        )
        far_sum = jnp.einsum(
            "grjtu,jugh->jtgrh", paired, far_values, preferred_element_type=jnp.float32
        )
        far_sum = far_sum.reshape(row_count, local_groups, per_group, head_size)
        accum = accum * jnp.transpose(shrink, (2, 0, 1))[..., None] + far_sum
        running_max = new_max
    attended = (accum / jnp.transpose(total, (2, 0, 1))[..., None]).astype(jnp.bfloat16)
    attended = attended.reshape(row_count, local_groups, per_group * head_size)
    tile_count = lax.axis_size("kvh") * lax.axis_size("sub")
    tile_cols = width // tile_count
    owner_index = lax.axis_index("kvh") * lax.axis_size("sub") + lax.axis_index("sub")
    owned = lax.dynamic_slice_in_dim(normed, owner_index * tile_cols, tile_cols, 1)
    seq_count = lax.axis_size("seq")
    inverse_count = 1.0 / (row_count * seq_count)
    gram_sum = lax.psum_scatter(
        (
            jnp.einsum("tc,tr->cr", normed, owned, preferred_element_type=jnp.float32)
            * inverse_count
        ).astype(jnp.bfloat16),
        "seq",
        scatter_dimension=0,
        tiled=True,
    ).astype(jnp.float32)
    gram_tile = gram_sum
    return (attended, gram_tile)


def solution(mesh):
    placed = (
        P(("grp", "seq"), ("kvh", "sub")),
        P(),
        P(None, "kvh", "sub"),
        P("sub", "kvh", None),
        P("sub", "kvh", None),
        P(),
    )
    return jax.shard_map(
        body,
        mesh=mesh,
        in_specs=placed,
        out_specs=(P(("grp", "seq"), "kvh", "sub"), P(("grp", "seq"), ("kvh", "sub"))),
        check_vma=False,
    )
```

profile of v0, /device:TPU:0, one launch (start us, length us, event | category | flops | bytes accessed | tf_op | source)
XLA Modules:
  0.0 238.9 jit_solution(13191938020074221671)
XLA Ops:
  8.0 38.8 %all-gather.2.cloned.1.call-done = bf16[512,4096]{1,0:T(8,128)(2,1)} async-done(((bf16[512,1024]{1,0:T(8,128)(2,1)}), bf16[512,4096]{1,0:T(8,128)(2,1)}) %all-gather.2.cloned.1.call-update) | async-done | bytes 4194320 | tf_op jit(solution)/shard_map/all_gather | solution.py:63
  46.8 3.2 %fusion = f32[512]{0:T(512)S(1)} fusion(bf16[512,4096]{1,0:T(8,128)(2,1)} %all-gather.2.cloned.1.call-done), kind=kLoop, calls=%fused_computation.3 | loop fusion | flops 6290944 | bytes 4196352 | tf_op jit(solution)/shard_map/reduce_sum | solution.py:65
  50.2 1.6 fusion.2
  51.8 2.0 copy-done.2
  53.8 7.0 %multiply_convert_fusion = bf16[4096,1024]{1,0:T(8,128)(2,1)} fusion(bf16[512,4096]{1,0:T(8,128)(2,1)S(1)} %fusion.2, s32[]{:T(128)S(6)} %select_n.127), kind=kOutput, calls=%fused_computation | convolution fusion | flops 4303355904 | bytes 13631492 | tf_op jit(solution)/shard_map/tc,tr->cr/dot_general | solution.py:152
  60.9 3.3 %copy.58 = bf16[2048,4,128]{2,0,1:T(8,128)(2,1)} copy(bf16[2048,4,128]{2,1,0:T(4,128)(2,1)} %param.10) | data formatting | bytes 4194304 | tf_op args[4]
  64.5 2.7 %copy.60 = bf16[2048,4,128]{0,2,1:T(8,128)(2,1)} copy(bf16[2048,4,128]{2,1,0:T(4,128)(2,1)S(1)} %copy-done.7) | data formatting | bytes 4194304 | tf_op args[3]
  73.0 1.4 select_reduce_fusion
  74.7 3.7 %fusion.31 = f32[512,4,128]{2,0,1:T(8,128)S(1)} fusion(bf16[512,4096]{1,0:T(8,128)(2,1)} %copy-done.2, s32[]{:T(128)S(6)} %select_n.114, bf16[2048,4,128]{2,1,0:T(4,128)(2,1)} %param.10), kind=kOutput, calls=%fused_computation.42 | convolution fusion | flops 1073741824 | bytes 5242884 | tf_op jit(solution)/shard_map/td,dgh->tgh/dot_general | solution.py:94
  78.4 3.0 %fusion.51 = bf16[512,4,128]{2,0,1:T(8,128)(2,1)S(1)} fusion(f32[512,4,128]{2,0,1:T(8,128)S(1)} %fusion.31, bf16[2048,4,128]{2,0,1:T(8,128)(2,1)} %collective-permute-done, bf16[512,4096]{1,0:T(8,128)(2,1)S(1)} %copy-done.3, s32[]{:T(128)S(6)} %select_n.116), kind=kOutput, calls=%fused_computation.58 | convolution fusion | flops 1074266112 | bytes 5767172 | tf_op jit(solution)/shard_map/td,dgh->tgh/dot_general | solution.py:94
  82.3 2.4 %collective-permute-start.8 = (bf16[256,4,128]{2,0,1:T(8,128)(2,1)}, bf16[256,4,128]{2,0,1:T(8,128)(2,1)}, u32[]{:S(2)}, u32[]{:S(2)}) collective-permute-start(bf16[256,4,128]{2,0,1:T(8,128)(2,1)} %constant_dynamic-slice_fusion.1), channel_id=1, source_target_pairs={{0,8},{8,0},{4,12},{12,4},{1,9},{9,1},{5,13},{13,5},{2,10},{10,2},... | collective-permute-start | bytes 786440 | tf_op jit(solution)/shard_map/ppermute | solution.py:18
  84.7 1.5 collective-permute-start.4
  87.5 2.9 %fusion.34 = f32[512,512]{0,1:S(1)} fusion(bf16[2048,512]{0,1:T(8,128)(2,1)} %bitcast.8, bf16[512,4096]{1,0:T(8,128)(2,1)S(1)} %copy-done.3, s32[]{:T(128)S(6)} %select_n.116), kind=kOutput, calls=%fused_computation.47 | convolution fusion | flops 1073741824 | bytes 5242884
  92.5 7.3 %fusion.3 = f32[512,4,256]{0,2,1:T(8,128)S(1)} fusion(bf16[4096,4,256]{2,1,0:T(4,128)(2,1)} %param.8, bf16[512,4096]{1,0:T(8,128)(2,1)S(1)} %copy-done.3), kind=kOutput, calls=%fused_computation.7 | convolution fusion | flops 4294967296 | bytes 14680064 | tf_op jit(solution)/shard_map/td,dgc->tgc/dot_general | solution.py:76
  100.0 1.9 copy.105
  102.0 2.0 copy.104
  104.0 2.8 %subtract_convert_fusion = (bf16[512,4,2,64]{3,0,2,1:T(8,128)(2,1)S(1)}, bf16[512,4,2,64]{3,0,2,1:T(8,128)(2,1)S(1)}) fusion(f32[512,4,2,64]{3,0,2,1:T(8,128)} %copy.105, f32[512,4,2,64]{3,0,2,1:T(8,128)} %copy.104, f32[512,64]{1,0:T(8,128)S(1)} %copy.66, f32[512,64]{1,0:T(8,128)S(1)} %copy.64), kind=kLoop, calls=%fused_computation.45 | loop fusion | flops 2097152 | bytes 3407872 | tf_op jit(solution)/shard_map/convert.4
  106.8 2.3 fusion.7
  109.2 1.8 fusion.5
  110.9 1.5 copy-done.1
  112.4 19.4 %collective-permute-done.6 = bf16[256,4,128]{0,2,1:T(8,128)(2,1)} collective-permute-done((bf16[256,4,128]{0,2,1:T(8,128)(2,1)}, bf16[256,4,128]{0,2,1:T(8,128)(2,1)}, u32[]{:S(2)}, u32[]{:S(2)}) %collective-permute-start.6) | collective-permute-done | bytes 262176 | tf_op jit(solution)/shard_map/ppermute | solution.py:18
  133.0 1.8 copy.70
  139.5 1.8 copy.79
  141.3 1.8 copy.71
  143.1 1.9 constant_dynamic-update-slice_fusion
  145.0 1.9 constant_dynamic-update-slice_fusion.4
  146.8 2.2 bitcast_reduce_fusion.1
  154.4 1.7 slice-done.1
  156.1 2.5 %fusion.33 = bf16[512,4,2,128]{0,3,2,1:T(8,128)(2,1)S(1)} fusion(f32[512,4,2,128]{0,3,2,1:T(8,128)S(1)} %bitcast.166, f32[512,4,2,128]{0,3,2,1:T(8,128)S(1)} %bitcast.165, f32[4,512,512,2]{2,1,3,0:T(8,128)S(1)} %bitcast.159, f32[4,2,512]{2,1,0:T(2,128)S(1)} %get-tuple-element.36, pred[512,512]{0,1:T(8,128)(4,1)S(1)} %fusion.59, ...), kind=kOutput, calls=%fused_computation.46 | convolution fusion | flops 548405248 | bytes 14483456 | tf_op jit(solution)/shard_map/grtu,ugh->tgrh/dot_general | solution.py:112
  158.6 1.4 copy.83
  160.0 67.9 %reduce-scatter.2.cloned.1.call-done = bf16[1024,1024]{1,0:T(8,128)(2,1)} async-done(((bf16[4096,1024]{1,0:T(8,128)(2,1)}), bf16[1024,1024]{1,0:T(8,128)(2,1)}) %reduce-scatter.2.cloned.1.call-update) | async-done | bytes 2097168 | tf_op jit(solution)/shard_map/reduce_scatter | solution.py:150
  228.0 4.1 %convert_element_type.49 = f32[1024,1024]{1,0:T(8,128)} convert(bf16[1024,1024]{1,0:T(8,128)(2,1)} %reduce-scatter.2.cloned.1.call-done) | non-fusion elementwise | flops 1048576 | bytes 6291456 | tf_op jit(solution)/shard_map/convert_element_type | solution.py:158
  (91 shorter events, 22.9 us)
Async XLA Ops:
  7.2 42.8 %copy-start.11 = (f32[4096]{0:T(1024)S(1)}, f32[4096]{0:T(1024)}, u32[]{:S(2)}) copy-start(f32[4096]{0:T(1024)} %param.7) | copy-start | bytes 49156
  7.2 39.6 %all-gather.2.cloned.1.call-start = ((), (), s32[]{:S(2)}) async-start(), calls=%async_computation.1 | async-start | bytes 5242880 | tf_op jit(solution)/shard_map/all_gather | solution.py:63
  7.9 220.0 %reduce-scatter.2.cloned.1.call-start = ((), (), s32[]{:S(2)}) async-start(), calls=%async_computation.2 | async-start | bytes 10485760 | tf_op jit(solution)/shard_map/reduce_scatter | solution.py:150
  46.8 3.4 %copy-start = (bf16[512,4096]{1,0:T(8,128)(2,1)S(1)}, bf16[512,4096]{1,0:T(8,128)(2,1)}, u32[]{:S(2)}) copy-start(bf16[512,4096]{1,0:T(8,128)(2,1)} %all-gather.2.cloned.1.call-done) | copy-start | bytes 12582916
  51.8 2.0 copy-start.2
  60.9 3.6 %copy-start.7 = (bf16[2048,4,128]{2,1,0:T(4,128)(2,1)S(1)}, bf16[2048,4,128]{2,1,0:T(4,128)(2,1)}, u32[]{:S(2)}) copy-start(bf16[2048,4,128]{2,1,0:T(4,128)(2,1)} %param.9) | copy-start | bytes 6291460
  60.9 6.6 %copy-start.12 = (s32[3,8]{1,0:T(4,128)S(1)}, s32[3,8]{1,0:T(4,128)}, u32[]{:S(2)}) copy-start(s32[3,8]{1,0:T(4,128)} %param.11) | copy-start | bytes 292
  64.2 14.2 %collective-permute-start = (bf16[2048,4,128]{2,0,1:T(8,128)(2,1)}, bf16[2048,4,128]{2,0,1:T(8,128)(2,1)}, u32[]{:S(2)}, u32[]{:S(2)}) collective-permute-start(bf16[2048,4,128]{2,0,1:T(8,128)(2,1)} %copy.58), channel_id=1, source_target_pairs={{0,1},{1,0},{2,3},{3,2},{4,5},{5,4},{6,7},{7,6},{8,9},{9,8},{10,11... | collective-permute-start | bytes 6291464 | tf_op jit(solution)/shard_map/ppermute | solution.py:90
  67.2 20.3 %collective-permute-start.1 = (bf16[2048,4,128]{0,2,1:T(8,128)(2,1)}, bf16[2048,4,128]{0,2,1:T(8,128)(2,1)}, u32[]{:S(2)}, u32[]{:S(2)}) collective-permute-start(bf16[2048,4,128]{0,2,1:T(8,128)(2,1)} %copy.60), channel_id=1, source_target_pairs={{0,1},{1,0},{2,3},{3,2},{4,5},{5,4},{6,7},{7,6},{8,9},{9,8},{10,11... | collective-permute-start | bytes 6291464 | tf_op jit(solution)/shard_map/ppermute | solution.py:90
  74.7 3.7 %copy-start.3 = (bf16[512,4096]{1,0:T(8,128)(2,1)S(1)}, bf16[512,4096]{1,0:T(8,128)(2,1)}, u32[]{:S(2)}) copy-start(bf16[512,4096]{1,0:T(8,128)(2,1)} %copy-done.2) | copy-start | bytes 12582916
  78.4 7.8 %copy-start.8 = (bf16[2048,4,128]{0,2,1:T(8,128)(2,1)S(1)}, bf16[2048,4,128]{0,2,1:T(8,128)(2,1)}, u32[]{:S(2)}) copy-start(bf16[2048,4,128]{0,2,1:T(8,128)(2,1)} %copy.60) | copy-start | bytes 6291460
  81.4 8.9 %copy-start.9 = (bf16[512,4,128]{2,0,1:T(8,128)(2,1)}, bf16[512,4,128]{2,0,1:T(8,128)(2,1)S(1)}, u32[]{:S(2)}) copy-start(bf16[512,4,128]{2,0,1:T(8,128)(2,1)S(1)} %fusion.51) | copy-start | bytes 1572868
  82.3 53.0 %collective-permute-start.8 = (bf16[256,4,128]{2,0,1:T(8,128)(2,1)}, bf16[256,4,128]{2,0,1:T(8,128)(2,1)}, u32[]{:S(2)}, u32[]{:S(2)}) collective-permute-start(bf16[256,4,128]{2,0,1:T(8,128)(2,1)} %constant_dynamic-slice_fusion.1), channel_id=1, source_target_pairs={{0,8},{8,0},{4,12},{12,4},{1,9},{9,1},{5,13},{13,5},{2,10},{10,2},... | collective-permute-start | bytes 786440 | tf_op jit(solution)/shard_map/ppermute | solution.py:18
  84.7 51.9 %collective-permute-start.4 = (bf16[256,4,128]{2,0,1:T(8,128)(2,1)}, bf16[256,4,128]{2,0,1:T(8,128)(2,1)}, u32[]{:S(2)}, u32[]{:S(2)}) collective-permute-start(bf16[256,4,128]{2,0,1:T(8,128)(2,1)} %constant_dynamic-slice_fusion.1), channel_id=1, source_target_pairs={{0,4},{4,0},{8,12},{12,8},{1,5},{5,1},{9,13},{13,9},{2,6},{6,2},{1... | collective-permute-start | bytes 786440 | tf_op jit(solution)/shard_map/ppermute | solution.py:18
  91.5 40.3 %collective-permute-start.6 = (bf16[256,4,128]{0,2,1:T(8,128)(2,1)}, bf16[256,4,128]{0,2,1:T(8,128)(2,1)}, u32[]{:S(2)}, u32[]{:S(2)}) collective-permute-start(bf16[256,4,128]{0,2,1:T(8,128)(2,1)} %fusion.70), channel_id=1, source_target_pairs={{0,8},{8,0},{4,12},{12,4},{1,9},{9,1},{5,13},{13,5},{2,10},{10,2},... | collective-permute-start | bytes 786440 | tf_op jit(solution)/shard_map/ppermute | solution.py:18
  92.0 41.0 %collective-permute-start.2 = (bf16[256,4,128]{0,2,1:T(8,128)(2,1)}, bf16[256,4,128]{0,2,1:T(8,128)(2,1)}, u32[]{:S(2)}, u32[]{:S(2)}) collective-permute-start(bf16[256,4,128]{0,2,1:T(8,128)(2,1)} %fusion.70), channel_id=1, source_target_pairs={{0,4},{4,0},{8,12},{12,8},{1,5},{5,1},{9,13},{13,9},{2,6},{6,2},{1... | collective-permute-start | bytes 786440 | tf_op jit(solution)/shard_map/ppermute | solution.py:18
  109.1 3.2 %copy-start.1 = (f32[4,512,512,2]{2,1,3,0:T(8,128)}, f32[4,512,512,2]{2,1,3,0:T(8,128)S(1)}, u32[]{:S(2)}) copy-start(f32[4,512,512,2]{2,1,3,0:T(8,128)S(1)} %get-tuple-element.37) | copy-start | bytes 25165828
  132.9 6.6 %collective-permute-start.7 = (bf16[256,4,128]{0,2,1:T(8,128)(2,1)}, bf16[256,4,128]{0,2,1:T(8,128)(2,1)}, u32[]{:S(2)}, u32[]{:S(2)}) collective-permute-start(bf16[256,4,128]{0,2,1:T(8,128)(2,1)} %collective-permute-done.6), channel_id=1, source_target_pairs={{0,1},{1,0},{2,3},{3,2},{4,5},{5,4},{6,7},{7,6},{8,9},{9,8},{10,11... | collective-permute-start | bytes 786440 | tf_op jit(solution)/shard_map/ppermute | solution.py:26
  134.8 6.5 %collective-permute-start.3 = (bf16[256,4,128]{0,2,1:T(8,128)(2,1)}, bf16[256,4,128]{0,2,1:T(8,128)(2,1)}, u32[]{:S(2)}, u32[]{:S(2)}) collective-permute-start(bf16[256,4,128]{0,2,1:T(8,128)(2,1)} %collective-permute-done.2), channel_id=1, source_target_pairs={{0,1},{1,0},{2,3},{3,2},{4,5},{5,4},{6,7},{7,6},{8,9},{9,8},{10,11... | collective-permute-start | bytes 786440 | tf_op jit(solution)/shard_map/ppermute | solution.py:26
  135.3 7.8 %collective-permute-start.9 = (bf16[256,4,128]{2,0,1:T(8,128)(2,1)}, bf16[256,4,128]{2,0,1:T(8,128)(2,1)}, u32[]{:S(2)}, u32[]{:S(2)}) collective-permute-start(bf16[256,4,128]{2,0,1:T(8,128)(2,1)} %collective-permute-done.8), channel_id=1, source_target_pairs={{0,1},{1,0},{2,3},{3,2},{4,5},{5,4},{6,7},{7,6},{8,9},{9,8},{10,11... | collective-permute-start | bytes 786440 | tf_op jit(solution)/shard_map/ppermute | solution.py:26
  136.5 0.8 copy-start.4
  136.5 8.5 %collective-permute-start.5 = (bf16[256,4,128]{2,0,1:T(8,128)(2,1)}, bf16[256,4,128]{2,0,1:T(8,128)(2,1)}, u32[]{:S(2)}, u32[]{:S(2)}) collective-permute-start(bf16[256,4,128]{2,0,1:T(8,128)(2,1)} %collective-permute-done.4), channel_id=1, source_target_pairs={{0,1},{1,0},{2,3},{3,2},{4,5},{5,4},{6,7},{7,6},{8,9},{9,8},{10,11... | collective-permute-start | bytes 786440 | tf_op jit(solution)/shard_map/ppermute | solution.py:26
  138.3 1.2 copy-start.5
  152.0 1.1 copy-start.6
  152.0 2.4 slice-start
  153.1 3.0 %slice-start.1 = ((s8[8388608]{0:T(1024)(128)(4,1)}), s8[4194304]{0:T(1024)(128)(4,1)S(1)}, s32[]{:S(2)}) async-start(s8[8388608]{0:T(1024)(128)(4,1)} %bitcast.158), calls=%async_computation.4 | async-start | bytes 8388608
  153.1 3.0 %copy-start.10 = (bf16[512,4,128]{2,0,1:T(8,128)(2,1)S(1)}, bf16[512,4,128]{2,0,1:T(8,128)(2,1)}, u32[]{:S(2)}) copy-start(bf16[512,4,128]{2,0,1:T(8,128)(2,1)} %copy-done.9) | copy-start | bytes 1572868
Sparse Core Ops, SparseCore 0:
  9.5 37.1 all-gather.1
  61.0 166.9 reduce-scatter.1
where the time goes:
time: 239 us
  waiting for transfers between devices  127 us (53%)
  local copies, waits for them, and re-layouts  34.6 us (14%)
  matrix products  34.6 us (14%)
  other arithmetic  21.7 us (9%)
  between operations  14.5 us (6%)
  starting transfers between devices  6.64 us (3%)
    reduce_scatter x1, waiting for transfers between devices, body(): lax.psum_scatter((jnp.einsum('tc,tr->cr', normed, owned, preferred_elemen...  67.9 us
    all_gather x1, waiting for transfers between devices, body(): gathered = lax.all_gather(tokens, ('kvh', 'sub'), axis=1, tiled=True)  38.8 us
    ppermute x4, waiting for transfers between devices, from_partner(): return lax.ppermute(block, axis, route)  19.4 us
    unnamed x35, local copies, waits for them, and re-layouts  17.3 us
    dot_general x1, matrix products, body(): jnp.einsum('td,dgc->tgc', normed, w_query, preferred_element_type=jnp.flo...  7.27 us
    dot_general x1, matrix products, body(): jnp.einsum('tc,tr->cr', normed, owned, preferred_element_type=jnp.float32)  7 us
    dynamic_update_slice x6, local copies, waits for them, and re-layouts, split_send(): lax.dynamic_update_slice_in_dim(full, whole[shift][n], source * share, 0)  6.87 us
    dot_general x2, matrix products, body(): jnp.einsum('td,dgh->tgh', rows, value_part, preferred_element_type=jnp.fl...  6.7 us
  transfers between devices with their start and end apart: 12, of which 3 were waited for; matrix products, arithmetic and copies ran while one was open for 29% of the time, Pallas kernels for 0%

commit v1 on v0

--- a/solution.py
+++ b/solution.py
@@ -60,7 +60,15 @@
 
 
 def body(tokens, norm_gain, w_query, w_key, w_value, links):
-    gathered = lax.all_gather(tokens, ("kvh", "sub"), axis=1, tiled=True)
+    lanes = lax.all_gather(tokens, "kvh", axis=0, tiled=False)
+    sub_total = lax.axis_size("sub")
+    lane_index = lax.axis_index("sub")
+    copies = swap_halves(lanes, sub_total, lane_index)
+    ordered = [
+        lax.select_n((lane_index - lane) % sub_total, *copies) for lane in range(sub_total)
+    ]
+    stacked = jnp.stack(ordered, axis=1)
+    gathered = jnp.transpose(stacked, (2, 0, 1, 3)).reshape(tokens.shape[0], -1)
     widened = gathered.astype(jnp.float32)
     mean_square = jnp.mean(widened * widened, axis=-1, keepdims=True)
     normed = (widened * lax.rsqrt(mean_square + 1e-05) * norm_gain).astype(jnp.bfloat16)

time: 239 us -> 271 us (1.13)
  local copies, waits for them, and re-layouts: 34.6 us -> 80.2 us
  waiting for transfers between devices: 127 us -> 107 us
  other arithmetic: 21.7 us -> 25.2 us
    convert_element_type x0 -> x2, local copies, waits for them, and re-layouts: none -> 23 us  [body(): widened = gathered.astype(jnp.float32)]
    reduce_scatter x1, waiting for transfers between devices: 67.9 us -> 50 us  [body(): lax.psum_scatter((jnp.einsum('tc,tr->cr', normed, owned, preferred_elemen...]
    dot_general x0 -> x1, local copies, waits for them, and re-layouts: none -> 13.8 us  [body(): jnp.einsum('td,dgc->tgc', normed, w_query, preferred_element_type=jnp.flo...]
    mul x0 -> x3, local copies, waits for them, and re-layouts: none -> 6.33 us  [body(): widened * lax.rsqrt(mean_square + 1e-05) * norm_gain]
    ppermute x4, waiting for transfers between devices: 19.4 us -> 14.1 us  [from_partner(): return lax.ppermute(block, axis, route)]
    ppermute x4 -> x5, waiting for transfers between devices: 0.01 us -> 4.51 us  [swap_halves(): whole[shift] = lax.ppermute(pieces, 'sub', route)]
    convert_element_type x1, other arithmetic: 1.62 us -> 4.71 us  [body(): (widened * lax.rsqrt(mean_square + 1e-05) * norm_gain).astype(jnp.bfloat16)]
    mul x0 -> x1, other arithmetic: none -> 2.82 us  [body(): widened * lax.rsqrt(mean_square + 1e-05) * norm_gain]
  transfers between devices with their start and end apart: 12 -> 13, of which waited for: 3 -> 4; matrix products, arithmetic and copies ran while one was open for 29% -> 34% of each run, Pallas kernels for 0% -> 0%
where the time goes in v1:
time: 271 us; the launch traced here: 269 us
  waiting for transfers between devices  107 us (39%)
  local copies, waits for them, and re-layouts  80.2 us (30%)
  matrix products  36 us (13%)
  other arithmetic  25.2 us (9%)
  between operations  14.5 us (5%)
  starting transfers between devices  6.74 us (2%)
    reduce_scatter x1, waiting for transfers between devices, body(): lax.psum_scatter((jnp.einsum('tc,tr->cr', normed, owned, preferred_elemen...  50 us
    all_gather x1, waiting for transfers between devices, body(): lanes = lax.all_gather(tokens, 'kvh', axis=0, tiled=False)  37.4 us
    convert_element_type x2, local copies, waits for them, and re-layouts, body(): widened = gathered.astype(jnp.float32)  23 us
    unnamed x27, local copies, waits for them, and re-layouts  16 us
    ppermute x4, waiting for transfers between devices, from_partner(): return lax.ppermute(block, axis, route)  14.1 us
    dot_general x1, local copies, waits for them, and re-layouts, body(): jnp.einsum('td,dgc->tgc', normed, w_query, preferred_element_type=jnp.flo...  13.8 us
    dot_general x1, matrix products, body(): jnp.einsum('td,dgc->tgc', normed, w_query, preferred_element_type=jnp.flo...  8.37 us
    dynamic_update_slice x6, local copies, waits for them, and re-layouts, split_send(): lax.dynamic_update_slice_in_dim(full, whole[shift][n], source * share, 0)  8.08 us
  transfers between devices with their start and end apart: 13, of which 4 were waited for; matrix products, arithmetic and copies ran while one was open for 34% of the time, Pallas kernels for 0%

profile of v1, /device:TPU:0, one launch (start us, length us, event | category | flops | bytes accessed | tf_op | source)
XLA Modules:
  0.0 269.4 jit_solution(1851980646299447295)
XLA Ops:
  7.9 37.4 %all-gather.3.cloned.1.call-done = bf16[1024,1024]{1,0:T(8,128)(2,1)} async-done(((bf16[512,1024]{1,0:T(8,128)(2,1)}), bf16[1024,1024]{1,0:T(8,128)(2,1)}) %all-gather.3.cloned.1.call-update) | async-done | bytes 2097168 | tf_op jit(solution)/shard_map/all_gather | solution.py:63
  45.4 4.5 %collective-permute-done = bf16[2,512,1024]{2,1,0:T(8,128)(2,1)} collective-permute-done((bf16[2,512,1024]{2,1,0:T(8,128)(2,1)}, bf16[2,512,1024]{2,1,0:T(8,128)(2,1)}, u32[]{:S(2)}, u32[]{:S(2)}) %collective-permute-start) | collective-permute-done | bytes 2097184 | tf_op jit(solution)/shard_map/ppermute | solution.py:26
  49.9 2.5 select_bitcast_fusion.1
  54.7 11.2 %copy.84 = f32[512,2,2,1024]{3,2,1,0:T(2,128)} copy(f32[512,2,2,1024]{3,0,1,2:T(8,128)S(1)} %convert_bitcast_fusion) | data formatting | bytes 16777216 | tf_op jit(solution)/shard_map/convert_element_type | solution.py:72
  65.9 11.8 %reshape.333 = f32[512,4096]{1,0:T(8,128)} reshape(f32[512,2,2,1024]{3,2,1,0:T(2,128)} %copy.84) | data formatting | bytes 16777216 | tf_op jit(solution)/shard_map/convert_element_type | solution.py:72
  77.7 4.7 %multiply_convert_fusion.1 = bf16[512,4096]{1,0:T(8,128)(2,1)S(1)} fusion(f32[512,4096]{1,0:T(8,128)} %reshape.333, f32[4096]{0:T(1024)S(1)} %copy-done.8, f32[512]{0:T(512)S(1)} %add_rsqrt_fusion), kind=kLoop, calls=%fused_computation.9 | loop fusion | flops 6291456 | bytes 12601344 | tf_op jit(solution)/shard_map/convert_element_type | solution.py:74
  82.4 2.0 copy-done.3
  84.4 7.0 %multiply_convert_fusion = bf16[4096,1024]{1,0:T(8,128)(2,1)} fusion(bf16[512,4096]{1,0:T(8,128)(2,1)S(1)} %multiply_convert_fusion.1, s32[]{:T(128)S(6)} %select_n.155), kind=kOutput, calls=%fused_computation | convolution fusion | flops 4303355904 | bytes 13631492 | tf_op jit(solution)/shard_map/tc,tr->cr/dot_general | solution.py:160
  91.4 3.2 %copy.85 = bf16[2048,4,128]{2,0,1:T(8,128)(2,1)} copy(bf16[2048,4,128]{2,1,0:T(4,128)(2,1)} %param.10) | data formatting | bytes 4194304 | tf_op args[4]
  94.8 4.5 %copy.87 = bf16[2048,4,128]{0,2,1:T(8,128)(2,1)} copy(bf16[2048,4,128]{2,1,0:T(4,128)(2,1)} %param.9) | data formatting | bytes 4194304 | tf_op args[3]
  101.6 13.8 %copy.127 = bf16[4,256,4096]{2,1,0:T(8,128)(2,1)} copy(bf16[4,256,4096]{1,0,2:T(4,128)(2,1)} %bitcast.172) | data formatting | bytes 16777216 | tf_op jit(solution)/shard_map/td,dgc->tgc/dot_general | solution.py:84
  120.4 3.6 %fusion.29 = f32[512,4,128]{2,0,1:T(8,128)S(1)} fusion(bf16[512,4096]{1,0:T(8,128)(2,1)} %copy-done.3, s32[]{:T(128)S(6)} %select_n.143, bf16[2048,4,128]{2,1,0:T(4,128)(2,1)} %param.10), kind=kOutput, calls=%fused_computation.43 | convolution fusion | flops 1073741824 | bytes 5242884 | tf_op jit(solution)/shard_map/td,dgh->tgh/dot_general | solution.py:102
  124.0 3.0 %fusion.49 = bf16[512,4,128]{2,0,1:T(8,128)(2,1)S(1)} fusion(f32[512,4,128]{2,0,1:T(8,128)S(1)} %fusion.29, bf16[2048,4,128]{2,0,1:T(8,128)(2,1)} %collective-permute-done.1, bf16[512,4096]{1,0:T(8,128)(2,1)S(1)} %copy-done.4, s32[]{:T(128)S(6)} %select_n.144), kind=kOutput, calls=%fused_computation.59 | convolution fusion | flops 1074266112 | bytes 5767172 | tf_op jit(solution)/shard_map/td,dgh->tgh/dot_general | solution.py:102
  127.9 2.4 collective-permute-start.9
  133.1 3.0 %fusion.32 = f32[512,512]{0,1:S(1)} fusion(bf16[2048,512]{0,1:T(8,128)(2,1)} %bitcast.12, bf16[512,4096]{1,0:T(8,128)(2,1)S(1)} %copy-done.4, s32[]{:T(128)S(6)} %select_n.144), kind=kOutput, calls=%fused_computation.48 | convolution fusion | flops 1073741824 | bytes 5242884
  137.6 2.8 %fusion.8 = bf16[512,2,2,1024]{3,0,1,2:T(8,128)(2,1)} fusion(f32[2,2,1024]{2,0,1:T(2,128)S(1)} %copy.89, f32[512]{0:T(512)S(1)} %add_rsqrt_fusion, bf16[2,1,512,1024]{3,2,0,1:T(8,128)(2,1)S(1)} %copy-done.1, bf16[2,1,512,1024]{3,2,0,1:T(8,128)(2,1)S(1)} %get-tuple-element.19), kind=kLoop, calls=%fused_computation.14 | loop fusion | flops 10485760 | bytes 8407040 | tf_op jit(solution)/shard_map/mul | solution.py:74
  140.5 6.3 %copy.90 = bf16[512,2,2,1024]{0,3,2,1:T(8,128)(2,1)} copy(bf16[512,2,2,1024]{3,0,1,2:T(8,128)(2,1)} %fusion.8) | data formatting | bytes 8388608 | tf_op jit(solution)/shard_map/mul | solution.py:74
  146.8 8.4 %fusion.98 = f32[512,4,2,128]{0,3,2,1:T(8,128)S(1)} fusion(bf16[512,4096,1,1]{0,1,3,2:T(8,128)(2,1)} %bitcast.176, bf16[4,2,128,4096]{3,2,1,0:T(8,128)(2,1)} %bitcast.175), kind=kOutput, calls=%fused_computation.148 | convolution fusion | flops 4294967296 | bytes 14680064 | tf_op jit(solution)/shard_map/td,dgc->tgc/dot_general | solution.py:84
  157.1 3.2 %copy-done.2 = f32[4,512,512,2]{2,1,3,0:T(8,128)} copy-done((f32[4,512,512,2]{2,1,3,0:T(8,128)}, f32[4,512,512,2]{2,1,3,0:T(8,128)S(1)}, u32[]{:S(2)}) %copy-start.2) | copy-done | bytes 8388632
  160.3 1.8 fusion.3
  163.7 14.1 %collective-permute-done.7 = bf16[256,4,128]{0,2,1:T(8,128)(2,1)} collective-permute-done((bf16[256,4,128]{0,2,1:T(8,128)(2,1)S(1)}, bf16[256,4,128]{0,2,1:T(8,128)(2,1)}, u32[]{:S(2)}, u32[]{:S(2)}) %collective-permute-start.7) | collective-permute-done | bytes 262176 | tf_op jit(solution)/shard_map/ppermute | solution.py:18
  179.1 1.8 copy.97
  183.9 1.7 constant_dynamic-update-slice_fusion.1
  186.5 1.7 constant_dynamic-update-slice_fusion.5
  188.2 1.8 copy.106
  190.0 1.8 copy.98
  191.8 1.8 constant_dynamic-update-slice_fusion
  193.6 1.8 constant_dynamic-update-slice_fusion.4
  201.6 1.9 fusion.40
  204.6 2.5 fusion.31
  208.5 50.0 %reduce-scatter.2.cloned.1.call-done = bf16[1024,1024]{1,0:T(8,128)(2,1)} async-done(((bf16[4096,1024]{1,0:T(8,128)(2,1)}), bf16[1024,1024]{1,0:T(8,128)(2,1)}) %reduce-scatter.2.cloned.1.call-update) | async-done | bytes 2097168 | tf_op jit(solution)/shard_map/reduce_scatter | solution.py:158
  258.5 4.1 %convert_element_type.67 = f32[1024,1024]{1,0:T(8,128)} convert(bf16[1024,1024]{1,0:T(8,128)(2,1)} %reduce-scatter.2.cloned.1.call-done) | non-fusion elementwise | flops 1048576 | bytes 6291456 | tf_op jit(solution)/shard_map/convert_element_type | solution.py:166
  (95 shorter events, 32.9 us)
Async XLA Ops:
  7.2 38.2 %all-gather.3.cloned.1.call-start = ((), (), s32[]{:S(2)}) async-start(), calls=%async_computation.2 | async-start | bytes 3145728 | tf_op jit(solution)/shard_map/all_gather | solution.py:63
  7.9 250.6 %reduce-scatter.2.cloned.1.call-start = ((), (), s32[]{:S(2)}) async-start(), calls=%async_computation.1 | async-start | bytes 10485760 | tf_op jit(solution)/shard_map/reduce_scatter | solution.py:158
  45.4 4.5 %collective-permute-start = (bf16[2,512,1024]{2,1,0:T(8,128)(2,1)}, bf16[2,512,1024]{2,1,0:T(8,128)(2,1)}, u32[]{:S(2)}, u32[]{:S(2)}) collective-permute-start(bf16[2,512,1024]{2,1,0:T(8,128)(2,1)} %bitcast.179), channel_id=1, source_target_pairs={{0,1},{1,0},{2,3},{3,2},{4,5},{5,4},{6,7},{7,6},{8,9},{9,8},{10,11... | collective-permute-start | bytes 6291464 | tf_op jit(solution)/shard_map/ppermute | solution.py:26
  52.4 1.3 copy-start
  65.9 11.8 %copy-start.8 = (f32[4096]{0:T(1024)S(1)}, f32[4096]{0:T(1024)}, u32[]{:S(2)}) copy-start(f32[4096]{0:T(1024)} %param.7) | copy-start | bytes 49156
  82.4 2.0 copy-start.3
  91.4 8.3 %copy-start.9 = (s32[3,8]{1,0:T(4,128)S(1)}, s32[3,8]{1,0:T(4,128)}, u32[]{:S(2)}) copy-start(s32[3,8]{1,0:T(4,128)} %param.11) | copy-start | bytes 292
  94.7 29.3 %collective-permute-start.1 = (bf16[2048,4,128]{2,0,1:T(8,128)(2,1)}, bf16[2048,4,128]{2,0,1:T(8,128)(2,1)}, u32[]{:S(2)}, u32[]{:S(2)}) collective-permute-start(bf16[2048,4,128]{2,0,1:T(8,128)(2,1)} %copy.85), channel_id=1, source_target_pairs={{0,1},{1,0},{2,3},{3,2},{4,5},{5,4},{6,7},{7,6},{8,9},{9,8},{10,11... | collective-permute-start | bytes 6291464 | tf_op jit(solution)/shard_map/ppermute | solution.py:98
  99.3 33.7 %collective-permute-start.2 = (bf16[2048,4,128]{0,2,1:T(8,128)(2,1)}, bf16[2048,4,128]{0,2,1:T(8,128)(2,1)}, u32[]{:S(2)}, u32[]{:S(2)}) collective-permute-start(bf16[2048,4,128]{0,2,1:T(8,128)(2,1)} %copy.87), channel_id=1, source_target_pairs={{0,1},{1,0},{2,3},{3,2},{4,5},{5,4},{6,7},{7,6},{8,9},{9,8},{10,11... | collective-permute-start | bytes 6291464 | tf_op jit(solution)/shard_map/ppermute | solution.py:98
  120.4 3.7 %copy-start.4 = (bf16[512,4096]{1,0:T(8,128)(2,1)S(1)}, bf16[512,4096]{1,0:T(8,128)(2,1)}, u32[]{:S(2)}) copy-start(bf16[512,4096]{1,0:T(8,128)(2,1)} %copy-done.3) | copy-start | bytes 12582916
  124.0 7.7 %copy-start.5 = (bf16[2048,4,128]{0,2,1:T(8,128)(2,1)S(1)}, bf16[2048,4,128]{0,2,1:T(8,128)(2,1)}, u32[]{:S(2)}) copy-start(bf16[2048,4,128]{0,2,1:T(8,128)(2,1)} %copy.87) | copy-start | bytes 6291460
  127.1 9.0 %copy-start.6 = (bf16[512,4,128]{2,0,1:T(8,128)(2,1)}, bf16[512,4,128]{2,0,1:T(8,128)(2,1)S(1)}, u32[]{:S(2)}) copy-start(bf16[512,4,128]{2,0,1:T(8,128)(2,1)S(1)} %fusion.49) | copy-start | bytes 1572868
  127.9 53.4 %collective-permute-start.9 = (bf16[256,4,128]{2,0,1:T(8,128)(2,1)}, bf16[256,4,128]{2,0,1:T(8,128)(2,1)}, u32[]{:S(2)}, u32[]{:S(2)}) collective-permute-start(bf16[256,4,128]{2,0,1:T(8,128)(2,1)} %constant_dynamic-slice_fusion.1), channel_id=1, source_target_pairs={{0,8},{8,0},{4,12},{12,4},{1,9},{9,1},{5,13},{13,5},{2,10},{10,2},... | collective-permute-start | bytes 786440 | tf_op jit(solution)/shard_map/ppermute | solution.py:18
  130.3 52.4 %collective-permute-start.5 = (bf16[256,4,128]{2,0,1:T(8,128)(2,1)}, bf16[256,4,128]{2,0,1:T(8,128)(2,1)}, u32[]{:S(2)}, u32[]{:S(2)}) collective-permute-start(bf16[256,4,128]{2,0,1:T(8,128)(2,1)} %constant_dynamic-slice_fusion.1), channel_id=1, source_target_pairs={{0,4},{4,0},{8,12},{12,8},{1,5},{5,1},{9,13},{13,9},{2,6},{6,2},{1... | collective-permute-start | bytes 786440 | tf_op jit(solution)/shard_map/ppermute | solution.py:18
  136.0 1.6 copy-start.1
  136.5 41.3 %collective-permute-start.7 = (bf16[256,4,128]{0,2,1:T(8,128)(2,1)S(1)}, bf16[256,4,128]{0,2,1:T(8,128)(2,1)}, u32[]{:S(2)}, u32[]{:S(2)}) collective-permute-start(bf16[256,4,128]{0,2,1:T(8,128)(2,1)S(1)} %fusion.64), channel_id=1, source_target_pairs={{0,8},{8,0},{4,12},{12,4},{1,9},{9,1},{5,13},{13,5},{2,10},{10,2},... | collective-permute-start | bytes 786440 | tf_op jit(solution)/shard_map/ppermute | solution.py:18
  137.1 42.0 %collective-permute-start.3 = (bf16[256,4,128]{0,2,1:T(8,128)(2,1)S(1)}, bf16[256,4,128]{0,2,1:T(8,128)(2,1)}, u32[]{:S(2)}, u32[]{:S(2)}) collective-permute-start(bf16[256,4,128]{0,2,1:T(8,128)(2,1)S(1)} %fusion.64), channel_id=1, source_target_pairs={{0,4},{4,0},{8,12},{12,8},{1,5},{5,1},{9,13},{13,9},{2,6},{6,2},{1... | collective-permute-start | bytes 786440 | tf_op jit(solution)/shard_map/ppermute | solution.py:18
  157.0 3.2 %copy-start.2 = (f32[4,512,512,2]{2,1,3,0:T(8,128)}, f32[4,512,512,2]{2,1,3,0:T(8,128)S(1)}, u32[]{:S(2)}) copy-start(f32[4,512,512,2]{2,1,3,0:T(8,128)S(1)} %get-tuple-element.39) | copy-start | bytes 25165828
  178.9 9.3 %collective-permute-start.8 = (bf16[256,4,128]{0,2,1:T(8,128)(2,1)}, bf16[256,4,128]{0,2,1:T(8,128)(2,1)}, u32[]{:S(2)}, u32[]{:S(2)}) collective-permute-start(bf16[256,4,128]{0,2,1:T(8,128)(2,1)} %collective-permute-done.7), channel_id=1, source_target_pairs={{0,1},{1,0},{2,3},{3,2},{4,5},{5,4},{6,7},{7,6},{8,9},{9,8},{10,11... | collective-permute-start | bytes 786440 | tf_op jit(solution)/shard_map/ppermute | solution.py:26
  180.9 9.1 %collective-permute-start.4 = (bf16[256,4,128]{0,2,1:T(8,128)(2,1)}, bf16[256,4,128]{0,2,1:T(8,128)(2,1)}, u32[]{:S(2)}, u32[]{:S(2)}) collective-permute-start(bf16[256,4,128]{0,2,1:T(8,128)(2,1)} %collective-permute-done.3), channel_id=1, source_target_pairs={{0,1},{1,0},{2,3},{3,2},{4,5},{5,4},{6,7},{7,6},{8,9},{9,8},{10,11... | collective-permute-start | bytes 786440 | tf_op jit(solution)/shard_map/ppermute | solution.py:26
  181.3 10.5 %collective-permute-start.10 = (bf16[256,4,128]{2,0,1:T(8,128)(2,1)}, bf16[256,4,128]{2,0,1:T(8,128)(2,1)}, u32[]{:S(2)}, u32[]{:S(2)}) collective-permute-start(bf16[256,4,128]{2,0,1:T(8,128)(2,1)} %collective-permute-done.9), channel_id=1, source_target_pairs={{0,1},{1,0},{2,3},{3,2},{4,5},{5,4},{6,7},{7,6},{8,9},{9,8},{10,11... | collective-permute-start | bytes 786440 | tf_op jit(solution)/shard_map/ppermute | solution.py:26
  182.6 11.0 %collective-permute-start.6 = (bf16[256,4,128]{2,0,1:T(8,128)(2,1)}, bf16[256,4,128]{2,0,1:T(8,128)(2,1)}, u32[]{:S(2)}, u32[]{:S(2)}) collective-permute-start(bf16[256,4,128]{2,0,1:T(8,128)(2,1)} %collective-permute-done.5), channel_id=1, source_target_pairs={{0,1},{1,0},{2,3},{3,2},{4,5},{5,4},{6,7},{7,6},{8,9},{9,8},{10,11... | collective-permute-start | bytes 786440 | tf_op jit(solution)/shard_map/ppermute | solution.py:26
  200.6 3.2 %slice-start = ((s8[8388608]{0:T(1024)(128)(4,1)}), s8[4194304]{0:T(1024)(128)(4,1)S(1)}, s32[]{:S(2)}) async-start(s8[8388608]{0:T(1024)(128)(4,1)} %bitcast.173), calls=%async_computation.3 | async-start | bytes 8388608
  201.6 3.0 %slice-start.1 = ((s8[8388608]{0:T(1024)(128)(4,1)}), s8[4194304]{0:T(1024)(128)(4,1)S(1)}, s32[]{:S(2)}) async-start(s8[8388608]{0:T(1024)(128)(4,1)} %bitcast.173), calls=%async_computation.4 | async-start | bytes 8388608
  201.6 3.0 %copy-start.7 = (bf16[512,4,128]{2,0,1:T(8,128)(2,1)S(1)}, bf16[512,4,128]{2,0,1:T(8,128)(2,1)}, u32[]{:S(2)}) copy-start(bf16[512,4,128]{2,0,1:T(8,128)(2,1)} %copy-done.6) | copy-start | bytes 1572868
Sparse Core Ops, SparseCore 0:
  9.5 35.8 all-gather.2
  91.6 166.9 reduce-scatter.1

commit v2 on v0

--- a/solution.py
+++ b/solution.py
@@ -60,7 +60,23 @@
 
 
 def body(tokens, norm_gain, w_query, w_key, w_value, links):
-    gathered = lax.all_gather(tokens, ("kvh", "sub"), axis=1, tiled=True)
+    kvh_total = lax.axis_size("kvh")
+    kvh_at = lax.axis_index("kvh")
+    sub_total = lax.axis_size("sub")
+    lane_index = lax.axis_index("sub")
+    across = [tokens]
+    for shift in range(1, kvh_total):
+        route = [(j, (j + shift) % kvh_total) for j in range(kvh_total)]
+        across.append(lax.ppermute(tokens, "kvh", route))
+    pieces = []
+    for shift in range(kvh_total):
+        pieces.extend(swap_halves(across[shift], sub_total, lane_index))
+    blocks = []
+    for owner_kvh in range(kvh_total):
+        for owner_sub in range(sub_total):
+            pick = ((kvh_at - owner_kvh) % kvh_total) * sub_total + (lane_index - owner_sub) % sub_total
+            blocks.append(lax.select_n(pick, *pieces))
+    gathered = jnp.concatenate(blocks, axis=1)
     widened = gathered.astype(jnp.float32)
     mean_square = jnp.mean(widened * widened, axis=-1, keepdims=True)
     normed = (widened * lax.rsqrt(mean_square + 1e-05) * norm_gain).astype(jnp.bfloat16)

time: 239 us -> 229 us (0.958)
  waiting for transfers between devices: 127 us -> 116 us
  starting transfers between devices: 6.64 us -> 9.69 us
    all_gather x1 -> x0, waiting for transfers between devices: 38.8 us -> none  [body(): gathered = lax.all_gather(tokens, ('kvh', 'sub'), axis=1, tiled=True)]
    ppermute x0 -> x1, waiting for transfers between devices: none -> 23.4 us  [body(): across.append(lax.ppermute(tokens, 'kvh', route))]
    ppermute x0 -> x1, starting transfers between devices: none -> 3.03 us  [body(): across.append(lax.ppermute(tokens, 'kvh', route))]
    ppermute x4 -> x6, waiting for transfers between devices: 0.01 us -> 2.67 us  [swap_halves(): whole[shift] = lax.ppermute(pieces, 'sub', route)]
    unnamed x35 -> x37, local copies, waits for them, and re-layouts: 17.3 us -> 17 us
  transfers between devices with their start and end apart: 12 -> 14, of which waited for: 3 -> 4; matrix products, arithmetic and copies ran while one was open for 29% -> 30% of each run, Pallas kernels for 0% -> 0%
where the time goes in v2:
time: 229 us
  waiting for transfers between devices  116 us (51%)
  local copies, waits for them, and re-layouts  34.9 us (15%)
  matrix products  32.6 us (14%)
  other arithmetic  21 us (9%)
  between operations  14.4 us (6%)
  starting transfers between devices  9.69 us (4%)
    reduce_scatter x1, waiting for transfers between devices, body(): lax.psum_scatter((jnp.einsum('tc,tr->cr', normed, owned, preferred_elemen...  69.6 us
    ppermute x1, waiting for transfers between devices, body(): across.append(lax.ppermute(tokens, 'kvh', route))  23.4 us
    ppermute x4, waiting for transfers between devices, from_partner(): return lax.ppermute(block, axis, route)  20.4 us
    unnamed x37, local copies, waits for them, and re-layouts  17 us
    dot_general x1, matrix products, body(): jnp.einsum('td,dgc->tgc', normed, w_query, preferred_element_type=jnp.flo...  7.24 us
    dot_general x1, matrix products, body(): jnp.einsum('tc,tr->cr', normed, owned, preferred_element_type=jnp.float32)  7 us
    dynamic_update_slice x6, local copies, waits for them, and re-layouts, split_send(): lax.dynamic_update_slice_in_dim(full, whole[shift][n], source * share, 0)  6.85 us
    ppermute x4, starting transfers between devices, from_partner(): return lax.ppermute(block, axis, route)  4.95 us
  transfers between devices with their start and end apart: 14, of which 4 were waited for; matrix products, arithmetic and copies ran while one was open for 30% of the time, Pallas kernels for 0%

profile of v2, /device:TPU:0, one launch (start us, length us, event | category | flops | bytes accessed | tf_op | source)
XLA Modules:
  0.0 228.7 jit_solution(6640550967098099929)
XLA Ops:
  7.2 3.0 %collective-permute-start.1 = (bf16[512,1024]{1,0:T(8,128)(2,1)}, bf16[512,1024]{1,0:T(8,128)(2,1)S(1)}, u32[]{:S(2)}, u32[]{:S(2)}) collective-permute-start(bf16[512,1024]{1,0:T(8,128)(2,1)} %param.6), channel_id=1, source_target_pairs={{0,2},{2,0},{1,3},{3,1},{4,6},{6,4},{5,7},{7,5},{8,10},{10,8},{9,1... | collective-permute-start | bytes 3145736 | tf_op jit(solution)/shard_map/ppermute | solution.py:70
  10.2 23.4 %collective-permute-done.1 = bf16[512,1024]{1,0:T(8,128)(2,1)S(1)} collective-permute-done((bf16[512,1024]{1,0:T(8,128)(2,1)}, bf16[512,1024]{1,0:T(8,128)(2,1)S(1)}, u32[]{:S(2)}, u32[]{:S(2)}) %collective-permute-start.1) | collective-permute-done | bytes 1048608 | tf_op jit(solution)/shard_map/ppermute | solution.py:70
  33.6 2.7 %collective-permute-done.2 = bf16[512,1024]{1,0:T(8,128)(2,1)S(1)} collective-permute-done((bf16[512,1024]{1,0:T(8,128)(2,1)S(1)}, bf16[512,1024]{1,0:T(8,128)(2,1)S(1)}, u32[]{:S(2)}, u32[]{:S(2)}) %collective-permute-start.2) | collective-permute-done | bytes 1048608 | tf_op jit(solution)/shard_map/ppermute | solution.py:26
  36.3 1.5 select_select_fusion.3
  40.2 2.0 copy-done.1
  42.2 7.0 %multiply_convert_fusion = bf16[4096,1024]{1,0:T(8,128)(2,1)} fusion(bf16[512,4096]{1,0:T(8,128)(2,1)S(1)} %fusion.2, s32[]{:T(128)S(6)} %select_n.293), kind=kOutput, calls=%fused_computation | convolution fusion | flops 4303355904 | bytes 13631492 | tf_op jit(solution)/shard_map/tc,tr->cr/dot_general | solution.py:168
  49.3 3.4 %copy.58 = bf16[2048,4,128]{2,0,1:T(8,128)(2,1)} copy(bf16[2048,4,128]{2,1,0:T(4,128)(2,1)} %param.10) | data formatting | bytes 4194304 | tf_op args[4]
  52.8 2.7 %copy.60 = bf16[2048,4,128]{0,2,1:T(8,128)(2,1)} copy(bf16[2048,4,128]{2,1,0:T(4,128)(2,1)S(1)} %copy-done.6) | data formatting | bytes 4194304 | tf_op args[3]
  62.1 1.7 select_reduce_fusion
  64.1 3.5 %fusion.29 = f32[512,4,128]{2,0,1:T(8,128)S(1)} fusion(bf16[2048,4,128]{2,0,1:T(8,128)(2,1)} %collective-permute-done.3, bf16[512,4096]{1,0:T(8,128)(2,1)} %copy-done.1, s32[]{:T(128)S(6)} %select_n.282), kind=kOutput, calls=%fused_computation.41 | convolution fusion | flops 1073741824 | bytes 5242884 | tf_op jit(solution)/shard_map/td,dgh->tgh/dot_general | solution.py:110
  69.7 2.9 %collective-permute-start.11 = (bf16[256,4,128]{2,0,1:T(8,128)(2,1)}, bf16[256,4,128]{2,0,1:T(8,128)(2,1)}, u32[]{:S(2)}, u32[]{:S(2)}) collective-permute-start(bf16[256,4,128]{2,0,1:T(8,128)(2,1)} %constant_dynamic-slice_fusion.1), channel_id=1, source_target_pairs={{0,8},{8,0},{4,12},{12,4},{1,9},{9,1},{5,13},{13,5},{2,10},{10,2},... | collective-permute-start | bytes 786440 | tf_op jit(solution)/shard_map/ppermute | solution.py:18
  72.6 1.6 collective-permute-start.7
  75.5 2.9 %fusion.34 = f32[512,512]{0,1:S(1)} fusion(bf16[2048,512]{0,1:T(8,128)(2,1)} %bitcast.8, bf16[512,4096]{1,0:T(8,128)(2,1)S(1)} %copy-done.2, s32[]{:T(128)S(6)} %select_n.282), kind=kOutput, calls=%fused_computation.48 | convolution fusion | flops 1073741824 | bytes 5242884
  80.0 7.2 %fusion.3 = f32[512,4,256]{0,2,1:T(8,128)S(1)} fusion(bf16[4096,4,256]{2,1,0:T(4,128)(2,1)} %param.8, bf16[512,4096]{1,0:T(8,128)(2,1)S(1)} %copy-done.2), kind=kOutput, calls=%fused_computation.7 | convolution fusion | flops 4294967296 | bytes 14680064 | tf_op jit(solution)/shard_map/td,dgc->tgc/dot_general | solution.py:92
  87.4 1.9 copy.105
  89.4 2.0 copy.104
  91.4 2.8 %subtract_convert_fusion = (bf16[512,4,2,64]{3,0,2,1:T(8,128)(2,1)S(1)}, bf16[512,4,2,64]{3,0,2,1:T(8,128)(2,1)S(1)}) fusion(f32[512,4,2,64]{3,0,2,1:T(8,128)} %copy.105, f32[512,4,2,64]{3,0,2,1:T(8,128)} %copy.104, f32[512,64]{1,0:T(8,128)S(1)} %copy-done.9, f32[512,64]{1,0:T(8,128)S(1)} %copy.64), kind=kLoop, calls=%fused_computation.46 | loop fusion | flops 2097152 | bytes 3407872 | tf_op jit(solution)/shard_map/convert.4
  94.2 2.3 %fusion.7 = (f32[4,2,512]{2,1,0:T(2,128)S(1)}, f32[4,512,512,2]{2,1,3,0:T(8,128)S(1)}) fusion(pred[512,512]{0,1:T(8,128)(4,1)S(1)} %fusion.59, bf16[512,4,2,64]{3,0,2,1:T(8,128)(2,1)S(1)} %get-tuple-element.14, bf16[512,4,2,64]{3,0,2,1:T(8,128)(2,1)S(1)} %get-tuple-element.13, bf16[512,4,64]{0,2,1:T(8,128)(2,1)S(1)} %get-tuple-element.25, ...), kind=kOutput, calls=%fused_computation.12 | convolution fusion | flops 546304000 | bytes 10240000 | tf_op jit(solution)/shard_map/tgrh,ugh->grtu/dot_general | solution.py:118
  96.5 1.8 fusion.5
  98.3 1.5 copy-done
  99.7 20.4 %collective-permute-done.9 = bf16[256,4,128]{0,2,1:T(8,128)(2,1)} collective-permute-done((bf16[256,4,128]{0,2,1:T(8,128)(2,1)}, bf16[256,4,128]{0,2,1:T(8,128)(2,1)}, u32[]{:S(2)}, u32[]{:S(2)}) %collective-permute-start.9) | collective-permute-done | bytes 262176 | tf_op jit(solution)/shard_map/ppermute | solution.py:18
  121.5 1.8 copy.70
  128.0 1.8 copy.79
  129.7 1.8 copy.71
  131.5 1.8 constant_dynamic-update-slice_fusion
  133.4 1.9 constant_dynamic-update-slice_fusion.4
  135.3 2.2 bitcast_reduce_fusion.1
  142.8 1.5 slice-done.1
  144.3 2.5 %fusion.33 = bf16[512,4,2,128]{0,3,2,1:T(8,128)(2,1)S(1)} fusion(f32[512,4,2,128]{0,3,2,1:T(8,128)S(1)} %bitcast.166, f32[512,4,2,128]{0,3,2,1:T(8,128)S(1)} %bitcast.165, f32[4,512,512,2]{2,1,3,0:T(8,128)S(1)} %bitcast.159, f32[4,2,512]{2,1,0:T(2,128)S(1)} %get-tuple-element.40, pred[512,512]{0,1:T(8,128)(4,1)S(1)} %fusion.59, ...), kind=kOutput, calls=%fused_computation.47 | convolution fusion | flops 548405248 | bytes 14483456 | tf_op jit(solution)/shard_map/grtu,ugh->tgrh/dot_general | solution.py:128
  146.8 1.4 copy.83
  148.2 69.6 %reduce-scatter.2.cloned.1.call-done = bf16[1024,1024]{1,0:T(8,128)(2,1)} async-done(((bf16[4096,1024]{1,0:T(8,128)(2,1)}), bf16[1024,1024]{1,0:T(8,128)(2,1)}) %reduce-scatter.2.cloned.1.call-update) | async-done | bytes 2097168 | tf_op jit(solution)/shard_map/reduce_scatter | solution.py:166
  217.8 4.1 %convert_element_type.49 = f32[1024,1024]{1,0:T(8,128)} convert(bf16[1024,1024]{1,0:T(8,128)(2,1)} %reduce-scatter.2.cloned.1.call-done) | non-fusion elementwise | flops 1048576 | bytes 6291456 | tf_op jit(solution)/shard_map/convert_element_type | solution.py:174
  (97 shorter events, 25.9 us)
Async XLA Ops:
  7.2 210.6 %reduce-scatter.2.cloned.1.call-start = ((), (), s32[]{:S(2)}) async-start(), calls=%async_computation.1 | async-start | bytes 10485760 | tf_op jit(solution)/shard_map/reduce_scatter | solution.py:166
  7.2 26.4 %collective-permute-start.1 = (bf16[512,1024]{1,0:T(8,128)(2,1)}, bf16[512,1024]{1,0:T(8,128)(2,1)S(1)}, u32[]{:S(2)}, u32[]{:S(2)}) collective-permute-start(bf16[512,1024]{1,0:T(8,128)(2,1)} %param.6), channel_id=1, source_target_pairs={{0,2},{2,0},{1,3},{3,1},{4,6},{6,4},{5,7},{7,5},{8,10},{10,8},{9,1... | collective-permute-start | bytes 3145736 | tf_op jit(solution)/shard_map/ppermute | solution.py:70
  10.2 23.4 %collective-permute-start = (bf16[512,1024]{1,0:T(8,128)(2,1)}, bf16[512,1024]{1,0:T(8,128)(2,1)S(1)}, u32[]{:S(2)}, u32[]{:S(2)}) collective-permute-start(bf16[512,1024]{1,0:T(8,128)(2,1)} %param.6), channel_id=1, source_target_pairs={{0,1},{1,0},{2,3},{3,2},{4,5},{5,4},{6,7},{7,6},{8,9},{9,8},{10,11... | collective-permute-start | bytes 3145736 | tf_op jit(solution)/shard_map/ppermute | solution.py:26
  33.6 2.7 %collective-permute-start.2 = (bf16[512,1024]{1,0:T(8,128)(2,1)S(1)}, bf16[512,1024]{1,0:T(8,128)(2,1)S(1)}, u32[]{:S(2)}, u32[]{:S(2)}) collective-permute-start(bf16[512,1024]{1,0:T(8,128)(2,1)S(1)} %collective-permute-done.1), channel_id=1, source_target_pairs={{0,1},{1,0},{2,3},{3,2},{4,5},{5,4},{6,7},{7,6},{8,9},{9,8},{10,11... | collective-permute-start | bytes 3145736 | tf_op jit(solution)/shard_map/ppermute | solution.py:26
  37.8 1.0 copy-start.12
  40.2 2.0 copy-start.1
  49.2 3.5 %copy-start.6 = (bf16[2048,4,128]{2,1,0:T(4,128)(2,1)S(1)}, bf16[2048,4,128]{2,1,0:T(4,128)(2,1)}, u32[]{:S(2)}) copy-start(bf16[2048,4,128]{2,1,0:T(4,128)(2,1)} %param.9) | copy-start | bytes 6291460
  49.3 6.6 %copy-start.13 = (s32[3,8]{1,0:T(4,128)S(1)}, s32[3,8]{1,0:T(4,128)}, u32[]{:S(2)}) copy-start(s32[3,8]{1,0:T(4,128)} %param.11) | copy-start | bytes 292
  52.6 11.5 %collective-permute-start.3 = (bf16[2048,4,128]{2,0,1:T(8,128)(2,1)}, bf16[2048,4,128]{2,0,1:T(8,128)(2,1)}, u32[]{:S(2)}, u32[]{:S(2)}) collective-permute-start(bf16[2048,4,128]{2,0,1:T(8,128)(2,1)} %copy.58), channel_id=1, source_target_pairs={{0,1},{1,0},{2,3},{3,2},{4,5},{5,4},{6,7},{7,6},{8,9},{9,8},{10,11... | collective-permute-start | bytes 6291464 | tf_op jit(solution)/shard_map/ppermute | solution.py:106
  55.5 20.0 %collective-permute-start.4 = (bf16[2048,4,128]{0,2,1:T(8,128)(2,1)}, bf16[2048,4,128]{0,2,1:T(8,128)(2,1)}, u32[]{:S(2)}, u32[]{:S(2)}) collective-permute-start(bf16[2048,4,128]{0,2,1:T(8,128)(2,1)} %copy.60), channel_id=1, source_target_pairs={{0,1},{1,0},{2,3},{3,2},{4,5},{5,4},{6,7},{7,6},{8,9},{9,8},{10,11... | collective-permute-start | bytes 6291464 | tf_op jit(solution)/shard_map/ppermute | solution.py:106
  60.6 7.0 %copy-start.7 = (bf16[2048,4,128]{2,1,0:T(4,128)(2,1)S(1)}, bf16[2048,4,128]{2,1,0:T(4,128)(2,1)}, u32[]{:S(2)}) copy-start(bf16[2048,4,128]{2,1,0:T(4,128)(2,1)} %param.10) | copy-start | bytes 6291460
  61.4 6.2 %copy-start.2 = (bf16[512,4096]{1,0:T(8,128)(2,1)S(1)}, bf16[512,4096]{1,0:T(8,128)(2,1)}, u32[]{:S(2)}) copy-start(bf16[512,4096]{1,0:T(8,128)(2,1)} %copy-done.1) | copy-start | bytes 12582916
  67.6 6.6 %copy-start.8 = (bf16[2048,4,128]{0,2,1:T(8,128)(2,1)S(1)}, bf16[2048,4,128]{0,2,1:T(8,128)(2,1)}, u32[]{:S(2)}) copy-start(bf16[2048,4,128]{0,2,1:T(8,128)(2,1)} %copy.60) | copy-start | bytes 6291460
  68.9 9.5 %copy-start.10 = (bf16[512,4,128]{2,0,1:T(8,128)(2,1)}, bf16[512,4,128]{2,0,1:T(8,128)(2,1)S(1)}, u32[]{:S(2)}) copy-start(bf16[512,4,128]{2,0,1:T(8,128)(2,1)S(1)} %fusion.51) | copy-start | bytes 1572868
  69.7 54.0 %collective-permute-start.11 = (bf16[256,4,128]{2,0,1:T(8,128)(2,1)}, bf16[256,4,128]{2,0,1:T(8,128)(2,1)}, u32[]{:S(2)}, u32[]{:S(2)}) collective-permute-start(bf16[256,4,128]{2,0,1:T(8,128)(2,1)} %constant_dynamic-slice_fusion.1), channel_id=1, source_target_pairs={{0,8},{8,0},{4,12},{12,4},{1,9},{9,1},{5,13},{13,5},{2,10},{10,2},... | collective-permute-start | bytes 786440 | tf_op jit(solution)/shard_map/ppermute | solution.py:18
  72.6 52.4 %collective-permute-start.7 = (bf16[256,4,128]{2,0,1:T(8,128)(2,1)}, bf16[256,4,128]{2,0,1:T(8,128)(2,1)}, u32[]{:S(2)}, u32[]{:S(2)}) collective-permute-start(bf16[256,4,128]{2,0,1:T(8,128)(2,1)} %constant_dynamic-slice_fusion.1), channel_id=1, source_target_pairs={{0,4},{4,0},{8,12},{12,8},{1,5},{5,1},{9,13},{13,9},{2,6},{6,2},{1... | collective-permute-start | bytes 786440 | tf_op jit(solution)/shard_map/ppermute | solution.py:18
  79.5 40.6 %collective-permute-start.9 = (bf16[256,4,128]{0,2,1:T(8,128)(2,1)}, bf16[256,4,128]{0,2,1:T(8,128)(2,1)}, u32[]{:S(2)}, u32[]{:S(2)}) collective-permute-start(bf16[256,4,128]{0,2,1:T(8,128)(2,1)} %fusion.70), channel_id=1, source_target_pairs={{0,8},{8,0},{4,12},{12,4},{1,9},{9,1},{5,13},{13,5},{2,10},{10,2},... | collective-permute-start | bytes 786440 | tf_op jit(solution)/shard_map/ppermute | solution.py:18
  79.8 41.7 %collective-permute-start.5 = (bf16[256,4,128]{0,2,1:T(8,128)(2,1)}, bf16[256,4,128]{0,2,1:T(8,128)(2,1)}, u32[]{:S(2)}, u32[]{:S(2)}) collective-permute-start(bf16[256,4,128]{0,2,1:T(8,128)(2,1)} %fusion.70), channel_id=1, source_target_pairs={{0,4},{4,0},{8,12},{12,8},{1,5},{5,1},{9,13},{13,9},{2,6},{6,2},{1... | collective-permute-start | bytes 786440 | tf_op jit(solution)/shard_map/ppermute | solution.py:18
  87.4 3.9 %copy-start.9 = (f32[512,64]{1,0:T(8,128)S(1)}, f32[512,64]{1,0:T(8,128)}, u32[]{:S(2)}) copy-start(f32[512,64]{1,0:T(8,128)} %copy.66) | copy-start | bytes 393220
  96.5 3.2 %copy-start = (f32[4,512,512,2]{2,1,3,0:T(8,128)}, f32[4,512,512,2]{2,1,3,0:T(8,128)S(1)}, u32[]{:S(2)}) copy-start(f32[4,512,512,2]{2,1,3,0:T(8,128)S(1)} %get-tuple-element.41) | copy-start | bytes 25165828
  121.3 6.7 %collective-permute-start.10 = (bf16[256,4,128]{0,2,1:T(8,128)(2,1)}, bf16[256,4,128]{0,2,1:T(8,128)(2,1)}, u32[]{:S(2)}, u32[]{:S(2)}) collective-permute-start(bf16[256,4,128]{0,2,1:T(8,128)(2,1)} %collective-permute-done.9), channel_id=1, source_target_pairs={{0,1},{1,0},{2,3},{3,2},{4,5},{5,4},{6,7},{7,6},{8,9},{9,8},{10,11... | collective-permute-start | bytes 786440 | tf_op jit(solution)/shard_map/ppermute | solution.py:26
  123.2 6.5 %collective-permute-start.6 = (bf16[256,4,128]{0,2,1:T(8,128)(2,1)}, bf16[256,4,128]{0,2,1:T(8,128)(2,1)}, u32[]{:S(2)}, u32[]{:S(2)}) collective-permute-start(bf16[256,4,128]{0,2,1:T(8,128)(2,1)} %collective-permute-done.5), channel_id=1, source_target_pairs={{0,1},{1,0},{2,3},{3,2},{4,5},{5,4},{6,7},{7,6},{8,9},{9,8},{10,11... | collective-permute-start | bytes 786440 | tf_op jit(solution)/shard_map/ppermute | solution.py:26
  123.7 7.9 %collective-permute-start.12 = (bf16[256,4,128]{2,0,1:T(8,128)(2,1)}, bf16[256,4,128]{2,0,1:T(8,128)(2,1)}, u32[]{:S(2)}, u32[]{:S(2)}) collective-permute-start(bf16[256,4,128]{2,0,1:T(8,128)(2,1)} %collective-permute-done.11), channel_id=1, source_target_pairs={{0,1},{1,0},{2,3},{3,2},{4,5},{5,4},{6,7},{7,6},{8,9},{9,8},{10,11... | collective-permute-start | bytes 786440 | tf_op jit(solution)/shard_map/ppermute | solution.py:26
  125.0 0.8 copy-start.3
  125.0 8.4 %collective-permute-start.8 = (bf16[256,4,128]{2,0,1:T(8,128)(2,1)}, bf16[256,4,128]{2,0,1:T(8,128)(2,1)}, u32[]{:S(2)}, u32[]{:S(2)}) collective-permute-start(bf16[256,4,128]{2,0,1:T(8,128)(2,1)} %collective-permute-done.7), channel_id=1, source_target_pairs={{0,1},{1,0},{2,3},{3,2},{4,5},{5,4},{6,7},{7,6},{8,9},{9,8},{10,11... | collective-permute-start | bytes 786440 | tf_op jit(solution)/shard_map/ppermute | solution.py:26
  126.7 1.2 copy-start.4
  140.4 1.1 copy-start.5
  140.5 2.4 %slice-start = ((s8[8388608]{0:T(1024)(128)(4,1)}), s8[4194304]{0:T(1024)(128)(4,1)S(1)}, s32[]{:S(2)}) async-start(s8[8388608]{0:T(1024)(128)(4,1)} %bitcast.158), calls=%async_computation.2 | async-start | bytes 8388608
  141.5 2.8 %slice-start.1 = ((s8[8388608]{0:T(1024)(128)(4,1)}), s8[4194304]{0:T(1024)(128)(4,1)S(1)}, s32[]{:S(2)}) async-start(s8[8388608]{0:T(1024)(128)(4,1)} %bitcast.158), calls=%async_computation.3 | async-start | bytes 8388608
  141.5 2.8 %copy-start.11 = (bf16[512,4,128]{2,0,1:T(8,128)(2,1)S(1)}, bf16[512,4,128]{2,0,1:T(8,128)(2,1)}, u32[]{:S(2)}) copy-start(bf16[512,4,128]{2,0,1:T(8,128)(2,1)} %copy-done.10) | copy-start | bytes 1572868
Sparse Core Ops, SparseCore 0:
  49.4 168.3 reduce-scatter.1

commit v3 on v2

--- a/solution.py
+++ b/solution.py
@@ -162,16 +162,33 @@
     owner_index = lax.axis_index("kvh") * lax.axis_size("sub") + lax.axis_index("sub")
     owned = lax.dynamic_slice_in_dim(normed, owner_index * tile_cols, tile_cols, 1)
     seq_count = lax.axis_size("seq")
+    band = width // seq_count
     inverse_count = 1.0 / (row_count * seq_count)
-    gram_sum = lax.psum_scatter(
-        (
-            jnp.einsum("tc,tr->cr", normed, owned, preferred_element_type=jnp.float32)
-            * inverse_count
-        ).astype(jnp.bfloat16),
-        "seq",
-        scatter_dimension=0,
-        tiled=True,
+    partial = (
+        jnp.einsum("tc,tr->cr", normed, owned, preferred_element_type=jnp.float32)
+        * inverse_count
+    )
+    split = tile_cols // 2
+    offloaded = lax.psum_scatter(
+        partial[:, :split].astype(jnp.bfloat16), "seq", scatter_dimension=0, tiled=True
     ).astype(jnp.float32)
+    rest = partial[:, split:]
+
+    def piece(dest):
+        dest = jnp.clip(dest, 0, seq_count - 1)
+        return lax.dynamic_slice_in_dim(rest, dest * band, band, 0)
+
+    from_left = jnp.zeros((band, tile_cols - split), jnp.bfloat16)
+    from_right = jnp.zeros((band, tile_cols - split), jnp.bfloat16)
+    for step in range(1, seq_count):
+        up = piece(seq_index + seq_count - step) + from_left.astype(jnp.float32)
+        down = piece(seq_index - seq_count + step) + from_right.astype(jnp.float32)
+        up_route = [(c, c + 1) for c in range(step) if c + 1 < seq_count]
+        down_route = [(c, c - 1) for c in range(seq_count - step, seq_count) if c >= 1]
+        from_left = lax.ppermute(up.astype(jnp.bfloat16), "seq", up_route)
+        from_right = lax.ppermute(down.astype(jnp.bfloat16), "seq", down_route)
+    stepped = piece(seq_index) + from_left.astype(jnp.float32) + from_right.astype(jnp.float32)
+    gram_sum = jnp.concatenate([offloaded, stepped], axis=1)
     gram_tile = gram_sum
     return (attended, gram_tile)
 

time: 229 us -> 268 us (1.17)
  starting transfers between devices: 9.69 us -> 29 us
  local copies, waits for them, and re-layouts: 34.9 us -> 48.6 us
  other arithmetic: 21 us -> 30 us
  waiting for transfers between devices: 116 us -> 113 us
    ppermute x0 -> x6, waiting for transfers between devices: none -> 96.4 us  [the longest x3 74.2 us: body(): from_left = lax.ppermute(up.astype(jnp.bfloat16), 'seq', up_route)]
    reduce_scatter x1, waiting for transfers between devices: 69.6 us -> 0.02 us  [body(): lax.psum_scatter(partial[:, :split].astype(jnp.bfloat16), 'seq', scatter_...]
    ppermute x4, waiting for transfers between devices: 20.4 us -> 0.01 us  [from_partner(): return lax.ppermute(block, axis, route)]
    ppermute x0 -> x6, starting transfers between devices: none -> 19.2 us  [the longest x3 15.4 us: body(): from_left = lax.ppermute(up.astype(jnp.bfloat16), 'seq', up_route)]
    ppermute x1, waiting for transfers between devices: 23.4 us -> 16.4 us  [body(): across.append(lax.ppermute(tokens, 'kvh', route))]
    slice x0 -> x2, local copies, waits for them, and re-layouts: none -> 6.39 us  [the longest x1 3.81 us: body(): rest = partial[:, split:]]
    convert_element_type x1 -> x4, other arithmetic: 4.07 us -> 10.4 us  [the longest x2 6.9 us: body(): from_left = lax.ppermute(up.astype(jnp.bfloat16), 'seq', up_route)]
    convert_element_type x0 -> x1, local copies, waits for them, and re-layouts: none -> 4.04 us  [body(): from_left = lax.ppermute(up.astype(jnp.bfloat16), 'seq', up_route)]
  transfers between devices with their start and end apart: 14 -> 20, of which waited for: 4 -> 5; matrix products, arithmetic and copies ran while one was open for 30% -> 37% of each run, Pallas kernels for 0% -> 0%
where the time goes in v3:
time: 268 us; the launch traced here: 267 us
  waiting for transfers between devices  113 us (42%)
  local copies, waits for them, and re-layouts  48.6 us (18%)
  matrix products  32.2 us (12%)
  other arithmetic  30 us (11%)
  starting transfers between devices  29 us (11%)
  between operations  14.8 us (6%)
    ppermute x3, waiting for transfers between devices, body(): from_left = lax.ppermute(up.astype(jnp.bfloat16), 'seq', up_route)  74.2 us
    ppermute x3, waiting for transfers between devices, body(): from_right = lax.ppermute(down.astype(jnp.bfloat16), 'seq', down_route)  22.2 us
    unnamed x52, local copies, waits for them, and re-layouts  20.4 us
    ppermute x1, waiting for transfers between devices, body(): across.append(lax.ppermute(tokens, 'kvh', route))  16.4 us
    ppermute x3, starting transfers between devices, body(): from_left = lax.ppermute(up.astype(jnp.bfloat16), 'seq', up_route)  15.4 us
    dot_general x1, matrix products, body(): jnp.einsum('td,dgc->tgc', normed, w_query, preferred_element_type=jnp.flo...  8.5 us
    convert_element_type x2, other arithmetic, body(): from_left = lax.ppermute(up.astype(jnp.bfloat16), 'seq', up_route)  6.9 us
    dynamic_update_slice x6, local copies, waits for them, and re-layouts, split_send(): lax.dynamic_update_slice_in_dim(full, whole[shift][n], source * share, 0)  6.01 us
  transfers between devices with their start and end apart: 20, of which 5 were waited for; matrix products, arithmetic and copies ran while one was open for 37% of the time, Pallas kernels for 0%

profile of v3, /device:TPU:0, one launch (start us, length us, event | category | flops | bytes accessed | tf_op | source)
XLA Modules:
  0.0 267.4 jit_solution(17406383727706635470)
XLA Ops:
  7.2 3.0 %collective-permute-start.1 = (bf16[512,1024]{1,0:T(8,128)(2,1)}, bf16[512,1024]{1,0:T(8,128)(2,1)}, u32[]{:S(2)}, u32[]{:S(2)}) collective-permute-start(bf16[512,1024]{1,0:T(8,128)(2,1)} %param.6), channel_id=1, source_target_pairs={{0,2},{2,0},{1,3},{3,1},{4,6},{6,4},{5,7},{7,5},{8,10},{10,8},{9,1... | collective-permute-start | bytes 3145736 | tf_op jit(solution)/shard_map/ppermute | solution.py:70
  10.3 3.2 %copy.60 = bf16[2048,4,128]{2,0,1:T(8,128)(2,1)} copy(bf16[2048,4,128]{2,1,0:T(4,128)(2,1)} %param.10) | data formatting | bytes 4194304 | tf_op args[4]
  14.0 2.7 %copy.62 = bf16[2048,4,128]{0,2,1:T(8,128)(2,1)} copy(bf16[2048,4,128]{2,1,0:T(4,128)(2,1)S(1)} %copy-done.10) | data formatting | bytes 4194304 | tf_op args[3]
  17.4 16.4 %collective-permute-done.1 = bf16[512,1024]{1,0:T(8,128)(2,1)} collective-permute-done((bf16[512,1024]{1,0:T(8,128)(2,1)}, bf16[512,1024]{1,0:T(8,128)(2,1)}, u32[]{:S(2)}, u32[]{:S(2)}) %collective-permute-start.1) | collective-permute-done | bytes 1048608 | tf_op jit(solution)/shard_map/ppermute | solution.py:70
  46.1 4.4 %fusion.29 = f32[512,4,128]{2,0,1:T(8,128)S(1)} fusion(bf16[2048,4,128]{2,0,1:T(8,128)(2,1)} %collective-permute-done.3, bf16[512,4096]{1,0:T(8,128)(2,1)S(1)} %fusion.2, s32[]{:T(128)S(6)} %select_n.303), kind=kOutput, calls=%fused_computation.43 | convolution fusion | flops 1073741824 | bytes 5242884 | tf_op jit(solution)/shard_map/td,dgh->tgh/dot_general | solution.py:110
  52.6 2.8 %collective-permute-start.11 = (bf16[256,4,128]{2,0,1:T(8,128)(2,1)}, bf16[256,4,128]{2,0,1:T(8,128)(2,1)}, u32[]{:S(2)}, u32[]{:S(2)}) collective-permute-start(bf16[256,4,128]{2,0,1:T(8,128)(2,1)} %constant_dynamic-slice_fusion.1), channel_id=1, source_target_pairs={{0,8},{8,0},{4,12},{12,4},{1,9},{9,1},{5,13},{13,5},{2,10},{10,2},... | collective-permute-start | bytes 786440 | tf_op jit(solution)/shard_map/ppermute | solution.py:18
  58.3 2.9 %fusion.34 = f32[512,512]{0,1:S(1)} fusion(bf16[2048,512]{0,1:T(8,128)(2,1)} %bitcast.8, bf16[512,4096]{1,0:T(8,128)(2,1)S(1)} %fusion.2, s32[]{:T(128)S(6)} %select_n.303), kind=kOutput, calls=%fused_computation.57 | convolution fusion | flops 1073741824 | bytes 5242884
  62.9 4.9 %broadcast_multiply_fusion = f32[4096,1024]{0,1:T(8,128)S(1)} fusion(bf16[512,4096]{1,0:T(8,128)(2,1)S(1)} %fusion.2, s32[]{:T(128)S(6)} %select_n.314), kind=kOutput, calls=%fused_computation.9 | convolution fusion | flops 4299161600 | bytes 22020100 | tf_op jit(solution)/shard_map/tc,tr->cr/dot_general | solution.py:168
  67.8 3.8 %slice.51 = f32[4096,512]{0,1:T(8,128)} slice(f32[4096,1024]{0,1:T(8,128)S(1)} %broadcast_multiply_fusion), slice={[0:4096], [512:1024]} | slice | bytes 16777216 | tf_op jit(solution)/shard_map/slice | solution.py:175
  71.6 2.6 slice.57
  74.2 8.5 %fusion.3 = f32[512,4,256]{0,2,1:T(8,128)S(1)} fusion(bf16[4096,4,256]{2,1,0:T(4,128)(2,1)} %param.8, bf16[512,4096]{1,0:T(8,128)(2,1)} %copy-done.3), kind=kOutput, calls=%fused_computation.7 | convolution fusion | flops 4294967296 | bytes 14680064 | tf_op jit(solution)/shard_map/td,dgc->tgc/dot_general | solution.py:92
  82.9 1.9 copy.108
  84.8 2.0 copy.107
  86.8 4.0 %dynamic-slice_convert_fusion.1 = (bf16[1024,512]{0,1:T(8,128)(2,1)}, bf16[1024,512]{0,1:T(8,128)(2,1)}) fusion(f32[4096,512]{0,1:T(8,128)} %slice.51, s32[]{:T(128)S(6)} %select_n.318, s32[]{:T(128)S(6)} %select_n.321), kind=kLoop, calls=%fused_computation.53 | loop fusion | bytes 4194312 | tf_op jit(solution)/shard_map/convert_element_type | solution.py:188
  90.9 4.8 %collective-permute-start.13 = (bf16[1024,512]{0,1:T(8,128)(2,1)}, bf16[1024,512]{0,1:T(8,128)(2,1)}, u32[]{:S(2)}, u32[]{:S(2)}) collective-permute-start(bf16[1024,512]{0,1:T(8,128)(2,1)} %get-tuple-element.15), channel_id=1, source_target_pairs={{0,4},{1,5},{2,6},{3,7},{16,20},{17,21},{18,22},{19,23}} | collective-permute-start | bytes 3145736 | tf_op jit(solution)/shard_map/ppermute | solution.py:188
  96.3 2.3 fusion.7
  113.0 27.4 %collective-permute-done.13 = bf16[1024,512]{0,1:T(8,128)(2,1)} collective-permute-done((bf16[1024,512]{0,1:T(8,128)(2,1)}, bf16[1024,512]{0,1:T(8,128)(2,1)}, u32[]{:S(2)}, u32[]{:S(2)}) %collective-permute-start.13) | collective-permute-done | bytes 1048608 | tf_op jit(solution)/shard_map/ppermute | solution.py:188
  140.4 3.2 %add_convert_fusion.3 = bf16[1024,512]{0,1:T(8,128)(2,1)} fusion(bf16[1024,512]{0,1:T(8,128)(2,1)} %collective-permute-done.13, f32[4096,512]{0,1:T(8,128)} %slice.51, s32[]{:T(128)S(6)} %select_n.317), kind=kLoop, calls=%fused_computation.52 | loop fusion | flops 1572864 | bytes 4194308 | tf_op jit(solution)/shard_map/convert_element_type | solution.py:188
  143.6 5.5 %collective-permute-start.14 = (bf16[1024,512]{0,1:T(8,128)(2,1)}, bf16[1024,512]{0,1:T(8,128)(2,1)}, u32[]{:S(2)}, u32[]{:S(2)}) collective-permute-start(bf16[1024,512]{0,1:T(8,128)(2,1)} %add_convert_fusion.3), channel_id=1, source_target_pairs={{0,4},{4,8},{1,5},{5,9},{2,6},{6,10},{3,7},{7,11},{16,20},{20,24},... | collective-permute-start | bytes 3145736 | tf_op jit(solution)/shard_map/ppermute | solution.py:188
  150.9 1.8 copy.73
  152.7 1.9 constant_dynamic-update-slice_fusion.4
  157.0 36.5 %collective-permute-done.14 = bf16[1024,512]{0,1:T(8,128)(2,1)} collective-permute-done((bf16[1024,512]{0,1:T(8,128)(2,1)}, bf16[1024,512]{0,1:T(8,128)(2,1)}, u32[]{:S(2)}, u32[]{:S(2)}) %collective-permute-start.14) | collective-permute-done | bytes 1048608 | tf_op jit(solution)/shard_map/ppermute | solution.py:188
  193.6 3.7 %add_convert_fusion.2 = (bf16[1024,512]{0,1:T(8,128)(2,1)S(1)}, bf16[1024,512]{0,1:T(8,128)(2,1)S(1)}) fusion(bf16[1024,512]{0,1:T(8,128)(2,1)} %collective-permute-done.14, f32[4096,512]{0,1:T(8,128)} %slice.51, s32[]{:T(128)S(6)} %select_n.316, bf16[1024,512]{0,1:T(8,128)(2,1)} %collective-permute-done.16, s32[]{:T(128)S(6)} %select_n.320), kind=kLoop, calls=%fused_computation.51 | loop fusion | flops 3145728 | bytes 8388616 | tf_op jit(solution)/shard_map/convert_element_type | solution.py:188
  201.1 5.2 %collective-permute-start.15 = (bf16[1024,512]{0,1:T(8,128)(2,1)S(1)}, bf16[1024,512]{0,1:T(8,128)(2,1)S(1)}, u32[]{:S(2)}, u32[]{:S(2)}) collective-permute-start(bf16[1024,512]{0,1:T(8,128)(2,1)S(1)} %get-tuple-element.13), channel_id=1, source_target_pairs={{0,4},{4,8},{8,12},{1,5},{5,9},{9,13},{2,6},{6,10},{10,14},{3,7},{... | collective-permute-start | bytes 3145736 | tf_op jit(solution)/shard_map/ppermute | solution.py:188
  206.3 2.0 add_convert_fusion
  210.7 3.3 %fusion.33 = bf16[512,4,2,128]{0,3,2,1:T(8,128)(2,1)} fusion(f32[512,4,2,128]{0,3,2,1:T(8,128)S(1)} %bitcast.165, f32[512,4,2,128]{0,3,2,1:T(8,128)S(1)} %bitcast.166, f32[4,512,512,2]{2,1,3,0:T(8,128)S(1)} %bitcast.159, f32[4,2,512]{2,1,0:T(2,128)S(1)} %get-tuple-element.44, pred[512,512]{0,1:T(8,128)(4,1)S(1)} %fusion.59, ...), kind=kOutput, calls=%fused_computation.56 | convolution fusion | flops 548405248 | bytes 14483456 | tf_op jit(solution)/shard_map/grtu,ugh->tgrh/dot_general | solution.py:128
  213.9 2.4 copy.85
  216.3 10.3 %collective-permute-done.15 = bf16[1024,512]{0,1:T(8,128)(2,1)S(1)} collective-permute-done((bf16[1024,512]{0,1:T(8,128)(2,1)S(1)}, bf16[1024,512]{0,1:T(8,128)(2,1)S(1)}, u32[]{:S(2)}, u32[]{:S(2)}) %collective-permute-start.15) | collective-permute-done | bytes 1048608 | tf_op jit(solution)/shard_map/ppermute | solution.py:188
  226.6 22.2 %collective-permute-done.18 = bf16[1024,512]{0,1:T(8,128)(2,1)} collective-permute-done((bf16[1024,512]{0,1:T(8,128)(2,1)S(1)}, bf16[1024,512]{0,1:T(8,128)(2,1)}, u32[]{:S(2)}, u32[]{:S(2)}) %collective-permute-start.18) | collective-permute-done | bytes 1048608 | tf_op jit(solution)/shard_map/ppermute | solution.py:189
  248.8 2.4 convert_add_fusion
  252.7 2.5 pad_maximum_fusion.1
  255.2 5.3 %copy.86 = f32[1024,1024]{1,0:T(8,128)} copy(f32[1024,1024]{0,1:T(8,128)} %pad_maximum_fusion.1) | data formatting | bytes 8388608
  (132 shorter events, 46.9 us)
Async XLA Ops:
  7.2 34.5 %copy-start.13 = (bf16[512,1024]{1,0:T(8,128)(2,1)S(1)}, bf16[512,1024]{1,0:T(8,128)(2,1)}, u32[]{:S(2)}) copy-start(bf16[512,1024]{1,0:T(8,128)(2,1)} %param.6) | copy-start | bytes 3145732
  7.2 9.5 %copy-start.20 = (s32[3,8]{1,0:T(4,128)S(1)}, s32[3,8]{1,0:T(4,128)}, u32[]{:S(2)}) copy-start(s32[3,8]{1,0:T(4,128)} %param.11) | copy-start | bytes 292
  7.2 244.0 %reduce-scatter.2.cloned.1.call-start = ((), (), s32[]{:S(2)}) async-start(), calls=%async_computation.1 | async-start | bytes 5242880 | tf_op jit(solution)/shard_map/reduce_scatter | solution.py:172
  7.2 26.5 %collective-permute-start.1 = (bf16[512,1024]{1,0:T(8,128)(2,1)}, bf16[512,1024]{1,0:T(8,128)(2,1)}, u32[]{:S(2)}, u32[]{:S(2)}) collective-permute-start(bf16[512,1024]{1,0:T(8,128)(2,1)} %param.6), channel_id=1, source_target_pairs={{0,2},{2,0},{1,3},{3,1},{4,6},{6,4},{5,7},{7,5},{8,10},{10,8},{9,1... | collective-permute-start | bytes 3145736 | tf_op jit(solution)/shard_map/ppermute | solution.py:70
  10.3 31.4 %collective-permute-start = (bf16[512,1024]{1,0:T(8,128)(2,1)}, bf16[512,1024]{1,0:T(8,128)(2,1)}, u32[]{:S(2)}, u32[]{:S(2)}) collective-permute-start(bf16[512,1024]{1,0:T(8,128)(2,1)} %param.6), channel_id=1, source_target_pairs={{0,1},{1,0},{2,3},{3,2},{4,5},{5,4},{6,7},{7,6},{8,9},{9,8},{10,11... | collective-permute-start | bytes 3145736 | tf_op jit(solution)/shard_map/ppermute | solution.py:26
  13.5 32.6 %collective-permute-start.3 = (bf16[2048,4,128]{2,0,1:T(8,128)(2,1)}, bf16[2048,4,128]{2,0,1:T(8,128)(2,1)}, u32[]{:S(2)}, u32[]{:S(2)}) collective-permute-start(bf16[2048,4,128]{2,0,1:T(8,128)(2,1)} %copy.60), channel_id=1, source_target_pairs={{0,1},{1,0},{2,3},{3,2},{4,5},{5,4},{6,7},{7,6},{8,9},{9,8},{10,11... | collective-permute-start | bytes 6291464 | tf_op jit(solution)/shard_map/ppermute | solution.py:106
  16.7 41.6 %collective-permute-start.4 = (bf16[2048,4,128]{0,2,1:T(8,128)(2,1)}, bf16[2048,4,128]{0,2,1:T(8,128)(2,1)}, u32[]{:S(2)}, u32[]{:S(2)}) collective-permute-start(bf16[2048,4,128]{0,2,1:T(8,128)(2,1)} %copy.62), channel_id=1, source_target_pairs={{0,1},{1,0},{2,3},{3,2},{4,5},{5,4},{6,7},{7,6},{8,9},{9,8},{10,11... | collective-permute-start | bytes 6291464 | tf_op jit(solution)/shard_map/ppermute | solution.py:106
  33.7 7.9 %collective-permute-start.2 = (bf16[512,1024]{1,0:T(8,128)(2,1)}, bf16[512,1024]{1,0:T(8,128)(2,1)S(1)}, u32[]{:S(2)}, u32[]{:S(2)}) collective-permute-start(bf16[512,1024]{1,0:T(8,128)(2,1)} %collective-permute-done.1), channel_id=1, source_target_pairs={{0,1},{1,0},{2,3},{3,2},{4,5},{5,4},{6,7},{7,6},{8,9},{9,8},{10,11... | collective-permute-start | bytes 3145736 | tf_op jit(solution)/shard_map/ppermute | solution.py:26
  46.1 16.8 %copy-start.3 = (bf16[512,4096]{1,0:T(8,128)(2,1)}, bf16[512,4096]{1,0:T(8,128)(2,1)S(1)}, u32[]{:S(2)}) copy-start(bf16[512,4096]{1,0:T(8,128)(2,1)S(1)} %fusion.2) | copy-start | bytes 12582916
  51.8 9.4 %copy-start.17 = (bf16[512,4,128]{2,0,1:T(8,128)(2,1)}, bf16[512,4,128]{2,0,1:T(8,128)(2,1)S(1)}, u32[]{:S(2)}) copy-start(bf16[512,4,128]{2,0,1:T(8,128)(2,1)S(1)} %fusion.51) | copy-start | bytes 1572868
  52.6 55.1 %collective-permute-start.11 = (bf16[256,4,128]{2,0,1:T(8,128)(2,1)}, bf16[256,4,128]{2,0,1:T(8,128)(2,1)}, u32[]{:S(2)}, u32[]{:S(2)}) collective-permute-start(bf16[256,4,128]{2,0,1:T(8,128)(2,1)} %constant_dynamic-slice_fusion.1), channel_id=1, source_target_pairs={{0,8},{8,0},{4,12},{12,4},{1,9},{9,1},{5,13},{13,5},{2,10},{10,2},... | collective-permute-start | bytes 786440 | tf_op jit(solution)/shard_map/ppermute | solution.py:18
  55.5 52.8 %collective-permute-start.7 = (bf16[256,4,128]{2,0,1:T(8,128)(2,1)}, bf16[256,4,128]{2,0,1:T(8,128)(2,1)}, u32[]{:S(2)}, u32[]{:S(2)}) collective-permute-start(bf16[256,4,128]{2,0,1:T(8,128)(2,1)} %constant_dynamic-slice_fusion.1), channel_id=1, source_target_pairs={{0,4},{4,0},{8,12},{12,8},{1,5},{5,1},{9,13},{13,9},{2,6},{6,2},{1... | collective-permute-start | bytes 786440 | tf_op jit(solution)/shard_map/ppermute | solution.py:18
  62.4 39.5 %collective-permute-start.9 = (bf16[256,4,128]{0,2,1:T(8,128)(2,1)}, bf16[256,4,128]{0,2,1:T(8,128)(2,1)}, u32[]{:S(2)}, u32[]{:S(2)}) collective-permute-start(bf16[256,4,128]{0,2,1:T(8,128)(2,1)} %fusion.70), channel_id=1, source_target_pairs={{0,8},{8,0},{4,12},{12,4},{1,9},{9,1},{5,13},{13,5},{2,10},{10,2},... | collective-permute-start | bytes 786440 | tf_op jit(solution)/shard_map/ppermute | solution.py:18
  62.7 41.9 %collective-permute-start.5 = (bf16[256,4,128]{0,2,1:T(8,128)(2,1)}, bf16[256,4,128]{0,2,1:T(8,128)(2,1)}, u32[]{:S(2)}, u32[]{:S(2)}) collective-permute-start(bf16[256,4,128]{0,2,1:T(8,128)(2,1)} %fusion.70), channel_id=1, source_target_pairs={{0,4},{4,0},{8,12},{12,8},{1,5},{5,1},{9,13},{13,9},{2,6},{6,2},{1... | collective-permute-start | bytes 786440 | tf_op jit(solution)/shard_map/ppermute | solution.py:18
  84.8 10.8 %copy-start.15 = (f32[512,64]{1,0:T(8,128)S(1)}, f32[512,64]{1,0:T(8,128)}, u32[]{:S(2)}) copy-start(f32[512,64]{1,0:T(8,128)} %copy.68) | copy-start | bytes 393220
  84.8 10.8 %copy-start.16 = (f32[512,64]{1,0:T(8,128)S(1)}, f32[512,64]{1,0:T(8,128)}, u32[]{:S(2)}) copy-start(f32[512,64]{1,0:T(8,128)} %copy.66) | copy-start | bytes 393220
  86.8 8.9 %copy-start.1 = (f32[512,4,2,64]{3,0,2,1:T(8,128)S(1)}, f32[512,4,2,64]{3,0,2,1:T(8,128)}, u32[]{:S(2)}) copy-start(f32[512,4,2,64]{3,0,2,1:T(8,128)} %copy.108) | copy-start | bytes 3145732
  86.8 8.9 %copy-start.2 = (f32[512,4,2,64]{3,0,2,1:T(8,128)S(1)}, f32[512,4,2,64]{3,0,2,1:T(8,128)}, u32[]{:S(2)}) copy-start(f32[512,4,2,64]{3,0,2,1:T(8,128)} %copy.107) | copy-start | bytes 3145732
  90.9 49.5 %collective-permute-start.13 = (bf16[1024,512]{0,1:T(8,128)(2,1)}, bf16[1024,512]{0,1:T(8,128)(2,1)}, u32[]{:S(2)}, u32[]{:S(2)}) collective-permute-start(bf16[1024,512]{0,1:T(8,128)(2,1)} %get-tuple-element.15), channel_id=1, source_target_pairs={{0,4},{1,5},{2,6},{3,7},{16,20},{17,21},{18,22},{19,23}} | collective-permute-start | bytes 3145736 | tf_op jit(solution)/shard_map/ppermute | solution.py:188
  101.9 55.2 %collective-permute-start.16 = (bf16[1024,512]{0,1:T(8,128)(2,1)}, bf16[1024,512]{0,1:T(8,128)(2,1)}, u32[]{:S(2)}, u32[]{:S(2)}) collective-permute-start(bf16[1024,512]{0,1:T(8,128)(2,1)} %get-tuple-element.16), channel_id=1, source_target_pairs={{12,8},{13,9},{14,10},{15,11},{28,24},{29,25},{30,26},{31,27}} | collective-permute-start | bytes 3145736 | tf_op jit(solution)/shard_map/ppermute | solution.py:189
  104.6 6.0 %collective-permute-start.10 = (bf16[256,4,128]{0,2,1:T(8,128)(2,1)}, bf16[256,4,128]{0,2,1:T(8,128)(2,1)}, u32[]{:S(2)}, u32[]{:S(2)}) collective-permute-start(bf16[256,4,128]{0,2,1:T(8,128)(2,1)} %collective-permute-done.9), channel_id=1, source_target_pairs={{0,1},{1,0},{2,3},{3,2},{4,5},{5,4},{6,7},{7,6},{8,9},{9,8},{10,11... | collective-permute-start | bytes 786440 | tf_op jit(solution)/shard_map/ppermute | solution.py:26
  107.7 41.4 %collective-permute-start.12 = (bf16[256,4,128]{2,0,1:T(8,128)(2,1)}, bf16[256,4,128]{2,0,1:T(8,128)(2,1)}, u32[]{:S(2)}, u32[]{:S(2)}) collective-permute-start(bf16[256,4,128]{2,0,1:T(8,128)(2,1)} %collective-permute-done.11), channel_id=1, source_target_pairs={{0,1},{1,0},{2,3},{3,2},{4,5},{5,4},{6,7},{7,6},{8,9},{9,8},{10,11... | collective-permute-start | bytes 786440 | tf_op jit(solution)/shard_map/ppermute | solution.py:26
  108.3 44.5 %collective-permute-start.8 = (bf16[256,4,128]{2,0,1:T(8,128)(2,1)}, bf16[256,4,128]{2,0,1:T(8,128)(2,1)}, u32[]{:S(2)}, u32[]{:S(2)}) collective-permute-start(bf16[256,4,128]{2,0,1:T(8,128)(2,1)} %collective-permute-done.7), channel_id=1, source_target_pairs={{0,1},{1,0},{2,3},{3,2},{4,5},{5,4},{6,7},{7,6},{8,9},{9,8},{10,11... | collective-permute-start | bytes 786440 | tf_op jit(solution)/shard_map/ppermute | solution.py:26
  110.7 40.3 %collective-permute-start.6 = (bf16[256,4,128]{0,2,1:T(8,128)(2,1)}, bf16[256,4,128]{0,2,1:T(8,128)(2,1)}, u32[]{:S(2)}, u32[]{:S(2)}) collective-permute-start(bf16[256,4,128]{0,2,1:T(8,128)(2,1)} %collective-permute-done.5), channel_id=1, source_target_pairs={{0,1},{1,0},{2,3},{3,2},{4,5},{5,4},{6,7},{7,6},{8,9},{9,8},{10,11... | collective-permute-start | bytes 786440 | tf_op jit(solution)/shard_map/ppermute | solution.py:26
  113.0 36.1 %copy-start.7 = (bf16[512,4,128]{2,0,1:T(8,128)(2,1)S(1)}, bf16[512,4,128]{2,0,1:T(8,128)(2,1)}, u32[]{:S(2)}) copy-start(bf16[512,4,128]{2,0,1:T(8,128)(2,1)} %copy-done.6) | copy-start | bytes 1572868
  113.0 36.1 %copy-start.14 = (bf16[256,4,128]{2,0,1:T(8,128)(2,1)S(1)}, bf16[256,4,128]{2,0,1:T(8,128)(2,1)}, u32[]{:S(2)}) copy-start(bf16[256,4,128]{2,0,1:T(8,128)(2,1)} %copy.81) | copy-start | bytes 786436
  143.6 49.9 %collective-permute-start.14 = (bf16[1024,512]{0,1:T(8,128)(2,1)}, bf16[1024,512]{0,1:T(8,128)(2,1)}, u32[]{:S(2)}, u32[]{:S(2)}) collective-permute-start(bf16[1024,512]{0,1:T(8,128)(2,1)} %add_convert_fusion.3), channel_id=1, source_target_pairs={{0,4},{4,8},{1,5},{5,9},{2,6},{6,10},{3,7},{7,11},{16,20},{20,24},... | collective-permute-start | bytes 3145736 | tf_op jit(solution)/shard_map/ppermute | solution.py:188
  197.2 9.0 %collective-permute-start.17 = (bf16[1024,512]{0,1:T(8,128)(2,1)S(1)}, bf16[1024,512]{0,1:T(8,128)(2,1)S(1)}, u32[]{:S(2)}, u32[]{:S(2)}) collective-permute-start(bf16[1024,512]{0,1:T(8,128)(2,1)S(1)} %get-tuple-element.14), channel_id=1, source_target_pairs={{8,4},{12,8},{9,5},{13,9},{10,6},{14,10},{11,7},{15,11},{24,20},{2... | collective-permute-start | bytes 3145736 | tf_op jit(solution)/shard_map/ppermute | solution.py:189
  200.5 9.7 %slice-start = ((s8[8388608]{0:T(1024)(128)(4,1)}), s8[4194304]{0:T(1024)(128)(4,1)S(1)}, s32[]{:S(2)}) async-start(s8[8388608]{0:T(1024)(128)(4,1)} %bitcast.158), calls=%async_computation.2 | async-start | bytes 8388608
  201.1 9.1 %slice-start.1 = ((s8[8388608]{0:T(1024)(128)(4,1)}), s8[4194304]{0:T(1024)(128)(4,1)S(1)}, s32[]{:S(2)}) async-start(s8[8388608]{0:T(1024)(128)(4,1)} %bitcast.158), calls=%async_computation.3 | async-start | bytes 8388608
  201.1 25.5 %collective-permute-start.15 = (bf16[1024,512]{0,1:T(8,128)(2,1)S(1)}, bf16[1024,512]{0,1:T(8,128)(2,1)S(1)}, u32[]{:S(2)}, u32[]{:S(2)}) collective-permute-start(bf16[1024,512]{0,1:T(8,128)(2,1)S(1)} %get-tuple-element.13), channel_id=1, source_target_pairs={{0,4},{4,8},{8,12},{1,5},{5,9},{9,13},{2,6},{6,10},{10,14},{3,7},{... | collective-permute-start | bytes 3145736 | tf_op jit(solution)/shard_map/ppermute | solution.py:188
  208.3 40.6 %collective-permute-start.18 = (bf16[1024,512]{0,1:T(8,128)(2,1)S(1)}, bf16[1024,512]{0,1:T(8,128)(2,1)}, u32[]{:S(2)}, u32[]{:S(2)}) collective-permute-start(bf16[1024,512]{0,1:T(8,128)(2,1)S(1)} %add_convert_fusion), channel_id=1, source_target_pairs={{4,0},{8,4},{12,8},{5,1},{9,5},{13,9},{6,2},{10,6},{14,10},{7,3},{... | collective-permute-start | bytes 3145736 | tf_op jit(solution)/shard_map/ppermute | solution.py:189
  (11 other events, 28.9 us)
Sparse Core Ops, SparseCore 0:
  74.3 121.1 reduce-scatter.1

commit v4 on v2

--- a/solution.py
+++ b/solution.py
@@ -162,16 +162,28 @@
     owner_index = lax.axis_index("kvh") * lax.axis_size("sub") + lax.axis_index("sub")
     owned = lax.dynamic_slice_in_dim(normed, owner_index * tile_cols, tile_cols, 1)
     seq_count = lax.axis_size("seq")
+    band = width // seq_count
     inverse_count = 1.0 / (row_count * seq_count)
-    gram_sum = lax.psum_scatter(
-        (
-            jnp.einsum("tc,tr->cr", normed, owned, preferred_element_type=jnp.float32)
-            * inverse_count
-        ).astype(jnp.bfloat16),
-        "seq",
-        scatter_dimension=0,
-        tiled=True,
-    ).astype(jnp.float32)
+    share = row_count // sub_count
+    all_owned = lax.all_gather(owned, "seq", axis=0, tiled=True)
+    mine = lax.dynamic_slice_in_dim(normed, seq_index * band, band, 1)
+    gram_sum = jnp.einsum("tc,tr->cr", mine, owned, preferred_element_type=jnp.float32)
+    my_rows = lax.dynamic_slice_in_dim(normed, sub_index * share, share, 0)
+    for shift in range(1, seq_count):
+        target = (seq_index + shift) % seq_count
+        outgoing = lax.dynamic_slice_in_dim(my_rows, target * band, band, 1)
+        route = [(j, (j + shift) % seq_count) for j in range(seq_count)]
+        incoming = lax.ppermute(outgoing, "seq", route)
+        halves = swap_halves(incoming, sub_count, sub_index)
+        source = (seq_index - shift) % seq_count
+        their_owned = lax.dynamic_slice_in_dim(all_owned, source * row_count, row_count, 0)
+        for lane_shift in range(sub_count):
+            half_at = (sub_index - lane_shift) % sub_count
+            their_rows = lax.dynamic_slice_in_dim(their_owned, half_at * share, share, 0)
+            gram_sum = gram_sum + jnp.einsum(
+                "tc,tr->cr", halves[lane_shift], their_rows, preferred_element_type=jnp.float32
+            )
+    gram_sum = gram_sum * inverse_count
     gram_tile = gram_sum
     return (attended, gram_tile)
 

time: 229 us -> 219 us (0.956)
  waiting for transfers between devices: 116 us -> 87.6 us
  matrix products: 32.6 us -> 42.9 us
  local copies, waits for them, and re-layouts: 34.9 us -> 41.7 us
  starting transfers between devices: 9.69 us -> 15.3 us
  other arithmetic: 21 us -> 16.1 us
    reduce_scatter x1 -> x0, waiting for transfers between devices: 69.6 us -> none  [body(): lax.psum_scatter((jnp.einsum('tc,tr->cr', normed, owned, preferred_elemen...]
    ppermute x0 -> x3, waiting for transfers between devices: none -> 60.3 us  [body(): incoming = lax.ppermute(outgoing, 'seq', route)]
    ppermute x4, waiting for transfers between devices: 20.4 us -> 0.01 us  [from_partner(): return lax.ppermute(block, axis, route)]
    all_gather x0 -> x1, waiting for transfers between devices: none -> 10.9 us  [body(): all_owned = lax.all_gather(owned, 'seq', axis=0, tiled=True)]
    dot_general x1 -> x7, matrix products: 7 us -> 16.4 us  [the longest x6 11.9 us: body(): jnp.einsum('tc,tr->cr', halves[lane_shift], their_rows, preferred_element...]
    ppermute x1, waiting for transfers between devices: 23.4 us -> 16.4 us  [body(): across.append(lax.ppermute(tokens, 'kvh', route))]
    ppermute x0 -> x3, starting transfers between devices: none -> 5.02 us  [body(): incoming = lax.ppermute(outgoing, 'seq', route)]
    dynamic_slice x0 -> x2, local copies, waits for them, and re-layouts: none -> 4.75 us  [the longest x1 3.68 us: body(): outgoing = lax.dynamic_slice_in_dim(my_rows, target * band, band, 1)]
  transfers between devices with their start and end apart: 14 -> 20, of which waited for: 4 -> 3; matrix products, arithmetic and copies ran while one was open for 30% -> 41% of each run, Pallas kernels for 0% -> 0%
where the time goes in v4:
time: 219 us; the launch traced here: 218 us
  waiting for transfers between devices  87.6 us (40%)
  matrix products  42.9 us (20%)
  local copies, waits for them, and re-layouts  41.7 us (19%)
  other arithmetic  16.1 us (7%)
  starting transfers between devices  15.3 us (7%)
  between operations  14.8 us (7%)
    ppermute x3, waiting for transfers between devices, body(): incoming = lax.ppermute(outgoing, 'seq', route)  60.3 us
    unnamed x49, local copies, waits for them, and re-layouts  16.7 us
    ppermute x1, waiting for transfers between devices, body(): across.append(lax.ppermute(tokens, 'kvh', route))  16.4 us
    dot_general x6, matrix products, body(): jnp.einsum('tc,tr->cr', halves[lane_shift], their_rows, preferred_element...  11.9 us
    all_gather x1, waiting for transfers between devices, body(): all_owned = lax.all_gather(owned, 'seq', axis=0, tiled=True)  10.9 us
    dot_general x1, matrix products, body(): jnp.einsum('td,dgc->tgc', normed, w_query, preferred_element_type=jnp.flo...  8.37 us
    dynamic_update_slice x6, local copies, waits for them, and re-layouts, split_send(): lax.dynamic_update_slice_in_dim(full, whole[shift][n], source * share, 0)  6.82 us
    dot_general x2, matrix products, body(): jnp.einsum('td,dgh->tgh', rows, value_part, preferred_element_type=jnp.fl...  5.68 us
  transfers between devices with their start and end apart: 20, of which 3 were waited for; matrix products, arithmetic and copies ran while one was open for 41% of the time, Pallas kernels for 0%

profile of v4, /device:TPU:0, one launch (start us, length us, event | category | flops | bytes accessed | tf_op | source)
XLA Modules:
  0.0 218.4 jit_solution(15621678332138186840)
XLA Ops:
  7.2 3.0 %collective-permute-start.1 = (bf16[512,1024]{1,0:T(8,128)(2,1)}, bf16[512,1024]{1,0:T(8,128)(2,1)}, u32[]{:S(2)}, u32[]{:S(2)}) collective-permute-start(bf16[512,1024]{1,0:T(8,128)(2,1)} %param.6), channel_id=1, source_target_pairs={{0,2},{2,0},{1,3},{3,1},{4,6},{6,4},{5,7},{7,5},{8,10},{10,8},{9,1... | collective-permute-start | bytes 3145736 | tf_op jit(solution)/shard_map/ppermute | solution.py:70
  10.3 3.2 %copy.58 = bf16[2048,4,128]{2,0,1:T(8,128)(2,1)} copy(bf16[2048,4,128]{2,1,0:T(4,128)(2,1)} %param.10) | data formatting | bytes 4194304 | tf_op args[4]
  14.0 2.7 %copy.60 = bf16[2048,4,128]{0,2,1:T(8,128)(2,1)} copy(bf16[2048,4,128]{2,1,0:T(4,128)(2,1)S(1)} %copy-done.10) | data formatting | bytes 4194304 | tf_op args[3]
  17.4 16.4 %collective-permute-done.1 = bf16[512,1024]{1,0:T(8,128)(2,1)} collective-permute-done((bf16[512,1024]{1,0:T(8,128)(2,1)}, bf16[512,1024]{1,0:T(8,128)(2,1)}, u32[]{:S(2)}, u32[]{:S(2)}) %collective-permute-start.1) | collective-permute-done | bytes 1048608 | tf_op jit(solution)/shard_map/ppermute | solution.py:70
  41.9 1.8 select_select_fusion.3
  46.1 4.4 %fusion.29 = f32[512,4,128]{2,0,1:T(8,128)S(1)} fusion(bf16[2048,4,128]{2,0,1:T(8,128)(2,1)} %collective-permute-done.3, bf16[512,4096]{1,0:T(8,128)(2,1)S(1)} %fusion.2, s32[]{:T(128)S(6)} %select_n.364), kind=kOutput, calls=%fused_computation.41 | convolution fusion | flops 1073741824 | bytes 5242884 | tf_op jit(solution)/shard_map/td,dgh->tgh/dot_general | solution.py:110
  52.6 2.8 %collective-permute-start.11 = (bf16[256,4,128]{2,0,1:T(8,128)(2,1)}, bf16[256,4,128]{2,0,1:T(8,128)(2,1)}, u32[]{:S(2)}, u32[]{:S(2)}) collective-permute-start(bf16[256,4,128]{2,0,1:T(8,128)(2,1)} %constant_dynamic-slice_fusion.2), channel_id=1, source_target_pairs={{0,8},{8,0},{4,12},{12,4},{1,9},{9,1},{5,13},{13,5},{2,10},{10,2},... | collective-permute-start | bytes 786440 | tf_op jit(solution)/shard_map/ppermute | solution.py:18
  55.5 1.6 collective-permute-start.7
  58.5 2.9 %fusion.34 = f32[512,512]{0,1:S(1)} fusion(bf16[2048,512]{0,1:T(8,128)(2,1)} %bitcast.8, bf16[512,4096]{1,0:T(8,128)(2,1)S(1)} %fusion.2, s32[]{:T(128)S(6)} %select_n.364), kind=kOutput, calls=%fused_computation.48 | convolution fusion | flops 1073741824 | bytes 5242884
  63.0 8.4 %fusion.3 = f32[512,4,256]{0,2,1:T(8,128)} fusion(bf16[4096,4,256]{2,1,0:T(4,128)(2,1)} %param.8, bf16[512,4096]{1,0:T(8,128)(2,1)S(1)} %fusion.2), kind=kOutput, calls=%fused_computation.6 | convolution fusion | flops 4294967296 | bytes 14680064 | tf_op jit(solution)/shard_map/td,dgc->tgc/dot_general | solution.py:92
  72.5 1.8 fusion.115
  74.3 2.0 copy.105
  76.3 1.9 copy.104
  78.2 3.7 %fusion.114 = (bf16[256,1024]{1,0:T(8,128)(2,1)}, bf16[256,1024]{1,0:T(8,128)(2,1)}, bf16[256,1024]{1,0:T(8,128)(2,1)}) fusion(bf16[512,4096]{1,0:T(8,128)(2,1)} %copy-done, s32[]{:T(128)S(6)} %select_n.377, s32[]{:T(128)S(6)} %select_n.380, s32[]{:T(128)S(6)} %select_n.394, s32[]{:T(128)S(6)} %select_n.388), kind=kLoop, calls=%fused_computation.165 | loop fusion | bytes 3145744 | tf_op jit(solution)/shard_map/dynamic_slice | solution.py:174
  81.9 3.9 %collective-permute-start.17 = (bf16[256,1024]{1,0:T(8,128)(2,1)}, bf16[256,1024]{1,0:T(8,128)(2,1)}, u32[]{:S(2)}, u32[]{:S(2)}) collective-permute-start(bf16[256,1024]{1,0:T(8,128)(2,1)} %get-tuple-element.20), channel_id=1, source_target_pairs={{0,12},{4,0},{8,4},{12,8},{1,13},{5,1},{9,5},{13,9},{2,14},{6,2},{... | collective-permute-start | bytes 1572872 | tf_op jit(solution)/shard_map/ppermute | solution.py:176
  85.8 2.1 subtract_convert_fusion
  87.9 2.3 %fusion.7 = (f32[4,2,512]{2,1,0:T(2,128)S(1)}, f32[4,512,512,2]{2,1,3,0:T(8,128)S(1)}) fusion(pred[512,512]{0,1:T(8,128)(4,1)S(1)} %fusion.60, bf16[512,4,2,64]{3,0,2,1:T(8,128)(2,1)S(1)} %get-tuple-element.14, bf16[512,4,2,64]{3,0,2,1:T(8,128)(2,1)S(1)} %get-tuple-element.13, bf16[512,4,64]{0,2,1:T(8,128)(2,1)S(1)} %get-tuple-element.28, ...), kind=kOutput, calls=%fused_computation.11 | convolution fusion | flops 546304000 | bytes 10240000 | tf_op jit(solution)/shard_map/tgrh,ugh->grtu/dot_general | solution.py:118
  90.3 1.8 fusion.5
  93.5 4.5 %fusion.58 = f32[1024,1024]{1,0:T(8,128)} fusion(bf16[512,1024]{1,0:T(8,128)(2,1)S(1)} %copy-done.3, bf16[512,4096]{1,0:T(8,128)(2,1)} %copy-done, s32[]{:T(128)S(6)} %select_n.375), kind=kOutput, calls=%fused_computation.65 | convolution fusion | flops 1073741824 | bytes 6291460 | tf_op jit(solution)/shard_map/tc,tr->cr/dot_general | solution.py:170
  99.2 1.8 copy.70
  105.8 1.8 copy.79
  108.7 1.8 copy.71
  110.5 1.8 constant_dynamic-update-slice_fusion
  112.3 1.9 constant_dynamic-update-slice_fusion.4
  120.6 1.5 slice-done.1
  122.1 2.5 %fusion.33 = bf16[512,4,2,128]{0,3,2,1:T(8,128)(2,1)S(1)} fusion(f32[512,4,2,128]{0,3,2,1:T(8,128)S(1)} %bitcast.171, f32[512,4,2,128]{0,3,2,1:T(8,128)S(1)} %bitcast.172, f32[4,512,512,2]{2,1,3,0:T(8,128)S(1)} %bitcast.165, f32[4,2,512]{2,1,0:T(2,128)S(1)} %get-tuple-element.43, pred[512,512]{0,1:T(8,128)(4,1)S(1)} %fusion.60, ...), kind=kOutput, calls=%fused_computation.47 | convolution fusion | flops 548405248 | bytes 14483456 | tf_op jit(solution)/shard_map/grtu,ugh->tgrh/dot_general | solution.py:128
  126.0 60.3 %collective-permute-done.15 = bf16[256,1024]{1,0:T(8,128)(2,1)} collective-permute-done((bf16[256,1024]{1,0:T(8,128)(2,1)}, bf16[256,1024]{1,0:T(8,128)(2,1)}, u32[]{:S(2)}, u32[]{:S(2)}) %collective-permute-start.15) | collective-permute-done | bytes 524320 | tf_op jit(solution)/shard_map/ppermute | solution.py:176
  186.9 10.9 %all-gather.2.cloned.1.call-done = bf16[2048,1024]{1,0:T(8,128)(2,1)} async-done(((bf16[512,1024]{1,0:T(8,128)(2,1)}), bf16[2048,1024]{1,0:T(8,128)(2,1)}) %all-gather.2.cloned.1.call-update) | async-done | bytes 4194320 | tf_op jit(solution)/shard_map/all_gather | solution.py:168
  197.8 2.1 fusion.72
  200.3 1.8 fusion.76
  202.1 1.8 fusion.80
  206.9 4.7 %add_multiply_fusion = f32[1024,1024]{1,0:T(8,128)} fusion(f32[1024,1024]{1,0:T(8,128)S(1)} %fusion.72, f32[1024,1024]{1,0:T(8,128)S(1)} %fusion.74, f32[1024,1024]{1,0:T(8,128)S(1)} %fusion.76, f32[1024,1024]{1,0:T(8,128)S(1)} %fusion.78, f32[1024,1024]{1,0:T(8,128)S(1)} %copy-done.4, f32[1024,1024]{1,0:T(8,128)S(1)} %fusion.80, ...), kind=kOutput, calls=%fused_computation.21 | convolution fusion | flops 544210944 | bytes 30408708 | tf_op jit(solution)/shard_map/tc,tr->cr/dot_general | solution.py:183
  (128 shorter events, 37.8 us)
Async XLA Ops:
  7.2 34.7 %copy-start.13 = (bf16[512,1024]{1,0:T(8,128)(2,1)S(1)}, bf16[512,1024]{1,0:T(8,128)(2,1)}, u32[]{:S(2)}) copy-start(bf16[512,1024]{1,0:T(8,128)(2,1)} %param.6) | copy-start | bytes 3145732
  7.2 6.9 %copy-start.10 = (bf16[2048,4,128]{2,1,0:T(4,128)(2,1)S(1)}, bf16[2048,4,128]{2,1,0:T(4,128)(2,1)}, u32[]{:S(2)}) copy-start(bf16[2048,4,128]{2,1,0:T(4,128)(2,1)} %param.9) | copy-start | bytes 6291460
  7.2 9.5 %copy-start.19 = (s32[3,8]{1,0:T(4,128)S(1)}, s32[3,8]{1,0:T(4,128)}, u32[]{:S(2)}) copy-start(s32[3,8]{1,0:T(4,128)} %param.11) | copy-start | bytes 292
  7.2 190.6 %all-gather.2.cloned.1.call-start = ((), (), s32[]{:S(2)}) async-start(), calls=%async_computation | async-start | bytes 5242880 | tf_op jit(solution)/shard_map/all_gather | solution.py:168
  7.2 26.5 %collective-permute-start.1 = (bf16[512,1024]{1,0:T(8,128)(2,1)}, bf16[512,1024]{1,0:T(8,128)(2,1)}, u32[]{:S(2)}, u32[]{:S(2)}) collective-permute-start(bf16[512,1024]{1,0:T(8,128)(2,1)} %param.6), channel_id=1, source_target_pairs={{0,2},{2,0},{1,3},{3,1},{4,6},{6,4},{5,7},{7,5},{8,10},{10,8},{9,1... | collective-permute-start | bytes 3145736 | tf_op jit(solution)/shard_map/ppermute | solution.py:70
  10.3 31.6 %collective-permute-start = (bf16[512,1024]{1,0:T(8,128)(2,1)}, bf16[512,1024]{1,0:T(8,128)(2,1)}, u32[]{:S(2)}, u32[]{:S(2)}) collective-permute-start(bf16[512,1024]{1,0:T(8,128)(2,1)} %param.6), channel_id=1, source_target_pairs={{0,1},{1,0},{2,3},{3,2},{4,5},{5,4},{6,7},{7,6},{8,9},{9,8},{10,11... | collective-permute-start | bytes 3145736 | tf_op jit(solution)/shard_map/ppermute | solution.py:26
  13.5 32.6 %collective-permute-start.3 = (bf16[2048,4,128]{2,0,1:T(8,128)(2,1)}, bf16[2048,4,128]{2,0,1:T(8,128)(2,1)}, u32[]{:S(2)}, u32[]{:S(2)}) collective-permute-start(bf16[2048,4,128]{2,0,1:T(8,128)(2,1)} %copy.58), channel_id=1, source_target_pairs={{0,1},{1,0},{2,3},{3,2},{4,5},{5,4},{6,7},{7,6},{8,9},{9,8},{10,11... | collective-permute-start | bytes 6291464 | tf_op jit(solution)/shard_map/ppermute | solution.py:106
  16.7 41.7 %collective-permute-start.4 = (bf16[2048,4,128]{0,2,1:T(8,128)(2,1)}, bf16[2048,4,128]{0,2,1:T(8,128)(2,1)}, u32[]{:S(2)}, u32[]{:S(2)}) collective-permute-start(bf16[2048,4,128]{0,2,1:T(8,128)(2,1)} %copy.60), channel_id=1, source_target_pairs={{0,1},{1,0},{2,3},{3,2},{4,5},{5,4},{6,7},{7,6},{8,9},{9,8},{10,11... | collective-permute-start | bytes 6291464 | tf_op jit(solution)/shard_map/ppermute | solution.py:106
  33.7 8.1 %collective-permute-start.2 = (bf16[512,1024]{1,0:T(8,128)(2,1)}, bf16[512,1024]{1,0:T(8,128)(2,1)S(1)}, u32[]{:S(2)}, u32[]{:S(2)}) collective-permute-start(bf16[512,1024]{1,0:T(8,128)(2,1)} %collective-permute-done.1), channel_id=1, source_target_pairs={{0,1},{1,0},{2,3},{3,2},{4,5},{5,4},{6,7},{7,6},{8,9},{9,8},{10,11... | collective-permute-start | bytes 3145736 | tf_op jit(solution)/shard_map/ppermute | solution.py:26
  46.1 25.3 %copy-start = (bf16[512,4096]{1,0:T(8,128)(2,1)}, bf16[512,4096]{1,0:T(8,128)(2,1)S(1)}, u32[]{:S(2)}) copy-start(bf16[512,4096]{1,0:T(8,128)(2,1)S(1)} %fusion.2) | copy-start | bytes 12582916
  46.1 4.4 %copy-start.11 = (bf16[2048,4,128]{2,1,0:T(4,128)(2,1)S(1)}, bf16[2048,4,128]{2,1,0:T(4,128)(2,1)}, u32[]{:S(2)}) copy-start(bf16[2048,4,128]{2,1,0:T(4,128)(2,1)} %param.10) | copy-start | bytes 6291460
  50.5 6.5 %copy-start.12 = (bf16[2048,4,128]{0,2,1:T(8,128)(2,1)S(1)}, bf16[2048,4,128]{0,2,1:T(8,128)(2,1)}, u32[]{:S(2)}) copy-start(bf16[2048,4,128]{0,2,1:T(8,128)(2,1)} %copy.60) | copy-start | bytes 6291460
  51.8 9.5 %copy-start.16 = (bf16[512,4,128]{2,0,1:T(8,128)(2,1)}, bf16[512,4,128]{2,0,1:T(8,128)(2,1)S(1)}, u32[]{:S(2)}) copy-start(bf16[512,4,128]{2,0,1:T(8,128)(2,1)S(1)} %fusion.51) | copy-start | bytes 1572868
  52.6 48.9 %collective-permute-start.11 = (bf16[256,4,128]{2,0,1:T(8,128)(2,1)}, bf16[256,4,128]{2,0,1:T(8,128)(2,1)}, u32[]{:S(2)}, u32[]{:S(2)}) collective-permute-start(bf16[256,4,128]{2,0,1:T(8,128)(2,1)} %constant_dynamic-slice_fusion.2), channel_id=1, source_target_pairs={{0,8},{8,0},{4,12},{12,4},{1,9},{9,1},{5,13},{13,5},{2,10},{10,2},... | collective-permute-start | bytes 786440 | tf_op jit(solution)/shard_map/ppermute | solution.py:18
  55.5 47.2 %collective-permute-start.7 = (bf16[256,4,128]{2,0,1:T(8,128)(2,1)}, bf16[256,4,128]{2,0,1:T(8,128)(2,1)}, u32[]{:S(2)}, u32[]{:S(2)}) collective-permute-start(bf16[256,4,128]{2,0,1:T(8,128)(2,1)} %constant_dynamic-slice_fusion.2), channel_id=1, source_target_pairs={{0,4},{4,0},{8,12},{12,8},{1,5},{5,1},{9,13},{13,9},{2,6},{6,2},{1... | collective-permute-start | bytes 786440 | tf_op jit(solution)/shard_map/ppermute | solution.py:18
  62.5 35.5 %collective-permute-start.9 = (bf16[256,4,128]{0,2,1:T(8,128)(2,1)}, bf16[256,4,128]{0,2,1:T(8,128)(2,1)}, u32[]{:S(2)}, u32[]{:S(2)}) collective-permute-start(bf16[256,4,128]{0,2,1:T(8,128)(2,1)} %fusion.82), channel_id=1, source_target_pairs={{0,8},{8,0},{4,12},{12,4},{1,9},{9,1},{5,13},{13,5},{2,10},{10,2},... | collective-permute-start | bytes 786440 | tf_op jit(solution)/shard_map/ppermute | solution.py:18
  62.8 36.4 %collective-permute-start.5 = (bf16[256,4,128]{0,2,1:T(8,128)(2,1)}, bf16[256,4,128]{0,2,1:T(8,128)(2,1)}, u32[]{:S(2)}, u32[]{:S(2)}) collective-permute-start(bf16[256,4,128]{0,2,1:T(8,128)(2,1)} %fusion.82), channel_id=1, source_target_pairs={{0,4},{4,0},{8,12},{12,8},{1,5},{5,1},{9,13},{13,9},{2,6},{6,2},{1... | collective-permute-start | bytes 786440 | tf_op jit(solution)/shard_map/ppermute | solution.py:18
  74.3 11.5 %copy-start.14 = (f32[512,64]{1,0:T(8,128)S(1)}, f32[512,64]{1,0:T(8,128)}, u32[]{:S(2)}) copy-start(f32[512,64]{1,0:T(8,128)} %copy.66) | copy-start | bytes 393220
  74.3 11.5 %copy-start.15 = (f32[512,64]{1,0:T(8,128)S(1)}, f32[512,64]{1,0:T(8,128)}, u32[]{:S(2)}) copy-start(f32[512,64]{1,0:T(8,128)} %copy.64) | copy-start | bytes 393220
  78.2 7.6 %copy-start.2 = (f32[512,4,2,64]{3,0,2,1:T(8,128)S(1)}, f32[512,4,2,64]{3,0,2,1:T(8,128)}, u32[]{:S(2)}) copy-start(f32[512,4,2,64]{3,0,2,1:T(8,128)} %copy.105) | copy-start | bytes 3145732
  81.9 105.0 %collective-permute-start.17 = (bf16[256,1024]{1,0:T(8,128)(2,1)}, bf16[256,1024]{1,0:T(8,128)(2,1)}, u32[]{:S(2)}, u32[]{:S(2)}) collective-permute-start(bf16[256,1024]{1,0:T(8,128)(2,1)} %get-tuple-element.20), channel_id=1, source_target_pairs={{0,12},{4,0},{8,4},{12,8},{1,13},{5,1},{9,5},{13,9},{2,14},{6,2},{... | collective-permute-start | bytes 1572872 | tf_op jit(solution)/shard_map/ppermute | solution.py:176
  90.3 3.3 %copy-start.1 = (f32[4,512,512,2]{2,1,3,0:T(8,128)}, f32[4,512,512,2]{2,1,3,0:T(8,128)S(1)}, u32[]{:S(2)}) copy-start(f32[4,512,512,2]{2,1,3,0:T(8,128)S(1)} %get-tuple-element.44) | copy-start | bytes 25165828
  90.3 3.3 %copy-start.3 = (bf16[512,1024]{1,0:T(8,128)(2,1)S(1)}, bf16[512,1024]{1,0:T(8,128)(2,1)}, u32[]{:S(2)}) copy-start(bf16[512,1024]{1,0:T(8,128)(2,1)} %constant_dynamic-slice_fusion) | copy-start | bytes 3145732
  99.1 6.6 %collective-permute-start.10 = (bf16[256,4,128]{0,2,1:T(8,128)(2,1)}, bf16[256,4,128]{0,2,1:T(8,128)(2,1)}, u32[]{:S(2)}, u32[]{:S(2)}) collective-permute-start(bf16[256,4,128]{0,2,1:T(8,128)(2,1)} %collective-permute-done.9), channel_id=1, source_target_pairs={{0,1},{1,0},{2,3},{3,2},{4,5},{5,4},{6,7},{7,6},{8,9},{9,8},{10,11... | collective-permute-start | bytes 786440 | tf_op jit(solution)/shard_map/ppermute | solution.py:26
  101.0 6.6 %collective-permute-start.6 = (bf16[256,4,128]{0,2,1:T(8,128)(2,1)}, bf16[256,4,128]{0,2,1:T(8,128)(2,1)}, u32[]{:S(2)}, u32[]{:S(2)}) collective-permute-start(bf16[256,4,128]{0,2,1:T(8,128)(2,1)} %collective-permute-done.5), channel_id=1, source_target_pairs={{0,1},{1,0},{2,3},{3,2},{4,5},{5,4},{6,7},{7,6},{8,9},{9,8},{10,11... | collective-permute-start | bytes 786440 | tf_op jit(solution)/shard_map/ppermute | solution.py:26
  101.5 9.0 %collective-permute-start.12 = (bf16[256,4,128]{2,0,1:T(8,128)(2,1)}, bf16[256,4,128]{2,0,1:T(8,128)(2,1)}, u32[]{:S(2)}, u32[]{:S(2)}) collective-permute-start(bf16[256,4,128]{2,0,1:T(8,128)(2,1)} %collective-permute-done.11), channel_id=1, source_target_pairs={{0,1},{1,0},{2,3},{3,2},{4,5},{5,4},{6,7},{7,6},{8,9},{9,8},{10,11... | collective-permute-start | bytes 786440 | tf_op jit(solution)/shard_map/ppermute | solution.py:26
  102.7 9.6 %collective-permute-start.8 = (bf16[256,4,128]{2,0,1:T(8,128)(2,1)}, bf16[256,4,128]{2,0,1:T(8,128)(2,1)}, u32[]{:S(2)}, u32[]{:S(2)}) collective-permute-start(bf16[256,4,128]{2,0,1:T(8,128)(2,1)} %collective-permute-done.7), channel_id=1, source_target_pairs={{0,1},{1,0},{2,3},{3,2},{4,5},{5,4},{6,7},{7,6},{8,9},{9,8},{10,11... | collective-permute-start | bytes 786440 | tf_op jit(solution)/shard_map/ppermute | solution.py:26
  105.7 80.6 %collective-permute-start.15 = (bf16[256,1024]{1,0:T(8,128)(2,1)}, bf16[256,1024]{1,0:T(8,128)(2,1)}, u32[]{:S(2)}, u32[]{:S(2)}) collective-permute-start(bf16[256,1024]{1,0:T(8,128)(2,1)} %get-tuple-element.21), channel_id=1, source_target_pairs={{0,8},{4,12},{8,0},{12,4},{1,9},{5,13},{9,1},{13,5},{2,10},{6,14},... | collective-permute-start | bytes 1572872 | tf_op jit(solution)/shard_map/ppermute | solution.py:176
  107.6 78.7 %collective-permute-start.13 = (bf16[256,1024]{1,0:T(8,128)(2,1)}, bf16[256,1024]{1,0:T(8,128)(2,1)}, u32[]{:S(2)}, u32[]{:S(2)}) collective-permute-start(bf16[256,1024]{1,0:T(8,128)(2,1)} %get-tuple-element.19), channel_id=1, source_target_pairs={{0,4},{4,8},{8,12},{12,0},{1,5},{5,9},{9,13},{13,1},{2,6},{6,10},{... | collective-permute-start | bytes 1572872 | tf_op jit(solution)/shard_map/ppermute | solution.py:176
  186.3 17.6 %collective-permute-start.16 = (bf16[256,1024]{1,0:T(8,128)(2,1)}, bf16[256,1024]{1,0:T(8,128)(2,1)S(1)}, u32[]{:S(2)}, u32[]{:S(2)}) collective-permute-start(bf16[256,1024]{1,0:T(8,128)(2,1)} %collective-permute-done.15), channel_id=1, source_target_pairs={{0,1},{1,0},{2,3},{3,2},{4,5},{5,4},{6,7},{7,6},{8,9},{9,8},{10,11... | collective-permute-start | bytes 1572872 | tf_op jit(solution)/shard_map/ppermute | solution.py:26
  186.3 18.4 %collective-permute-start.14 = (bf16[256,1024]{1,0:T(8,128)(2,1)}, bf16[256,1024]{1,0:T(8,128)(2,1)S(1)}, u32[]{:S(2)}, u32[]{:S(2)}) collective-permute-start(bf16[256,1024]{1,0:T(8,128)(2,1)} %collective-permute-done.13), channel_id=1, source_target_pairs={{0,1},{1,0},{2,3},{3,2},{4,5},{5,4},{6,7},{7,6},{8,9},{9,8},{10,11... | collective-permute-start | bytes 1572872 | tf_op jit(solution)/shard_map/ppermute | solution.py:26
  186.8 18.6 %collective-permute-start.18 = (bf16[256,1024]{1,0:T(8,128)(2,1)}, bf16[256,1024]{1,0:T(8,128)(2,1)}, u32[]{:S(2)}, u32[]{:S(2)}) collective-permute-start(bf16[256,1024]{1,0:T(8,128)(2,1)} %collective-permute-done.17), channel_id=1, source_target_pairs={{0,1},{1,0},{2,3},{3,2},{4,5},{5,4},{6,7},{7,6},{8,9},{9,8},{10,11... | collective-permute-start | bytes 1572872 | tf_op jit(solution)/shard_map/ppermute | solution.py:26
  (10 other events, 17.7 us)
Sparse Core Ops, SparseCore 0:
  72.6 125.1 all-gather.1

commit v5 on v4

--- a/solution.py
+++ b/solution.py
@@ -79,7 +79,8 @@
     gathered = jnp.concatenate(blocks, axis=1)
     widened = gathered.astype(jnp.float32)
     mean_square = jnp.mean(widened * widened, axis=-1, keepdims=True)
-    normed = (widened * lax.rsqrt(mean_square + 1e-05) * norm_gain).astype(jnp.bfloat16)
+    row_scale = lax.rsqrt(mean_square + 1e-05)[:, 0]
+    normed = (widened * row_scale[:, None] * norm_gain).astype(jnp.bfloat16)
     row_count = normed.shape[0]
     block_len = row_count // 2
     width = normed.shape[1]
@@ -165,7 +166,8 @@
     band = width // seq_count
     inverse_count = 1.0 / (row_count * seq_count)
     share = row_count // sub_count
-    all_owned = lax.all_gather(owned, "seq", axis=0, tiled=True)
+    raw_columns = lax.all_gather(tokens, "seq", axis=0, tiled=True)
+    column_gain = lax.dynamic_slice_in_dim(norm_gain, owner_index * tile_cols, tile_cols, 0)
     mine = lax.dynamic_slice_in_dim(normed, seq_index * band, band, 1)
     gram_sum = jnp.einsum("tc,tr->cr", mine, owned, preferred_element_type=jnp.float32)
     my_rows = lax.dynamic_slice_in_dim(normed, sub_index * share, share, 0)
@@ -173,10 +175,13 @@
         target = (seq_index + shift) % seq_count
         outgoing = lax.dynamic_slice_in_dim(my_rows, target * band, band, 1)
         route = [(j, (j + shift) % seq_count) for j in range(seq_count)]
-        incoming = lax.ppermute(outgoing, "seq", route)
+        incoming, their_scale = lax.ppermute((outgoing, row_scale), "seq", route)
         halves = swap_halves(incoming, sub_count, sub_index)
         source = (seq_index - shift) % seq_count
-        their_owned = lax.dynamic_slice_in_dim(all_owned, source * row_count, row_count, 0)
+        their_raw = lax.dynamic_slice_in_dim(raw_columns, source * row_count, row_count, 0)
+        their_owned = (
+            their_raw.astype(jnp.float32) * their_scale[:, None] * column_gain
+        ).astype(jnp.bfloat16)
         for lane_shift in range(sub_count):
             half_at = (sub_index - lane_shift) % sub_count
             their_rows = lax.dynamic_slice_in_dim(their_owned, half_at * share, share, 0)

time: 219 us -> 192 us (0.88)
  waiting for transfers between devices: 87.6 us -> 55.2 us
  starting transfers between devices: 15.3 us -> 20 us
  other arithmetic: 16.1 us -> 19.4 us
    ppermute x3 -> x6, waiting for transfers between devices: 60.3 us -> 27.2 us  [body(): incoming, their_scale = lax.ppermute((outgoing, row_scale), 'seq', route)]
    ppermute x4, waiting for transfers between devices: 0.01 us -> 11.7 us  [from_partner(): return lax.ppermute(block, axis, route)]
    all_gather x1, waiting for transfers between devices: 10.9 us -> 0.01 us  [body(): raw_columns = lax.all_gather(tokens, 'seq', axis=0, tiled=True)]
    ppermute x3 -> x6, starting transfers between devices: 5.02 us -> 10.3 us  [body(): incoming, their_scale = lax.ppermute((outgoing, row_scale), 'seq', route)]
    convert_element_type x1 -> x2, other arithmetic: 1.39 us -> 4.03 us  [the longest x1 2.64 us: body(): their_owned = (their_raw.astype(jnp.float32) * their_scale[:, None] * col...]
    dot_general x2, matrix products: 0.99 us -> 3.38 us  [body(): jnp.einsum('grjtu,jugh->jtgrh', paired, far_values, preferred_element_typ...]
    unnamed x49 -> x41, local copies, waits for them, and re-layouts: 16.7 us -> 16.7 us
  transfers between devices with their start and end apart: 20 -> 23, of which waited for: 3 -> 4; matrix products, arithmetic and copies ran while one was open for 41% -> 48% of each run, Pallas kernels for 0% -> 0%
where the time goes in v5:
time: 192 us
  waiting for transfers between devices  55.2 us (29%)
  matrix products  41.7 us (22%)
  local copies, waits for them, and re-layouts  40.3 us (21%)
  starting transfers between devices  20 us (10%)
  other arithmetic  19.4 us (10%)
  between operations  14.8 us (8%)
    ppermute x6, waiting for transfers between devices, body(): incoming, their_scale = lax.ppermute((outgoing, row_scale), 'seq', route)  27.2 us
    unnamed x41, local copies, waits for them, and re-layouts  16.7 us
    ppermute x1, waiting for transfers between devices, body(): across.append(lax.ppermute(tokens, 'kvh', route))  16.2 us
    ppermute x4, waiting for transfers between devices, from_partner(): return lax.ppermute(block, axis, route)  11.7 us
    dot_general x6, matrix products, body(): jnp.einsum('tc,tr->cr', halves[lane_shift], their_rows, preferred_element...  10.9 us
    ppermute x6, starting transfers between devices, body(): incoming, their_scale = lax.ppermute((outgoing, row_scale), 'seq', route)  10.3 us
    dynamic_update_slice x6, local copies, waits for them, and re-layouts, split_send(): lax.dynamic_update_slice_in_dim(full, whole[shift][n], source * share, 0)  8.09 us
    dot_general x1, matrix products, body(): jnp.einsum('td,dgc->tgc', normed, w_query, preferred_element_type=jnp.flo...  7.05 us
  transfers between devices with their start and end apart: 23, of which 4 were waited for; matrix products, arithmetic and copies ran while one was open for 48% of the time, Pallas kernels for 0%

profile of v5, /device:TPU:0, one launch (start us, length us, event | category | flops | bytes accessed | tf_op | source)
XLA Modules:
  0.0 191.6 jit_solution(11812582252716886410)
XLA Ops:
  7.2 3.0 %collective-permute-start.1 = (bf16[512,1024]{1,0:T(8,128)(2,1)}, bf16[512,1024]{1,0:T(8,128)(2,1)}, u32[]{:S(2)}, u32[]{:S(2)}) collective-permute-start(bf16[512,1024]{1,0:T(8,128)(2,1)} %param.6), channel_id=1, source_target_pairs={{0,2},{2,0},{1,3},{3,1},{4,6},{6,4},{5,7},{7,5},{8,10},{10,8},{9,1... | collective-permute-start | bytes 3145736 | tf_op jit(solution)/shard_map/ppermute | solution.py:70
  10.3 3.3 %copy.58 = bf16[2048,4,128]{2,0,1:T(8,128)(2,1)} copy(bf16[2048,4,128]{2,1,0:T(4,128)(2,1)} %param.10) | data formatting | bytes 4194304 | tf_op args[4]
  14.1 2.7 %copy.60 = bf16[2048,4,128]{0,2,1:T(8,128)(2,1)} copy(bf16[2048,4,128]{2,1,0:T(4,128)(2,1)S(1)} %copy-done.6) | data formatting | bytes 4194304 | tf_op args[3]
  17.5 16.2 %collective-permute-done.1 = bf16[512,1024]{1,0:T(8,128)(2,1)} collective-permute-done((bf16[512,1024]{1,0:T(8,128)(2,1)}, bf16[512,1024]{1,0:T(8,128)(2,1)}, u32[]{:S(2)}, u32[]{:S(2)}) %collective-permute-start.1) | collective-permute-done | bytes 1048608 | tf_op jit(solution)/shard_map/ppermute | solution.py:70
  46.1 4.4 %fusion.29 = f32[512,4,128]{2,0,1:T(8,128)S(1)} fusion(bf16[2048,4,128]{2,0,1:T(8,128)(2,1)} %collective-permute-done.3, bf16[512,4096]{1,0:T(8,128)(2,1)S(1)} %fusion.2, s32[]{:T(128)S(6)} %select_n.355), kind=kOutput, calls=%fused_computation.41 | convolution fusion | flops 1073741824 | bytes 5242884 | tf_op jit(solution)/shard_map/td,dgh->tgh/dot_general | solution.py:111
  52.6 2.9 %collective-permute-start.11 = (bf16[256,4,128]{2,0,1:T(8,128)(2,1)}, bf16[256,4,128]{2,0,1:T(8,128)(2,1)}, u32[]{:S(2)}, u32[]{:S(2)}) collective-permute-start(bf16[256,4,128]{2,0,1:T(8,128)(2,1)} %constant_dynamic-slice_fusion.1), channel_id=1, source_target_pairs={{0,8},{8,0},{4,12},{12,4},{1,9},{9,1},{5,13},{13,5},{2,10},{10,2},... | collective-permute-start | bytes 786440 | tf_op jit(solution)/shard_map/ppermute | solution.py:18
  58.4 2.9 %fusion.34 = f32[512,512]{0,1:S(1)} fusion(bf16[2048,512]{0,1:T(8,128)(2,1)} %bitcast.8, bf16[512,4096]{1,0:T(8,128)(2,1)S(1)} %fusion.2, s32[]{:T(128)S(6)} %select_n.355), kind=kOutput, calls=%fused_computation.51 | convolution fusion | flops 1073741824 | bytes 5242884
  63.0 1.8 collective-permute-start.14
  64.8 7.1 %fusion.3 = f32[512,4,256]{0,2,1:T(8,128)S(1)} fusion(bf16[4096,4,256]{2,1,0:T(4,128)(2,1)} %param.8, bf16[512,4096]{1,0:T(8,128)(2,1)S(1)} %fusion.2), kind=kOutput, calls=%fused_computation.6 | convolution fusion | flops 4294967296 | bytes 14680064 | tf_op jit(solution)/shard_map/td,dgc->tgc/dot_general | solution.py:93
  72.1 2.0 %copy.105 = f32[512,4,2,64]{3,0,2,1:T(8,128)} copy(f32[512,4,2,64]{0,3,2,1:T(8,128)S(1)} %get-tuple-element.29) | data formatting | bytes 2097152
  74.1 1.9 %copy.104 = f32[512,4,2,64]{3,0,2,1:T(8,128)} copy(f32[512,4,2,64]{0,3,2,1:T(8,128)S(1)} %get-tuple-element.30) | data formatting | bytes 2097152
  76.0 2.8 %subtract_convert_fusion = (bf16[512,4,2,64]{3,0,2,1:T(8,128)(2,1)S(1)}, bf16[512,4,2,64]{3,0,2,1:T(8,128)(2,1)S(1)}) fusion(f32[512,4,2,64]{3,0,2,1:T(8,128)} %copy.105, f32[512,4,2,64]{3,0,2,1:T(8,128)} %copy.104, f32[512,64]{1,0:T(8,128)S(1)} %copy-done.9, f32[512,64]{1,0:T(8,128)S(1)} %copy-done.10), kind=kLoop, calls=%fused_computation.49 | loop fusion | flops 2097152 | bytes 3407872 | tf_op jit(solution)/shard_map/convert.4
  78.8 2.3 %fusion.7 = (f32[4,2,512]{2,1,0:T(2,128)S(1)}, f32[4,512,512,2]{2,1,3,0:T(8,128)S(1)}) fusion(pred[512,512]{0,1:T(8,128)(4,1)S(1)} %fusion.61, bf16[512,4,2,64]{3,0,2,1:T(8,128)(2,1)S(1)} %get-tuple-element.14, bf16[512,4,2,64]{3,0,2,1:T(8,128)(2,1)S(1)} %get-tuple-element.13, bf16[512,4,64]{0,2,1:T(8,128)(2,1)S(1)} %get-tuple-element.31, ...), kind=kOutput, calls=%fused_computation.11 | convolution fusion | flops 546304000 | bytes 10240000 | tf_op jit(solution)/shard_map/tgrh,ugh->grtu/dot_general | solution.py:119
  83.0 2.5 %copy-done.3 = f32[4,512,512,2]{2,1,3,0:T(8,128)} copy-done((f32[4,512,512,2]{2,1,3,0:T(8,128)}, f32[4,512,512,2]{2,1,3,0:T(8,128)S(1)}, u32[]{:S(2)}) %copy-start.3) | copy-done | bytes 8388632
  86.4 3.3 %fusion.58 = f32[1024,1024]{1,0:T(8,128)} fusion(bf16[512,4096]{1,0:T(8,128)(2,1)S(1)} %copy-done.2, s32[]{:T(128)} %select_n.367, s32[]{:T(128)S(6)} %select_n.366), kind=kOutput, calls=%fused_computation.68 | convolution fusion | flops 1073741824 | bytes 6291464 | tf_op jit(solution)/shard_map/tc,tr->cr/dot_general | solution.py:172
  89.7 2.1 %fusion.115 = (bf16[256,1024]{1,0:T(8,128)(2,1)}, bf16[256,1024]{1,0:T(8,128)(2,1)}, bf16[256,1024]{1,0:T(8,128)(2,1)}) fusion(bf16[512,4096]{1,0:T(8,128)(2,1)S(1)} %copy-done.2, s32[]{:T(128)S(6)} %select_n.368, s32[]{:T(128)S(6)} %select_n.371, s32[]{:T(128)S(6)} %select_n.381, s32[]{:T(128)S(6)} %select_n.376), kind=kLoop, calls=%fused_computation.168 | loop fusion | bytes 3145744 | tf_op jit(solution)/shard_map/dynamic_slice | solution.py:176
  91.8 10.4 %collective-permute-done.9 = bf16[256,4,128]{0,2,1:T(8,128)(2,1)} collective-permute-done((bf16[256,4,128]{0,2,1:T(8,128)(2,1)}, bf16[256,4,128]{0,2,1:T(8,128)(2,1)}, u32[]{:S(2)}, u32[]{:S(2)}) %collective-permute-start.9) | collective-permute-done | bytes 262176 | tf_op jit(solution)/shard_map/ppermute | solution.py:18
  104.7 1.8 copy.70
  113.4 1.8 copy.79
  115.2 4.4 %collective-permute-start.20 = (f32[512]{0:T(512)S(1)}, f32[512]{0:T(512)S(1)}, u32[]{:S(2)}, u32[]{:S(2)}) collective-permute-start(f32[512]{0:T(512)S(1)} %add_rsqrt_fusion), channel_id=1, source_target_pairs={{0,12},{4,0},{8,4},{12,8},{1,13},{5,1},{9,5},{13,9},{2,14},{6,2},{... | collective-permute-start | bytes 6152 | tf_op jit(solution)/shard_map/ppermute | solution.py:178
  119.6 1.8 copy.71
  121.4 1.8 constant_dynamic-update-slice_fusion
  123.2 2.0 %collective-permute-start.16 = (bf16[256,1024]{1,0:T(8,128)(2,1)}, bf16[256,1024]{1,0:T(8,128)(2,1)}, u32[]{:S(2)}, u32[]{:S(2)}) collective-permute-start(bf16[256,1024]{1,0:T(8,128)(2,1)} %get-tuple-element.24), channel_id=1, source_target_pairs={{0,8},{4,12},{8,0},{12,4},{1,9},{5,13},{9,1},{13,5},{2,10},{6,14},... | collective-permute-start | bytes 1572872 | tf_op jit(solution)/shard_map/ppermute | solution.py:178
  125.3 1.8 constant_dynamic-update-slice_fusion.4
  133.0 1.8 fusion.42
  135.9 2.0 %collective-permute-start.13 = (bf16[256,1024]{1,0:T(8,128)(2,1)S(1)}, bf16[256,1024]{1,0:T(8,128)(2,1)S(1)}, u32[]{:S(2)}, u32[]{:S(2)}) collective-permute-start(bf16[256,1024]{1,0:T(8,128)(2,1)S(1)} %copy-done.11), channel_id=1, source_target_pairs={{0,4},{4,8},{8,12},{12,0},{1,5},{5,9},{9,13},{13,1},{2,6},{6,10},{... | collective-permute-start | bytes 1572872 | tf_op jit(solution)/shard_map/ppermute | solution.py:178
  138.0 2.5 %fusion.33 = bf16[512,4,2,128]{0,3,2,1:T(8,128)(2,1)S(1)} fusion(f32[512,4,2,128]{0,3,2,1:T(8,128)S(1)} %bitcast.168, f32[512,4,2,128]{0,3,2,1:T(8,128)S(1)} %bitcast.169, f32[4,512,512,2]{2,1,3,0:T(8,128)S(1)} %bitcast.164, f32[4,2,512]{2,1,0:T(2,128)S(1)} %get-tuple-element.46, pred[512,512]{0,1:T(8,128)(4,1)S(1)} %fusion.61, ...), kind=kOutput, calls=%fused_computation.50 | convolution fusion | flops 548405248 | bytes 14483456 | tf_op jit(solution)/shard_map/grtu,ugh->tgrh/dot_general | solution.py:129
  141.9 27.2 %collective-permute-done.16 = bf16[256,1024]{1,0:T(8,128)(2,1)} collective-permute-done((bf16[256,1024]{1,0:T(8,128)(2,1)}, bf16[256,1024]{1,0:T(8,128)(2,1)}, u32[]{:S(2)}, u32[]{:S(2)}) %collective-permute-start.16) | collective-permute-done | bytes 524320 | tf_op jit(solution)/shard_map/ppermute | solution.py:178
  169.7 2.6 %multiply_convert_fusion.2 = (bf16[512,1024]{1,0:T(8,128)(2,1)S(1)}, bf16[512,1024]{1,0:T(8,128)(2,1)S(1)}, bf16[512,1024]{1,0:T(8,128)(2,1)S(1)}) fusion(f32[1024]{0:T(1024)S(1)} %dynamic-slice-done, f32[512]{0:T(512)S(1)} %collective-permute-done.14, bf16[2048,1024]{1,0:T(8,128)(2,1)} %all-gather.2.cloned.1.call-done, s32[]{:T(128)S(6)} %select_n.373, ...), kind=kLoop, calls=%fused_computation.47 | loop fusion | flops 6291456 | bytes 6301708 | tf_op jit(solution)/shard_map/convert_element_type | solution.py:184
  172.4 2.2 %fusion.73 = f32[1024,1024]{1,0:T(8,128)S(1)} fusion(bf16[256,1024]{1,0:T(8,128)(2,1)} %collective-permute-done.19, bf16[512,1024]{1,0:T(8,128)(2,1)S(1)} %get-tuple-element.21, s32[]{:T(128)S(6)} %select_n.362), kind=kOutput, calls=%fused_computation.90 | convolution fusion | flops 536870912 | bytes 5242884 | tf_op jit(solution)/shard_map/tc,tr->cr/dot_general | solution.py:188
  174.6 1.8 fusion.77
  180.1 4.7 %add_multiply_fusion = f32[1024,1024]{1,0:T(8,128)} fusion(f32[1024,1024]{1,0:T(8,128)S(1)} %fusion.73, f32[1024,1024]{1,0:T(8,128)S(1)} %fusion.75, f32[1024,1024]{1,0:T(8,128)S(1)} %fusion.77, f32[1024,1024]{1,0:T(8,128)S(1)} %fusion.79, f32[1024,1024]{1,0:T(8,128)S(1)} %copy-done, f32[1024,1024]{1,0:T(8,128)S(1)} %fusion.81, ...), kind=kOutput, calls=%fused_computation.21 | convolution fusion | flops 544210944 | bytes 30408708 | tf_op jit(solution)/shard_map/tc,tr->cr/dot_general | solution.py:188
  (128 shorter events, 44.8 us)
Async XLA Ops:
  7.2 7.0 %copy-start.6 = (bf16[2048,4,128]{2,1,0:T(4,128)(2,1)S(1)}, bf16[2048,4,128]{2,1,0:T(4,128)(2,1)}, u32[]{:S(2)}) copy-start(bf16[2048,4,128]{2,1,0:T(4,128)(2,1)} %param.9) | copy-start | bytes 6291460
  7.2 162.5 %all-gather.2.cloned.1.call-start = ((), (), s32[]{:S(2)}) async-start(), calls=%async_computation | async-start | bytes 5242880 | tf_op jit(solution)/shard_map/all_gather | solution.py:169
  7.2 26.5 %collective-permute-start.1 = (bf16[512,1024]{1,0:T(8,128)(2,1)}, bf16[512,1024]{1,0:T(8,128)(2,1)}, u32[]{:S(2)}, u32[]{:S(2)}) collective-permute-start(bf16[512,1024]{1,0:T(8,128)(2,1)} %param.6), channel_id=1, source_target_pairs={{0,2},{2,0},{1,3},{3,1},{4,6},{6,4},{5,7},{7,5},{8,10},{10,8},{9,1... | collective-permute-start | bytes 3145736 | tf_op jit(solution)/shard_map/ppermute | solution.py:70
  10.3 31.6 %collective-permute-start = (bf16[512,1024]{1,0:T(8,128)(2,1)}, bf16[512,1024]{1,0:T(8,128)(2,1)}, u32[]{:S(2)}, u32[]{:S(2)}) collective-permute-start(bf16[512,1024]{1,0:T(8,128)(2,1)} %param.6), channel_id=1, source_target_pairs={{0,1},{1,0},{2,3},{3,2},{4,5},{5,4},{6,7},{7,6},{8,9},{9,8},{10,11... | collective-permute-start | bytes 3145736 | tf_op jit(solution)/shard_map/ppermute | solution.py:26
  10.3 6.5 %copy-start.15 = (s32[3,8]{1,0:T(4,128)S(1)}, s32[3,8]{1,0:T(4,128)}, u32[]{:S(2)}) copy-start(s32[3,8]{1,0:T(4,128)} %param.11) | copy-start | bytes 292
  10.3 31.6 %copy-start.5 = (bf16[512,1024]{1,0:T(8,128)(2,1)S(1)}, bf16[512,1024]{1,0:T(8,128)(2,1)}, u32[]{:S(2)}) copy-start(bf16[512,1024]{1,0:T(8,128)(2,1)} %param.6) | copy-start | bytes 3145732
  13.6 32.5 %collective-permute-start.3 = (bf16[2048,4,128]{2,0,1:T(8,128)(2,1)}, bf16[2048,4,128]{2,0,1:T(8,128)(2,1)}, u32[]{:S(2)}, u32[]{:S(2)}) collective-permute-start(bf16[2048,4,128]{2,0,1:T(8,128)(2,1)} %copy.58), channel_id=1, source_target_pairs={{0,1},{1,0},{2,3},{3,2},{4,5},{5,4},{6,7},{7,6},{8,9},{9,8},{10,11... | collective-permute-start | bytes 6291464 | tf_op jit(solution)/shard_map/ppermute | solution.py:107
  16.8 41.6 %collective-permute-start.4 = (bf16[2048,4,128]{0,2,1:T(8,128)(2,1)}, bf16[2048,4,128]{0,2,1:T(8,128)(2,1)}, u32[]{:S(2)}, u32[]{:S(2)}) collective-permute-start(bf16[2048,4,128]{0,2,1:T(8,128)(2,1)} %copy.60), channel_id=1, source_target_pairs={{0,1},{1,0},{2,3},{3,2},{4,5},{5,4},{6,7},{7,6},{8,9},{9,8},{10,11... | collective-permute-start | bytes 6291464 | tf_op jit(solution)/shard_map/ppermute | solution.py:107
  33.7 8.1 %collective-permute-start.2 = (bf16[512,1024]{1,0:T(8,128)(2,1)}, bf16[512,1024]{1,0:T(8,128)(2,1)S(1)}, u32[]{:S(2)}, u32[]{:S(2)}) collective-permute-start(bf16[512,1024]{1,0:T(8,128)(2,1)} %collective-permute-done.1), channel_id=1, source_target_pairs={{0,1},{1,0},{2,3},{3,2},{4,5},{5,4},{6,7},{7,6},{8,9},{9,8},{10,11... | collective-permute-start | bytes 3145736 | tf_op jit(solution)/shard_map/ppermute | solution.py:26
  46.1 18.7 %copy-start.1 = (bf16[512,4096]{1,0:T(8,128)(2,1)}, bf16[512,4096]{1,0:T(8,128)(2,1)S(1)}, u32[]{:S(2)}) copy-start(bf16[512,4096]{1,0:T(8,128)(2,1)S(1)} %fusion.2) | copy-start | bytes 12582916
  50.5 6.5 %copy-start.8 = (bf16[2048,4,128]{0,2,1:T(8,128)(2,1)S(1)}, bf16[2048,4,128]{0,2,1:T(8,128)(2,1)}, u32[]{:S(2)}) copy-start(bf16[2048,4,128]{0,2,1:T(8,128)(2,1)} %copy.60) | copy-start | bytes 6291460
  51.8 9.5 %copy-start.12 = (bf16[512,4,128]{2,0,1:T(8,128)(2,1)}, bf16[512,4,128]{2,0,1:T(8,128)(2,1)S(1)}, u32[]{:S(2)}) copy-start(bf16[512,4,128]{2,0,1:T(8,128)(2,1)S(1)} %fusion.51) | copy-start | bytes 1572868
  52.6 53.9 %collective-permute-start.11 = (bf16[256,4,128]{2,0,1:T(8,128)(2,1)}, bf16[256,4,128]{2,0,1:T(8,128)(2,1)}, u32[]{:S(2)}, u32[]{:S(2)}) collective-permute-start(bf16[256,4,128]{2,0,1:T(8,128)(2,1)} %constant_dynamic-slice_fusion.1), channel_id=1, source_target_pairs={{0,8},{8,0},{4,12},{12,4},{1,9},{9,1},{5,13},{13,5},{2,10},{10,2},... | collective-permute-start | bytes 786440 | tf_op jit(solution)/shard_map/ppermute | solution.py:18
  55.5 52.7 %collective-permute-start.7 = (bf16[256,4,128]{2,0,1:T(8,128)(2,1)}, bf16[256,4,128]{2,0,1:T(8,128)(2,1)}, u32[]{:S(2)}, u32[]{:S(2)}) collective-permute-start(bf16[256,4,128]{2,0,1:T(8,128)(2,1)} %constant_dynamic-slice_fusion.1), channel_id=1, source_target_pairs={{0,4},{4,0},{8,12},{12,8},{1,5},{5,1},{9,13},{13,9},{2,6},{6,2},{1... | collective-permute-start | bytes 786440 | tf_op jit(solution)/shard_map/ppermute | solution.py:18
  62.4 39.8 %collective-permute-start.9 = (bf16[256,4,128]{0,2,1:T(8,128)(2,1)}, bf16[256,4,128]{0,2,1:T(8,128)(2,1)}, u32[]{:S(2)}, u32[]{:S(2)}) collective-permute-start(bf16[256,4,128]{0,2,1:T(8,128)(2,1)} %fusion.83), channel_id=1, source_target_pairs={{0,8},{8,0},{4,12},{12,4},{1,9},{9,1},{5,13},{13,5},{2,10},{10,2},... | collective-permute-start | bytes 786440 | tf_op jit(solution)/shard_map/ppermute | solution.py:18
  62.8 41.9 %collective-permute-start.5 = (bf16[256,4,128]{0,2,1:T(8,128)(2,1)}, bf16[256,4,128]{0,2,1:T(8,128)(2,1)}, u32[]{:S(2)}, u32[]{:S(2)}) collective-permute-start(bf16[256,4,128]{0,2,1:T(8,128)(2,1)} %fusion.83), channel_id=1, source_target_pairs={{0,4},{4,0},{8,12},{12,8},{1,5},{5,1},{9,13},{13,9},{2,6},{6,2},{1... | collective-permute-start | bytes 786440 | tf_op jit(solution)/shard_map/ppermute | solution.py:18
  63.0 72.5 %collective-permute-start.14 = (f32[512]{0:T(512)S(1)}, f32[512]{0:T(512)S(1)}, u32[]{:S(2)}, u32[]{:S(2)}) collective-permute-start(f32[512]{0:T(512)S(1)} %add_rsqrt_fusion), channel_id=1, source_target_pairs={{0,4},{4,8},{8,12},{12,0},{1,5},{5,9},{9,13},{13,1},{2,6},{6,10},{... | collective-permute-start | bytes 6152 | tf_op jit(solution)/shard_map/ppermute | solution.py:178
  81.2 5.2 %copy-start.2 = (bf16[512,4096]{1,0:T(8,128)(2,1)S(1)}, bf16[512,4096]{1,0:T(8,128)(2,1)}, u32[]{:S(2)}) copy-start(bf16[512,4096]{1,0:T(8,128)(2,1)} %copy-done.1) | copy-start | bytes 12582916
  103.4 10.0 %collective-permute-start.10 = (bf16[256,4,128]{0,2,1:T(8,128)(2,1)}, bf16[256,4,128]{0,2,1:T(8,128)(2,1)}, u32[]{:S(2)}, u32[]{:S(2)}) collective-permute-start(bf16[256,4,128]{0,2,1:T(8,128)(2,1)} %collective-permute-done.9), channel_id=1, source_target_pairs={{0,1},{1,0},{2,3},{3,2},{4,5},{5,4},{6,7},{7,6},{8,9},{9,8},{10,11... | collective-permute-start | bytes 786440 | tf_op jit(solution)/shard_map/ppermute | solution.py:26
  106.5 8.8 %collective-permute-start.6 = (bf16[256,4,128]{0,2,1:T(8,128)(2,1)}, bf16[256,4,128]{0,2,1:T(8,128)(2,1)}, u32[]{:S(2)}, u32[]{:S(2)}) collective-permute-start(bf16[256,4,128]{0,2,1:T(8,128)(2,1)} %collective-permute-done.5), channel_id=1, source_target_pairs={{0,1},{1,0},{2,3},{3,2},{4,5},{5,4},{6,7},{7,6},{8,9},{9,8},{10,11... | collective-permute-start | bytes 786440 | tf_op jit(solution)/shard_map/ppermute | solution.py:26
  106.5 14.9 %collective-permute-start.12 = (bf16[256,4,128]{2,0,1:T(8,128)(2,1)}, bf16[256,4,128]{2,0,1:T(8,128)(2,1)}, u32[]{:S(2)}, u32[]{:S(2)}) collective-permute-start(bf16[256,4,128]{2,0,1:T(8,128)(2,1)} %collective-permute-done.11), channel_id=1, source_target_pairs={{0,1},{1,0},{2,3},{3,2},{4,5},{5,4},{6,7},{7,6},{8,9},{9,8},{10,11... | collective-permute-start | bytes 786440 | tf_op jit(solution)/shard_map/ppermute | solution.py:26
  108.2 15.1 %collective-permute-start.8 = (bf16[256,4,128]{2,0,1:T(8,128)(2,1)}, bf16[256,4,128]{2,0,1:T(8,128)(2,1)}, u32[]{:S(2)}, u32[]{:S(2)}) collective-permute-start(bf16[256,4,128]{2,0,1:T(8,128)(2,1)} %collective-permute-done.7), channel_id=1, source_target_pairs={{0,1},{1,0},{2,3},{3,2},{4,5},{5,4},{6,7},{7,6},{8,9},{9,8},{10,11... | collective-permute-start | bytes 786440 | tf_op jit(solution)/shard_map/ppermute | solution.py:26
  113.4 56.3 %collective-permute-start.17 = (f32[512]{0:T(512)S(1)}, f32[512]{0:T(512)S(1)}, u32[]{:S(2)}, u32[]{:S(2)}) collective-permute-start(f32[512]{0:T(512)S(1)} %add_rsqrt_fusion), channel_id=1, source_target_pairs={{0,8},{4,12},{8,0},{12,4},{1,9},{5,13},{9,1},{13,5},{2,10},{6,14},... | collective-permute-start | bytes 6152 | tf_op jit(solution)/shard_map/ppermute | solution.py:178
  115.2 54.5 %collective-permute-start.20 = (f32[512]{0:T(512)S(1)}, f32[512]{0:T(512)S(1)}, u32[]{:S(2)}, u32[]{:S(2)}) collective-permute-start(f32[512]{0:T(512)S(1)} %add_rsqrt_fusion), channel_id=1, source_target_pairs={{0,12},{4,0},{8,4},{12,8},{1,13},{5,1},{9,5},{13,9},{2,14},{6,2},{... | collective-permute-start | bytes 6152 | tf_op jit(solution)/shard_map/ppermute | solution.py:178
  121.4 48.2 %collective-permute-start.19 = (bf16[256,1024]{1,0:T(8,128)(2,1)}, bf16[256,1024]{1,0:T(8,128)(2,1)}, u32[]{:S(2)}, u32[]{:S(2)}) collective-permute-start(bf16[256,1024]{1,0:T(8,128)(2,1)} %get-tuple-element.23), channel_id=1, source_target_pairs={{0,12},{4,0},{8,4},{12,8},{1,13},{5,1},{9,5},{13,9},{2,14},{6,2},{... | collective-permute-start | bytes 1572872 | tf_op jit(solution)/shard_map/ppermute | solution.py:178
  123.2 45.9 %collective-permute-start.16 = (bf16[256,1024]{1,0:T(8,128)(2,1)}, bf16[256,1024]{1,0:T(8,128)(2,1)}, u32[]{:S(2)}, u32[]{:S(2)}) collective-permute-start(bf16[256,1024]{1,0:T(8,128)(2,1)} %get-tuple-element.24), channel_id=1, source_target_pairs={{0,8},{4,12},{8,0},{12,4},{1,9},{5,13},{9,1},{13,5},{2,10},{6,14},... | collective-permute-start | bytes 1572872 | tf_op jit(solution)/shard_map/ppermute | solution.py:178
  132.0 5.9 %slice-start = ((s8[8388608]{0:T(1024)(128)(4,1)}), s8[4194304]{0:T(1024)(128)(4,1)S(1)}, s32[]{:S(2)}) async-start(s8[8388608]{0:T(1024)(128)(4,1)} %bitcast.163), calls=%async_computation.1 | async-start | bytes 8388608
  135.9 33.2 %collective-permute-start.13 = (bf16[256,1024]{1,0:T(8,128)(2,1)S(1)}, bf16[256,1024]{1,0:T(8,128)(2,1)S(1)}, u32[]{:S(2)}, u32[]{:S(2)}) collective-permute-start(bf16[256,1024]{1,0:T(8,128)(2,1)S(1)} %copy-done.11), channel_id=1, source_target_pairs={{0,4},{4,8},{8,12},{12,0},{1,5},{5,9},{9,13},{13,1},{2,6},{6,10},{... | collective-permute-start | bytes 1572872 | tf_op jit(solution)/shard_map/ppermute | solution.py:178
  138.0 31.8 %dynamic-slice-start = ((f32[4096]{0:T(1024)}, s32[]{:T(128)}), f32[1024]{0:T(1024)S(1)}, s32[]{:S(2)}) async-start(f32[4096]{0:T(1024)} %param.7, s32[]{:T(128)} %select_n.367), calls=%async_computation.3 | async-start | bytes 8704 | tf_op jit(solution)/shard_map/dynamic_slice | solution.py:170
  169.1 7.2 %collective-permute-start.18 = (bf16[256,1024]{1,0:T(8,128)(2,1)}, bf16[256,1024]{1,0:T(8,128)(2,1)S(1)}, u32[]{:S(2)}, u32[]{:S(2)}) collective-permute-start(bf16[256,1024]{1,0:T(8,128)(2,1)} %collective-permute-done.16), channel_id=1, source_target_pairs={{0,1},{1,0},{2,3},{3,2},{4,5},{5,4},{6,7},{7,6},{8,9},{9,8},{10,11... | collective-permute-start | bytes 1572872 | tf_op jit(solution)/shard_map/ppermute | solution.py:26
  169.1 8.8 %collective-permute-start.15 = (bf16[256,1024]{1,0:T(8,128)(2,1)S(1)}, bf16[256,1024]{1,0:T(8,128)(2,1)S(1)}, u32[]{:S(2)}, u32[]{:S(2)}) collective-permute-start(bf16[256,1024]{1,0:T(8,128)(2,1)S(1)} %collective-permute-done.13), channel_id=1, source_target_pairs={{0,1},{1,0},{2,3},{3,2},{4,5},{5,4},{6,7},{7,6},{8,9},{9,8},{10,11... | collective-permute-start | bytes 1572872 | tf_op jit(solution)/shard_map/ppermute | solution.py:26
  169.6 9.0 %collective-permute-start.21 = (bf16[256,1024]{1,0:T(8,128)(2,1)}, bf16[256,1024]{1,0:T(8,128)(2,1)}, u32[]{:S(2)}, u32[]{:S(2)}) collective-permute-start(bf16[256,1024]{1,0:T(8,128)(2,1)} %collective-permute-done.19), channel_id=1, source_target_pairs={{0,1},{1,0},{2,3},{3,2},{4,5},{5,4},{6,7},{7,6},{8,9},{9,8},{10,11... | collective-permute-start | bytes 1572872 | tf_op jit(solution)/shard_map/ppermute | solution.py:26
  (10 other events, 32.8 us)
Sparse Core Ops, SparseCore 0:
  10.4 104.9 all-gather.1

commit v6 on v2

--- a/solution.py
+++ b/solution.py
@@ -79,7 +79,8 @@
     gathered = jnp.concatenate(blocks, axis=1)
     widened = gathered.astype(jnp.float32)
     mean_square = jnp.mean(widened * widened, axis=-1, keepdims=True)
-    normed = (widened * lax.rsqrt(mean_square + 1e-05) * norm_gain).astype(jnp.bfloat16)
+    row_scale = lax.rsqrt(mean_square + 1e-05)[:, 0]
+    normed = (widened * row_scale[:, None] * norm_gain).astype(jnp.bfloat16)
     row_count = normed.shape[0]
     block_len = row_count // 2
     width = normed.shape[1]
@@ -95,6 +96,40 @@
     ).astype(jnp.bfloat16)
     sub_count = lax.axis_size("sub")
     sub_index = lax.axis_index("sub")
+    tile_count = lax.axis_size("kvh") * lax.axis_size("sub")
+    tile_cols = width // tile_count
+    owner_index = lax.axis_index("kvh") * lax.axis_size("sub") + lax.axis_index("sub")
+    owned = lax.dynamic_slice_in_dim(normed, owner_index * tile_cols, tile_cols, 1)
+    seq_count = lax.axis_size("seq")
+    band = width // seq_count
+    inverse_count = 1.0 / (row_count * seq_count)
+    share = row_count // sub_count
+    raw_parts = [tokens]
+    for shift in range(1, seq_count):
+        route = [(j, (j + shift) % seq_count) for j in range(seq_count)]
+        raw_parts.append(lax.ppermute(tokens, "seq", route))
+    column_gain = lax.dynamic_slice_in_dim(norm_gain, owner_index * tile_cols, tile_cols, 0)
+    mine = lax.dynamic_slice_in_dim(normed, seq_index * band, band, 1)
+    gram_sum = jnp.einsum("tc,tr->cr", mine, owned, preferred_element_type=jnp.float32)
+    my_rows = lax.dynamic_slice_in_dim(normed, sub_index * share, share, 0)
+    for shift in range(1, seq_count):
+        target = (seq_index + shift) % seq_count
+        outgoing = lax.dynamic_slice_in_dim(my_rows, target * band, band, 1)
+        route = [(j, (j + shift) % seq_count) for j in range(seq_count)]
+        incoming, their_scale = lax.ppermute((outgoing, row_scale), "seq", route)
+        halves = swap_halves(incoming, sub_count, sub_index)
+        source = (seq_index - shift) % seq_count
+        their_raw = raw_parts[shift]
+        their_owned = (
+            their_raw.astype(jnp.float32) * their_scale[:, None] * column_gain
+        ).astype(jnp.bfloat16)
+        for lane_shift in range(sub_count):
+            half_at = (sub_index - lane_shift) % sub_count
+            their_rows = lax.dynamic_slice_in_dim(their_owned, half_at * share, share, 0)
+            gram_sum = gram_sum + jnp.einsum(
+                "tc,tr->cr", halves[lane_shift], their_rows, preferred_element_type=jnp.float32
+            )
+    gram_sum = gram_sum * inverse_count
     row_share = w_key.shape[0]
     key_more = None
     value_more = None
@@ -157,21 +192,6 @@
         running_max = new_max
     attended = (accum / jnp.transpose(total, (2, 0, 1))[..., None]).astype(jnp.bfloat16)
     attended = attended.reshape(row_count, local_groups, per_group * head_size)
-    tile_count = lax.axis_size("kvh") * lax.axis_size("sub")
-    tile_cols = width // tile_count
-    owner_index = lax.axis_index("kvh") * lax.axis_size("sub") + lax.axis_index("sub")
-    owned = lax.dynamic_slice_in_dim(normed, owner_index * tile_cols, tile_cols, 1)
-    seq_count = lax.axis_size("seq")
-    inverse_count = 1.0 / (row_count * seq_count)
-    gram_sum = lax.psum_scatter(
-        (
-            jnp.einsum("tc,tr->cr", normed, owned, preferred_element_type=jnp.float32)
-            * inverse_count
-        ).astype(jnp.bfloat16),
-        "seq",
-        scatter_dimension=0,
-        tiled=True,
-    ).astype(jnp.float32)
     gram_tile = gram_sum
     return (attended, gram_tile)
 

time: 229 us -> 197 us (0.86)
  waiting for transfers between devices: 116 us -> 29.9 us
  starting transfers between devices: 9.69 us -> 59.1 us
  between operations: 14.4 us -> 1.26 us
  local copies, waits for them, and re-layouts: 34.9 us -> 43.2 us
  matrix products: 32.6 us -> 40.3 us
    reduce_scatter x1 -> x0, waiting for transfers between devices: 69.6 us -> none  [body(): lax.psum_scatter((jnp.einsum('tc,tr->cr', normed, owned, preferred_elemen...]
    ppermute x0 -> x9, starting transfers between devices: none -> 33.1 us  [the longest x6 27.6 us: body(): incoming, their_scale = lax.ppermute((outgoing, row_scale), 'seq', route)]
    ppermute x4, starting transfers between devices: 4.95 us -> 21.2 us  [from_partner(): return lax.ppermute(block, axis, route)]
    ppermute x4, waiting for transfers between devices: 20.4 us -> 5.99 us  [from_partner(): return lax.ppermute(block, axis, route)]
    dot_general x1 -> x7, matrix products: 7 us -> 14.7 us  [the longest x6 11.4 us: body(): jnp.einsum('tc,tr->cr', halves[lane_shift], their_rows, preferred_element...]
    ppermute x0 -> x9, waiting for transfers between devices: none -> 7.35 us  [the longest x6 7.35 us: body(): incoming, their_scale = lax.ppermute((outgoing, row_scale), 'seq', route)]
    ppermute x1, waiting for transfers between devices: 23.4 us -> 16.5 us  [body(): across.append(lax.ppermute(tokens, 'kvh', route))]
    dynamic_update_slice x6, local copies, waits for them, and re-layouts: 6.85 us -> 10.6 us  [split_send(): lax.dynamic_update_slice_in_dim(full, whole[shift][n], source * share, 0)]
  transfers between devices with their start and end apart: 14 -> 25, of which waited for: 4 -> 4; matrix products, arithmetic and copies ran while one was open for 30% -> 51% of each run, Pallas kernels for 0% -> 0%
where the time goes in v6:
time: 197 us; the launch traced here: 196 us
  starting transfers between devices  59.1 us (30%)
  local copies, waits for them, and re-layouts  43.2 us (22%)
  matrix products  40.3 us (20%)
  waiting for transfers between devices  29.9 us (15%)
  other arithmetic  22.7 us (12%)
    ppermute x6, starting transfers between devices, body(): incoming, their_scale = lax.ppermute((outgoing, row_scale), 'seq', route)  27.6 us
    ppermute x4, starting transfers between devices, from_partner(): return lax.ppermute(block, axis, route)  21.2 us
    ppermute x1, waiting for transfers between devices, body(): across.append(lax.ppermute(tokens, 'kvh', route))  16.5 us
    unnamed x43, local copies, waits for them, and re-layouts  13.7 us
    dot_general x6, matrix products, body(): jnp.einsum('tc,tr->cr', halves[lane_shift], their_rows, preferred_element...  11.4 us
    dynamic_update_slice x6, local copies, waits for them, and re-layouts, split_send(): lax.dynamic_update_slice_in_dim(full, whole[shift][n], source * share, 0)  10.6 us
    ppermute x6, waiting for transfers between devices, body(): incoming, their_scale = lax.ppermute((outgoing, row_scale), 'seq', route)  7.35 us
    dot_general x1, matrix products, body(): jnp.einsum('td,dgc->tgc', normed, w_query, preferred_element_type=jnp.flo...  7.06 us
  transfers between devices with their start and end apart: 25, of which 4 were waited for; matrix products, arithmetic and copies ran while one was open for 51% of the time, Pallas kernels for 0%

profile of v6, /device:TPU:0, one launch (start us, length us, event | category | flops | bytes accessed | tf_op | source)
XLA Modules:
  0.0 196.3 jit_solution(13602200477281479326)
XLA Ops:
  0.6 3.0 %collective-permute-start.1 = (bf16[512,1024]{1,0:T(8,128)(2,1)}, bf16[512,1024]{1,0:T(8,128)(2,1)}, u32[]{:S(2)}, u32[]{:S(2)}) collective-permute-start(bf16[512,1024]{1,0:T(8,128)(2,1)} %param.6), channel_id=1, source_target_pairs={{0,2},{2,0},{1,3},{3,1},{4,6},{6,4},{5,7},{7,5},{8,10},{10,8},{9,1... | collective-permute-start | bytes 3145736 | tf_op jit(solution)/shard_map/ppermute | solution.py:70
  5.3 2.6 %collective-permute-start.18 = (bf16[512,1024]{1,0:T(8,128)(2,1)}, bf16[512,1024]{1,0:T(8,128)(2,1)}, u32[]{:S(2)}, u32[]{:S(2)}) collective-permute-start(bf16[512,1024]{1,0:T(8,128)(2,1)} %param.6), channel_id=1, source_target_pairs={{0,8},{4,12},{8,0},{12,4},{1,9},{5,13},{9,1},{13,5},{2,10},{6,14},... | collective-permute-start | bytes 3145736 | tf_op jit(solution)/shard_map/ppermute | solution.py:110
  10.6 16.5 %collective-permute-done.1 = bf16[512,1024]{1,0:T(8,128)(2,1)} collective-permute-done((bf16[512,1024]{1,0:T(8,128)(2,1)}, bf16[512,1024]{1,0:T(8,128)(2,1)}, u32[]{:S(2)}, u32[]{:S(2)}) %collective-permute-start.1) | collective-permute-done | bytes 1048608 | tf_op jit(solution)/shard_map/ppermute | solution.py:70
  28.6 3.3 %copy.58 = bf16[2048,4,128]{2,0,1:T(8,128)(2,1)} copy(bf16[2048,4,128]{2,1,0:T(4,128)(2,1)} %param.10) | data formatting | bytes 4194304 | tf_op args[4]
  31.9 2.7 %copy.60 = bf16[2048,4,128]{0,2,1:T(8,128)(2,1)} copy(bf16[2048,4,128]{2,1,0:T(4,128)(2,1)S(1)} %copy-done.7) | data formatting | bytes 4194304 | tf_op args[3]
  41.7 2.1 %select_select_fusion.3 = (bf16[512,1024]{1,0:T(8,128)(2,1)S(1)}, bf16[512,1024]{1,0:T(8,128)(2,1)S(1)}, bf16[512,1024]{1,0:T(8,128)(2,1)S(1)}, bf16[512,1024]{1,0:T(8,128)(2,1)S(1)}) fusion(bf16[512,1024]{1,0:T(8,128)(2,1)} %collective-permute-done.1, bf16[512,1024]{1,0:T(8,128)(2,1)} %collective-permute-done.2, bf16[512,1024]{1,0:T(8,128)(2,1)S(1)} %copy-done.10, ...), kind=kLoop, calls=%fused_computation.75 | loop fusion | flops 6291456 | bytes 8388620 | tf_op jit(solution)/shard_map/select_n | solution.py:78
  47.8 1.9 collective-permute-start.15
  50.9 2.1 %fusion.51 = bf16[512,4,128]{2,0,1:T(8,128)(2,1)} fusion(f32[512,4,128]{2,0,1:T(8,128)S(1)} %fusion.29, bf16[512,4096]{1,0:T(8,128)(2,1)S(1)} %fusion.2, s32[]{:T(128)S(6)} %select_n.333, bf16[2048,4,128]{2,1,0:T(4,128)(2,1)S(1)} %copy-done.8), kind=kOutput, calls=%fused_computation.62 | convolution fusion | flops 1074266112 | bytes 5767172 | tf_op jit(solution)/shard_map/td,dgh->tgh/dot_general | solution.py:145
  53.0 2.6 %collective-permute-start.19 = (f32[512]{0:T(512)S(1)}, f32[512]{0:T(512)S(1)}, u32[]{:S(2)}, u32[]{:S(2)}) collective-permute-start(f32[512]{0:T(512)S(1)} %add_rsqrt_fusion), channel_id=1, source_target_pairs={{0,8},{4,12},{8,0},{12,4},{1,9},{5,13},{9,1},{13,5},{2,10},{6,14},... | collective-permute-start | bytes 6152 | tf_op jit(solution)/shard_map/ppermute | solution.py:119
  58.0 7.1 %fusion.3 = f32[512,4,256]{0,2,1:T(8,128)S(1)} fusion(bf16[4096,4,256]{2,1,0:T(4,128)(2,1)} %param.8, bf16[512,4096]{1,0:T(8,128)(2,1)S(1)} %fusion.2), kind=kOutput, calls=%fused_computation.6 | convolution fusion | flops 4294967296 | bytes 14680064 | tf_op jit(solution)/shard_map/td,dgc->tgc/dot_general | solution.py:93
  65.3 1.9 copy.105
  67.3 2.0 copy.104
  69.2 2.9 %subtract_convert_fusion = (bf16[512,4,2,64]{3,0,2,1:T(8,128)(2,1)S(1)}, bf16[512,4,2,64]{3,0,2,1:T(8,128)(2,1)S(1)}) fusion(f32[512,4,2,64]{3,0,2,1:T(8,128)} %copy.105, f32[512,4,2,64]{3,0,2,1:T(8,128)} %copy.104, f32[512,64]{1,0:T(8,128)} %copy.66, f32[512,64]{1,0:T(8,128)} %copy.64), kind=kLoop, calls=%fused_computation.49 | loop fusion | flops 2097152 | bytes 3407872 | tf_op jit(solution)/shard_map/convert.4
  72.2 2.3 %fusion.7 = (f32[4,2,512]{2,1,0:T(2,128)S(1)}, f32[4,512,512,2]{2,1,3,0:T(8,128)S(1)}) fusion(pred[512,512]{0,1:T(8,128)(4,1)S(1)} %fusion.61, bf16[512,4,2,64]{3,0,2,1:T(8,128)(2,1)S(1)} %get-tuple-element.14, bf16[512,4,2,64]{3,0,2,1:T(8,128)(2,1)S(1)} %get-tuple-element.13, bf16[512,4,64]{0,2,1:T(8,128)(2,1)S(1)} %copy-done.11, ...), kind=kOutput, calls=%fused_computation.11 | convolution fusion | flops 546304000 | bytes 10240000 | tf_op jit(solution)/shard_map/tgrh,ugh->grtu/dot_general | solution.py:153
  74.6 2.6 %fusion.115 = (bf16[256,1024]{1,0:T(8,128)(2,1)}, bf16[256,1024]{1,0:T(8,128)(2,1)}, bf16[256,1024]{1,0:T(8,128)(2,1)}) fusion(bf16[512,4096]{1,0:T(8,128)(2,1)S(1)} %copy-done.2, s32[]{:T(128)S(6)} %select_n.347, s32[]{:T(128)S(6)} %select_n.350, s32[]{:T(128)S(6)} %select_n.356, s32[]{:T(128)S(6)} %select_n.353), kind=kLoop, calls=%fused_computation.168 | loop fusion | bytes 3145744 | tf_op jit(solution)/shard_map/dynamic_slice | solution.py:117
  78.5 3.3 %fusion.58 = f32[1024,1024]{1,0:T(8,128)} fusion(bf16[512,4096]{1,0:T(8,128)(2,1)S(1)} %copy-done.2, s32[]{:T(128)} %select_n.346, s32[]{:T(128)S(6)} %select_n.345), kind=kOutput, calls=%fused_computation.68 | convolution fusion | flops 1073741824 | bytes 6291464 | tf_op jit(solution)/shard_map/tc,tr->cr/dot_general | solution.py:113
  86.1 20.7 %collective-permute-start.7 = (bf16[256,4,128]{2,0,1:T(8,128)(2,1)}, bf16[256,4,128]{2,0,1:T(8,128)(2,1)}, u32[]{:S(2)}, u32[]{:S(2)}) collective-permute-start(bf16[256,4,128]{2,0,1:T(8,128)(2,1)} %constant_dynamic-slice_fusion.1), channel_id=1, source_target_pairs={{0,4},{4,0},{8,12},{12,8},{1,5},{5,1},{9,13},{13,9},{2,6},{6,2},{1... | collective-permute-start | bytes 786440 | tf_op jit(solution)/shard_map/ppermute | solution.py:18
  106.9 4.2 %collective-permute-start.21 = (bf16[256,1024]{1,0:T(8,128)(2,1)}, bf16[256,1024]{1,0:T(8,128)(2,1)}, u32[]{:S(2)}, u32[]{:S(2)}) collective-permute-start(bf16[256,1024]{1,0:T(8,128)(2,1)} %get-tuple-element.20), channel_id=1, source_target_pairs={{0,12},{4,0},{8,4},{12,8},{1,13},{5,1},{9,5},{13,9},{2,14},{6,2},{... | collective-permute-start | bytes 1572872 | tf_op jit(solution)/shard_map/ppermute | solution.py:119
  111.2 4.0 %multiply_convert_fusion.2 = (bf16[512,1024]{1,0:T(8,128)(2,1)}, bf16[512,1024]{1,0:T(8,128)(2,1)}, bf16[512,1024]{1,0:T(8,128)(2,1)S(1)}) fusion(bf16[512,1024]{1,0:T(8,128)(2,1)} %collective-permute-done.14, f32[1024]{0:T(1024)S(1)} %dynamic-slice-done, f32[512]{0:T(512)S(1)} %collective-permute-done.15, f32[512]{0:T(512)S(1)} %collective-permute-done.19, ...), kind=kLoop, calls=%fused_computation.47 | loop fusion | flops 6291456 | bytes 6301696 | tf_op jit(solution)/shard_map/convert_element_type | solution.py:125
  115.2 4.3 %collective-permute-done.9 = bf16[256,4,128]{0,2,1:T(8,128)(2,1)} collective-permute-done((bf16[256,4,128]{0,2,1:T(8,128)(2,1)}, bf16[256,4,128]{0,2,1:T(8,128)(2,1)}, u32[]{:S(2)}, u32[]{:S(2)}) %collective-permute-start.9) | collective-permute-done | bytes 262176 | tf_op jit(solution)/shard_map/ppermute | solution.py:18
  133.0 15.0 %collective-permute-start.17 = (bf16[256,1024]{1,0:T(8,128)(2,1)}, bf16[256,1024]{1,0:T(8,128)(2,1)}, u32[]{:S(2)}, u32[]{:S(2)}) collective-permute-start(bf16[256,1024]{1,0:T(8,128)(2,1)} %get-tuple-element.21), channel_id=1, source_target_pairs={{0,8},{4,12},{8,0},{12,4},{1,9},{5,13},{9,1},{13,5},{2,10},{6,14},... | collective-permute-start | bytes 1572872 | tf_op jit(solution)/shard_map/ppermute | solution.py:119
  150.5 2.5 %collective-permute-start.13 = (bf16[256,1024]{1,0:T(8,128)(2,1)}, bf16[256,1024]{1,0:T(8,128)(2,1)}, u32[]{:S(2)}, u32[]{:S(2)}) collective-permute-start(bf16[256,1024]{1,0:T(8,128)(2,1)} %get-tuple-element.19), channel_id=1, source_target_pairs={{0,4},{4,8},{8,12},{12,0},{1,5},{5,9},{9,13},{13,1},{2,6},{6,10},{... | collective-permute-start | bytes 1572872 | tf_op jit(solution)/shard_map/ppermute | solution.py:119
  156.6 2.0 constant_dynamic-update-slice_fusion
  158.6 2.2 %bitcast_reduce_fusion = (f32[4,2,2,256]{3,1,2,0:T(2,128)S(1)}, f32[4,2,256,256,2]{3,2,4,1,0:T(8,128)S(1)}) fusion(f32[2,256]{1,0:T(2,128)S(1)} %add.291, bf16[2,256,4,128,1]{3,1,4,0,2:T(8,128)(2,1)} %bitcast.33, bf16[2,256,4,2,64]{4,1,0,3,2:T(8,128)(2,1)S(1)} %bitcast.161, bf16[2,256,4,2,64]{4,1,0,3,2:T(8,128)(2,1)S(1)} %bitcast.159), kind=kOutput, calls=%fused_computation.15 | convolution fusion | flops 273674240 | bytes 5785600 | tf_op jit(solution)/shard_map/jtgrh,jugh->grjtu/dot_general | solution.py:173
  160.8 1.9 constant_dynamic-update-slice_fusion.4
  162.7 2.2 %bitcast_reduce_fusion.1 = (f32[4,2,2,256]{3,1,2,0:T(2,128)S(1)}, f32[4,2,256,256,2]{3,2,4,1,0:T(8,128)S(1)}) fusion(f32[2,256]{1,0:T(2,128)S(1)} %add.286, bf16[2,256,4,128,1]{3,1,4,0,2:T(8,128)(2,1)} %bitcast.18, bf16[2,256,4,2,64]{4,1,0,3,2:T(8,128)(2,1)S(1)} %bitcast.162, bf16[2,256,4,2,64]{4,1,0,3,2:T(8,128)(2,1)S(1)} %bitcast.160), kind=kOutput, calls=%fused_computation.18 | convolution fusion | flops 273674240 | bytes 5785600 | tf_op jit(solution)/shard_map/jtgrh,jugh->grjtu/dot_general | solution.py:173
  168.7 1.8 fusion.42
  171.6 2.5 %fusion.33 = bf16[512,4,2,128]{0,3,2,1:T(8,128)(2,1)S(1)} fusion(f32[512,4,2,128]{0,3,2,1:T(8,128)S(1)} %bitcast.166, f32[512,4,2,128]{0,3,2,1:T(8,128)S(1)} %bitcast.167, f32[4,512,512,2]{2,1,3,0:T(8,128)S(1)} %bitcast.164, f32[4,2,512]{2,1,0:T(2,128)S(1)} %get-tuple-element.46, pred[512,512]{0,1:T(8,128)(4,1)S(1)} %fusion.61, ...), kind=kOutput, calls=%fused_computation.50 | convolution fusion | flops 548405248 | bytes 14483456 | tf_op jit(solution)/shard_map/grtu,ugh->tgrh/dot_general | solution.py:163
  175.5 7.3 %collective-permute-done.17 = bf16[256,1024]{1,0:T(8,128)(2,1)} collective-permute-done((bf16[256,1024]{1,0:T(8,128)(2,1)}, bf16[256,1024]{1,0:T(8,128)(2,1)}, u32[]{:S(2)}, u32[]{:S(2)}) %collective-permute-start.17) | collective-permute-done | bytes 524320 | tf_op jit(solution)/shard_map/ppermute | solution.py:119
  185.2 1.9 fusion.77
  187.1 1.8 fusion.81
  191.8 4.5 %add_multiply_fusion = f32[1024,1024]{1,0:T(8,128)} fusion(f32[1024,1024]{1,0:T(8,128)S(1)} %fusion.73, f32[1024,1024]{1,0:T(8,128)S(1)} %fusion.75, f32[1024,1024]{1,0:T(8,128)S(1)} %fusion.77, f32[1024,1024]{1,0:T(8,128)S(1)} %fusion.79, f32[1024,1024]{1,0:T(8,128)S(1)} %copy-done, f32[1024,1024]{1,0:T(8,128)S(1)} %fusion.81, ...), kind=kOutput, calls=%fused_computation.21 | convolution fusion | flops 544210944 | bytes 30408708 | tf_op jit(solution)/shard_map/tc,tr->cr/dot_general | solution.py:129
  (133 shorter events, 57.5 us)
Async XLA Ops:
  0.6 31.3 %copy-start.7 = (bf16[2048,4,128]{2,1,0:T(4,128)(2,1)S(1)}, bf16[2048,4,128]{2,1,0:T(4,128)(2,1)}, u32[]{:S(2)}) copy-start(bf16[2048,4,128]{2,1,0:T(4,128)(2,1)} %param.9) | copy-start | bytes 6291460
  0.6 26.5 %collective-permute-start.1 = (bf16[512,1024]{1,0:T(8,128)(2,1)}, bf16[512,1024]{1,0:T(8,128)(2,1)}, u32[]{:S(2)}, u32[]{:S(2)}) collective-permute-start(bf16[512,1024]{1,0:T(8,128)(2,1)} %param.6), channel_id=1, source_target_pairs={{0,2},{2,0},{1,3},{3,1},{4,6},{6,4},{5,7},{7,5},{8,10},{10,8},{9,1... | collective-permute-start | bytes 3145736 | tf_op jit(solution)/shard_map/ppermute | solution.py:70
  3.7 37.5 %collective-permute-start = (bf16[512,1024]{1,0:T(8,128)(2,1)}, bf16[512,1024]{1,0:T(8,128)(2,1)}, u32[]{:S(2)}, u32[]{:S(2)}) collective-permute-start(bf16[512,1024]{1,0:T(8,128)(2,1)} %param.6), channel_id=1, source_target_pairs={{0,1},{1,0},{2,3},{3,2},{4,5},{5,4},{6,7},{7,6},{8,9},{9,8},{10,11... | collective-permute-start | bytes 3145736 | tf_op jit(solution)/shard_map/ppermute | solution.py:26
  3.7 79.9 %collective-permute-start.14 = (bf16[512,1024]{1,0:T(8,128)(2,1)}, bf16[512,1024]{1,0:T(8,128)(2,1)}, u32[]{:S(2)}, u32[]{:S(2)}) collective-permute-start(bf16[512,1024]{1,0:T(8,128)(2,1)} %param.6), channel_id=1, source_target_pairs={{0,4},{4,8},{8,12},{12,0},{1,5},{5,9},{9,13},{13,1},{2,6},{6,10},{... | collective-permute-start | bytes 3145736 | tf_op jit(solution)/shard_map/ppermute | solution.py:110
  5.3 80.4 %collective-permute-start.18 = (bf16[512,1024]{1,0:T(8,128)(2,1)}, bf16[512,1024]{1,0:T(8,128)(2,1)}, u32[]{:S(2)}, u32[]{:S(2)}) collective-permute-start(bf16[512,1024]{1,0:T(8,128)(2,1)} %param.6), channel_id=1, source_target_pairs={{0,8},{4,12},{8,0},{12,4},{1,9},{5,13},{9,1},{13,5},{2,10},{6,14},... | collective-permute-start | bytes 3145736 | tf_op jit(solution)/shard_map/ppermute | solution.py:110
  7.8 78.2 %collective-permute-start.22 = (bf16[512,1024]{1,0:T(8,128)(2,1)}, bf16[512,1024]{1,0:T(8,128)(2,1)}, u32[]{:S(2)}, u32[]{:S(2)}) collective-permute-start(bf16[512,1024]{1,0:T(8,128)(2,1)} %param.6), channel_id=1, source_target_pairs={{0,12},{4,0},{8,4},{12,8},{1,13},{5,1},{9,5},{13,9},{2,14},{6,2},{... | collective-permute-start | bytes 3145736 | tf_op jit(solution)/shard_map/ppermute | solution.py:110
  27.1 14.4 %collective-permute-start.2 = (bf16[512,1024]{1,0:T(8,128)(2,1)}, bf16[512,1024]{1,0:T(8,128)(2,1)}, u32[]{:S(2)}, u32[]{:S(2)}) collective-permute-start(bf16[512,1024]{1,0:T(8,128)(2,1)} %collective-permute-done.1), channel_id=1, source_target_pairs={{0,1},{1,0},{2,3},{3,2},{4,5},{5,4},{6,7},{7,6},{8,9},{9,8},{10,11... | collective-permute-start | bytes 3145736 | tf_op jit(solution)/shard_map/ppermute | solution.py:26
  28.6 13.1 %copy-start.10 = (bf16[512,1024]{1,0:T(8,128)(2,1)S(1)}, bf16[512,1024]{1,0:T(8,128)(2,1)}, u32[]{:S(2)}) copy-start(bf16[512,1024]{1,0:T(8,128)(2,1)} %param.6) | copy-start | bytes 3145732
  41.2 6.6 %collective-permute-start.3 = (bf16[2048,4,128]{2,0,1:T(8,128)(2,1)}, bf16[2048,4,128]{2,0,1:T(8,128)(2,1)S(1)}, u32[]{:S(2)}, u32[]{:S(2)}) collective-permute-start(bf16[2048,4,128]{2,0,1:T(8,128)(2,1)} %copy.58), channel_id=1, source_target_pairs={{0,1},{1,0},{2,3},{3,2},{4,5},{5,4},{6,7},{7,6},{8,9},{9,8},{10,11... | collective-permute-start | bytes 6291464 | tf_op jit(solution)/shard_map/ppermute | solution.py:141
  41.6 11.4 %collective-permute-start.4 = (bf16[2048,4,128]{0,2,1:T(8,128)(2,1)}, bf16[2048,4,128]{0,2,1:T(8,128)(2,1)S(1)}, u32[]{:S(2)}, u32[]{:S(2)}) collective-permute-start(bf16[2048,4,128]{0,2,1:T(8,128)(2,1)} %copy.60), channel_id=1, source_target_pairs={{0,1},{1,0},{2,3},{3,2},{4,5},{5,4},{6,7},{7,6},{8,9},{9,8},{10,11... | collective-permute-start | bytes 6291464 | tf_op jit(solution)/shard_map/ppermute | solution.py:141
  46.3 11.8 %copy-start.1 = (bf16[512,4096]{1,0:T(8,128)(2,1)}, bf16[512,4096]{1,0:T(8,128)(2,1)S(1)}, u32[]{:S(2)}) copy-start(bf16[512,4096]{1,0:T(8,128)(2,1)S(1)} %fusion.2) | copy-start | bytes 12582916
  47.8 59.0 %collective-permute-start.15 = (f32[512]{0:T(512)S(1)}, f32[512]{0:T(512)S(1)}, u32[]{:S(2)}, u32[]{:S(2)}) collective-permute-start(f32[512]{0:T(512)S(1)} %add_rsqrt_fusion), channel_id=1, source_target_pairs={{0,4},{4,8},{8,12},{12,0},{1,5},{5,9},{9,13},{13,1},{2,6},{6,10},{... | collective-permute-start | bytes 6152 | tf_op jit(solution)/shard_map/ppermute | solution.py:119
  53.0 53.8 %collective-permute-start.19 = (f32[512]{0:T(512)S(1)}, f32[512]{0:T(512)S(1)}, u32[]{:S(2)}, u32[]{:S(2)}) collective-permute-start(f32[512]{0:T(512)S(1)} %add_rsqrt_fusion), channel_id=1, source_target_pairs={{0,8},{4,12},{8,0},{12,4},{1,9},{5,13},{9,1},{13,5},{2,10},{6,14},... | collective-permute-start | bytes 6152 | tf_op jit(solution)/shard_map/ppermute | solution.py:119
  74.6 7.2 %copy-start.3 = (f32[4,512,512,2]{2,1,3,0:T(8,128)}, f32[4,512,512,2]{2,1,3,0:T(8,128)S(1)}, u32[]{:S(2)}) copy-start(f32[4,512,512,2]{2,1,3,0:T(8,128)S(1)} %get-tuple-element.47) | copy-start | bytes 25165828
  81.8 29.4 %dynamic-slice-start = ((f32[4096]{0:T(1024)}, s32[]{:T(128)}), f32[1024]{0:T(1024)S(1)}, s32[]{:S(2)}) async-start(f32[4096]{0:T(1024)} %param.7, s32[]{:T(128)} %select_n.346), calls=%async_computation.2 | async-start | bytes 8704 | tf_op jit(solution)/shard_map/dynamic_slice | solution.py:111
  83.6 23.4 %collective-permute-start.23 = (f32[512]{0:T(512)S(1)}, f32[512]{0:T(512)S(1)}, u32[]{:S(2)}, u32[]{:S(2)}) collective-permute-start(f32[512]{0:T(512)S(1)} %add_rsqrt_fusion), channel_id=1, source_target_pairs={{0,12},{4,0},{8,4},{12,8},{1,13},{5,1},{9,5},{13,9},{2,14},{6,2},{... | collective-permute-start | bytes 6152 | tf_op jit(solution)/shard_map/ppermute | solution.py:119
  85.7 41.6 %collective-permute-start.11 = (bf16[256,4,128]{2,0,1:T(8,128)(2,1)}, bf16[256,4,128]{2,0,1:T(8,128)(2,1)}, u32[]{:S(2)}, u32[]{:S(2)}) collective-permute-start(bf16[256,4,128]{2,0,1:T(8,128)(2,1)} %constant_dynamic-slice_fusion.1), channel_id=1, source_target_pairs={{0,8},{8,0},{4,12},{12,4},{1,9},{9,1},{5,13},{13,5},{2,10},{10,2},... | collective-permute-start | bytes 786440 | tf_op jit(solution)/shard_map/ppermute | solution.py:18
  86.1 46.9 %collective-permute-start.7 = (bf16[256,4,128]{2,0,1:T(8,128)(2,1)}, bf16[256,4,128]{2,0,1:T(8,128)(2,1)}, u32[]{:S(2)}, u32[]{:S(2)}) collective-permute-start(bf16[256,4,128]{2,0,1:T(8,128)(2,1)} %constant_dynamic-slice_fusion.1), channel_id=1, source_target_pairs={{0,4},{4,0},{8,12},{12,8},{1,5},{5,1},{9,13},{13,9},{2,6},{6,2},{1... | collective-permute-start | bytes 786440 | tf_op jit(solution)/shard_map/ppermute | solution.py:18
  106.8 12.7 %collective-permute-start.9 = (bf16[256,4,128]{0,2,1:T(8,128)(2,1)}, bf16[256,4,128]{0,2,1:T(8,128)(2,1)}, u32[]{:S(2)}, u32[]{:S(2)}) collective-permute-start(bf16[256,4,128]{0,2,1:T(8,128)(2,1)} %fusion.83), channel_id=1, source_target_pairs={{0,8},{8,0},{4,12},{12,4},{1,9},{9,1},{5,13},{13,5},{2,10},{10,2},... | collective-permute-start | bytes 786440 | tf_op jit(solution)/shard_map/ppermute | solution.py:18
  106.8 18.7 %collective-permute-start.5 = (bf16[256,4,128]{0,2,1:T(8,128)(2,1)}, bf16[256,4,128]{0,2,1:T(8,128)(2,1)}, u32[]{:S(2)}, u32[]{:S(2)}) collective-permute-start(bf16[256,4,128]{0,2,1:T(8,128)(2,1)} %fusion.83), channel_id=1, source_target_pairs={{0,4},{4,0},{8,12},{12,8},{1,5},{5,1},{9,13},{13,9},{2,6},{6,2},{1... | collective-permute-start | bytes 786440 | tf_op jit(solution)/shard_map/ppermute | solution.py:18
  106.9 75.9 %collective-permute-start.21 = (bf16[256,1024]{1,0:T(8,128)(2,1)}, bf16[256,1024]{1,0:T(8,128)(2,1)}, u32[]{:S(2)}, u32[]{:S(2)}) collective-permute-start(bf16[256,1024]{1,0:T(8,128)(2,1)} %get-tuple-element.20), channel_id=1, source_target_pairs={{0,12},{4,0},{8,4},{12,8},{1,13},{5,1},{9,5},{13,9},{2,14},{6,2},{... | collective-permute-start | bytes 1572872 | tf_op jit(solution)/shard_map/ppermute | solution.py:119
  115.2 68.1 %copy-start.4 = (bf16[512,1024]{1,0:T(8,128)(2,1)}, bf16[512,1024]{1,0:T(8,128)(2,1)S(1)}, u32[]{:S(2)}) copy-start(bf16[512,1024]{1,0:T(8,128)(2,1)S(1)} %get-tuple-element.32) | copy-start | bytes 3145732
  123.8 26.8 %collective-permute-start.10 = (bf16[256,4,128]{0,2,1:T(8,128)(2,1)}, bf16[256,4,128]{0,2,1:T(8,128)(2,1)}, u32[]{:S(2)}, u32[]{:S(2)}) collective-permute-start(bf16[256,4,128]{0,2,1:T(8,128)(2,1)} %collective-permute-done.9), channel_id=1, source_target_pairs={{0,1},{1,0},{2,3},{3,2},{4,5},{5,4},{6,7},{7,6},{8,9},{9,8},{10,11... | collective-permute-start | bytes 786440 | tf_op jit(solution)/shard_map/ppermute | solution.py:26
  127.3 27.5 %collective-permute-start.6 = (bf16[256,4,128]{0,2,1:T(8,128)(2,1)}, bf16[256,4,128]{0,2,1:T(8,128)(2,1)}, u32[]{:S(2)}, u32[]{:S(2)}) collective-permute-start(bf16[256,4,128]{0,2,1:T(8,128)(2,1)} %collective-permute-done.5), channel_id=1, source_target_pairs={{0,1},{1,0},{2,3},{3,2},{4,5},{5,4},{6,7},{7,6},{8,9},{9,8},{10,11... | collective-permute-start | bytes 786440 | tf_op jit(solution)/shard_map/ppermute | solution.py:26
  127.3 29.3 %collective-permute-start.12 = (bf16[256,4,128]{2,0,1:T(8,128)(2,1)}, bf16[256,4,128]{2,0,1:T(8,128)(2,1)}, u32[]{:S(2)}, u32[]{:S(2)}) collective-permute-start(bf16[256,4,128]{2,0,1:T(8,128)(2,1)} %collective-permute-done.11), channel_id=1, source_target_pairs={{0,1},{1,0},{2,3},{3,2},{4,5},{5,4},{6,7},{7,6},{8,9},{9,8},{10,11... | collective-permute-start | bytes 786440 | tf_op jit(solution)/shard_map/ppermute | solution.py:26
  133.0 49.9 %collective-permute-start.17 = (bf16[256,1024]{1,0:T(8,128)(2,1)}, bf16[256,1024]{1,0:T(8,128)(2,1)}, u32[]{:S(2)}, u32[]{:S(2)}) collective-permute-start(bf16[256,1024]{1,0:T(8,128)(2,1)} %get-tuple-element.21), channel_id=1, source_target_pairs={{0,8},{4,12},{8,0},{12,4},{1,9},{5,13},{9,1},{13,5},{2,10},{6,14},... | collective-permute-start | bytes 1572872 | tf_op jit(solution)/shard_map/ppermute | solution.py:119
  150.5 34.6 %collective-permute-start.13 = (bf16[256,1024]{1,0:T(8,128)(2,1)}, bf16[256,1024]{1,0:T(8,128)(2,1)}, u32[]{:S(2)}, u32[]{:S(2)}) collective-permute-start(bf16[256,1024]{1,0:T(8,128)(2,1)} %get-tuple-element.19), channel_id=1, source_target_pairs={{0,4},{4,8},{8,12},{12,0},{1,5},{5,9},{9,13},{13,1},{2,6},{6,10},{... | collective-permute-start | bytes 1572872 | tf_op jit(solution)/shard_map/ppermute | solution.py:119
  154.8 6.0 %collective-permute-start.8 = (bf16[256,4,128]{2,0,1:T(8,128)(2,1)}, bf16[256,4,128]{2,0,1:T(8,128)(2,1)}, u32[]{:S(2)}, u32[]{:S(2)}) collective-permute-start(bf16[256,4,128]{2,0,1:T(8,128)(2,1)} %collective-permute-done.7), channel_id=1, source_target_pairs={{0,1},{1,0},{2,3},{3,2},{4,5},{5,4},{6,7},{7,6},{8,9},{9,8},{10,11... | collective-permute-start | bytes 786440 | tf_op jit(solution)/shard_map/ppermute | solution.py:26
  175.5 9.7 %copy-start.6 = (bf16[512,1024]{1,0:T(8,128)(2,1)S(1)}, bf16[512,1024]{1,0:T(8,128)(2,1)}, u32[]{:S(2)}) copy-start(bf16[512,1024]{1,0:T(8,128)(2,1)} %get-tuple-element.31) | copy-start | bytes 3145732
  182.8 6.1 %collective-permute-start.20 = (bf16[256,1024]{1,0:T(8,128)(2,1)}, bf16[256,1024]{1,0:T(8,128)(2,1)S(1)}, u32[]{:S(2)}, u32[]{:S(2)}) collective-permute-start(bf16[256,1024]{1,0:T(8,128)(2,1)} %collective-permute-done.17), channel_id=1, source_target_pairs={{0,1},{1,0},{2,3},{3,2},{4,5},{5,4},{6,7},{7,6},{8,9},{9,8},{10,11... | collective-permute-start | bytes 1572872 | tf_op jit(solution)/shard_map/ppermute | solution.py:26
  182.8 7.6 %collective-permute-start.24 = (bf16[256,1024]{1,0:T(8,128)(2,1)}, bf16[256,1024]{1,0:T(8,128)(2,1)S(1)}, u32[]{:S(2)}, u32[]{:S(2)}) collective-permute-start(bf16[256,1024]{1,0:T(8,128)(2,1)} %collective-permute-done.21), channel_id=1, source_target_pairs={{0,1},{1,0},{2,3},{3,2},{4,5},{5,4},{6,7},{7,6},{8,9},{9,8},{10,11... | collective-permute-start | bytes 1572872 | tf_op jit(solution)/shard_map/ppermute | solution.py:26
  185.1 4.5 %collective-permute-start.16 = (bf16[256,1024]{1,0:T(8,128)(2,1)}, bf16[256,1024]{1,0:T(8,128)(2,1)S(1)}, u32[]{:S(2)}, u32[]{:S(2)}) collective-permute-start(bf16[256,1024]{1,0:T(8,128)(2,1)} %collective-permute-done.13), channel_id=1, source_target_pairs={{0,1},{1,0},{2,3},{3,2},{4,5},{5,4},{6,7},{7,6},{8,9},{9,8},{10,11... | collective-permute-start | bytes 1572872 | tf_op jit(solution)/shard_map/ppermute | solution.py:26
  (13 other events, 34.5 us)

commit v7 on v5

--- a/solution.py
+++ b/solution.py
@@ -104,7 +104,8 @@
             key_part, value_part = w_key, w_value
         else:
             route = [(j, (j + shift) % sub_count) for j in range(sub_count)]
-            key_part, value_part = lax.ppermute((w_key, w_value), "sub", route)
+            weight_pair = lax.ppermute(jnp.stack([w_key, w_value]), "sub", route)
+            key_part, value_part = weight_pair[0], weight_pair[1]
         source = (sub_index - shift) % sub_count
         rows = lax.dynamic_slice_in_dim(normed, source * row_share, row_share, 1)
         key_step = jnp.einsum("td,dgh->tgh", rows, key_part, preferred_element_type=jnp.float32)
@@ -131,7 +132,9 @@
     )
     query_pairs = queries.reshape(2, block_len, local_groups, per_group, head_size)
     for section in range(1, lax.axis_size("seq").bit_length()):
-        far_keys, far_values = split_send((keys, values), "seq", section - 1)
+        (far_pair,) = split_send((jnp.stack([keys, values]).swapaxes(0, 1),), "seq", section - 1)
+        far_keys = far_pair[:, 0]
+        far_values = far_pair[:, 1]
         far_keys = far_keys.reshape(2, block_len, local_groups, head_size)
         far_values = far_values.reshape(2, block_len, local_groups, head_size)
         linked = lax.dynamic_slice_in_dim(links[section], seq_index * 2, 2) != block_ids

time: 192 us -> 193 us (level)
  waiting for transfers between devices: 55.2 us -> 71 us
  local copies, waits for them, and re-layouts: 40.3 us -> 28.6 us
  starting transfers between devices: 20 us -> 14.5 us
  other arithmetic: 19.4 us -> 21.9 us
    ppermute x4 -> x2, waiting for transfers between devices: 11.7 us -> 20 us  [from_partner(): return lax.ppermute(block, axis, route)]
    dynamic_update_slice x6 -> x4, local copies, waits for them, and re-layouts: 8.09 us -> 0.29 us  [split_send(): lax.dynamic_update_slice_in_dim(full, whole[shift][n], source * share, 0)]
    squeeze x0 -> x2, local copies, waits for them, and re-layouts: none -> 7.05 us  [body(): key_part, value_part = (weight_pair[0], weight_pair[1])]
    ppermute x6, waiting for transfers between devices: 27.2 us -> 33.9 us  [body(): incoming, their_scale = lax.ppermute((outgoing, row_scale), 'seq', route)]
    ppermute x4 -> x0, local copies, waits for them, and re-layouts: 6.48 us -> none  [the longest x2 3.58 us: swap_halves(): whole[shift] = lax.ppermute(pieces, 'sub', route)]
    unnamed x41 -> x36, local copies, waits for them, and re-layouts: 16.7 us -> 10.5 us
    ppermute x4 -> x2, starting transfers between devices: 4.95 us -> 1.09 us  [from_partner(): return lax.ppermute(block, axis, route)]
    dot_general x0 -> x2, local copies, waits for them, and re-layouts: none -> 2.85 us  [body(): jnp.einsum('td,dgh->tgh', rows, key_part, preferred_element_type=jnp.floa...]
  transfers between devices with their start and end apart: 23 -> 18, of which waited for: 4 -> 3; matrix products, arithmetic and copies ran while one was open for 48% -> 44% of each run, Pallas kernels for 0% -> 0%
where the time goes in v7:
time: 193 us; the launch traced here: 192 us
  waiting for transfers between devices  71 us (37%)
  matrix products  41.9 us (22%)
  local copies, waits for them, and re-layouts  28.6 us (15%)
  other arithmetic  21.9 us (11%)
  between operations  14.6 us (8%)
  starting transfers between devices  14.5 us (8%)
    ppermute x6, waiting for transfers between devices, body(): incoming, their_scale = lax.ppermute((outgoing, row_scale), 'seq', route)  33.9 us
    ppermute x2, waiting for transfers between devices, from_partner(): return lax.ppermute(block, axis, route)  20 us
    ppermute x1, waiting for transfers between devices, body(): across.append(lax.ppermute(tokens, 'kvh', route))  17 us
    unnamed x36, local copies, waits for them, and re-layouts  10.5 us
    dot_general x6, matrix products, body(): jnp.einsum('tc,tr->cr', halves[lane_shift], their_rows, preferred_element...  9.58 us
    ppermute x6, starting transfers between devices, body(): incoming, their_scale = lax.ppermute((outgoing, row_scale), 'seq', route)  8.77 us
    dot_general x1, matrix products, body(): jnp.einsum('td,dgc->tgc', normed, w_query, preferred_element_type=jnp.flo...  8.29 us
    squeeze x2, local copies, waits for them, and re-layouts, body(): key_part, value_part = (weight_pair[0], weight_pair[1])  7.05 us
  transfers between devices with their start and end apart: 18, of which 3 were waited for; matrix products, arithmetic and copies ran while one was open for 44% of the time, Pallas kernels for 0%

profile of v7, /device:TPU:0, one launch (start us, length us, event | category | flops | bytes accessed | tf_op | source)
XLA Modules:
  0.0 192.4 jit_solution(8244212212001185448)
XLA Ops:
  7.2 3.0 %collective-permute-start.1 = (bf16[512,1024]{1,0:T(8,128)(2,1)}, bf16[512,1024]{1,0:T(8,128)(2,1)}, u32[]{:S(2)}, u32[]{:S(2)}) collective-permute-start(bf16[512,1024]{1,0:T(8,128)(2,1)} %param.6), channel_id=1, source_target_pairs={{0,2},{2,0},{1,3},{3,1},{4,6},{6,4},{5,7},{7,5},{8,10},{10,8},{9,1... | collective-permute-start | bytes 3145736 | tf_op jit(solution)/shard_map/ppermute | solution.py:70
  10.3 2.8 %copy_bitcast_fusion = (bf16[1,2048,4,128]{3,1,2,0:T(8,128)(2,1)S(1)}, bf16[1,2048,4,128]{3,1,2,0:T(8,128)(2,1)S(1)}) fusion(bf16[2048,4,128]{2,1,0:T(4,128)(2,1)} %param.9, bf16[2048,4,128]{2,1,0:T(4,128)(2,1)} %param.10), kind=kLoop, calls=%fused_computation.48 | loop fusion | bytes 8388608 | tf_op jit(solution)/shard_map/stack | solution.py:107
  13.1 2.4 %pad_maximum_fusion.1 = bf16[2,2048,4,128]{3,1,2,0:T(8,128)(2,1)} fusion(bf16[1,2048,4,128]{3,1,2,0:T(8,128)(2,1)S(1)} %get-tuple-element.57, bf16[1,2048,4,128]{3,1,2,0:T(8,128)(2,1)S(1)} %get-tuple-element.56), kind=kLoop, calls=%fused_computation.14 | loop fusion | flops 2097152 | bytes 8388608 | tf_op jit(solution)/shard_map/stack | solution.py:107
  16.7 17.0 %collective-permute-done.1 = bf16[512,1024]{1,0:T(8,128)(2,1)} collective-permute-done((bf16[512,1024]{1,0:T(8,128)(2,1)}, bf16[512,1024]{1,0:T(8,128)(2,1)}, u32[]{:S(2)}, u32[]{:S(2)}) %collective-permute-start.1) | collective-permute-done | bytes 1048608 | tf_op jit(solution)/shard_map/ppermute | solution.py:70
  34.3 2.7 %copy.53 = bf16[2048,4,128]{0,2,1:T(8,128)(2,1)} copy(bf16[2048,4,128]{2,1,0:T(4,128)(2,1)S(1)} %copy-done.5) | data formatting | bytes 4194304 | tf_op args[3]
  37.0 2.5 %select_reduce_fusion.1 = (f32[512]{0:T(512)S(1)}, f32[512]{0:T(512)S(1)}) fusion(f32[]{:T(128)} %bitcast.45, f32[]{:T(128)} %bitcast.44, f32[]{:T(128)} %bitcast.32, f32[]{:T(128)} %bitcast.31), kind=kLoop, calls=%fused_computation.155 | loop fusion | flops 7168 | bytes 4112 | tf_op jit(solution)/shard_map/gather | solution.py:141
  41.9 1.8 multiply_cosine_fusion
  43.7 2.1 %select_select_fusion.3 = (bf16[512,1024]{1,0:T(8,128)(2,1)S(1)}, bf16[512,1024]{1,0:T(8,128)(2,1)S(1)}, bf16[512,1024]{1,0:T(8,128)(2,1)S(1)}, bf16[512,1024]{1,0:T(8,128)(2,1)S(1)}) fusion(bf16[512,1024]{1,0:T(8,128)(2,1)} %collective-permute-done.1, bf16[512,1024]{1,0:T(8,128)(2,1)} %collective-permute-done.2, bf16[512,1024]{1,0:T(8,128)(2,1)S(1)} %copy-done.7, ...), kind=kLoop, calls=%fused_computation.86 | loop fusion | flops 6291456 | bytes 8388620 | tf_op jit(solution)/shard_map/select_n | solution.py:78
  46.9 1.8 collective-permute-start.9
  48.7 2.6 %collective-permute-start.12 = (f32[512]{0:T(512)S(1)}, f32[512]{0:T(512)S(1)}, u32[]{:S(2)}, u32[]{:S(2)}) collective-permute-start(f32[512]{0:T(512)S(1)} %add_rsqrt_fusion), channel_id=1, source_target_pairs={{0,8},{4,12},{8,0},{12,4},{1,9},{5,13},{9,1},{13,5},{2,10},{6,14},... | collective-permute-start | bytes 6152 | tf_op jit(solution)/shard_map/ppermute | solution.py:181
  52.6 1.4 fusion.2
  54.0 1.9 %copy-done.1 = bf16[512,4096]{1,0:T(8,128)(2,1)} copy-done((bf16[512,4096]{1,0:T(8,128)(2,1)}, bf16[512,4096]{1,0:T(8,128)(2,1)S(1)}, u32[]{:S(2)}) %copy-start.1) | copy-done | bytes 4194328
  57.6 8.3 %fusion.3 = f32[512,4,256]{0,2,1:T(8,128)S(1)} fusion(bf16[4096,4,256]{2,1,0:T(4,128)(2,1)} %param.8, bf16[512,4096]{1,0:T(8,128)(2,1)} %copy-done.1), kind=kOutput, calls=%fused_computation.6 | convolution fusion | flops 4294967296 | bytes 14680064 | tf_op jit(solution)/shard_map/td,dgc->tgc/dot_general | solution.py:93
  66.1 2.0 %copy.91 = f32[512,4,2,64]{3,0,2,1:T(8,128)} copy(f32[512,4,2,64]{0,3,2,1:T(8,128)S(1)} %get-tuple-element.29) | data formatting | bytes 2097152
  68.1 1.9 copy.90
  70.0 5.0 %fusion.63 = f32[1024,1024]{1,0:T(8,128)} fusion(bf16[512,4096]{1,0:T(8,128)(2,1)} %copy-done.1, s32[]{:T(128)} %select_n.353, s32[]{:T(128)S(6)} %select_n.352), kind=kOutput, calls=%fused_computation.77 | convolution fusion | flops 1073741824 | bytes 6291972 | tf_op jit(solution)/shard_map/tc,tr->cr/dot_general | solution.py:175
  75.6 3.0 %slice_bitcast_fusion = bf16[2048,4,128]{2,0,1:T(8,128)(2,1)} fusion(bf16[2,2048,4,128]{3,1,2,0:T(8,128)(2,1)} %collective-permute-done.3), kind=kLoop, calls=%fused_computation.33 | loop fusion | bytes 4194304 | tf_op jit(solution)/shard_map/squeeze | solution.py:108
  78.6 4.0 %copy.54 = bf16[2048,4,128]{0,2,1:T(8,128)(2,1)} copy(bf16[2048,4,128]{2,0,1:T(8,128)(2,1)} %slice_bitcast_fusion) | data formatting | bytes 4194304 | tf_op jit(solution)/shard_map/squeeze | solution.py:108
  82.6 4.5 %fusion.35 = f32[512,512]{0,1} fusion(bf16[2048,512]{0,1:T(8,128)(2,1)} %bitcast.182, bf16[512,4096]{1,0:T(8,128)(2,1)} %copy-done.1, s32[]{:T(128)S(6)} %select_n.341), kind=kOutput, calls=%fused_computation.57 | convolution fusion | flops 1073741824 | bytes 5242884
  87.1 2.5 %copy.56 = f32[512,4,128]{2,0,1:T(8,128)} copy(f32[512,4,128]{0,2,1:T(8,128)} %bitcast.189) | data formatting | bytes 2097152 | tf_op jit(solution)/shard_map/td,dgh->tgh/dot_general | solution.py:111
  91.0 3.6 %fusion.21 = f32[512,4,128]{2,0,1:T(8,128)S(1)} fusion(bf16[2,2048,4,128]{3,1,2,0:T(8,128)(2,1)} %collective-permute-done.3, bf16[512,4096]{1,0:T(8,128)(2,1)} %copy-done.1, s32[]{:T(128)S(6)} %select_n.341), kind=kOutput, calls=%fused_computation.35 | convolution fusion | flops 1073741824 | bytes 5242884 | tf_op jit(solution)/shard_map/td,dgh->tgh/dot_general | solution.py:112
  97.8 2.1 %fusion.121 = (bf16[256,1024]{1,0:T(8,128)(2,1)}, bf16[256,1024]{1,0:T(8,128)(2,1)}, bf16[256,1024]{1,0:T(8,128)(2,1)}) fusion(bf16[512,4096]{1,0:T(8,128)(2,1)S(1)} %copy-done.2, s32[]{:T(128)S(6)} %select_n.354, s32[]{:T(128)S(6)} %select_n.357, s32[]{:T(128)S(6)} %select_n.367, s32[]{:T(128)S(6)} %select_n.362), kind=kLoop, calls=%fused_computation.172 | loop fusion | bytes 3145744 | tf_op jit(solution)/shard_map/dynamic_slice | solution.py:179
  99.9 2.5 %fusion.7 = (f32[4,2,512]{2,1,0:T(2,128)S(1)}, f32[4,512,512,2]{2,1,3,0:T(8,128)S(1)}) fusion(pred[512,512]{0,1:T(8,128)(4,1)S(1)} %fusion.66, bf16[512,4,2,64]{3,0,2,1:T(8,128)(2,1)S(1)} %get-tuple-element.14, bf16[512,4,2,64]{3,0,2,1:T(8,128)(2,1)S(1)} %get-tuple-element.13, bf16[512,4,64]{2,0,1:T(8,128)(2,1)S(1)} %get-tuple-element.31, ...), kind=kOutput, calls=%fused_computation.11 | convolution fusion | flops 546304000 | bytes 10240000 | tf_op jit(solution)/shard_map/tgrh,ugh->grtu/dot_general | solution.py:120
  102.4 20.0 %collective-permute-done.6 = bf16[256,2,4,128]{3,0,2,1:T(8,128)(2,1)S(1)} collective-permute-done((bf16[256,2,4,128]{3,0,2,1:T(8,128)(2,1)S(1)}, bf16[256,2,4,128]{3,0,2,1:T(8,128)(2,1)S(1)}, u32[]{:S(2)}, u32[]{:S(2)}) %collective-permute-start.6) | collective-permute-done | bytes 524320 | tf_op jit(solution)/shard_map/ppermute | solution.py:18
  123.0 1.8 fusion.5
  132.4 2.0 %collective-permute-start.8 = (bf16[256,1024]{1,0:T(8,128)(2,1)}, bf16[256,1024]{1,0:T(8,128)(2,1)S(1)}, u32[]{:S(2)}, u32[]{:S(2)}) collective-permute-start(bf16[256,1024]{1,0:T(8,128)(2,1)} %get-tuple-element.22), channel_id=1, source_target_pairs={{0,4},{4,8},{8,12},{12,0},{1,5},{5,9},{9,13},{13,1},{2,6},{6,10},{... | collective-permute-start | bytes 1572872 | tf_op jit(solution)/shard_map/ppermute | solution.py:181
  134.5 2.5 %fusion.33 = bf16[512,4,2,128]{0,3,2,1:T(8,128)(2,1)S(1)} fusion(f32[512,4,2,128]{0,3,2,1:T(8,128)S(1)} %bitcast.179, f32[512,4,2,128]{0,3,2,1:T(8,128)S(1)} %bitcast.180, f32[4,512,512,2]{2,1,3,0:T(8,128)S(1)} %get-tuple-element.51, f32[4,2,512]{2,1,0:T(2,128)S(1)} %get-tuple-element.50, pred[512,512]{0,1:T(8,128)(4,1)S(1)} %fusion.66, ...), kind=kOutput, calls=%fused_computation.54 | convolution fusion | flops 548405248 | bytes 14483456 | tf_op jit(solution)/shard_map/grtu,ugh->tgrh/dot_general | solution.py:130
  137.0 1.4 copy.71
  138.4 33.9 %collective-permute-done.11 = bf16[256,1024]{1,0:T(8,128)(2,1)S(1)} collective-permute-done((bf16[256,1024]{1,0:T(8,128)(2,1)}, bf16[256,1024]{1,0:T(8,128)(2,1)S(1)}, u32[]{:S(2)}, u32[]{:S(2)}) %collective-permute-start.11) | collective-permute-done | bytes 524320 | tf_op jit(solution)/shard_map/ppermute | solution.py:181
  172.9 2.6 %multiply_convert_fusion.2 = (bf16[512,1024]{1,0:T(8,128)(2,1)S(1)}, bf16[512,1024]{1,0:T(8,128)(2,1)S(1)}, bf16[512,1024]{1,0:T(8,128)(2,1)S(1)}) fusion(f32[1024]{0:T(1024)S(1)} %dynamic-slice-done, f32[512]{0:T(512)S(1)} %collective-permute-done.9, bf16[2048,1024]{1,0:T(8,128)(2,1)} %all-gather.2.cloned.1.call-done, s32[]{:T(128)S(6)} %select_n.359, ...), kind=kLoop, calls=%fused_computation.51 | loop fusion | flops 6291456 | bytes 6301708 | tf_op jit(solution)/shard_map/convert_element_type | solution.py:187
  178.6 1.9 %fusion.87 = f32[1024,1024]{1,0:T(8,128)S(1)} fusion(bf16[256,1024]{1,0:T(8,128)(2,1)} %collective-permute-done.10, bf16[512,1024]{1,0:T(8,128)(2,1)S(1)} %get-tuple-element.19, s32[]{:T(128)S(6)} %select_n.349), kind=kOutput, calls=%fused_computation.109 | convolution fusion | flops 536870912 | bytes 5242884 | tf_op jit(solution)/shard_map/tc,tr->cr/dot_general | solution.py:191
  180.9 4.7 %add_multiply_fusion = f32[1024,1024]{1,0:T(8,128)} fusion(f32[1024,1024]{1,0:T(8,128)S(1)} %fusion.81, f32[1024,1024]{1,0:T(8,128)S(1)} %fusion.83, f32[1024,1024]{1,0:T(8,128)S(1)} %fusion.85, f32[1024,1024]{1,0:T(8,128)S(1)} %fusion.87, f32[1024,1024]{1,0:T(8,128)S(1)} %copy-done, f32[1024,1024]{1,0:T(8,128)S(1)} %fusion.89, ...), kind=kOutput, calls=%fused_computation.22 | convolution fusion | flops 544210944 | bytes 30408708 | tf_op jit(solution)/shard_map/tc,tr->cr/dot_general | solution.py:191
  (109 shorter events, 25.5 us)
Async XLA Ops:
  7.2 165.7 %all-gather.2.cloned.1.call-start = ((), (), s32[]{:S(2)}) async-start(), calls=%async_computation | async-start | bytes 5242880 | tf_op jit(solution)/shard_map/all_gather | solution.py:172
  7.2 26.5 %collective-permute-start.1 = (bf16[512,1024]{1,0:T(8,128)(2,1)}, bf16[512,1024]{1,0:T(8,128)(2,1)}, u32[]{:S(2)}, u32[]{:S(2)}) collective-permute-start(bf16[512,1024]{1,0:T(8,128)(2,1)} %param.6), channel_id=1, source_target_pairs={{0,2},{2,0},{1,3},{3,1},{4,6},{6,4},{5,7},{7,5},{8,10},{10,8},{9,1... | collective-permute-start | bytes 3145736 | tf_op jit(solution)/shard_map/ppermute | solution.py:70
  10.2 33.4 %collective-permute-start = (bf16[512,1024]{1,0:T(8,128)(2,1)}, bf16[512,1024]{1,0:T(8,128)(2,1)}, u32[]{:S(2)}, u32[]{:S(2)}) collective-permute-start(bf16[512,1024]{1,0:T(8,128)(2,1)} %param.6), channel_id=1, source_target_pairs={{0,1},{1,0},{2,3},{3,2},{4,5},{5,4},{6,7},{7,6},{8,9},{9,8},{10,11... | collective-permute-start | bytes 3145736 | tf_op jit(solution)/shard_map/ppermute | solution.py:26
  13.0 2.9 %copy-start.15 = (s32[3,8]{1,0:T(4,128)S(1)}, s32[3,8]{1,0:T(4,128)}, u32[]{:S(2)}) copy-start(s32[3,8]{1,0:T(4,128)} %param.11) | copy-start | bytes 292
  13.1 21.3 %copy-start.5 = (bf16[2048,4,128]{2,1,0:T(4,128)(2,1)S(1)}, bf16[2048,4,128]{2,1,0:T(4,128)(2,1)}, u32[]{:S(2)}) copy-start(bf16[2048,4,128]{2,1,0:T(4,128)(2,1)} %param.9) | copy-start | bytes 6291460
  15.4 28.2 %copy-start.7 = (bf16[512,1024]{1,0:T(8,128)(2,1)S(1)}, bf16[512,1024]{1,0:T(8,128)(2,1)}, u32[]{:S(2)}) copy-start(bf16[512,1024]{1,0:T(8,128)(2,1)} %param.6) | copy-start | bytes 3145732
  15.4 60.1 %collective-permute-start.3 = (bf16[2,2048,4,128]{3,1,2,0:T(8,128)(2,1)}, bf16[2,2048,4,128]{3,1,2,0:T(8,128)(2,1)}, u32[]{:S(2)}, u32[]{:S(2)}) collective-permute-start(bf16[2,2048,4,128]{3,1,2,0:T(8,128)(2,1)} %pad_maximum_fusion.1), channel_id=1, source_target_pairs={{0,1},{1,0},{2,3},{3,2},{4,5},{5,4},{6,7},{7,6},{8,9},{9,8},{10,11... | collective-permute-start | bytes 12582920 | tf_op jit(solution)/shard_map/ppermute | solution.py:107
  33.7 10.0 %collective-permute-start.2 = (bf16[512,1024]{1,0:T(8,128)(2,1)}, bf16[512,1024]{1,0:T(8,128)(2,1)}, u32[]{:S(2)}, u32[]{:S(2)}) collective-permute-start(bf16[512,1024]{1,0:T(8,128)(2,1)} %collective-permute-done.1), channel_id=1, source_target_pairs={{0,1},{1,0},{2,3},{3,2},{4,5},{5,4},{6,7},{7,6},{8,9},{9,8},{10,11... | collective-permute-start | bytes 3145736 | tf_op jit(solution)/shard_map/ppermute | solution.py:26
  45.8 6.8 %copy-start.14 = (f32[4096]{0:T(1024)S(1)}, f32[4096]{0:T(1024)}, u32[]{:S(2)}) copy-start(f32[4096]{0:T(1024)} %param.7) | copy-start | bytes 49156
  46.8 9.1 %copy-start.12 = (bf16[2048,4,128]{0,2,1:T(8,128)(2,1)S(1)}, bf16[2048,4,128]{0,2,1:T(8,128)(2,1)}, u32[]{:S(2)}) copy-start(bf16[2048,4,128]{0,2,1:T(8,128)(2,1)} %copy.53) | copy-start | bytes 6291460
  46.9 85.6 %collective-permute-start.9 = (f32[512]{0:T(512)S(1)}, f32[512]{0:T(512)S(1)}, u32[]{:S(2)}, u32[]{:S(2)}) collective-permute-start(f32[512]{0:T(512)S(1)} %add_rsqrt_fusion), channel_id=1, source_target_pairs={{0,4},{4,8},{8,12},{12,0},{1,5},{5,9},{9,13},{13,1},{2,6},{6,10},{... | collective-permute-start | bytes 6152 | tf_op jit(solution)/shard_map/ppermute | solution.py:181
  48.7 124.2 %collective-permute-start.12 = (f32[512]{0:T(512)S(1)}, f32[512]{0:T(512)S(1)}, u32[]{:S(2)}, u32[]{:S(2)}) collective-permute-start(f32[512]{0:T(512)S(1)} %add_rsqrt_fusion), channel_id=1, source_target_pairs={{0,8},{4,12},{8,0},{12,4},{1,9},{5,13},{9,1},{13,5},{2,10},{6,14},... | collective-permute-start | bytes 6152 | tf_op jit(solution)/shard_map/ppermute | solution.py:181
  51.3 121.6 %collective-permute-start.15 = (f32[512]{0:T(512)S(1)}, f32[512]{0:T(512)S(1)}, u32[]{:S(2)}, u32[]{:S(2)}) collective-permute-start(f32[512]{0:T(512)S(1)} %add_rsqrt_fusion), channel_id=1, source_target_pairs={{0,12},{4,0},{8,4},{12,8},{1,13},{5,1},{9,5},{13,9},{2,14},{6,2},{... | collective-permute-start | bytes 6152 | tf_op jit(solution)/shard_map/ppermute | solution.py:181
  70.0 5.0 %copy-start.3 = (f32[512,4,2,64]{3,0,2,1:T(8,128)S(1)}, f32[512,4,2,64]{3,0,2,1:T(8,128)}, u32[]{:S(2)}) copy-start(f32[512,4,2,64]{3,0,2,1:T(8,128)} %copy.91) | copy-start | bytes 3145732
  70.0 5.0 %copy-start.4 = (f32[512,4,2,64]{3,0,2,1:T(8,128)S(1)}, f32[512,4,2,64]{3,0,2,1:T(8,128)}, u32[]{:S(2)}) copy-start(f32[512,4,2,64]{3,0,2,1:T(8,128)} %copy.90) | copy-start | bytes 3145732
  70.0 5.0 %copy-start.8 = (f32[512,64]{1,0:T(8,128)S(1)}, f32[512,64]{1,0:T(8,128)}, u32[]{:S(2)}) copy-start(f32[512,64]{1,0:T(8,128)} %get-tuple-element.37) | copy-start | bytes 393220
  70.0 5.0 %copy-start.10 = (f32[512,64]{1,0:T(8,128)S(1)}, f32[512,64]{1,0:T(8,128)}, u32[]{:S(2)}) copy-start(f32[512,64]{1,0:T(8,128)} %get-tuple-element.38) | copy-start | bytes 393220
  91.0 3.7 %copy-start.9 = (f32[512,64]{1,0:T(8,128)S(1)}, f32[512,64]{1,0:T(8,128)}, u32[]{:S(2)}) copy-start(f32[512,64]{1,0:T(8,128)} %get-tuple-element.37) | copy-start | bytes 393220
  91.0 3.7 %copy-start.11 = (f32[512,64]{1,0:T(8,128)S(1)}, f32[512,64]{1,0:T(8,128)}, u32[]{:S(2)}) copy-start(f32[512,64]{1,0:T(8,128)} %get-tuple-element.38) | copy-start | bytes 393220
  91.0 4.1 %copy-start.2 = (bf16[512,4096]{1,0:T(8,128)(2,1)S(1)}, bf16[512,4096]{1,0:T(8,128)(2,1)}, u32[]{:S(2)}) copy-start(bf16[512,4096]{1,0:T(8,128)(2,1)} %copy-done.1) | copy-start | bytes 12582916
  91.0 4.3 %copy-start.13 = (bf16[2048,4,128]{2,1,0:T(4,128)(2,1)S(1)}, bf16[2048,4,128]{2,1,0:T(4,128)(2,1)}, u32[]{:S(2)}) copy-start(bf16[2048,4,128]{2,1,0:T(4,128)(2,1)} %param.10) | copy-start | bytes 6291460
  96.7 25.7 %collective-permute-start.6 = (bf16[256,2,4,128]{3,0,2,1:T(8,128)(2,1)S(1)}, bf16[256,2,4,128]{3,0,2,1:T(8,128)(2,1)S(1)}, u32[]{:S(2)}, u32[]{:S(2)}) collective-permute-start(bf16[256,2,4,128]{3,0,2,1:T(8,128)(2,1)S(1)} %fusion.74), channel_id=1, source_target_pairs={{0,8},{8,0},{4,12},{12,4},{1,9},{9,1},{5,13},{13,5},{2,10},{10,2},... | collective-permute-start | bytes 1572872 | tf_op jit(solution)/shard_map/ppermute | solution.py:18
  97.0 25.5 %collective-permute-start.4 = (bf16[256,2,4,128]{3,0,2,1:T(8,128)(2,1)S(1)}, bf16[256,2,4,128]{3,0,2,1:T(8,128)(2,1)S(1)}, u32[]{:S(2)}, u32[]{:S(2)}) collective-permute-start(bf16[256,2,4,128]{3,0,2,1:T(8,128)(2,1)S(1)} %fusion.74), channel_id=1, source_target_pairs={{0,4},{4,0},{8,12},{12,8},{1,5},{5,1},{9,13},{13,9},{2,6},{6,2},{1... | collective-permute-start | bytes 1572872 | tf_op jit(solution)/shard_map/ppermute | solution.py:18
  122.5 2.7 %collective-permute-start.7 = (bf16[256,2,4,128]{3,0,2,1:T(8,128)(2,1)S(1)}, bf16[256,2,4,128]{3,0,2,1:T(8,128)(2,1)S(1)}, u32[]{:S(2)}, u32[]{:S(2)}) collective-permute-start(bf16[256,2,4,128]{3,0,2,1:T(8,128)(2,1)S(1)} %collective-permute-done.6), channel_id=1, source_target_pairs={{0,1},{1,0},{2,3},{3,2},{4,5},{5,4},{6,7},{7,6},{8,9},{9,8},{10,11... | collective-permute-start | bytes 1572872 | tf_op jit(solution)/shard_map/ppermute | solution.py:26
  122.5 3.7 %collective-permute-start.5 = (bf16[256,2,4,128]{3,0,2,1:T(8,128)(2,1)S(1)}, bf16[256,2,4,128]{3,0,2,1:T(8,128)(2,1)S(1)}, u32[]{:S(2)}, u32[]{:S(2)}) collective-permute-start(bf16[256,2,4,128]{3,0,2,1:T(8,128)(2,1)S(1)} %collective-permute-done.4), channel_id=1, source_target_pairs={{0,1},{1,0},{2,3},{3,2},{4,5},{5,4},{6,7},{7,6},{8,9},{9,8},{10,11... | collective-permute-start | bytes 1572872 | tf_op jit(solution)/shard_map/ppermute | solution.py:26
  125.2 47.6 %collective-permute-start.14 = (bf16[256,1024]{1,0:T(8,128)(2,1)}, bf16[256,1024]{1,0:T(8,128)(2,1)S(1)}, u32[]{:S(2)}, u32[]{:S(2)}) collective-permute-start(bf16[256,1024]{1,0:T(8,128)(2,1)} %get-tuple-element.23), channel_id=1, source_target_pairs={{0,12},{4,0},{8,4},{12,8},{1,13},{5,1},{9,5},{13,9},{2,14},{6,2},{... | collective-permute-start | bytes 1572872 | tf_op jit(solution)/shard_map/ppermute | solution.py:181
  126.2 46.1 %collective-permute-start.11 = (bf16[256,1024]{1,0:T(8,128)(2,1)}, bf16[256,1024]{1,0:T(8,128)(2,1)S(1)}, u32[]{:S(2)}, u32[]{:S(2)}) collective-permute-start(bf16[256,1024]{1,0:T(8,128)(2,1)} %get-tuple-element.24), channel_id=1, source_target_pairs={{0,8},{4,12},{8,0},{12,4},{1,9},{5,13},{9,1},{13,5},{2,10},{6,14},... | collective-permute-start | bytes 1572872 | tf_op jit(solution)/shard_map/ppermute | solution.py:181
  132.4 39.9 %collective-permute-start.8 = (bf16[256,1024]{1,0:T(8,128)(2,1)}, bf16[256,1024]{1,0:T(8,128)(2,1)S(1)}, u32[]{:S(2)}, u32[]{:S(2)}) collective-permute-start(bf16[256,1024]{1,0:T(8,128)(2,1)} %get-tuple-element.22), channel_id=1, source_target_pairs={{0,4},{4,8},{8,12},{12,0},{1,5},{5,9},{9,13},{13,1},{2,6},{6,10},{... | collective-permute-start | bytes 1572872 | tf_op jit(solution)/shard_map/ppermute | solution.py:181
  134.5 38.4 %dynamic-slice-start = ((f32[4096]{0:T(1024)}, s32[]{:T(128)}), f32[1024]{0:T(1024)S(1)}, s32[]{:S(2)}) async-start(f32[4096]{0:T(1024)} %param.7, s32[]{:T(128)} %select_n.353), calls=%async_computation.1 | async-start | bytes 8704 | tf_op jit(solution)/shard_map/dynamic_slice | solution.py:173
  172.3 4.8 %collective-permute-start.13 = (bf16[256,1024]{1,0:T(8,128)(2,1)S(1)}, bf16[256,1024]{1,0:T(8,128)(2,1)S(1)}, u32[]{:S(2)}, u32[]{:S(2)}) collective-permute-start(bf16[256,1024]{1,0:T(8,128)(2,1)S(1)} %collective-permute-done.11), channel_id=1, source_target_pairs={{0,1},{1,0},{2,3},{3,2},{4,5},{5,4},{6,7},{7,6},{8,9},{9,8},{10,11... | collective-permute-start | bytes 1572872 | tf_op jit(solution)/shard_map/ppermute | solution.py:26
  172.3 6.3 %collective-permute-start.10 = (bf16[256,1024]{1,0:T(8,128)(2,1)S(1)}, bf16[256,1024]{1,0:T(8,128)(2,1)}, u32[]{:S(2)}, u32[]{:S(2)}) collective-permute-start(bf16[256,1024]{1,0:T(8,128)(2,1)S(1)} %collective-permute-done.8), channel_id=1, source_target_pairs={{0,1},{1,0},{2,3},{3,2},{4,5},{5,4},{6,7},{7,6},{8,9},{9,8},{10,11... | collective-permute-start | bytes 1572872 | tf_op jit(solution)/shard_map/ppermute | solution.py:26
  172.8 7.7 %collective-permute-start.16 = (bf16[256,1024]{1,0:T(8,128)(2,1)S(1)}, bf16[256,1024]{1,0:T(8,128)(2,1)}, u32[]{:S(2)}, u32[]{:S(2)}) collective-permute-start(bf16[256,1024]{1,0:T(8,128)(2,1)S(1)} %collective-permute-done.14), channel_id=1, source_target_pairs={{0,1},{1,0},{2,3},{3,2},{4,5},{5,4},{6,7},{7,6},{8,9},{9,8},{10,11... | collective-permute-start | bytes 1572872 | tf_op jit(solution)/shard_map/ppermute | solution.py:26
  (3 other events, 5.8 us)
Sparse Core Ops, SparseCore 0:
  10.4 82.7 all-gather.1

commit v8 on v7

--- a/solution.py
+++ b/solution.py
@@ -42,6 +42,27 @@
             full = lax.dynamic_update_slice_in_dim(full, whole[shift][n], source * share, 0)
         out.append(full)
     return tuple(out)
+
+
+def xor_route(count, pattern):
+    return [(j, j ^ pattern) for j in range(count) if (j ^ pattern) < count]
+
+
+def send_with_rows(kv_pair, rows_out, pattern):
+    count = lax.axis_size("sub")
+    index = lax.axis_index("sub")
+    share = kv_pair.shape[0] // count
+    mine_kv = lax.dynamic_slice_in_dim(kv_pair, index * share, share, 0)
+    kv_width = mine_kv.size // share
+    packed = jnp.concatenate([mine_kv.reshape(share, kv_width), rows_out], axis=1)
+    got = lax.ppermute(packed, "seq", xor_route(lax.axis_size("seq"), pattern))
+    whole = swap_halves(got, count, index)
+    full = jnp.zeros_like(kv_pair)
+    for shift in range(count):
+        source = (index - shift) % count
+        part = whole[shift][:, :kv_width].reshape(mine_kv.shape)
+        full = lax.dynamic_update_slice_in_dim(full, part, source * share, 0)
+    return full, [w[:, kv_width:] for w in whole]
 
 
 def rotate(vectors, positions):
@@ -131,8 +152,16 @@
         "grtu,ugh->tgrh", weights.astype(jnp.bfloat16), values, preferred_element_type=jnp.float32
     )
     query_pairs = queries.reshape(2, block_len, local_groups, per_group, head_size)
-    for section in range(1, lax.axis_size("seq").bit_length()):
-        (far_pair,) = split_send((jnp.stack([keys, values]).swapaxes(0, 1),), "seq", section - 1)
+    seq_count = lax.axis_size("seq")
+    band = width // seq_count
+    share = row_count // sub_count
+    my_rows = lax.dynamic_slice_in_dim(normed, sub_index * share, share, 0)
+    kv_pair = jnp.stack([keys, values]).swapaxes(0, 1)
+    carried = {}
+    for section in range(1, seq_count.bit_length()):
+        pattern = 1 << (section - 1)
+        rider = lax.dynamic_slice_in_dim(my_rows, (seq_index ^ pattern) * band, band, 1)
+        far_pair, carried[pattern] = send_with_rows(kv_pair, rider, pattern)
         far_keys = far_pair[:, 0]
         far_values = far_pair[:, 1]
         far_keys = far_keys.reshape(2, block_len, local_groups, head_size)
@@ -173,14 +202,16 @@
     column_gain = lax.dynamic_slice_in_dim(norm_gain, owner_index * tile_cols, tile_cols, 0)
     mine = lax.dynamic_slice_in_dim(normed, seq_index * band, band, 1)
     gram_sum = jnp.einsum("tc,tr->cr", mine, owned, preferred_element_type=jnp.float32)
-    my_rows = lax.dynamic_slice_in_dim(normed, sub_index * share, share, 0)
-    for shift in range(1, seq_count):
-        target = (seq_index + shift) % seq_count
-        outgoing = lax.dynamic_slice_in_dim(my_rows, target * band, band, 1)
-        route = [(j, (j + shift) % seq_count) for j in range(seq_count)]
-        incoming, their_scale = lax.ppermute((outgoing, row_scale), "seq", route)
-        halves = swap_halves(incoming, sub_count, sub_index)
-        source = (seq_index - shift) % seq_count
+    for pattern in range(1, seq_count):
+        route = xor_route(seq_count, pattern)
+        their_scale = lax.ppermute(row_scale, "seq", route)
+        if pattern in carried:
+            halves = carried[pattern]
+        else:
+            outgoing = lax.dynamic_slice_in_dim(my_rows, (seq_index ^ pattern) * band, band, 1)
+            incoming = lax.ppermute(outgoing, "seq", route)
+            halves = swap_halves(incoming, sub_count, sub_index)
+        source = seq_index ^ pattern
         their_raw = lax.dynamic_slice_in_dim(raw_columns, source * row_count, row_count, 0)
         their_owned = (
             their_raw.astype(jnp.float32) * their_scale[:, None] * column_gain

time: 193 us -> 218 us (1.13)
  local copies, waits for them, and re-layouts: 28.6 us -> 44.5 us
  waiting for transfers between devices: 71 us -> 76.6 us
  other arithmetic: 21.9 us -> 27.3 us
    ppermute x8 -> x6, waiting for transfers between devices: 53.9 us -> 65.9 us  [the longest x2 65.9 us: send_with_rows(): got = lax.ppermute(packed, 'seq', xor_route(lax.axis_size('seq'), pattern))]
    slice x0 -> x5, local copies, waits for them, and re-layouts: none -> 8.66 us  [the longest x4 5.91 us: send_with_rows(): part = whole[shift][:, :kv_width].reshape(mine_kv.shape)]
    squeeze x2 -> x0, local copies, waits for them, and re-layouts: 7.05 us -> none  [body(): key_part, value_part = (weight_pair[0], weight_pair[1])]
    ppermute x1, waiting for transfers between devices: 17 us -> 10.6 us  [body(): across.append(lax.ppermute(tokens, 'kvh', route))]
    reshape x0 -> x5, local copies, waits for them, and re-layouts: none -> 6.16 us  [the longest x4 5.95 us: send_with_rows(): part = whole[shift][:, :kv_width].reshape(mine_kv.shape)]
    unnamed x36 -> x45, local copies, waits for them, and re-layouts: 10.5 us -> 16.6 us
    dot_general x2 -> x0, matrix products: 4.87 us -> none  [body(): jnp.einsum('td,dgh->tgh', rows, value_part, preferred_element_type=jnp.fl...]
    dot_general x6, matrix products: 9.58 us -> 14.1 us  [body(): jnp.einsum('tc,tr->cr', halves[lane_shift], their_rows, preferred_element...]
  transfers between devices with their start and end apart: 18 -> 14, of which waited for: 3 -> 2; matrix products, arithmetic and copies ran while one was open for 44% -> 48% of each run, Pallas kernels for 0% -> 0%
where the time goes in v8:
time: 218 us; the launch traced here: 217 us
  waiting for transfers between devices  76.6 us (35%)
  local copies, waits for them, and re-layouts  44.5 us (20%)
  matrix products  39.9 us (18%)
  other arithmetic  27.3 us (13%)
  between operations  14.6 us (7%)
  starting transfers between devices  13.7 us (6%)
    ppermute x2, waiting for transfers between devices, send_with_rows(): got = lax.ppermute(packed, 'seq', xor_route(lax.axis_size('seq'), pattern))  65.9 us
    unnamed x45, local copies, waits for them, and re-layouts  16.6 us
    dot_general x6, matrix products, body(): jnp.einsum('tc,tr->cr', halves[lane_shift], their_rows, preferred_element...  14.1 us
    ppermute x1, waiting for transfers between devices, body(): across.append(lax.ppermute(tokens, 'kvh', route))  10.6 us
    dot_general x1, matrix products, body(): jnp.einsum('td,dgc->tgc', normed, w_query, preferred_element_type=jnp.flo...  7.26 us
    reshape x4, local copies, waits for them, and re-layouts, send_with_rows(): part = whole[shift][:, :kv_width].reshape(mine_kv.shape)  5.95 us
    slice x4, local copies, waits for them, and re-layouts, send_with_rows(): part = whole[shift][:, :kv_width].reshape(mine_kv.shape)  5.91 us
    ppermute x3, starting transfers between devices, body(): their_scale = lax.ppermute(row_scale, 'seq', route)  5.2 us
  transfers between devices with their start and end apart: 14, of which 2 were waited for; matrix products, arithmetic and copies ran while one was open for 48% of the time, Pallas kernels for 0%

profile of v8, /device:TPU:0, one launch (start us, length us, event | category | flops | bytes accessed | tf_op | source)
XLA Modules:
  0.0 216.5 jit_solution(10649862171106024384)
XLA Ops:
  7.2 3.0 %collective-permute-start.1 = (bf16[512,1024]{1,0:T(8,128)(2,1)}, bf16[512,1024]{1,0:T(8,128)(2,1)}, u32[]{:S(2)}, u32[]{:S(2)}) collective-permute-start(bf16[512,1024]{1,0:T(8,128)(2,1)} %param.6), channel_id=1, source_target_pairs={{0,2},{2,0},{1,3},{3,1},{4,6},{6,4},{5,7},{7,5},{8,10},{10,8},{9,1... | collective-permute-start | bytes 3145736 | tf_op jit(solution)/shard_map/ppermute | solution.py:91
  10.3 4.4 %copy.59 = bf16[2048,4,128]{0,2,1:T(8,128)(2,1)} copy(bf16[2048,4,128]{2,1,0:T(4,128)(2,1)} %param.9) | data formatting | bytes 4194304 | tf_op args[3]
  14.7 3.0 %copy.58 = bf16[2048,4,128]{0,2,1:T(8,128)(2,1)S(1)} copy(bf16[2048,4,128]{2,1,0:T(4,128)(2,1)} %param.10) | data formatting | bytes 4194304 | tf_op args[4]
  17.6 4.3 %pad_maximum_fusion.1 = bf16[2,2048,4,128]{1,3,2,0:T(8,128)(2,1)} fusion(bf16[1,2048,4,128]{1,3,2,0:T(8,128)(2,1)S(1)} %bitcast.168, bf16[1,2048,4,128]{1,3,2,0:T(8,128)(2,1)} %bitcast.170), kind=kLoop, calls=%fused_computation.14 | loop fusion | flops 2097152 | bytes 8388608 | tf_op jit(solution)/shard_map/stack | solution.py:128
  23.2 10.6 %collective-permute-done.1 = bf16[512,1024]{1,0:T(8,128)(2,1)} collective-permute-done((bf16[512,1024]{1,0:T(8,128)(2,1)}, bf16[512,1024]{1,0:T(8,128)(2,1)}, u32[]{:S(2)}, u32[]{:S(2)}) %collective-permute-start.1) | collective-permute-done | bytes 1048608 | tf_op jit(solution)/shard_map/ppermute | solution.py:91
  34.4 2.5 %select_reduce_fusion.1 = (f32[512]{0:T(512)S(1)}, f32[512]{0:T(512)S(1)}) fusion(f32[]{:T(128)} %bitcast.49, f32[]{:T(128)} %bitcast.48, f32[]{:T(128)} %bitcast.35, f32[]{:T(128)} %bitcast.34), kind=kLoop, calls=%fused_computation.152 | loop fusion | flops 7168 | bytes 4112 | tf_op jit(solution)/shard_map/gather | solution.py:170
  42.2 2.1 select_select_fusion.3
  45.3 1.9 collective-permute-start.8
  47.2 2.6 %collective-permute-start.9 = (f32[512]{0:T(512)S(1)}, f32[512]{0:T(512)S(1)}, u32[]{:S(2)}, u32[]{:S(2)}) collective-permute-start(f32[512]{0:T(512)S(1)} %add_rsqrt_fusion), channel_id=1, source_target_pairs={{0,8},{4,12},{8,0},{12,4},{1,9},{5,13},{9,1},{13,5},{2,10},{6,14},... | collective-permute-start | bytes 6152 | tf_op jit(solution)/shard_map/ppermute | solution.py:207
  51.2 2.5 %fusion.111 = (bf16[256,1024]{1,0:T(8,128)(2,1)}, bf16[256,1024]{1,0:T(8,128)(2,1)}, bf16[256,1024]{1,0:T(8,128)(2,1)}) fusion(bf16[512,4096]{1,0:T(8,128)(2,1)S(1)} %fusion.2, s32[]{:T(128)S(6)} %select_n.324, s32[]{:T(128)S(6)} %select_n.338, s32[]{:T(128)S(6)} %select_n.331, s32[]{:T(128)S(6)} %select_n.326), kind=kLoop, calls=%fused_computation.169 | loop fusion | bytes 3145744 | tf_op jit(solution)/shard_map/dynamic_slice | solution.py:211
  53.7 7.3 %fusion.3 = f32[512,4,256]{0,2,1:T(8,128)S(1)} fusion(bf16[4096,4,256]{2,1,0:T(4,128)(2,1)} %param.8, bf16[512,4096]{1,0:T(8,128)(2,1)S(1)} %fusion.2), kind=kOutput, calls=%fused_computation.6 | convolution fusion | flops 4294967296 | bytes 14680064 | tf_op jit(solution)/shard_map/td,dgc->tgc/dot_general | solution.py:114
  65.5 2.7 %fusion.112 = (bf16[1,2048,4,128]{1,3,2,0:T(8,128)(2,1)S(1)}, bf16[1,2048,4,128]{1,3,2,0:T(8,128)(2,1)S(1)}) fusion(bf16[2,2048,4,128]{1,3,2,0:T(8,128)(2,1)} %collective-permute-done.3), kind=kLoop, calls=%fused_computation.170 | loop fusion | bytes 8388608 | tf_op jit(solution)/shard_map/slice | solution.py:129
  72.6 2.7 %pad_maximum_fusion.3 = (bf16[256,2048]{1,0:T(8,128)(2,1)}, bf16[256,2048]{1,0:T(8,128)(2,1)}) fusion(bf16[256,1024]{1,0:T(8,128)(2,1)S(1)} %copy.95, bf16[256,1024]{1,0:T(8,128)(2,1)} %get-tuple-element.24, bf16[256,1024]{1,0:T(8,128)(2,1)S(1)} %copy-done.10), kind=kLoop, calls=%fused_computation.61 | loop fusion | flops 3670016 | bytes 3670016 | tf_op jit(solution)/shard_map/concatenate | solution.py:57
  75.4 1.9 collective-permute-start.6
  77.3 2.5 %collective-permute-start.4 = (bf16[256,2048]{1,0:T(8,128)(2,1)}, bf16[256,2048]{1,0:T(8,128)(2,1)}, u32[]{:S(2)}, u32[]{:S(2)}) collective-permute-start(bf16[256,2048]{1,0:T(8,128)(2,1)} %get-tuple-element.39), channel_id=1, source_target_pairs={{0,4},{4,0},{8,12},{12,8},{1,5},{5,1},{9,13},{13,9},{2,6},{6,2},{1... | collective-permute-start | bytes 3145736 | tf_op jit(solution)/shard_map/ppermute | solution.py:58
  79.8 5.0 %fusion.50 = f32[1024,1024]{1,0:T(8,128)} fusion(bf16[512,4096]{1,0:T(8,128)(2,1)} %copy-done.1, s32[]{:T(128)} %select_n.334, s32[]{:T(128)S(6)} %select_n.333), kind=kOutput, calls=%fused_computation.70 | convolution fusion | flops 1073741824 | bytes 6291972 | tf_op jit(solution)/shard_map/tc,tr->cr/dot_general | solution.py:204
  84.8 1.9 copy.104
  86.8 2.0 copy.103
  88.7 2.9 %subtract_convert_fusion = (bf16[512,4,2,64]{3,0,2,1:T(8,128)(2,1)S(1)}, bf16[512,4,2,64]{3,0,2,1:T(8,128)(2,1)S(1)}) fusion(f32[512,4,2,64]{3,0,2,1:T(8,128)} %copy.104, f32[512,4,2,64]{3,0,2,1:T(8,128)} %copy.103, f32[512,64]{1,0:T(8,128)} %copy.66, f32[512,64]{1,0:T(8,128)} %copy.64), kind=kLoop, calls=%fused_computation.46 | loop fusion | flops 2097152 | bytes 3407872 | tf_op jit(solution)/shard_map/convert.8
  91.7 2.3 %fusion.7 = (f32[4,2,512]{2,1,0:T(2,128)S(1)}, f32[4,512,512,2]{2,1,3,0:T(8,128)S(1)}) fusion(pred[512,512]{0,1:T(8,128)(4,1)S(1)} %copy-done.11, bf16[512,4,2,64]{3,0,2,1:T(8,128)(2,1)S(1)} %get-tuple-element.14, bf16[512,4,2,64]{3,0,2,1:T(8,128)(2,1)S(1)} %get-tuple-element.13, bf16[512,4,64]{0,2,1:T(8,128)(2,1)S(1)} %copy-done.13, ...), kind=kOutput, calls=%fused_computation.11 | convolution fusion | flops 546304000 | bytes 10240000 | tf_op jit(solution)/shard_map/tgrh,ugh->grtu/dot_general | solution.py:141
  94.1 65.9 %collective-permute-done.6 = bf16[256,2048]{1,0:T(8,128)(2,1)} collective-permute-done((bf16[256,2048]{1,0:T(8,128)(2,1)}, bf16[256,2048]{1,0:T(8,128)(2,1)}, u32[]{:S(2)}, u32[]{:S(2)}) %collective-permute-start.6) | collective-permute-done | bytes 1048608 | tf_op jit(solution)/shard_map/ppermute | solution.py:58
  160.5 2.0 fusion.5
  168.8 1.9 slice.104
  170.7 2.2 %reshape.359 = bf16[256,2,4,128]{3,2,1,0:T(4,128)(2,1)} reshape(bf16[256,1024]{1,0:T(8,128)(2,1)} %slice.104) | data formatting | bytes 1048576 | tf_op jit(solution)/shard_map/reshape | solution.py:63
  172.9 1.9 slice.100
  174.7 2.2 %reshape.356 = bf16[256,2,4,128]{3,2,1,0:T(4,128)(2,1)} reshape(bf16[256,1024]{1,0:T(8,128)(2,1)} %slice.100) | data formatting | bytes 1048576 | tf_op jit(solution)/shard_map/reshape | solution.py:63
  177.0 2.2 %copy_dynamic-update-slice_fusion = (bf16[512,2,4,128]{3,0,2,1:T(8,128)(2,1)}, bf16[512,2,4,128]{3,0,2,1:T(8,128)(2,1)S(1)}) fusion(bf16[512,2,4,128]{3,0,2,1:T(8,128)(2,1)} %copy-done.7, s32[]{:T(128)S(6)} %select_n.328, bf16[256,2,4,128]{3,2,1,0:T(4,128)(2,1)} %reshape.359, bf16[512,2,4,128]{3,0,2,1:T(8,128)(2,1)S(1)} %copy_dynamic-update-slice_fusion.3, ...), kind=kLoop, calls=%fused_computation.101 | loop fusion | bytes 2097156 | tf_op jit(solution)/shard_map/dynamic_update_slice | solution.py:64
  188.4 2.6 %fusion.29 = bf16[512,4,2,128]{0,3,2,1:T(8,128)(2,1)S(1)} fusion(f32[512,4,2,128]{0,3,2,1:T(8,128)S(1)} %bitcast.173, f32[512,4,2,128]{0,3,2,1:T(8,128)S(1)} %bitcast.174, f32[4,512,512,2]{2,1,3,0:T(8,128)S(1)} %bitcast.167, f32[4,2,512]{2,1,0:T(2,128)S(1)} %get-tuple-element.54, pred[512,512]{0,1:T(8,128)(4,1)S(1)} %copy-done.11, ...), kind=kOutput, calls=%fused_computation.47 | convolution fusion | flops 548405248 | bytes 14483456 | tf_op jit(solution)/shard_map/grtu,ugh->tgrh/dot_general | solution.py:151
  192.4 2.6 %multiply_convert_fusion.2 = (bf16[512,1024]{1,0:T(8,128)(2,1)S(1)}, bf16[512,1024]{1,0:T(8,128)(2,1)S(1)}, bf16[512,1024]{1,0:T(8,128)(2,1)S(1)}) fusion(f32[1024]{0:T(1024)S(1)} %dynamic-slice-done, f32[512]{0:T(512)S(1)} %collective-permute-done.8, bf16[2048,1024]{1,0:T(8,128)(2,1)} %all-gather.2.cloned.1.call-done, s32[]{:T(128)S(6)} %select_n.335, ...), kind=kLoop, calls=%fused_computation.44 | loop fusion | flops 6291456 | bytes 6301708 | tf_op jit(solution)/shard_map/convert_element_type | solution.py:218
  195.1 2.2 %fusion.61 = f32[1024,1024]{1,0:T(8,128)S(1)} fusion(bf16[256,2048]{1,0:T(8,128)(2,1)} %collective-permute-done.7, bf16[512,1024]{1,0:T(8,128)(2,1)S(1)} %get-tuple-element.20, s32[]{:T(128)S(6)} %select_n.328), kind=kOutput, calls=%fused_computation.87 | convolution fusion | flops 536870912 | bytes 5242884 | tf_op jit(solution)/shard_map/tc,tr->cr/dot_general | solution.py:222
  202.7 1.9 fusion.75
  205.0 4.7 %add_multiply_fusion = f32[1024,1024]{1,0:T(8,128)} fusion(f32[1024,1024]{1,0:T(8,128)S(1)} %fusion.75, f32[1024,1024]{1,0:T(8,128)S(1)} %fusion.61, f32[1024,1024]{1,0:T(8,128)S(1)} %fusion.63, f32[1024,1024]{1,0:T(8,128)S(1)} %fusion.65, f32[1024,1024]{1,0:T(8,128)S(1)} %copy-done, f32[1024,1024]{1,0:T(8,128)S(1)} %fusion.67, ...), kind=kOutput, calls=%fused_computation.22 | convolution fusion | flops 544210944 | bytes 30408708 | tf_op jit(solution)/shard_map/tc,tr->cr/dot_general | solution.py:222
  (119 shorter events, 41.5 us)
Async XLA Ops:
  7.2 185.3 %all-gather.2.cloned.1.call-start = ((), (), s32[]{:S(2)}) async-start(), calls=%async_computation | async-start | bytes 5242880 | tf_op jit(solution)/shard_map/all_gather | solution.py:201
  7.2 26.5 %collective-permute-start.1 = (bf16[512,1024]{1,0:T(8,128)(2,1)}, bf16[512,1024]{1,0:T(8,128)(2,1)}, u32[]{:S(2)}, u32[]{:S(2)}) collective-permute-start(bf16[512,1024]{1,0:T(8,128)(2,1)} %param.6), channel_id=1, source_target_pairs={{0,2},{2,0},{1,3},{3,1},{4,6},{6,4},{5,7},{7,5},{8,10},{10,8},{9,1... | collective-permute-start | bytes 3145736 | tf_op jit(solution)/shard_map/ppermute | solution.py:91
  10.2 32.0 %collective-permute-start = (bf16[512,1024]{1,0:T(8,128)(2,1)}, bf16[512,1024]{1,0:T(8,128)(2,1)}, u32[]{:S(2)}, u32[]{:S(2)}) collective-permute-start(bf16[512,1024]{1,0:T(8,128)(2,1)} %param.6), channel_id=1, source_target_pairs={{0,1},{1,0},{2,3},{3,2},{4,5},{5,4},{6,7},{7,6},{8,9},{9,8},{10,11... | collective-permute-start | bytes 3145736 | tf_op jit(solution)/shard_map/ppermute | solution.py:26
  17.6 4.8 %copy-start.17 = (s32[3,8]{1,0:T(4,128)S(1)}, s32[3,8]{1,0:T(4,128)}, u32[]{:S(2)}) copy-start(s32[3,8]{1,0:T(4,128)} %param.11) | copy-start | bytes 292
  17.6 24.6 %copy-start.5 = (bf16[512,1024]{1,0:T(8,128)(2,1)S(1)}, bf16[512,1024]{1,0:T(8,128)(2,1)}, u32[]{:S(2)}) copy-start(bf16[512,1024]{1,0:T(8,128)(2,1)} %param.6) | copy-start | bytes 3145732
  21.9 43.6 %collective-permute-start.3 = (bf16[2,2048,4,128]{1,3,2,0:T(8,128)(2,1)}, bf16[2,2048,4,128]{1,3,2,0:T(8,128)(2,1)}, u32[]{:S(2)}, u32[]{:S(2)}) collective-permute-start(bf16[2,2048,4,128]{1,3,2,0:T(8,128)(2,1)} %pad_maximum_fusion.1), channel_id=1, source_target_pairs={{0,1},{1,0},{2,3},{3,2},{4,5},{5,4},{6,7},{7,6},{8,9},{9,8},{10,11... | collective-permute-start | bytes 12582920 | tf_op jit(solution)/shard_map/ppermute | solution.py:128
  33.7 8.5 %collective-permute-start.2 = (bf16[512,1024]{1,0:T(8,128)(2,1)}, bf16[512,1024]{1,0:T(8,128)(2,1)}, u32[]{:S(2)}, u32[]{:S(2)}) collective-permute-start(bf16[512,1024]{1,0:T(8,128)(2,1)} %collective-permute-done.1), channel_id=1, source_target_pairs={{0,1},{1,0},{2,3},{3,2},{4,5},{5,4},{6,7},{7,6},{8,9},{9,8},{10,11... | collective-permute-start | bytes 3145736 | tf_op jit(solution)/shard_map/ppermute | solution.py:26
  44.3 5.5 %copy-start.16 = (f32[4096]{0:T(1024)S(1)}, f32[4096]{0:T(1024)}, u32[]{:S(2)}) copy-start(f32[4096]{0:T(1024)} %param.7) | copy-start | bytes 49156
  45.3 147.1 %collective-permute-start.8 = (f32[512]{0:T(512)S(1)}, f32[512]{0:T(512)S(1)}, u32[]{:S(2)}, u32[]{:S(2)}) collective-permute-start(f32[512]{0:T(512)S(1)} %add_rsqrt_fusion), channel_id=1, source_target_pairs={{0,4},{4,0},{8,12},{12,8},{1,5},{5,1},{9,13},{13,9},{2,6},{6,2},{1... | collective-permute-start | bytes 6152 | tf_op jit(solution)/shard_map/ppermute | solution.py:207
  47.2 145.2 %collective-permute-start.9 = (f32[512]{0:T(512)S(1)}, f32[512]{0:T(512)S(1)}, u32[]{:S(2)}, u32[]{:S(2)}) collective-permute-start(f32[512]{0:T(512)S(1)} %add_rsqrt_fusion), channel_id=1, source_target_pairs={{0,8},{4,12},{8,0},{12,4},{1,9},{5,13},{9,1},{13,5},{2,10},{6,14},... | collective-permute-start | bytes 6152 | tf_op jit(solution)/shard_map/ppermute | solution.py:207
  51.2 18.8 %copy-start.1 = (bf16[512,4096]{1,0:T(8,128)(2,1)}, bf16[512,4096]{1,0:T(8,128)(2,1)S(1)}, u32[]{:S(2)}) copy-start(bf16[512,4096]{1,0:T(8,128)(2,1)S(1)} %fusion.2) | copy-start | bytes 12582916
  53.7 114.3 %collective-permute-start.10 = (bf16[256,1024]{1,0:T(8,128)(2,1)}, bf16[256,1024]{1,0:T(8,128)(2,1)}, u32[]{:S(2)}, u32[]{:S(2)}) collective-permute-start(bf16[256,1024]{1,0:T(8,128)(2,1)} %get-tuple-element.22), channel_id=1, source_target_pairs={{0,12},{4,8},{8,4},{12,0},{1,13},{5,9},{9,5},{13,1},{2,14},{6,10},... | collective-permute-start | bytes 1572872 | tf_op jit(solution)/shard_map/ppermute | solution.py:212
  61.0 2.0 copy-start.3
  70.0 1.6 copy-start.12
  70.0 1.6 copy-start.14
  72.6 12.2 %copy-start.6 = (f32[512,4,2,64]{0,3,2,1:T(8,128)S(1)}, f32[512,4,2,64]{0,3,2,1:T(8,128)}, u32[]{:S(2)}) copy-start(f32[512,4,2,64]{0,3,2,1:T(8,128)} %get-tuple-element.31) | copy-start | bytes 3145732
  75.4 84.6 %collective-permute-start.6 = (bf16[256,2048]{1,0:T(8,128)(2,1)}, bf16[256,2048]{1,0:T(8,128)(2,1)}, u32[]{:S(2)}, u32[]{:S(2)}) collective-permute-start(bf16[256,2048]{1,0:T(8,128)(2,1)} %get-tuple-element.40), channel_id=1, source_target_pairs={{0,8},{4,12},{8,0},{12,4},{1,9},{5,13},{9,1},{13,5},{2,10},{6,14},... | collective-permute-start | bytes 3145736 | tf_op jit(solution)/shard_map/ppermute | solution.py:58
  77.3 82.7 %collective-permute-start.4 = (bf16[256,2048]{1,0:T(8,128)(2,1)}, bf16[256,2048]{1,0:T(8,128)(2,1)}, u32[]{:S(2)}, u32[]{:S(2)}) collective-permute-start(bf16[256,2048]{1,0:T(8,128)(2,1)} %get-tuple-element.39), channel_id=1, source_target_pairs={{0,4},{4,0},{8,12},{12,8},{1,5},{5,1},{9,13},{13,9},{2,6},{6,2},{1... | collective-permute-start | bytes 3145736 | tf_op jit(solution)/shard_map/ppermute | solution.py:58
  88.7 3.0 %copy-start.11 = (pred[512,512]{0,1:T(8,128)(4,1)S(1)}, pred[512,512]{0,1:T(8,128)(4,1)}, u32[]{:S(2)}) copy-start(pred[512,512]{0,1:T(8,128)(4,1)} %fusion.53) | copy-start | bytes 786436
  88.7 3.0 %copy-start.13 = (bf16[512,4,64]{0,2,1:T(8,128)(2,1)S(1)}, bf16[512,4,64]{0,2,1:T(8,128)(2,1)}, u32[]{:S(2)}) copy-start(bf16[512,4,64]{0,2,1:T(8,128)(2,1)} %copy-done.12) | copy-start | bytes 786436
  88.7 3.0 %copy-start.15 = (bf16[512,4,64]{0,2,1:T(8,128)(2,1)S(1)}, bf16[512,4,64]{0,2,1:T(8,128)(2,1)}, u32[]{:S(2)}) copy-start(bf16[512,4,64]{0,2,1:T(8,128)(2,1)} %copy-done.14) | copy-start | bytes 786436
  94.1 68.4 %copy-start.2 = (f32[4,512,512,2]{2,1,3,0:T(8,128)}, f32[4,512,512,2]{2,1,3,0:T(8,128)S(1)}, u32[]{:S(2)}) copy-start(f32[4,512,512,2]{2,1,3,0:T(8,128)S(1)} %get-tuple-element.55) | copy-start | bytes 25165828
  160.0 8.8 %collective-permute-start.7 = (bf16[256,2048]{1,0:T(8,128)(2,1)}, bf16[256,2048]{1,0:T(8,128)(2,1)}, u32[]{:S(2)}, u32[]{:S(2)}) collective-permute-start(bf16[256,2048]{1,0:T(8,128)(2,1)} %collective-permute-done.6), channel_id=1, source_target_pairs={{0,1},{1,0},{2,3},{3,2},{4,5},{5,4},{6,7},{7,6},{8,9},{9,8},{10,11... | collective-permute-start | bytes 3145736 | tf_op jit(solution)/shard_map/ppermute | solution.py:26
  160.0 12.9 %collective-permute-start.5 = (bf16[256,2048]{1,0:T(8,128)(2,1)}, bf16[256,2048]{1,0:T(8,128)(2,1)}, u32[]{:S(2)}, u32[]{:S(2)}) collective-permute-start(bf16[256,2048]{1,0:T(8,128)(2,1)} %collective-permute-done.4), channel_id=1, source_target_pairs={{0,1},{1,0},{2,3},{3,2},{4,5},{5,4},{6,7},{7,6},{8,9},{9,8},{10,11... | collective-permute-start | bytes 3145736 | tf_op jit(solution)/shard_map/ppermute | solution.py:26
  168.0 24.4 %collective-permute-start.11 = (f32[512]{0:T(512)S(1)}, f32[512]{0:T(512)S(1)}, u32[]{:S(2)}, u32[]{:S(2)}) collective-permute-start(f32[512]{0:T(512)S(1)} %add_rsqrt_fusion), channel_id=1, source_target_pairs={{0,12},{4,8},{8,4},{12,0},{1,13},{5,9},{9,5},{13,1},{2,14},{6,10},... | collective-permute-start | bytes 6152 | tf_op jit(solution)/shard_map/ppermute | solution.py:207
  168.8 35.9 %collective-permute-start.12 = (bf16[256,1024]{1,0:T(8,128)(2,1)}, bf16[256,1024]{1,0:T(8,128)(2,1)}, u32[]{:S(2)}, u32[]{:S(2)}) collective-permute-start(bf16[256,1024]{1,0:T(8,128)(2,1)} %collective-permute-done.10), channel_id=1, source_target_pairs={{0,1},{1,0},{2,3},{3,2},{4,5},{5,4},{6,7},{7,6},{8,9},{9,8},{10,11... | collective-permute-start | bytes 1572872 | tf_op jit(solution)/shard_map/ppermute | solution.py:26
  184.7 2.2 %slice-start = ((s8[8388608]{0:T(1024)(128)(4,1)}), s8[4194304]{0:T(1024)(128)(4,1)S(1)}, s32[]{:S(2)}) async-start(s8[8388608]{0:T(1024)(128)(4,1)} %bitcast.166), calls=%async_computation.1 | async-start | bytes 8388608
  185.6 2.7 %slice-start.1 = ((s8[8388608]{0:T(1024)(128)(4,1)}), s8[4194304]{0:T(1024)(128)(4,1)S(1)}, s32[]{:S(2)}) async-start(s8[8388608]{0:T(1024)(128)(4,1)} %bitcast.166), calls=%async_computation.2 | async-start | bytes 8388608
  185.6 2.7 %copy-start.9 = (bf16[512,4,128]{0,2,1:T(8,128)(2,1)S(1)}, bf16[512,4,128]{0,2,1:T(8,128)(2,1)}, u32[]{:S(2)}) copy-start(bf16[512,4,128]{0,2,1:T(8,128)(2,1)} %copy-done.8) | copy-start | bytes 1572868
  188.4 4.1 %dynamic-slice-start = ((f32[4096]{0:T(1024)}, s32[]{:T(128)}), f32[1024]{0:T(1024)S(1)}, s32[]{:S(2)}) async-start(f32[4096]{0:T(1024)} %param.7, s32[]{:T(128)} %select_n.334), calls=%async_computation.3 | async-start | bytes 8704 | tf_op jit(solution)/shard_map/dynamic_slice | solution.py:202
  195.1 7.6 %copy-start.4 = (bf16[512,1024]{1,0:T(8,128)(2,1)}, bf16[512,1024]{1,0:T(8,128)(2,1)S(1)}, u32[]{:S(2)}) copy-start(bf16[512,1024]{1,0:T(8,128)(2,1)S(1)} %get-tuple-element.21) | copy-start | bytes 3145732
  202.7 2.3 %copy-start = (f32[1024,1024]{1,0:T(8,128)S(1)}, f32[1024,1024]{1,0:T(8,128)}, u32[]{:S(2)}) copy-start(f32[1024,1024]{1,0:T(8,128)} %fusion.50) | copy-start | bytes 12582916
  (3 other events, 3.6 us)
Sparse Core Ops, SparseCore 0:
  10.4 135.1 all-gather.1

commit v9 on v7

--- a/solution.py
+++ b/solution.py
@@ -131,8 +131,18 @@
         "grtu,ugh->tgrh", weights.astype(jnp.bfloat16), values, preferred_element_type=jnp.float32
     )
     query_pairs = queries.reshape(2, block_len, local_groups, per_group, head_size)
-    for section in range(1, lax.axis_size("seq").bit_length()):
-        (far_pair,) = split_send((jnp.stack([keys, values]).swapaxes(0, 1),), "seq", section - 1)
+    seq_count = lax.axis_size("seq")
+    band = width // seq_count
+    share = row_count // sub_count
+    my_rows = lax.dynamic_slice_in_dim(normed, sub_index * share, share, 0)
+    outgoing_rows = [
+        lax.dynamic_slice_in_dim(my_rows, ((seq_index + shift) % seq_count) * band, band, 1)
+        for shift in range(1, seq_count)
+    ]
+    kv_pair = jnp.stack([keys, values]).swapaxes(0, 1)
+    outgoing_rows, kv_pair = lax.optimization_barrier((outgoing_rows, kv_pair))
+    for section in range(1, seq_count.bit_length()):
+        (far_pair,) = split_send((kv_pair,), "seq", section - 1)
         far_keys = far_pair[:, 0]
         far_values = far_pair[:, 1]
         far_keys = far_keys.reshape(2, block_len, local_groups, head_size)
@@ -173,10 +183,8 @@
     column_gain = lax.dynamic_slice_in_dim(norm_gain, owner_index * tile_cols, tile_cols, 0)
     mine = lax.dynamic_slice_in_dim(normed, seq_index * band, band, 1)
     gram_sum = jnp.einsum("tc,tr->cr", mine, owned, preferred_element_type=jnp.float32)
-    my_rows = lax.dynamic_slice_in_dim(normed, sub_index * share, share, 0)
     for shift in range(1, seq_count):
-        target = (seq_index + shift) % seq_count
-        outgoing = lax.dynamic_slice_in_dim(my_rows, target * band, band, 1)
+        outgoing = outgoing_rows[shift - 1]
         route = [(j, (j + shift) % seq_count) for j in range(seq_count)]
         incoming, their_scale = lax.ppermute((outgoing, row_scale), "seq", route)
         halves = swap_halves(incoming, sub_count, sub_index)

time: 193 us -> 196 us (1.016)
  other arithmetic: 21.9 us -> 25.3 us
  local copies, waits for them, and re-layouts: 28.6 us -> 31.1 us
    another operation x2, other arithmetic: 1.02 us -> 4 us
    unnamed x36 -> x32, local copies, waits for them, and re-layouts: 10.5 us -> 11.3 us
  transfers between devices with their start and end apart: 18 -> 18, of which waited for: 3 -> 3; matrix products, arithmetic and copies ran while one was open for 44% -> 45% of each run, Pallas kernels for 0% -> 0%
where the time goes in v9:
time: 196 us; the launch traced here: 195 us
  waiting for transfers between devices  69.6 us (36%)
  matrix products  40.3 us (21%)
  local copies, waits for them, and re-layouts  31.1 us (16%)
  other arithmetic  25.3 us (13%)
  between operations  14.5 us (7%)
  starting transfers between devices  14.2 us (7%)
    ppermute x6, waiting for transfers between devices, body(): incoming, their_scale = lax.ppermute((outgoing, row_scale), 'seq', route)  33.8 us
    ppermute x2, waiting for transfers between devices, from_partner(): return lax.ppermute(block, axis, route)  18.8 us
    ppermute x1, waiting for transfers between devices, body(): across.append(lax.ppermute(tokens, 'kvh', route))  17 us
    unnamed x32, local copies, waits for them, and re-layouts  11.3 us
    dot_general x6, matrix products, body(): jnp.einsum('tc,tr->cr', halves[lane_shift], their_rows, preferred_element...  9.57 us
    ppermute x6, starting transfers between devices, body(): incoming, their_scale = lax.ppermute((outgoing, row_scale), 'seq', route)  8.38 us
    dot_general x1, matrix products, body(): jnp.einsum('td,dgc->tgc', normed, w_query, preferred_element_type=jnp.flo...  8.29 us
    squeeze x2, local copies, waits for them, and re-layouts, body(): key_part, value_part = (weight_pair[0], weight_pair[1])  7.05 us
  transfers between devices with their start and end apart: 18, of which 3 were waited for; matrix products, arithmetic and copies ran while one was open for 45% of the time, Pallas kernels for 0%

profile of v9, /device:TPU:0, one launch (start us, length us, event | category | flops | bytes accessed | tf_op | source)
XLA Modules:
  0.0 195.1 jit_solution(4782392224219918615)
XLA Ops:
  7.2 3.0 %collective-permute-start.1 = (bf16[512,1024]{1,0:T(8,128)(2,1)}, bf16[512,1024]{1,0:T(8,128)(2,1)}, u32[]{:S(2)}, u32[]{:S(2)}) collective-permute-start(bf16[512,1024]{1,0:T(8,128)(2,1)} %param.6), channel_id=1, source_target_pairs={{0,2},{2,0},{1,3},{3,1},{4,6},{6,4},{5,7},{7,5},{8,10},{10,8},{9,1... | collective-permute-start | bytes 3145736 | tf_op jit(solution)/shard_map/ppermute | solution.py:70
  10.3 2.8 %copy_bitcast_fusion = (bf16[1,2048,4,128]{3,1,2,0:T(8,128)(2,1)S(1)}, bf16[1,2048,4,128]{3,1,2,0:T(8,128)(2,1)S(1)}) fusion(bf16[2048,4,128]{2,1,0:T(4,128)(2,1)} %param.9, bf16[2048,4,128]{2,1,0:T(4,128)(2,1)} %param.10), kind=kLoop, calls=%fused_computation.48 | loop fusion | bytes 8388608 | tf_op jit(solution)/shard_map/stack | solution.py:107
  13.1 2.4 %pad_maximum_fusion.1 = bf16[2,2048,4,128]{3,1,2,0:T(8,128)(2,1)} fusion(bf16[1,2048,4,128]{3,1,2,0:T(8,128)(2,1)S(1)} %get-tuple-element.65, bf16[1,2048,4,128]{3,1,2,0:T(8,128)(2,1)S(1)} %get-tuple-element.64), kind=kLoop, calls=%fused_computation.14 | loop fusion | flops 2097152 | bytes 8388608 | tf_op jit(solution)/shard_map/stack | solution.py:107
  16.7 17.0 %collective-permute-done.1 = bf16[512,1024]{1,0:T(8,128)(2,1)} collective-permute-done((bf16[512,1024]{1,0:T(8,128)(2,1)}, bf16[512,1024]{1,0:T(8,128)(2,1)}, u32[]{:S(2)}, u32[]{:S(2)}) %collective-permute-start.1) | collective-permute-done | bytes 1048608 | tf_op jit(solution)/shard_map/ppermute | solution.py:70
  34.4 2.6 %copy.53 = bf16[2048,4,128]{0,2,1:T(8,128)(2,1)} copy(bf16[2048,4,128]{2,1,0:T(4,128)(2,1)S(1)} %copy-done.5) | data formatting | bytes 4194304 | tf_op args[3]
  37.0 2.6 %select_reduce_fusion.1 = (f32[512]{0:T(512)S(1)}, f32[512]{0:T(512)S(1)}) fusion(f32[]{:T(128)} %bitcast.45, f32[]{:T(128)} %bitcast.44, f32[]{:T(128)} %bitcast.32, f32[]{:T(128)} %bitcast.31), kind=kLoop, calls=%fused_computation.151 | loop fusion | flops 7168 | bytes 4112 | tf_op jit(solution)/shard_map/gather | solution.py:151
  42.1 1.8 multiply_cosine_fusion
  43.9 2.1 %select_select_fusion.3 = (bf16[512,1024]{1,0:T(8,128)(2,1)S(1)}, bf16[512,1024]{1,0:T(8,128)(2,1)S(1)}, bf16[512,1024]{1,0:T(8,128)(2,1)S(1)}, bf16[512,1024]{1,0:T(8,128)(2,1)S(1)}) fusion(bf16[512,1024]{1,0:T(8,128)(2,1)} %collective-permute-done.1, bf16[512,1024]{1,0:T(8,128)(2,1)} %collective-permute-done.2, bf16[512,1024]{1,0:T(8,128)(2,1)S(1)} %copy-done.7, ...), kind=kLoop, calls=%fused_computation.84 | loop fusion | flops 6291456 | bytes 8388620 | tf_op jit(solution)/shard_map/select_n | solution.py:78
  47.1 1.9 collective-permute-start.9
  49.0 2.6 %collective-permute-start.12 = (f32[512]{0:T(512)S(1)}, f32[512]{0:T(512)S(1)}, u32[]{:S(2)}, u32[]{:S(2)}) collective-permute-start(f32[512]{0:T(512)S(1)} %add_rsqrt_fusion), channel_id=1, source_target_pairs={{0,8},{4,12},{8,0},{12,4},{1,9},{5,13},{9,1},{13,5},{2,10},{6,14},... | collective-permute-start | bytes 6152 | tf_op jit(solution)/shard_map/ppermute | solution.py:189
  54.3 2.0 %copy-done.1 = bf16[512,4096]{1,0:T(8,128)(2,1)} copy-done((bf16[512,4096]{1,0:T(8,128)(2,1)}, bf16[512,4096]{1,0:T(8,128)(2,1)S(1)}, u32[]{:S(2)}) %copy-start.1) | copy-done | bytes 4194328
  57.9 8.3 %fusion.3 = f32[512,4,256]{0,2,1:T(8,128)S(1)} fusion(bf16[4096,4,256]{2,1,0:T(4,128)(2,1)} %param.8, bf16[512,4096]{1,0:T(8,128)(2,1)} %copy-done.1), kind=kOutput, calls=%fused_computation.6 | convolution fusion | flops 4294967296 | bytes 14680064 | tf_op jit(solution)/shard_map/td,dgc->tgc/dot_general | solution.py:93
  66.4 1.9 copy.91
  68.3 1.9 copy.90
  70.2 3.7 %fusion.118 = (bf16[256,1024]{1,0:T(8,128)(2,1)}, bf16[256,1024]{1,0:T(8,128)(2,1)}, bf16[256,1024]{1,0:T(8,128)(2,1)}) fusion(bf16[512,4096]{1,0:T(8,128)(2,1)} %copy-done.1, s32[]{:T(128)S(6)} %select_n.348, s32[]{:T(128)S(6)} %select_n.357, s32[]{:T(128)S(6)} %select_n.354, s32[]{:T(128)S(6)} %select_n.351), kind=kLoop, calls=%fused_computation.168 | loop fusion | bytes 3145744 | tf_op jit(solution)/shard_map/dynamic_slice | solution.py:139
  73.9 2.4 %subtract_convert_fusion = (bf16[512,4,2,64]{3,0,2,1:T(8,128)(2,1)S(1)}, bf16[512,4,2,64]{3,0,2,1:T(8,128)(2,1)S(1)}) fusion(f32[512,4,2,64]{3,0,2,1:T(8,128)S(1)} %copy-done.4, f32[512,4,2,64]{3,0,2,1:T(8,128)} %copy.90, f32[512,64]{1,0:T(8,128)} %get-tuple-element.46, f32[512,64]{1,0:T(8,128)} %get-tuple-element.45), kind=kLoop, calls=%fused_computation.53 | loop fusion | flops 2097152 | bytes 3407872 | tf_op jit(solution)/shard_map/convert.8
  76.9 2.9 %fusion.21 = f32[512,4,128]{2,0,1:T(8,128)S(1)} fusion(bf16[2,2048,4,128]{3,1,2,0:T(8,128)(2,1)} %collective-permute-done.3, bf16[512,4096]{1,0:T(8,128)(2,1)S(1)} %copy-done.2, s32[]{:T(128)S(6)} %select_n.341), kind=kOutput, calls=%fused_computation.35 | convolution fusion | flops 1073741824 | bytes 5242884 | tf_op jit(solution)/shard_map/td,dgh->tgh/dot_general | solution.py:112
  79.8 2.2 %fusion.54 = bf16[512,4,128]{2,0,1:T(8,128)(2,1)} fusion(f32[512,4,128]{2,0,1:T(8,128)S(1)} %fusion.21, bf16[2048,4,128]{2,1,0:T(4,128)(2,1)S(1)} %copy-done.9, bf16[512,4096]{1,0:T(8,128)(2,1)S(1)} %copy-done.2, s32[]{:T(128)S(6)} %select_n.340), kind=kOutput, calls=%fused_computation.68 | convolution fusion | flops 1074266112 | bytes 5767172 | tf_op jit(solution)/shard_map/td,dgh->tgh/dot_general | solution.py:112
  81.9 3.0 %slice_bitcast_fusion = bf16[2048,4,128]{2,0,1:T(8,128)(2,1)} fusion(bf16[2,2048,4,128]{3,1,2,0:T(8,128)(2,1)} %collective-permute-done.3), kind=kLoop, calls=%fused_computation.33 | loop fusion | bytes 4194304 | tf_op jit(solution)/shard_map/squeeze | solution.py:108
  85.0 4.0 %copy.54 = bf16[2048,4,128]{0,2,1:T(8,128)(2,1)} copy(bf16[2048,4,128]{2,0,1:T(8,128)(2,1)} %slice_bitcast_fusion) | data formatting | bytes 4194304 | tf_op jit(solution)/shard_map/squeeze | solution.py:108
  89.0 4.5 %fusion.35 = f32[512,512]{0,1} fusion(bf16[2048,512]{0,1:T(8,128)(2,1)} %bitcast.182, bf16[512,4096]{1,0:T(8,128)(2,1)} %copy-done.1, s32[]{:T(128)S(6)} %select_n.341), kind=kOutput, calls=%fused_computation.57 | convolution fusion | flops 1073741824 | bytes 5242884
  93.5 2.5 %copy.56 = f32[512,4,128]{2,0,1:T(8,128)} copy(f32[512,4,128]{0,2,1:T(8,128)} %bitcast.188) | data formatting | bytes 2097152 | tf_op jit(solution)/shard_map/td,dgh->tgh/dot_general | solution.py:111
  97.4 1.6 subtract_convert_fusion.1
  100.5 3.3 %fusion.63 = f32[1024,1024]{1,0:T(8,128)} fusion(bf16[512,4096]{1,0:T(8,128)(2,1)S(1)} %copy-done.3, s32[]{:T(128)} %select_n.363, s32[]{:T(128)S(6)} %select_n.362), kind=kOutput, calls=%fused_computation.75 | convolution fusion | flops 1073741824 | bytes 6291464 | tf_op jit(solution)/shard_map/tc,tr->cr/dot_general | solution.py:185
  103.9 2.5 %fusion.7 = (f32[4,2,512]{2,1,0:T(2,128)S(1)}, f32[4,512,512,2]{2,1,3,0:T(8,128)S(1)}) fusion(pred[512,512]{0,1:T(8,128)(4,1)S(1)} %fusion.66, bf16[512,4,2,64]{3,0,2,1:T(8,128)(2,1)S(1)} %get-tuple-element.22, bf16[512,4,2,64]{3,0,2,1:T(8,128)(2,1)S(1)} %get-tuple-element.21, bf16[512,4,64]{2,0,1:T(8,128)(2,1)S(1)} %get-tuple-element.40, ...), kind=kOutput, calls=%fused_computation.11 | convolution fusion | flops 546304000 | bytes 10240000 | tf_op jit(solution)/shard_map/tgrh,ugh->grtu/dot_general | solution.py:120
  106.3 18.8 %collective-permute-done.6 = bf16[256,2,4,128]{3,0,2,1:T(8,128)(2,1)S(1)} collective-permute-done((bf16[256,2,4,128]{3,0,2,1:T(8,128)(2,1)S(1)}, bf16[256,2,4,128]{3,0,2,1:T(8,128)(2,1)S(1)}, u32[]{:S(2)}, u32[]{:S(2)}) %collective-permute-start.6) | collective-permute-done | bytes 524320 | tf_op jit(solution)/shard_map/ppermute | solution.py:18
  125.6 1.8 fusion.5
  137.2 2.5 %fusion.33 = bf16[512,4,2,128]{0,3,2,1:T(8,128)(2,1)S(1)} fusion(f32[512,4,2,128]{0,3,2,1:T(8,128)S(1)} %bitcast.179, f32[512,4,2,128]{0,3,2,1:T(8,128)S(1)} %bitcast.180, f32[4,512,512,2]{2,1,3,0:T(8,128)S(1)} %get-tuple-element.59, f32[4,2,512]{2,1,0:T(2,128)S(1)} %get-tuple-element.58, pred[512,512]{0,1:T(8,128)(4,1)S(1)} %fusion.66, ...), kind=kOutput, calls=%fused_computation.54 | convolution fusion | flops 548405248 | bytes 14483456 | tf_op jit(solution)/shard_map/grtu,ugh->tgrh/dot_general | solution.py:130
  141.2 33.8 %collective-permute-done.11 = bf16[256,1024]{1,0:T(8,128)(2,1)S(1)} collective-permute-done((bf16[256,1024]{1,0:T(8,128)(2,1)}, bf16[256,1024]{1,0:T(8,128)(2,1)S(1)}, u32[]{:S(2)}, u32[]{:S(2)}) %collective-permute-start.11) | collective-permute-done | bytes 524320 | tf_op jit(solution)/shard_map/ppermute | solution.py:189
  175.6 2.6 %multiply_convert_fusion.2 = (bf16[512,1024]{1,0:T(8,128)(2,1)S(1)}, bf16[512,1024]{1,0:T(8,128)(2,1)S(1)}, bf16[512,1024]{1,0:T(8,128)(2,1)S(1)}) fusion(f32[1024]{0:T(1024)S(1)} %dynamic-slice-done, f32[512]{0:T(512)S(1)} %collective-permute-done.9, bf16[2048,1024]{1,0:T(8,128)(2,1)} %all-gather.2.cloned.1.call-done, s32[]{:T(128)S(6)} %select_n.365, ...), kind=kLoop, calls=%fused_computation.51 | loop fusion | flops 6291456 | bytes 6301708 | tf_op jit(solution)/shard_map/convert_element_type | solution.py:195
  181.3 1.9 fusion.84
  183.6 4.6 %add_multiply_fusion = f32[1024,1024]{1,0:T(8,128)} fusion(f32[1024,1024]{1,0:T(8,128)S(1)} %fusion.78, f32[1024,1024]{1,0:T(8,128)S(1)} %fusion.80, f32[1024,1024]{1,0:T(8,128)S(1)} %fusion.82, f32[1024,1024]{1,0:T(8,128)S(1)} %fusion.84, f32[1024,1024]{1,0:T(8,128)S(1)} %copy-done, f32[1024,1024]{1,0:T(8,128)S(1)} %fusion.86, ...), kind=kOutput, calls=%fused_computation.22 | convolution fusion | flops 544210944 | bytes 30408708 | tf_op jit(solution)/shard_map/tc,tr->cr/dot_general | solution.py:199
  (106 shorter events, 29.0 us)
Async XLA Ops:
  7.2 168.4 %all-gather.2.cloned.1.call-start = ((), (), s32[]{:S(2)}) async-start(), calls=%async_computation | async-start | bytes 5242880 | tf_op jit(solution)/shard_map/all_gather | solution.py:182
  7.2 26.5 %collective-permute-start.1 = (bf16[512,1024]{1,0:T(8,128)(2,1)}, bf16[512,1024]{1,0:T(8,128)(2,1)}, u32[]{:S(2)}, u32[]{:S(2)}) collective-permute-start(bf16[512,1024]{1,0:T(8,128)(2,1)} %param.6), channel_id=1, source_target_pairs={{0,2},{2,0},{1,3},{3,1},{4,6},{6,4},{5,7},{7,5},{8,10},{10,8},{9,1... | collective-permute-start | bytes 3145736 | tf_op jit(solution)/shard_map/ppermute | solution.py:70
  10.2 33.7 %collective-permute-start = (bf16[512,1024]{1,0:T(8,128)(2,1)}, bf16[512,1024]{1,0:T(8,128)(2,1)}, u32[]{:S(2)}, u32[]{:S(2)}) collective-permute-start(bf16[512,1024]{1,0:T(8,128)(2,1)} %param.6), channel_id=1, source_target_pairs={{0,1},{1,0},{2,3},{3,2},{4,5},{5,4},{6,7},{7,6},{8,9},{9,8},{10,11... | collective-permute-start | bytes 3145736 | tf_op jit(solution)/shard_map/ppermute | solution.py:26
  13.0 2.9 %copy-start.13 = (s32[3,8]{1,0:T(4,128)S(1)}, s32[3,8]{1,0:T(4,128)}, u32[]{:S(2)}) copy-start(s32[3,8]{1,0:T(4,128)} %param.11) | copy-start | bytes 292
  13.1 21.3 %copy-start.5 = (bf16[2048,4,128]{2,1,0:T(4,128)(2,1)S(1)}, bf16[2048,4,128]{2,1,0:T(4,128)(2,1)}, u32[]{:S(2)}) copy-start(bf16[2048,4,128]{2,1,0:T(4,128)(2,1)} %param.9) | copy-start | bytes 6291460
  15.4 28.5 %copy-start.7 = (bf16[512,1024]{1,0:T(8,128)(2,1)S(1)}, bf16[512,1024]{1,0:T(8,128)(2,1)}, u32[]{:S(2)}) copy-start(bf16[512,1024]{1,0:T(8,128)(2,1)} %param.6) | copy-start | bytes 3145732
  15.4 60.9 %collective-permute-start.3 = (bf16[2,2048,4,128]{3,1,2,0:T(8,128)(2,1)}, bf16[2,2048,4,128]{3,1,2,0:T(8,128)(2,1)}, u32[]{:S(2)}, u32[]{:S(2)}) collective-permute-start(bf16[2,2048,4,128]{3,1,2,0:T(8,128)(2,1)} %pad_maximum_fusion.1), channel_id=1, source_target_pairs={{0,1},{1,0},{2,3},{3,2},{4,5},{5,4},{6,7},{7,6},{8,9},{9,8},{10,11... | collective-permute-start | bytes 12582920 | tf_op jit(solution)/shard_map/ppermute | solution.py:107
  33.7 10.2 %collective-permute-start.2 = (bf16[512,1024]{1,0:T(8,128)(2,1)}, bf16[512,1024]{1,0:T(8,128)(2,1)}, u32[]{:S(2)}, u32[]{:S(2)}) collective-permute-start(bf16[512,1024]{1,0:T(8,128)(2,1)} %collective-permute-done.1), channel_id=1, source_target_pairs={{0,1},{1,0},{2,3},{3,2},{4,5},{5,4},{6,7},{7,6},{8,9},{9,8},{10,11... | collective-permute-start | bytes 3145736 | tf_op jit(solution)/shard_map/ppermute | solution.py:26
  46.1 6.8 %copy-start.12 = (f32[4096]{0:T(1024)S(1)}, f32[4096]{0:T(1024)}, u32[]{:S(2)}) copy-start(f32[4096]{0:T(1024)} %param.7) | copy-start | bytes 49156
  47.1 9.2 %copy-start.8 = (bf16[2048,4,128]{0,2,1:T(8,128)(2,1)S(1)}, bf16[2048,4,128]{0,2,1:T(8,128)(2,1)}, u32[]{:S(2)}) copy-start(bf16[2048,4,128]{0,2,1:T(8,128)(2,1)} %copy.53) | copy-start | bytes 6291460
  47.1 88.0 %collective-permute-start.9 = (f32[512]{0:T(512)S(1)}, f32[512]{0:T(512)S(1)}, u32[]{:S(2)}, u32[]{:S(2)}) collective-permute-start(f32[512]{0:T(512)S(1)} %add_rsqrt_fusion), channel_id=1, source_target_pairs={{0,4},{4,8},{8,12},{12,0},{1,5},{5,9},{9,13},{13,1},{2,6},{6,10},{... | collective-permute-start | bytes 6152 | tf_op jit(solution)/shard_map/ppermute | solution.py:189
  49.0 126.6 %collective-permute-start.12 = (f32[512]{0:T(512)S(1)}, f32[512]{0:T(512)S(1)}, u32[]{:S(2)}, u32[]{:S(2)}) collective-permute-start(f32[512]{0:T(512)S(1)} %add_rsqrt_fusion), channel_id=1, source_target_pairs={{0,8},{4,12},{8,0},{12,4},{1,9},{5,13},{9,1},{13,5},{2,10},{6,14},... | collective-permute-start | bytes 6152 | tf_op jit(solution)/shard_map/ppermute | solution.py:189
  51.5 124.0 %collective-permute-start.15 = (f32[512]{0:T(512)S(1)}, f32[512]{0:T(512)S(1)}, u32[]{:S(2)}, u32[]{:S(2)}) collective-permute-start(f32[512]{0:T(512)S(1)} %add_rsqrt_fusion), channel_id=1, source_target_pairs={{0,12},{4,0},{8,4},{12,8},{1,13},{5,1},{9,5},{13,9},{2,14},{6,2},{... | collective-permute-start | bytes 6152 | tf_op jit(solution)/shard_map/ppermute | solution.py:189
  54.2 2.0 %copy-start.1 = (bf16[512,4096]{1,0:T(8,128)(2,1)}, bf16[512,4096]{1,0:T(8,128)(2,1)S(1)}, u32[]{:S(2)}) copy-start(bf16[512,4096]{1,0:T(8,128)(2,1)S(1)} %fusion.2) | copy-start | bytes 12582916
  70.2 3.7 %copy-start.4 = (f32[512,4,2,64]{3,0,2,1:T(8,128)S(1)}, f32[512,4,2,64]{3,0,2,1:T(8,128)}, u32[]{:S(2)}) copy-start(f32[512,4,2,64]{3,0,2,1:T(8,128)} %copy.91) | copy-start | bytes 3145732
  73.9 3.0 %copy-start.2 = (bf16[512,4096]{1,0:T(8,128)(2,1)S(1)}, bf16[512,4096]{1,0:T(8,128)(2,1)}, u32[]{:S(2)}) copy-start(bf16[512,4096]{1,0:T(8,128)(2,1)} %copy-done.1) | copy-start | bytes 12582916
  76.3 3.5 %copy-start.9 = (bf16[2048,4,128]{2,1,0:T(4,128)(2,1)S(1)}, bf16[2048,4,128]{2,1,0:T(4,128)(2,1)}, u32[]{:S(2)}) copy-start(bf16[2048,4,128]{2,1,0:T(4,128)(2,1)} %param.10) | copy-start | bytes 6291460
  96.0 3.0 %copy-start.10 = (bf16[512,4,128]{2,0,1:T(8,128)(2,1)S(1)}, bf16[512,4,128]{2,0,1:T(8,128)(2,1)}, u32[]{:S(2)}) copy-start(bf16[512,4,128]{2,0,1:T(8,128)(2,1)} %fusion.54) | copy-start | bytes 1572868
  97.4 3.2 %copy-start.3 = (bf16[512,4096]{1,0:T(8,128)(2,1)S(1)}, bf16[512,4096]{1,0:T(8,128)(2,1)}, u32[]{:S(2)}) copy-start(bf16[512,4096]{1,0:T(8,128)(2,1)} %copy-done.1) | copy-start | bytes 12582916
  99.4 25.7 %collective-permute-start.6 = (bf16[256,2,4,128]{3,0,2,1:T(8,128)(2,1)S(1)}, bf16[256,2,4,128]{3,0,2,1:T(8,128)(2,1)S(1)}, u32[]{:S(2)}, u32[]{:S(2)}) collective-permute-start(bf16[256,2,4,128]{3,0,2,1:T(8,128)(2,1)S(1)} %constant_dynamic-slice_fusion.2), channel_id=1, source_target_pairs={{0,8},{8,0},{4,12},{12,4},{1,9},{9,1},{5,13},{13,5},{2,10},{10,2},... | collective-permute-start | bytes 1572872 | tf_op jit(solution)/shard_map/ppermute | solution.py:18
  99.6 25.5 %collective-permute-start.4 = (bf16[256,2,4,128]{3,0,2,1:T(8,128)(2,1)S(1)}, bf16[256,2,4,128]{3,0,2,1:T(8,128)(2,1)S(1)}, u32[]{:S(2)}, u32[]{:S(2)}) collective-permute-start(bf16[256,2,4,128]{3,0,2,1:T(8,128)(2,1)S(1)} %constant_dynamic-slice_fusion.2), channel_id=1, source_target_pairs={{0,4},{4,0},{8,12},{12,8},{1,5},{5,1},{9,13},{13,9},{2,6},{6,2},{1... | collective-permute-start | bytes 1572872 | tf_op jit(solution)/shard_map/ppermute | solution.py:18
  125.1 2.7 %collective-permute-start.7 = (bf16[256,2,4,128]{3,0,2,1:T(8,128)(2,1)S(1)}, bf16[256,2,4,128]{3,0,2,1:T(8,128)(2,1)S(1)}, u32[]{:S(2)}, u32[]{:S(2)}) collective-permute-start(bf16[256,2,4,128]{3,0,2,1:T(8,128)(2,1)S(1)} %collective-permute-done.6), channel_id=1, source_target_pairs={{0,1},{1,0},{2,3},{3,2},{4,5},{5,4},{6,7},{7,6},{8,9},{9,8},{10,11... | collective-permute-start | bytes 1572872 | tf_op jit(solution)/shard_map/ppermute | solution.py:26
  125.1 3.7 %collective-permute-start.5 = (bf16[256,2,4,128]{3,0,2,1:T(8,128)(2,1)S(1)}, bf16[256,2,4,128]{3,0,2,1:T(8,128)(2,1)S(1)}, u32[]{:S(2)}, u32[]{:S(2)}) collective-permute-start(bf16[256,2,4,128]{3,0,2,1:T(8,128)(2,1)S(1)} %collective-permute-done.4), channel_id=1, source_target_pairs={{0,1},{1,0},{2,3},{3,2},{4,5},{5,4},{6,7},{7,6},{8,9},{9,8},{10,11... | collective-permute-start | bytes 1572872 | tf_op jit(solution)/shard_map/ppermute | solution.py:26
  127.8 47.6 %collective-permute-start.14 = (bf16[256,1024]{1,0:T(8,128)(2,1)}, bf16[256,1024]{1,0:T(8,128)(2,1)S(1)}, u32[]{:S(2)}, u32[]{:S(2)}) collective-permute-start(bf16[256,1024]{1,0:T(8,128)(2,1)} %get-tuple-element.9), channel_id=1, source_target_pairs={{0,12},{4,0},{8,4},{12,8},{1,13},{5,1},{9,5},{13,9},{2,14},{6,2},{... | collective-permute-start | bytes 1572872 | tf_op jit(solution)/shard_map/ppermute | solution.py:189
  128.8 46.1 %collective-permute-start.11 = (bf16[256,1024]{1,0:T(8,128)(2,1)}, bf16[256,1024]{1,0:T(8,128)(2,1)S(1)}, u32[]{:S(2)}, u32[]{:S(2)}) collective-permute-start(bf16[256,1024]{1,0:T(8,128)(2,1)} %get-tuple-element.8), channel_id=1, source_target_pairs={{0,8},{4,12},{8,0},{12,4},{1,9},{5,13},{9,1},{13,5},{2,10},{6,14},... | collective-permute-start | bytes 1572872 | tf_op jit(solution)/shard_map/ppermute | solution.py:189
  135.6 39.4 %collective-permute-start.8 = (bf16[256,1024]{1,0:T(8,128)(2,1)S(1)}, bf16[256,1024]{1,0:T(8,128)(2,1)S(1)}, u32[]{:S(2)}, u32[]{:S(2)}) collective-permute-start(bf16[256,1024]{1,0:T(8,128)(2,1)S(1)} %copy-done.11), channel_id=1, source_target_pairs={{0,4},{4,8},{8,12},{12,0},{1,5},{5,9},{9,13},{13,1},{2,6},{6,10},{... | collective-permute-start | bytes 1572872 | tf_op jit(solution)/shard_map/ppermute | solution.py:189
  137.2 38.3 %dynamic-slice-start = ((f32[4096]{0:T(1024)}, s32[]{:T(128)}), f32[1024]{0:T(1024)S(1)}, s32[]{:S(2)}) async-start(f32[4096]{0:T(1024)} %param.7, s32[]{:T(128)} %select_n.363), calls=%async_computation.1 | async-start | bytes 8704 | tf_op jit(solution)/shard_map/dynamic_slice | solution.py:183
  175.0 4.8 %collective-permute-start.13 = (bf16[256,1024]{1,0:T(8,128)(2,1)S(1)}, bf16[256,1024]{1,0:T(8,128)(2,1)S(1)}, u32[]{:S(2)}, u32[]{:S(2)}) collective-permute-start(bf16[256,1024]{1,0:T(8,128)(2,1)S(1)} %collective-permute-done.11), channel_id=1, source_target_pairs={{0,1},{1,0},{2,3},{3,2},{4,5},{5,4},{6,7},{7,6},{8,9},{9,8},{10,11... | collective-permute-start | bytes 1572872 | tf_op jit(solution)/shard_map/ppermute | solution.py:26
  175.0 6.3 %collective-permute-start.10 = (bf16[256,1024]{1,0:T(8,128)(2,1)S(1)}, bf16[256,1024]{1,0:T(8,128)(2,1)}, u32[]{:S(2)}, u32[]{:S(2)}) collective-permute-start(bf16[256,1024]{1,0:T(8,128)(2,1)S(1)} %collective-permute-done.8), channel_id=1, source_target_pairs={{0,1},{1,0},{2,3},{3,2},{4,5},{5,4},{6,7},{7,6},{8,9},{9,8},{10,11... | collective-permute-start | bytes 1572872 | tf_op jit(solution)/shard_map/ppermute | solution.py:26
  175.5 7.7 %collective-permute-start.16 = (bf16[256,1024]{1,0:T(8,128)(2,1)S(1)}, bf16[256,1024]{1,0:T(8,128)(2,1)}, u32[]{:S(2)}, u32[]{:S(2)}) collective-permute-start(bf16[256,1024]{1,0:T(8,128)(2,1)S(1)} %collective-permute-done.14), channel_id=1, source_target_pairs={{0,1},{1,0},{2,3},{3,2},{4,5},{5,4},{6,7},{7,6},{8,9},{9,8},{10,11... | collective-permute-start | bytes 1572872 | tf_op jit(solution)/shard_map/ppermute | solution.py:26
  178.2 1.5 copy-start.6
  181.2 2.3 %copy-start = (f32[1024,1024]{1,0:T(8,128)S(1)}, f32[1024,1024]{1,0:T(8,128)}, u32[]{:S(2)}) copy-start(f32[1024,1024]{1,0:T(8,128)} %fusion.63) | copy-start | bytes 12582916
  (1 other events, 1.0 us)
Sparse Core Ops, SparseCore 0:
  10.4 82.7 all-gather.1

commit v10 on v9

--- a/solution.py
+++ b/solution.py
@@ -140,7 +140,13 @@
         for shift in range(1, seq_count)
     ]
     kv_pair = jnp.stack([keys, values]).swapaxes(0, 1)
-    outgoing_rows, kv_pair = lax.optimization_barrier((outgoing_rows, kv_pair))
+    received_scales = [
+        lax.ppermute(row_scale, "seq", [(j, (j + shift) % seq_count) for j in range(seq_count)])
+        for shift in range(1, seq_count)
+    ]
+    outgoing_rows, received_scales, kv_pair = lax.optimization_barrier(
+        (outgoing_rows, received_scales, kv_pair)
+    )
     for section in range(1, seq_count.bit_length()):
         (far_pair,) = split_send((kv_pair,), "seq", section - 1)
         far_keys = far_pair[:, 0]
@@ -186,7 +192,8 @@
     for shift in range(1, seq_count):
         outgoing = outgoing_rows[shift - 1]
         route = [(j, (j + shift) % seq_count) for j in range(seq_count)]
-        incoming, their_scale = lax.ppermute((outgoing, row_scale), "seq", route)
+        incoming = lax.ppermute(outgoing, "seq", route)
+        their_scale = received_scales[shift - 1]
         halves = swap_halves(incoming, sub_count, sub_index)
         source = (seq_index - shift) % seq_count
         their_raw = lax.dynamic_slice_in_dim(raw_columns, source * row_count, row_count, 0)

time: 196 us -> 204 us (1.041)
  waiting for transfers between devices: 69.6 us -> 74.2 us
  matrix products: 40.3 us -> 42.7 us
    ppermute x6, waiting for transfers between devices: 33.8 us -> 42.6 us  [the longest x3 42.6 us: body(): incoming = lax.ppermute(outgoing, 'seq', route)]
    ppermute x2, waiting for transfers between devices: 18.8 us -> 14.5 us  [from_partner(): return lax.ppermute(block, axis, route)]
    dot_general x6, matrix products: 9.57 us -> 11.7 us  [body(): jnp.einsum('tc,tr->cr', halves[lane_shift], their_rows, preferred_element...]
    unnamed x32 -> x36, local copies, waits for them, and re-layouts: 11.3 us -> 10.9 us
  transfers between devices with their start and end apart: 18 -> 18, of which waited for: 3 -> 4; matrix products, arithmetic and copies ran while one was open for 45% -> 45% of each run, Pallas kernels for 0% -> 0%
where the time goes in v10:
time: 204 us; the launch traced here: 203 us
  waiting for transfers between devices  74.2 us (36%)
  matrix products  42.7 us (21%)
  local copies, waits for them, and re-layouts  30.6 us (15%)
  other arithmetic  25.2 us (12%)
  starting transfers between devices  16.1 us (8%)
  between operations  14.6 us (7%)
    ppermute x3, waiting for transfers between devices, body(): incoming = lax.ppermute(outgoing, 'seq', route)  42.6 us
    ppermute x1, waiting for transfers between devices, body(): across.append(lax.ppermute(tokens, 'kvh', route))  17 us
    ppermute x2, waiting for transfers between devices, from_partner(): return lax.ppermute(block, axis, route)  14.5 us
    dot_general x6, matrix products, body(): jnp.einsum('tc,tr->cr', halves[lane_shift], their_rows, preferred_element...  11.7 us
    unnamed x36, local copies, waits for them, and re-layouts  10.9 us
    dot_general x1, matrix products, body(): jnp.einsum('td,dgc->tgc', normed, w_query, preferred_element_type=jnp.flo...  8.28 us
    squeeze x2, local copies, waits for them, and re-layouts, body(): key_part, value_part = (weight_pair[0], weight_pair[1])  7.05 us
    ppermute x3, starting transfers between devices, body(): lax.ppermute(row_scale, 'seq', [(j, (j + shift) % seq_count) for j in ran...  5.78 us
  transfers between devices with their start and end apart: 18, of which 4 were waited for; matrix products, arithmetic and copies ran while one was open for 45% of the time, Pallas kernels for 0%

profile of v10, /device:TPU:0, one launch (start us, length us, event | category | flops | bytes accessed | tf_op | source)
XLA Modules:
  0.0 203.4 jit_solution(11522255796091705143)
XLA Ops:
  7.2 3.0 %collective-permute-start.1 = (bf16[512,1024]{1,0:T(8,128)(2,1)}, bf16[512,1024]{1,0:T(8,128)(2,1)}, u32[]{:S(2)}, u32[]{:S(2)}) collective-permute-start(bf16[512,1024]{1,0:T(8,128)(2,1)} %param.6), channel_id=1, source_target_pairs={{0,2},{2,0},{1,3},{3,1},{4,6},{6,4},{5,7},{7,5},{8,10},{10,8},{9,1... | collective-permute-start | bytes 3145736 | tf_op jit(solution)/shard_map/ppermute | solution.py:70
  10.3 2.8 %copy_bitcast_fusion = (bf16[1,2048,4,128]{3,1,2,0:T(8,128)(2,1)S(1)}, bf16[1,2048,4,128]{3,1,2,0:T(8,128)(2,1)S(1)}) fusion(bf16[2048,4,128]{2,1,0:T(4,128)(2,1)} %param.9, bf16[2048,4,128]{2,1,0:T(4,128)(2,1)} %param.10), kind=kLoop, calls=%fused_computation.48 | loop fusion | bytes 8388608 | tf_op jit(solution)/shard_map/stack | solution.py:107
  13.1 2.4 %pad_maximum_fusion.1 = bf16[2,2048,4,128]{3,1,2,0:T(8,128)(2,1)} fusion(bf16[1,2048,4,128]{3,1,2,0:T(8,128)(2,1)S(1)} %get-tuple-element.71, bf16[1,2048,4,128]{3,1,2,0:T(8,128)(2,1)S(1)} %get-tuple-element.70), kind=kLoop, calls=%fused_computation.14 | loop fusion | flops 2097152 | bytes 8388608 | tf_op jit(solution)/shard_map/stack | solution.py:107
  16.7 17.0 %collective-permute-done.1 = bf16[512,1024]{1,0:T(8,128)(2,1)} collective-permute-done((bf16[512,1024]{1,0:T(8,128)(2,1)}, bf16[512,1024]{1,0:T(8,128)(2,1)}, u32[]{:S(2)}, u32[]{:S(2)}) %collective-permute-start.1) | collective-permute-done | bytes 1048608 | tf_op jit(solution)/shard_map/ppermute | solution.py:70
  34.4 2.6 %copy.53 = bf16[2048,4,128]{0,2,1:T(8,128)(2,1)} copy(bf16[2048,4,128]{2,1,0:T(4,128)(2,1)S(1)} %copy-done.5) | data formatting | bytes 4194304 | tf_op args[3]
  37.0 2.6 %select_reduce_fusion.1 = (f32[512]{0:T(512)S(1)}, f32[512]{0:T(512)S(1)}) fusion(f32[]{:T(128)} %bitcast.45, f32[]{:T(128)} %bitcast.44, f32[]{:T(128)} %bitcast.32, f32[]{:T(128)} %bitcast.31), kind=kLoop, calls=%fused_computation.151 | loop fusion | flops 7168 | bytes 4112 | tf_op jit(solution)/shard_map/gather | solution.py:157
  42.0 1.8 multiply_cosine_fusion
  43.9 2.1 %select_select_fusion.3 = (bf16[512,1024]{1,0:T(8,128)(2,1)S(1)}, bf16[512,1024]{1,0:T(8,128)(2,1)S(1)}, bf16[512,1024]{1,0:T(8,128)(2,1)S(1)}, bf16[512,1024]{1,0:T(8,128)(2,1)S(1)}) fusion(bf16[512,1024]{1,0:T(8,128)(2,1)} %collective-permute-done.1, bf16[512,1024]{1,0:T(8,128)(2,1)} %collective-permute-done.2, bf16[512,1024]{1,0:T(8,128)(2,1)S(1)} %copy-done.7, ...), kind=kLoop, calls=%fused_computation.84 | loop fusion | flops 6291456 | bytes 8388620 | tf_op jit(solution)/shard_map/select_n | solution.py:78
  47.1 1.9 collective-permute-start.4
  48.9 2.6 %collective-permute-start.5 = (f32[512]{0:T(512)S(1)}, f32[512]{0:T(512)S(1)}, u32[]{:S(2)}, u32[]{:S(2)}) collective-permute-start(f32[512]{0:T(512)S(1)} %add_rsqrt_fusion), channel_id=1, source_target_pairs={{0,8},{4,12},{8,0},{12,4},{1,9},{5,13},{9,1},{13,5},{2,10},{6,14},... | collective-permute-start | bytes 6152 | tf_op jit(solution)/shard_map/ppermute | solution.py:144
  54.2 2.0 copy-done.1
  57.8 8.3 %fusion.3 = f32[512,4,256]{0,2,1:T(8,128)S(1)} fusion(bf16[4096,4,256]{2,1,0:T(4,128)(2,1)} %param.8, bf16[512,4096]{1,0:T(8,128)(2,1)} %copy-done.1), kind=kOutput, calls=%fused_computation.6 | convolution fusion | flops 4294967296 | bytes 14680064 | tf_op jit(solution)/shard_map/td,dgc->tgc/dot_general | solution.py:93
  66.3 1.9 copy.91
  68.3 1.9 copy.90
  70.2 3.7 %fusion.118 = (bf16[256,1024]{1,0:T(8,128)(2,1)}, bf16[256,1024]{1,0:T(8,128)(2,1)}, bf16[256,1024]{1,0:T(8,128)(2,1)}) fusion(bf16[512,4096]{1,0:T(8,128)(2,1)} %copy-done.1, s32[]{:T(128)S(6)} %select_n.348, s32[]{:T(128)S(6)} %select_n.357, s32[]{:T(128)S(6)} %select_n.354, s32[]{:T(128)S(6)} %select_n.351), kind=kLoop, calls=%fused_computation.168 | loop fusion | bytes 3145744 | tf_op jit(solution)/shard_map/dynamic_slice | solution.py:139
  73.9 2.4 %subtract_convert_fusion = (bf16[512,4,2,64]{3,0,2,1:T(8,128)(2,1)S(1)}, bf16[512,4,2,64]{3,0,2,1:T(8,128)(2,1)S(1)}) fusion(f32[512,4,2,64]{3,0,2,1:T(8,128)S(1)} %copy-done.4, f32[512,4,2,64]{3,0,2,1:T(8,128)} %copy.90, f32[512,64]{1,0:T(8,128)} %get-tuple-element.52, f32[512,64]{1,0:T(8,128)} %get-tuple-element.51), kind=kLoop, calls=%fused_computation.53 | loop fusion | flops 2097152 | bytes 3407872 | tf_op jit(solution)/shard_map/convert.8
  76.9 2.9 %fusion.21 = f32[512,4,128]{2,0,1:T(8,128)S(1)} fusion(bf16[2,2048,4,128]{3,1,2,0:T(8,128)(2,1)} %collective-permute-done.3, bf16[512,4096]{1,0:T(8,128)(2,1)S(1)} %copy-done.2, s32[]{:T(128)S(6)} %select_n.341), kind=kOutput, calls=%fused_computation.35 | convolution fusion | flops 1073741824 | bytes 5242884 | tf_op jit(solution)/shard_map/td,dgh->tgh/dot_general | solution.py:112
  79.8 2.2 %fusion.54 = bf16[512,4,128]{2,0,1:T(8,128)(2,1)} fusion(f32[512,4,128]{2,0,1:T(8,128)S(1)} %fusion.21, bf16[2048,4,128]{2,1,0:T(4,128)(2,1)S(1)} %copy-done.9, bf16[512,4096]{1,0:T(8,128)(2,1)S(1)} %copy-done.2, s32[]{:T(128)S(6)} %select_n.340), kind=kOutput, calls=%fused_computation.68 | convolution fusion | flops 1074266112 | bytes 5767172 | tf_op jit(solution)/shard_map/td,dgh->tgh/dot_general | solution.py:112
  81.9 3.0 %slice_bitcast_fusion = bf16[2048,4,128]{2,0,1:T(8,128)(2,1)} fusion(bf16[2,2048,4,128]{3,1,2,0:T(8,128)(2,1)} %collective-permute-done.3), kind=kLoop, calls=%fused_computation.33 | loop fusion | bytes 4194304 | tf_op jit(solution)/shard_map/squeeze | solution.py:108
  85.0 4.0 %copy.54 = bf16[2048,4,128]{0,2,1:T(8,128)(2,1)} copy(bf16[2048,4,128]{2,0,1:T(8,128)(2,1)} %slice_bitcast_fusion) | data formatting | bytes 4194304 | tf_op jit(solution)/shard_map/squeeze | solution.py:108
  89.0 4.5 %fusion.35 = f32[512,512]{0,1} fusion(bf16[2048,512]{0,1:T(8,128)(2,1)} %bitcast.182, bf16[512,4096]{1,0:T(8,128)(2,1)} %copy-done.1, s32[]{:T(128)S(6)} %select_n.341), kind=kOutput, calls=%fused_computation.57 | convolution fusion | flops 1073741824 | bytes 5242884
  93.5 2.5 %copy.56 = f32[512,4,128]{2,0,1:T(8,128)} copy(f32[512,4,128]{0,2,1:T(8,128)} %bitcast.188) | data formatting | bytes 2097152 | tf_op jit(solution)/shard_map/td,dgh->tgh/dot_general | solution.py:111
  100.6 3.3 %fusion.63 = f32[1024,1024]{1,0:T(8,128)} fusion(bf16[512,4096]{1,0:T(8,128)(2,1)S(1)} %copy-done.3, s32[]{:T(128)} %select_n.363, s32[]{:T(128)S(6)} %select_n.362), kind=kOutput, calls=%fused_computation.75 | convolution fusion | flops 1073741824 | bytes 6291464 | tf_op jit(solution)/shard_map/tc,tr->cr/dot_general | solution.py:191
  103.9 3.3 %collective-permute-start.15 = (bf16[256,1024]{1,0:T(8,128)(2,1)S(1)}, bf16[256,1024]{1,0:T(8,128)(2,1)S(1)}, u32[]{:S(2)}, u32[]{:S(2)}) collective-permute-start(bf16[256,1024]{1,0:T(8,128)(2,1)S(1)} %copy-done.11), channel_id=1, source_target_pairs={{0,12},{4,0},{8,4},{12,8},{1,13},{5,1},{9,5},{13,9},{2,14},{6,2},{... | collective-permute-start | bytes 1572872 | tf_op jit(solution)/shard_map/ppermute | solution.py:195
  108.5 2.5 %fusion.7 = (f32[4,2,512]{2,1,0:T(2,128)S(1)}, f32[4,512,512,2]{2,1,3,0:T(8,128)S(1)}) fusion(pred[512,512]{0,1:T(8,128)(4,1)S(1)} %fusion.66, bf16[512,4,2,64]{3,0,2,1:T(8,128)(2,1)S(1)} %get-tuple-element.28, bf16[512,4,2,64]{3,0,2,1:T(8,128)(2,1)S(1)} %get-tuple-element.27, bf16[512,4,64]{2,0,1:T(8,128)(2,1)S(1)} %get-tuple-element.46, ...), kind=kOutput, calls=%fused_computation.11 | convolution fusion | flops 546304000 | bytes 10240000 | tf_op jit(solution)/shard_map/tgrh,ugh->grtu/dot_general | solution.py:120
  111.0 14.4 %collective-permute-done.9 = bf16[256,2,4,128]{3,0,2,1:T(8,128)(2,1)S(1)} collective-permute-done((bf16[256,2,4,128]{3,0,2,1:T(8,128)(2,1)S(1)}, bf16[256,2,4,128]{3,0,2,1:T(8,128)(2,1)S(1)}, u32[]{:S(2)}, u32[]{:S(2)}) %collective-permute-start.9) | collective-permute-done | bytes 524320 | tf_op jit(solution)/shard_map/ppermute | solution.py:18
  127.7 42.6 %collective-permute-done.13 = bf16[256,1024]{1,0:T(8,128)(2,1)} collective-permute-done((bf16[256,1024]{1,0:T(8,128)(2,1)S(1)}, bf16[256,1024]{1,0:T(8,128)(2,1)}, u32[]{:S(2)}, u32[]{:S(2)}) %collective-permute-start.13) | collective-permute-done | bytes 524320 | tf_op jit(solution)/shard_map/ppermute | solution.py:195
  177.6 2.8 %fusion.33 = bf16[512,4,2,128]{0,3,2,1:T(8,128)(2,1)S(1)} fusion(f32[512,4,2,128]{0,3,2,1:T(8,128)S(1)} %bitcast.179, f32[512,4,2,128]{0,3,2,1:T(8,128)S(1)} %bitcast.180, f32[4,512,512,2]{2,1,3,0:T(8,128)S(1)} %get-tuple-element.65, f32[4,2,512]{2,1,0:T(2,128)S(1)} %get-tuple-element.64, pred[512,512]{0,1:T(8,128)(4,1)S(1)} %fusion.66, ...), kind=kOutput, calls=%fused_computation.54 | convolution fusion | flops 548405248 | bytes 14483456 | tf_op jit(solution)/shard_map/grtu,ugh->tgrh/dot_general | solution.py:130
  181.8 2.6 %multiply_convert_fusion.2 = (bf16[512,1024]{1,0:T(8,128)(2,1)S(1)}, bf16[512,1024]{1,0:T(8,128)(2,1)S(1)}, bf16[512,1024]{1,0:T(8,128)(2,1)S(1)}) fusion(f32[1024]{0:T(1024)S(1)} %dynamic-slice-done, f32[512]{0:T(512)S(1)} %collective-permute-done.4, bf16[2048,1024]{1,0:T(8,128)(2,1)} %all-gather.2.cloned.1.call-done, s32[]{:T(128)S(6)} %select_n.365, ...), kind=kLoop, calls=%fused_computation.51 | loop fusion | flops 6291456 | bytes 6301708 | tf_op jit(solution)/shard_map/convert_element_type | solution.py:202
  187.1 1.8 fusion.80
  189.6 1.9 fusion.84
  191.9 4.7 %add_multiply_fusion = f32[1024,1024]{1,0:T(8,128)} fusion(f32[1024,1024]{1,0:T(8,128)S(1)} %fusion.78, f32[1024,1024]{1,0:T(8,128)S(1)} %fusion.80, f32[1024,1024]{1,0:T(8,128)S(1)} %fusion.82, f32[1024,1024]{1,0:T(8,128)S(1)} %fusion.84, f32[1024,1024]{1,0:T(8,128)S(1)} %copy-done, f32[1024,1024]{1,0:T(8,128)S(1)} %fusion.86, ...), kind=kOutput, calls=%fused_computation.22 | convolution fusion | flops 544210944 | bytes 30408708 | tf_op jit(solution)/shard_map/tc,tr->cr/dot_general | solution.py:206
  (110 shorter events, 30.8 us)
Async XLA Ops:
  7.2 174.7 %all-gather.2.cloned.1.call-start = ((), (), s32[]{:S(2)}) async-start(), calls=%async_computation | async-start | bytes 5242880 | tf_op jit(solution)/shard_map/all_gather | solution.py:188
  7.2 26.5 %collective-permute-start.1 = (bf16[512,1024]{1,0:T(8,128)(2,1)}, bf16[512,1024]{1,0:T(8,128)(2,1)}, u32[]{:S(2)}, u32[]{:S(2)}) collective-permute-start(bf16[512,1024]{1,0:T(8,128)(2,1)} %param.6), channel_id=1, source_target_pairs={{0,2},{2,0},{1,3},{3,1},{4,6},{6,4},{5,7},{7,5},{8,10},{10,8},{9,1... | collective-permute-start | bytes 3145736 | tf_op jit(solution)/shard_map/ppermute | solution.py:70
  10.2 33.7 %collective-permute-start = (bf16[512,1024]{1,0:T(8,128)(2,1)}, bf16[512,1024]{1,0:T(8,128)(2,1)}, u32[]{:S(2)}, u32[]{:S(2)}) collective-permute-start(bf16[512,1024]{1,0:T(8,128)(2,1)} %param.6), channel_id=1, source_target_pairs={{0,1},{1,0},{2,3},{3,2},{4,5},{5,4},{6,7},{7,6},{8,9},{9,8},{10,11... | collective-permute-start | bytes 3145736 | tf_op jit(solution)/shard_map/ppermute | solution.py:26
  13.0 2.9 %copy-start.15 = (s32[3,8]{1,0:T(4,128)S(1)}, s32[3,8]{1,0:T(4,128)}, u32[]{:S(2)}) copy-start(s32[3,8]{1,0:T(4,128)} %param.11) | copy-start | bytes 292
  13.1 21.3 %copy-start.5 = (bf16[2048,4,128]{2,1,0:T(4,128)(2,1)S(1)}, bf16[2048,4,128]{2,1,0:T(4,128)(2,1)}, u32[]{:S(2)}) copy-start(bf16[2048,4,128]{2,1,0:T(4,128)(2,1)} %param.9) | copy-start | bytes 6291460
  15.4 28.5 %copy-start.7 = (bf16[512,1024]{1,0:T(8,128)(2,1)S(1)}, bf16[512,1024]{1,0:T(8,128)(2,1)}, u32[]{:S(2)}) copy-start(bf16[512,1024]{1,0:T(8,128)(2,1)} %param.6) | copy-start | bytes 3145732
  15.4 60.8 %collective-permute-start.3 = (bf16[2,2048,4,128]{3,1,2,0:T(8,128)(2,1)}, bf16[2,2048,4,128]{3,1,2,0:T(8,128)(2,1)}, u32[]{:S(2)}, u32[]{:S(2)}) collective-permute-start(bf16[2,2048,4,128]{3,1,2,0:T(8,128)(2,1)} %pad_maximum_fusion.1), channel_id=1, source_target_pairs={{0,1},{1,0},{2,3},{3,2},{4,5},{5,4},{6,7},{7,6},{8,9},{9,8},{10,11... | collective-permute-start | bytes 12582920 | tf_op jit(solution)/shard_map/ppermute | solution.py:107
  33.7 10.2 %collective-permute-start.2 = (bf16[512,1024]{1,0:T(8,128)(2,1)}, bf16[512,1024]{1,0:T(8,128)(2,1)}, u32[]{:S(2)}, u32[]{:S(2)}) collective-permute-start(bf16[512,1024]{1,0:T(8,128)(2,1)} %collective-permute-done.1), channel_id=1, source_target_pairs={{0,1},{1,0},{2,3},{3,2},{4,5},{5,4},{6,7},{7,6},{8,9},{9,8},{10,11... | collective-permute-start | bytes 3145736 | tf_op jit(solution)/shard_map/ppermute | solution.py:26
  46.0 6.8 %copy-start.14 = (f32[4096]{0:T(1024)S(1)}, f32[4096]{0:T(1024)}, u32[]{:S(2)}) copy-start(f32[4096]{0:T(1024)} %param.7) | copy-start | bytes 49156
  47.1 9.2 %copy-start.8 = (bf16[2048,4,128]{0,2,1:T(8,128)(2,1)S(1)}, bf16[2048,4,128]{0,2,1:T(8,128)(2,1)}, u32[]{:S(2)}) copy-start(bf16[2048,4,128]{0,2,1:T(8,128)(2,1)} %copy.53) | copy-start | bytes 6291460
  47.1 52.3 %collective-permute-start.4 = (f32[512]{0:T(512)S(1)}, f32[512]{0:T(512)S(1)}, u32[]{:S(2)}, u32[]{:S(2)}) collective-permute-start(f32[512]{0:T(512)S(1)} %add_rsqrt_fusion), channel_id=1, source_target_pairs={{0,4},{4,8},{8,12},{12,0},{1,5},{5,9},{9,13},{13,1},{2,6},{6,10},{... | collective-permute-start | bytes 6152 | tf_op jit(solution)/shard_map/ppermute | solution.py:144
  48.9 50.5 %collective-permute-start.5 = (f32[512]{0:T(512)S(1)}, f32[512]{0:T(512)S(1)}, u32[]{:S(2)}, u32[]{:S(2)}) collective-permute-start(f32[512]{0:T(512)S(1)} %add_rsqrt_fusion), channel_id=1, source_target_pairs={{0,8},{4,12},{8,0},{12,4},{1,9},{5,13},{9,1},{13,5},{2,10},{6,14},... | collective-permute-start | bytes 6152 | tf_op jit(solution)/shard_map/ppermute | solution.py:144
  51.5 47.9 %collective-permute-start.6 = (f32[512]{0:T(512)S(1)}, f32[512]{0:T(512)S(1)}, u32[]{:S(2)}, u32[]{:S(2)}) collective-permute-start(f32[512]{0:T(512)S(1)} %add_rsqrt_fusion), channel_id=1, source_target_pairs={{0,12},{4,0},{8,4},{12,8},{1,13},{5,1},{9,5},{13,9},{2,14},{6,2},{... | collective-permute-start | bytes 6152 | tf_op jit(solution)/shard_map/ppermute | solution.py:144
  70.2 3.7 %copy-start.4 = (f32[512,4,2,64]{3,0,2,1:T(8,128)S(1)}, f32[512,4,2,64]{3,0,2,1:T(8,128)}, u32[]{:S(2)}) copy-start(f32[512,4,2,64]{3,0,2,1:T(8,128)} %copy.91) | copy-start | bytes 3145732
  73.9 3.0 %copy-start.2 = (bf16[512,4096]{1,0:T(8,128)(2,1)S(1)}, bf16[512,4096]{1,0:T(8,128)(2,1)}, u32[]{:S(2)}) copy-start(bf16[512,4096]{1,0:T(8,128)(2,1)} %copy-done.1) | copy-start | bytes 12582916
  76.3 3.5 %copy-start.9 = (bf16[2048,4,128]{2,1,0:T(4,128)(2,1)S(1)}, bf16[2048,4,128]{2,1,0:T(4,128)(2,1)}, u32[]{:S(2)}) copy-start(bf16[2048,4,128]{2,1,0:T(4,128)(2,1)} %param.10) | copy-start | bytes 6291460
  96.0 3.0 %copy-start.10 = (bf16[512,4,128]{2,0,1:T(8,128)(2,1)S(1)}, bf16[512,4,128]{2,0,1:T(8,128)(2,1)}, u32[]{:S(2)}) copy-start(bf16[512,4,128]{2,0,1:T(8,128)(2,1)} %fusion.54) | copy-start | bytes 1572868
  97.4 3.2 %copy-start.3 = (bf16[512,4096]{1,0:T(8,128)(2,1)S(1)}, bf16[512,4096]{1,0:T(8,128)(2,1)}, u32[]{:S(2)}) copy-start(bf16[512,4096]{1,0:T(8,128)(2,1)} %copy-done.1) | copy-start | bytes 12582916
  99.3 4.6 %copy-start.11 = (bf16[256,1024]{1,0:T(8,128)(2,1)S(1)}, bf16[256,1024]{1,0:T(8,128)(2,1)}, u32[]{:S(2)}) copy-start(bf16[256,1024]{1,0:T(8,128)(2,1)} %get-tuple-element.14) | copy-start | bytes 1572868
  99.4 7.9 %copy-start.13 = (bf16[256,1024]{1,0:T(8,128)(2,1)S(1)}, bf16[256,1024]{1,0:T(8,128)(2,1)}, u32[]{:S(2)}) copy-start(bf16[256,1024]{1,0:T(8,128)(2,1)} %get-tuple-element.12) | copy-start | bytes 1572868
  99.4 7.9 %copy-start.12 = (bf16[256,1024]{1,0:T(8,128)(2,1)S(1)}, bf16[256,1024]{1,0:T(8,128)(2,1)}, u32[]{:S(2)}) copy-start(bf16[256,1024]{1,0:T(8,128)(2,1)} %get-tuple-element.10) | copy-start | bytes 1572868
  99.5 26.0 %collective-permute-start.9 = (bf16[256,2,4,128]{3,0,2,1:T(8,128)(2,1)S(1)}, bf16[256,2,4,128]{3,0,2,1:T(8,128)(2,1)S(1)}, u32[]{:S(2)}, u32[]{:S(2)}) collective-permute-start(bf16[256,2,4,128]{3,0,2,1:T(8,128)(2,1)S(1)} %constant_dynamic-slice_fusion.2), channel_id=1, source_target_pairs={{0,8},{8,0},{4,12},{12,4},{1,9},{9,1},{5,13},{13,5},{2,10},{10,2},... | collective-permute-start | bytes 1572872 | tf_op jit(solution)/shard_map/ppermute | solution.py:18
  99.7 25.8 %collective-permute-start.7 = (bf16[256,2,4,128]{3,0,2,1:T(8,128)(2,1)S(1)}, bf16[256,2,4,128]{3,0,2,1:T(8,128)(2,1)S(1)}, u32[]{:S(2)}, u32[]{:S(2)}) collective-permute-start(bf16[256,2,4,128]{3,0,2,1:T(8,128)(2,1)S(1)} %constant_dynamic-slice_fusion.2), channel_id=1, source_target_pairs={{0,4},{4,0},{8,12},{12,8},{1,5},{5,1},{9,13},{13,9},{2,6},{6,2},{1... | collective-permute-start | bytes 1572872 | tf_op jit(solution)/shard_map/ppermute | solution.py:18
  103.9 66.9 %collective-permute-start.15 = (bf16[256,1024]{1,0:T(8,128)(2,1)S(1)}, bf16[256,1024]{1,0:T(8,128)(2,1)S(1)}, u32[]{:S(2)}, u32[]{:S(2)}) collective-permute-start(bf16[256,1024]{1,0:T(8,128)(2,1)S(1)} %copy-done.11), channel_id=1, source_target_pairs={{0,12},{4,0},{8,4},{12,8},{1,13},{5,1},{9,5},{13,9},{2,14},{6,2},{... | collective-permute-start | bytes 1572872 | tf_op jit(solution)/shard_map/ppermute | solution.py:195
  107.2 63.0 %collective-permute-start.13 = (bf16[256,1024]{1,0:T(8,128)(2,1)S(1)}, bf16[256,1024]{1,0:T(8,128)(2,1)}, u32[]{:S(2)}, u32[]{:S(2)}) collective-permute-start(bf16[256,1024]{1,0:T(8,128)(2,1)S(1)} %copy-done.13), channel_id=1, source_target_pairs={{0,8},{4,12},{8,0},{12,4},{1,9},{5,13},{9,1},{13,5},{2,10},{6,14},... | collective-permute-start | bytes 1572872 | tf_op jit(solution)/shard_map/ppermute | solution.py:195
  107.2 63.0 %collective-permute-start.11 = (bf16[256,1024]{1,0:T(8,128)(2,1)S(1)}, bf16[256,1024]{1,0:T(8,128)(2,1)S(1)}, u32[]{:S(2)}, u32[]{:S(2)}) collective-permute-start(bf16[256,1024]{1,0:T(8,128)(2,1)S(1)} %copy-done.12), channel_id=1, source_target_pairs={{0,4},{4,8},{8,12},{12,0},{1,5},{5,9},{9,13},{13,1},{2,6},{6,10},{... | collective-permute-start | bytes 1572872 | tf_op jit(solution)/shard_map/ppermute | solution.py:195
  125.4 45.9 %collective-permute-start.10 = (bf16[256,2,4,128]{3,0,2,1:T(8,128)(2,1)S(1)}, bf16[256,2,4,128]{3,0,2,1:T(8,128)(2,1)S(1)}, u32[]{:S(2)}, u32[]{:S(2)}) collective-permute-start(bf16[256,2,4,128]{3,0,2,1:T(8,128)(2,1)S(1)} %collective-permute-done.9), channel_id=1, source_target_pairs={{0,1},{1,0},{2,3},{3,2},{4,5},{5,4},{6,7},{7,6},{8,9},{9,8},{10,11... | collective-permute-start | bytes 1572872 | tf_op jit(solution)/shard_map/ppermute | solution.py:26
  125.5 45.9 %collective-permute-start.8 = (bf16[256,2,4,128]{3,0,2,1:T(8,128)(2,1)S(1)}, bf16[256,2,4,128]{3,0,2,1:T(8,128)(2,1)S(1)}, u32[]{:S(2)}, u32[]{:S(2)}) collective-permute-start(bf16[256,2,4,128]{3,0,2,1:T(8,128)(2,1)S(1)} %collective-permute-done.7), channel_id=1, source_target_pairs={{0,1},{1,0},{2,3},{3,2},{4,5},{5,4},{6,7},{7,6},{8,9},{9,8},{10,11... | collective-permute-start | bytes 1572872 | tf_op jit(solution)/shard_map/ppermute | solution.py:26
  170.3 16.8 %collective-permute-start.14 = (bf16[256,1024]{1,0:T(8,128)(2,1)}, bf16[256,1024]{1,0:T(8,128)(2,1)}, u32[]{:S(2)}, u32[]{:S(2)}) collective-permute-start(bf16[256,1024]{1,0:T(8,128)(2,1)} %collective-permute-done.13), channel_id=1, source_target_pairs={{0,1},{1,0},{2,3},{3,2},{4,5},{5,4},{6,7},{7,6},{8,9},{9,8},{10,11... | collective-permute-start | bytes 1572872 | tf_op jit(solution)/shard_map/ppermute | solution.py:26
  170.3 19.3 %collective-permute-start.12 = (bf16[256,1024]{1,0:T(8,128)(2,1)S(1)}, bf16[256,1024]{1,0:T(8,128)(2,1)}, u32[]{:S(2)}, u32[]{:S(2)}) collective-permute-start(bf16[256,1024]{1,0:T(8,128)(2,1)S(1)} %collective-permute-done.11), channel_id=1, source_target_pairs={{0,1},{1,0},{2,3},{3,2},{4,5},{5,4},{6,7},{7,6},{8,9},{9,8},{10,11... | collective-permute-start | bytes 1572872 | tf_op jit(solution)/shard_map/ppermute | solution.py:26
  170.8 20.8 %collective-permute-start.16 = (bf16[256,1024]{1,0:T(8,128)(2,1)S(1)}, bf16[256,1024]{1,0:T(8,128)(2,1)}, u32[]{:S(2)}, u32[]{:S(2)}) collective-permute-start(bf16[256,1024]{1,0:T(8,128)(2,1)S(1)} %collective-permute-done.15), channel_id=1, source_target_pairs={{0,1},{1,0},{2,3},{3,2},{4,5},{5,4},{6,7},{7,6},{8,9},{9,8},{10,11... | collective-permute-start | bytes 1572872 | tf_op jit(solution)/shard_map/ppermute | solution.py:26
  177.6 4.3 %dynamic-slice-start = ((f32[4096]{0:T(1024)}, s32[]{:T(128)}), f32[1024]{0:T(1024)S(1)}, s32[]{:S(2)}) async-start(f32[4096]{0:T(1024)} %param.7, s32[]{:T(128)} %select_n.363), calls=%async_computation.1 | async-start | bytes 8704 | tf_op jit(solution)/shard_map/dynamic_slice | solution.py:189
  (3 other events, 6.9 us)
Sparse Core Ops, SparseCore 0:
  10.4 82.7 all-gather.1

commit v11 on v7

--- a/solution.py
+++ b/solution.py
@@ -132,7 +132,7 @@
     )
     query_pairs = queries.reshape(2, block_len, local_groups, per_group, head_size)
     for section in range(1, lax.axis_size("seq").bit_length()):
-        (far_pair,) = split_send((jnp.stack([keys, values]).swapaxes(0, 1),), "seq", section - 1)
+        far_pair = from_partner(jnp.stack([keys, values]).swapaxes(0, 1), "seq", section - 1)
         far_keys = far_pair[:, 0]
         far_values = far_pair[:, 1]
         far_keys = far_keys.reshape(2, block_len, local_groups, head_size)

time: 193 us -> 215 us (1.11)
  waiting for transfers between devices: 71 us -> 92.6 us
    ppermute x2, waiting for transfers between devices: 20 us -> 42.8 us  [from_partner(): return lax.ppermute(block, axis, route)]
    unnamed x36 -> x34, local copies, waits for them, and re-layouts: 10.5 us -> 10.8 us
  transfers between devices with their start and end apart: 18 -> 16, of which waited for: 3 -> 3; matrix products, arithmetic and copies ran while one was open for 44% -> 41% of each run, Pallas kernels for 0% -> 0%
where the time goes in v11:
time: 215 us
  waiting for transfers between devices  92.6 us (43%)
  matrix products  41.3 us (19%)
  local copies, waits for them, and re-layouts  29.9 us (14%)
  other arithmetic  23.4 us (11%)
  between operations  14.5 us (7%)
  starting transfers between devices  13 us (6%)
    ppermute x2, waiting for transfers between devices, from_partner(): return lax.ppermute(block, axis, route)  42.8 us
    ppermute x6, waiting for transfers between devices, body(): incoming, their_scale = lax.ppermute((outgoing, row_scale), 'seq', route)  32.6 us
    ppermute x1, waiting for transfers between devices, body(): across.append(lax.ppermute(tokens, 'kvh', route))  17.1 us
    unnamed x34, local copies, waits for them, and re-layouts  10.8 us
    dot_general x6, matrix products, body(): jnp.einsum('tc,tr->cr', halves[lane_shift], their_rows, preferred_element...  9.59 us
    dot_general x1, matrix products, body(): jnp.einsum('td,dgc->tgc', normed, w_query, preferred_element_type=jnp.flo...  8.29 us
    ppermute x6, starting transfers between devices, body(): incoming, their_scale = lax.ppermute((outgoing, row_scale), 'seq', route)  7.9 us
    squeeze x2, local copies, waits for them, and re-layouts, body(): key_part, value_part = (weight_pair[0], weight_pair[1])  7.02 us
  transfers between devices with their start and end apart: 16, of which 3 were waited for; matrix products, arithmetic and copies ran while one was open for 41% of the time, Pallas kernels for 0%

profile of v11, /device:TPU:0, one launch (start us, length us, event | category | flops | bytes accessed | tf_op | source)
XLA Modules:
  0.0 214.6 jit_solution(11808144467932742418)
XLA Ops:
  7.2 3.0 %collective-permute-start.1 = (bf16[512,1024]{1,0:T(8,128)(2,1)}, bf16[512,1024]{1,0:T(8,128)(2,1)}, u32[]{:S(2)}, u32[]{:S(2)}) collective-permute-start(bf16[512,1024]{1,0:T(8,128)(2,1)} %param.6), channel_id=1, source_target_pairs={{0,2},{2,0},{1,3},{3,1},{4,6},{6,4},{5,7},{7,5},{8,10},{10,8},{9,1... | collective-permute-start | bytes 3145736 | tf_op jit(solution)/shard_map/ppermute | solution.py:70
  10.3 2.8 %copy_bitcast_fusion = (bf16[1,2048,4,128]{3,1,2,0:T(8,128)(2,1)S(1)}, bf16[1,2048,4,128]{3,1,2,0:T(8,128)(2,1)S(1)}) fusion(bf16[2048,4,128]{2,1,0:T(4,128)(2,1)} %param.9, bf16[2048,4,128]{2,1,0:T(4,128)(2,1)} %param.10), kind=kLoop, calls=%fused_computation.48 | loop fusion | bytes 8388608 | tf_op jit(solution)/shard_map/stack | solution.py:107
  13.1 2.4 %pad_maximum_fusion.1 = bf16[2,2048,4,128]{3,1,2,0:T(8,128)(2,1)} fusion(bf16[1,2048,4,128]{3,1,2,0:T(8,128)(2,1)S(1)} %get-tuple-element.55, bf16[1,2048,4,128]{3,1,2,0:T(8,128)(2,1)S(1)} %get-tuple-element.54), kind=kLoop, calls=%fused_computation.14 | loop fusion | flops 2097152 | bytes 8388608 | tf_op jit(solution)/shard_map/stack | solution.py:107
  16.6 17.1 %collective-permute-done.1 = bf16[512,1024]{1,0:T(8,128)(2,1)} collective-permute-done((bf16[512,1024]{1,0:T(8,128)(2,1)}, bf16[512,1024]{1,0:T(8,128)(2,1)}, u32[]{:S(2)}, u32[]{:S(2)}) %collective-permute-start.1) | collective-permute-done | bytes 1048608 | tf_op jit(solution)/shard_map/ppermute | solution.py:70
  34.3 2.7 %copy.33 = bf16[2048,4,128]{0,2,1:T(8,128)(2,1)} copy(bf16[2048,4,128]{2,1,0:T(4,128)(2,1)S(1)} %copy-done.5) | data formatting | bytes 4194304 | tf_op args[3]
  42.1 1.8 multiply_cosine_fusion
  43.9 2.1 select_select_fusion.3
  47.1 1.9 collective-permute-start.7
  49.0 2.6 %collective-permute-start.10 = (f32[512]{0:T(512)S(1)}, f32[512]{0:T(512)S(1)}, u32[]{:S(2)}, u32[]{:S(2)}) collective-permute-start(f32[512]{0:T(512)S(1)} %add_rsqrt_fusion), channel_id=1, source_target_pairs={{0,8},{4,12},{8,0},{12,4},{1,9},{5,13},{9,1},{13,5},{2,10},{6,14},... | collective-permute-start | bytes 6152 | tf_op jit(solution)/shard_map/ppermute | solution.py:181
  52.9 1.4 fusion.2
  54.3 1.9 copy-done.1
  57.8 8.3 %fusion.3 = f32[512,4,256]{0,2,1:T(8,128)S(1)} fusion(bf16[4096,4,256]{2,1,0:T(4,128)(2,1)} %param.8, bf16[512,4096]{1,0:T(8,128)(2,1)} %copy-done.1), kind=kOutput, calls=%fused_computation.6 | convolution fusion | flops 4294967296 | bytes 14680064 | tf_op jit(solution)/shard_map/td,dgc->tgc/dot_general | solution.py:93
  66.3 1.9 copy.71
  68.3 1.9 copy.70
  70.2 3.7 %fusion.118 = (bf16[256,1024]{1,0:T(8,128)(2,1)}, bf16[256,1024]{1,0:T(8,128)(2,1)}, bf16[256,1024]{1,0:T(8,128)(2,1)}) fusion(bf16[512,4096]{1,0:T(8,128)(2,1)} %copy-done.1, s32[]{:T(128)S(6)} %select_n.338, s32[]{:T(128)S(6)} %select_n.341, s32[]{:T(128)S(6)} %select_n.353, s32[]{:T(128)S(6)} %select_n.348), kind=kLoop, calls=%fused_computation.163 | loop fusion | bytes 3145744 | tf_op jit(solution)/shard_map/dynamic_slice | solution.py:179
  73.9 5.0 %fusion.63 = f32[1024,1024]{1,0:T(8,128)} fusion(bf16[512,4096]{1,0:T(8,128)(2,1)} %copy-done.1, s32[]{:T(128)} %select_n.336, s32[]{:T(128)S(6)} %select_n.335), kind=kOutput, calls=%fused_computation.75 | convolution fusion | flops 1073741824 | bytes 6291972 | tf_op jit(solution)/shard_map/tc,tr->cr/dot_general | solution.py:175
  79.5 3.0 %slice_bitcast_fusion = bf16[2048,4,128]{2,0,1:T(8,128)(2,1)} fusion(bf16[2,2048,4,128]{3,1,2,0:T(8,128)(2,1)} %collective-permute-done.3), kind=kLoop, calls=%fused_computation.33 | loop fusion | bytes 4194304 | tf_op jit(solution)/shard_map/squeeze | solution.py:108
  82.6 4.0 %copy.34 = bf16[2048,4,128]{0,2,1:T(8,128)(2,1)} copy(bf16[2048,4,128]{2,0,1:T(8,128)(2,1)} %slice_bitcast_fusion) | data formatting | bytes 4194304 | tf_op jit(solution)/shard_map/squeeze | solution.py:108
  86.6 4.5 %fusion.35 = f32[512,512]{0,1} fusion(bf16[2048,512]{0,1:T(8,128)(2,1)} %bitcast.182, bf16[512,4096]{1,0:T(8,128)(2,1)} %copy-done.1, s32[]{:T(128)S(6)} %select_n.327), kind=kOutput, calls=%fused_computation.57 | convolution fusion | flops 1073741824 | bytes 5242884
  91.0 2.5 %copy.36 = f32[512,4,128]{2,0,1:T(8,128)} copy(f32[512,4,128]{0,2,1:T(8,128)} %bitcast.189) | data formatting | bytes 2097152 | tf_op jit(solution)/shard_map/td,dgh->tgh/dot_general | solution.py:111
  93.6 1.5 add.279
  95.1 1.6 subtract_convert_fusion.1
  96.7 3.0 %fusion.21 = f32[512,4,128]{2,0,1:T(8,128)S(1)} fusion(bf16[2,2048,4,128]{3,1,2,0:T(8,128)(2,1)} %collective-permute-done.3, bf16[512,4096]{1,0:T(8,128)(2,1)S(1)} %copy-done.2, s32[]{:T(128)S(6)} %select_n.327), kind=kOutput, calls=%fused_computation.35 | convolution fusion | flops 1073741824 | bytes 5242884 | tf_op jit(solution)/shard_map/td,dgh->tgh/dot_general | solution.py:112
  102.2 2.5 %fusion.7 = (f32[4,2,512]{2,1,0:T(2,128)S(1)}, f32[4,512,512,2]{2,1,3,0:T(8,128)S(1)}) fusion(pred[512,512]{0,1:T(8,128)(4,1)S(1)} %fusion.66, bf16[512,4,2,64]{3,0,2,1:T(8,128)(2,1)S(1)} %get-tuple-element.12, bf16[512,4,2,64]{3,0,2,1:T(8,128)(2,1)S(1)} %get-tuple-element.11, bf16[512,4,64]{2,0,1:T(8,128)(2,1)S(1)} %get-tuple-element.30, ...), kind=kOutput, calls=%fused_computation.11 | convolution fusion | flops 546304000 | bytes 10240000 | tf_op jit(solution)/shard_map/tgrh,ugh->grtu/dot_general | solution.py:120
  104.7 1.8 fusion.5
  106.4 42.8 %collective-permute-done.5 = bf16[512,2,4,128]{3,0,2,1:T(8,128)(2,1)S(1)} collective-permute-done((bf16[512,2,4,128]{3,0,2,1:T(8,128)(2,1)S(1)}, bf16[512,2,4,128]{3,0,2,1:T(8,128)(2,1)S(1)}, u32[]{:S(2)}, u32[]{:S(2)}) %collective-permute-start.5) | collective-permute-done | bytes 1048608 | tf_op jit(solution)/shard_map/ppermute | solution.py:18
  157.9 2.5 %fusion.33 = bf16[512,4,2,128]{0,3,2,1:T(8,128)(2,1)S(1)} fusion(f32[512,4,2,128]{0,3,2,1:T(8,128)S(1)} %bitcast.179, f32[512,4,2,128]{0,3,2,1:T(8,128)S(1)} %bitcast.180, f32[4,512,512,2]{2,1,3,0:T(8,128)S(1)} %get-tuple-element.49, f32[4,2,512]{2,1,0:T(2,128)S(1)} %get-tuple-element.48, pred[512,512]{0,1:T(8,128)(4,1)S(1)} %fusion.66, ...), kind=kOutput, calls=%fused_computation.54 | convolution fusion | flops 548405248 | bytes 14483456 | tf_op jit(solution)/shard_map/grtu,ugh->tgrh/dot_general | solution.py:130
  160.5 1.4 copy.51
  161.9 32.6 %collective-permute-done.9 = bf16[256,1024]{1,0:T(8,128)(2,1)S(1)} collective-permute-done((bf16[256,1024]{1,0:T(8,128)(2,1)}, bf16[256,1024]{1,0:T(8,128)(2,1)S(1)}, u32[]{:S(2)}, u32[]{:S(2)}) %collective-permute-start.9) | collective-permute-done | bytes 524320 | tf_op jit(solution)/shard_map/ppermute | solution.py:181
  195.1 2.6 %multiply_convert_fusion.2 = (bf16[512,1024]{1,0:T(8,128)(2,1)S(1)}, bf16[512,1024]{1,0:T(8,128)(2,1)S(1)}, bf16[512,1024]{1,0:T(8,128)(2,1)S(1)}) fusion(f32[1024]{0:T(1024)S(1)} %dynamic-slice-done, f32[512]{0:T(512)S(1)} %collective-permute-done.7, bf16[2048,1024]{1,0:T(8,128)(2,1)} %all-gather.2.cloned.1.call-done, s32[]{:T(128)S(6)} %select_n.343, ...), kind=kLoop, calls=%fused_computation.51 | loop fusion | flops 6291456 | bytes 6301708 | tf_op jit(solution)/shard_map/convert_element_type | solution.py:187
  200.8 1.9 fusion.84
  203.1 4.7 %add_multiply_fusion = f32[1024,1024]{1,0:T(8,128)} fusion(f32[1024,1024]{1,0:T(8,128)S(1)} %fusion.78, f32[1024,1024]{1,0:T(8,128)S(1)} %fusion.80, f32[1024,1024]{1,0:T(8,128)S(1)} %fusion.82, f32[1024,1024]{1,0:T(8,128)S(1)} %fusion.84, f32[1024,1024]{1,0:T(8,128)S(1)} %copy-done, f32[1024,1024]{1,0:T(8,128)S(1)} %fusion.86, ...), kind=kOutput, calls=%fused_computation.22 | convolution fusion | flops 544210944 | bytes 30408708 | tf_op jit(solution)/shard_map/tc,tr->cr/dot_general | solution.py:191
  (97 shorter events, 26.7 us)
Async XLA Ops:
  7.2 187.9 %all-gather.2.cloned.1.call-start = ((), (), s32[]{:S(2)}) async-start(), calls=%async_computation | async-start | bytes 5242880 | tf_op jit(solution)/shard_map/all_gather | solution.py:172
  7.2 26.5 %collective-permute-start.1 = (bf16[512,1024]{1,0:T(8,128)(2,1)}, bf16[512,1024]{1,0:T(8,128)(2,1)}, u32[]{:S(2)}, u32[]{:S(2)}) collective-permute-start(bf16[512,1024]{1,0:T(8,128)(2,1)} %param.6), channel_id=1, source_target_pairs={{0,2},{2,0},{1,3},{3,1},{4,6},{6,4},{5,7},{7,5},{8,10},{10,8},{9,1... | collective-permute-start | bytes 3145736 | tf_op jit(solution)/shard_map/ppermute | solution.py:70
  10.2 33.7 %collective-permute-start = (bf16[512,1024]{1,0:T(8,128)(2,1)}, bf16[512,1024]{1,0:T(8,128)(2,1)}, u32[]{:S(2)}, u32[]{:S(2)}) collective-permute-start(bf16[512,1024]{1,0:T(8,128)(2,1)} %param.6), channel_id=1, source_target_pairs={{0,1},{1,0},{2,3},{3,2},{4,5},{5,4},{6,7},{7,6},{8,9},{9,8},{10,11... | collective-permute-start | bytes 3145736 | tf_op jit(solution)/shard_map/ppermute | solution.py:26
  13.0 2.9 %copy-start.14 = (s32[3,8]{1,0:T(4,128)S(1)}, s32[3,8]{1,0:T(4,128)}, u32[]{:S(2)}) copy-start(s32[3,8]{1,0:T(4,128)} %param.11) | copy-start | bytes 292
  13.1 21.3 %copy-start.5 = (bf16[2048,4,128]{2,1,0:T(4,128)(2,1)S(1)}, bf16[2048,4,128]{2,1,0:T(4,128)(2,1)}, u32[]{:S(2)}) copy-start(bf16[2048,4,128]{2,1,0:T(4,128)(2,1)} %param.9) | copy-start | bytes 6291460
  15.4 28.5 %copy-start.7 = (bf16[512,1024]{1,0:T(8,128)(2,1)S(1)}, bf16[512,1024]{1,0:T(8,128)(2,1)}, u32[]{:S(2)}) copy-start(bf16[512,1024]{1,0:T(8,128)(2,1)} %param.6) | copy-start | bytes 3145732
  15.4 64.1 %collective-permute-start.3 = (bf16[2,2048,4,128]{3,1,2,0:T(8,128)(2,1)}, bf16[2,2048,4,128]{3,1,2,0:T(8,128)(2,1)}, u32[]{:S(2)}, u32[]{:S(2)}) collective-permute-start(bf16[2,2048,4,128]{3,1,2,0:T(8,128)(2,1)} %pad_maximum_fusion.1), channel_id=1, source_target_pairs={{0,1},{1,0},{2,3},{3,2},{4,5},{5,4},{6,7},{7,6},{8,9},{9,8},{10,11... | collective-permute-start | bytes 12582920 | tf_op jit(solution)/shard_map/ppermute | solution.py:107
  33.7 10.2 %collective-permute-start.2 = (bf16[512,1024]{1,0:T(8,128)(2,1)}, bf16[512,1024]{1,0:T(8,128)(2,1)}, u32[]{:S(2)}, u32[]{:S(2)}) collective-permute-start(bf16[512,1024]{1,0:T(8,128)(2,1)} %collective-permute-done.1), channel_id=1, source_target_pairs={{0,1},{1,0},{2,3},{3,2},{4,5},{5,4},{6,7},{7,6},{8,9},{9,8},{10,11... | collective-permute-start | bytes 3145736 | tf_op jit(solution)/shard_map/ppermute | solution.py:26
  46.1 6.8 %copy-start.13 = (f32[4096]{0:T(1024)S(1)}, f32[4096]{0:T(1024)}, u32[]{:S(2)}) copy-start(f32[4096]{0:T(1024)} %param.7) | copy-start | bytes 49156
  47.1 9.1 %copy-start.10 = (bf16[2048,4,128]{0,2,1:T(8,128)(2,1)S(1)}, bf16[2048,4,128]{0,2,1:T(8,128)(2,1)}, u32[]{:S(2)}) copy-start(bf16[2048,4,128]{0,2,1:T(8,128)(2,1)} %copy.33) | copy-start | bytes 6291460
  47.1 109.1 %collective-permute-start.7 = (f32[512]{0:T(512)S(1)}, f32[512]{0:T(512)S(1)}, u32[]{:S(2)}, u32[]{:S(2)}) collective-permute-start(f32[512]{0:T(512)S(1)} %add_rsqrt_fusion), channel_id=1, source_target_pairs={{0,4},{4,8},{8,12},{12,0},{1,5},{5,9},{9,13},{13,1},{2,6},{6,10},{... | collective-permute-start | bytes 6152 | tf_op jit(solution)/shard_map/ppermute | solution.py:181
  49.0 146.2 %collective-permute-start.10 = (f32[512]{0:T(512)S(1)}, f32[512]{0:T(512)S(1)}, u32[]{:S(2)}, u32[]{:S(2)}) collective-permute-start(f32[512]{0:T(512)S(1)} %add_rsqrt_fusion), channel_id=1, source_target_pairs={{0,8},{4,12},{8,0},{12,4},{1,9},{5,13},{9,1},{13,5},{2,10},{6,14},... | collective-permute-start | bytes 6152 | tf_op jit(solution)/shard_map/ppermute | solution.py:181
  51.5 143.6 %collective-permute-start.13 = (f32[512]{0:T(512)S(1)}, f32[512]{0:T(512)S(1)}, u32[]{:S(2)}, u32[]{:S(2)}) collective-permute-start(f32[512]{0:T(512)S(1)} %add_rsqrt_fusion), channel_id=1, source_target_pairs={{0,12},{4,0},{8,4},{12,8},{1,13},{5,1},{9,5},{13,9},{2,14},{6,2},{... | collective-permute-start | bytes 6152 | tf_op jit(solution)/shard_map/ppermute | solution.py:181
  54.2 1.9 copy-start.1
  70.2 8.7 %copy-start.3 = (f32[512,4,2,64]{3,0,2,1:T(8,128)S(1)}, f32[512,4,2,64]{3,0,2,1:T(8,128)}, u32[]{:S(2)}) copy-start(f32[512,4,2,64]{3,0,2,1:T(8,128)} %copy.71) | copy-start | bytes 3145732
  70.2 8.7 %copy-start.4 = (f32[512,4,2,64]{3,0,2,1:T(8,128)S(1)}, f32[512,4,2,64]{3,0,2,1:T(8,128)}, u32[]{:S(2)}) copy-start(f32[512,4,2,64]{3,0,2,1:T(8,128)} %copy.70) | copy-start | bytes 3145732
  70.2 8.7 %copy-start.8 = (f32[512,64]{1,0:T(8,128)S(1)}, f32[512,64]{1,0:T(8,128)}, u32[]{:S(2)}) copy-start(f32[512,64]{1,0:T(8,128)} %get-tuple-element.35) | copy-start | bytes 393220
  70.2 8.7 %copy-start.9 = (f32[512,64]{1,0:T(8,128)S(1)}, f32[512,64]{1,0:T(8,128)}, u32[]{:S(2)}) copy-start(f32[512,64]{1,0:T(8,128)} %get-tuple-element.36) | copy-start | bytes 393220
  93.6 3.1 %copy-start.2 = (bf16[512,4096]{1,0:T(8,128)(2,1)S(1)}, bf16[512,4096]{1,0:T(8,128)(2,1)}, u32[]{:S(2)}) copy-start(bf16[512,4096]{1,0:T(8,128)(2,1)} %copy-done.1) | copy-start | bytes 12582916
  96.6 3.0 %copy-start.11 = (bf16[2048,4,128]{2,1,0:T(4,128)(2,1)S(1)}, bf16[2048,4,128]{2,1,0:T(4,128)(2,1)}, u32[]{:S(2)}) copy-start(bf16[2048,4,128]{2,1,0:T(4,128)(2,1)} %param.10) | copy-start | bytes 6291460
  101.2 48.0 %collective-permute-start.5 = (bf16[512,2,4,128]{3,0,2,1:T(8,128)(2,1)S(1)}, bf16[512,2,4,128]{3,0,2,1:T(8,128)(2,1)S(1)}, u32[]{:S(2)}, u32[]{:S(2)}) collective-permute-start(bf16[512,2,4,128]{3,0,2,1:T(8,128)(2,1)S(1)} %maximum_bitcast_fusion), channel_id=1, source_target_pairs={{0,8},{8,0},{4,12},{12,4},{1,9},{9,1},{5,13},{13,5},{2,10},{10,2},... | collective-permute-start | bytes 3145736 | tf_op jit(solution)/shard_map/ppermute | solution.py:18
  101.3 48.6 %collective-permute-start.4 = (bf16[512,2,4,128]{3,0,2,1:T(8,128)(2,1)S(1)}, bf16[512,2,4,128]{3,0,2,1:T(8,128)(2,1)S(1)}, u32[]{:S(2)}, u32[]{:S(2)}) collective-permute-start(bf16[512,2,4,128]{3,0,2,1:T(8,128)(2,1)S(1)} %maximum_bitcast_fusion), channel_id=1, source_target_pairs={{0,4},{4,0},{8,12},{12,8},{1,5},{5,1},{9,13},{13,9},{2,6},{6,2},{1... | collective-permute-start | bytes 3145736 | tf_op jit(solution)/shard_map/ppermute | solution.py:18
  149.2 45.8 %collective-permute-start.12 = (bf16[256,1024]{1,0:T(8,128)(2,1)}, bf16[256,1024]{1,0:T(8,128)(2,1)S(1)}, u32[]{:S(2)}, u32[]{:S(2)}) collective-permute-start(bf16[256,1024]{1,0:T(8,128)(2,1)} %get-tuple-element.21), channel_id=1, source_target_pairs={{0,12},{4,0},{8,4},{12,8},{1,13},{5,1},{9,5},{13,9},{2,14},{6,2},{... | collective-permute-start | bytes 1572872 | tf_op jit(solution)/shard_map/ppermute | solution.py:181
  150.0 44.6 %collective-permute-start.9 = (bf16[256,1024]{1,0:T(8,128)(2,1)}, bf16[256,1024]{1,0:T(8,128)(2,1)S(1)}, u32[]{:S(2)}, u32[]{:S(2)}) collective-permute-start(bf16[256,1024]{1,0:T(8,128)(2,1)} %get-tuple-element.22), channel_id=1, source_target_pairs={{0,8},{4,12},{8,0},{12,4},{1,9},{5,13},{9,1},{13,5},{2,10},{6,14},... | collective-permute-start | bytes 1572872 | tf_op jit(solution)/shard_map/ppermute | solution.py:181
  155.6 1.0 copy-start.12
  156.6 37.9 %collective-permute-start.6 = (bf16[256,1024]{1,0:T(8,128)(2,1)S(1)}, bf16[256,1024]{1,0:T(8,128)(2,1)S(1)}, u32[]{:S(2)}, u32[]{:S(2)}) collective-permute-start(bf16[256,1024]{1,0:T(8,128)(2,1)S(1)} %copy-done.12), channel_id=1, source_target_pairs={{0,4},{4,8},{8,12},{12,0},{1,5},{5,9},{9,13},{13,1},{2,6},{6,10},{... | collective-permute-start | bytes 1572872 | tf_op jit(solution)/shard_map/ppermute | solution.py:181
  157.9 37.2 %dynamic-slice-start = ((f32[4096]{0:T(1024)}, s32[]{:T(128)}), f32[1024]{0:T(1024)S(1)}, s32[]{:S(2)}) async-start(f32[4096]{0:T(1024)} %param.7, s32[]{:T(128)} %select_n.336), calls=%async_computation.1 | async-start | bytes 8704 | tf_op jit(solution)/shard_map/dynamic_slice | solution.py:173
  194.5 5.5 %collective-permute-start.11 = (bf16[256,1024]{1,0:T(8,128)(2,1)S(1)}, bf16[256,1024]{1,0:T(8,128)(2,1)S(1)}, u32[]{:S(2)}, u32[]{:S(2)}) collective-permute-start(bf16[256,1024]{1,0:T(8,128)(2,1)S(1)} %collective-permute-done.9), channel_id=1, source_target_pairs={{0,1},{1,0},{2,3},{3,2},{4,5},{5,4},{6,7},{7,6},{8,9},{9,8},{10,11... | collective-permute-start | bytes 1572872 | tf_op jit(solution)/shard_map/ppermute | solution.py:26
  194.5 6.3 %collective-permute-start.8 = (bf16[256,1024]{1,0:T(8,128)(2,1)S(1)}, bf16[256,1024]{1,0:T(8,128)(2,1)}, u32[]{:S(2)}, u32[]{:S(2)}) collective-permute-start(bf16[256,1024]{1,0:T(8,128)(2,1)S(1)} %collective-permute-done.6), channel_id=1, source_target_pairs={{0,1},{1,0},{2,3},{3,2},{4,5},{5,4},{6,7},{7,6},{8,9},{9,8},{10,11... | collective-permute-start | bytes 1572872 | tf_op jit(solution)/shard_map/ppermute | solution.py:26
  195.0 7.7 %collective-permute-start.14 = (bf16[256,1024]{1,0:T(8,128)(2,1)S(1)}, bf16[256,1024]{1,0:T(8,128)(2,1)}, u32[]{:S(2)}, u32[]{:S(2)}) collective-permute-start(bf16[256,1024]{1,0:T(8,128)(2,1)S(1)} %collective-permute-done.12), channel_id=1, source_target_pairs={{0,1},{1,0},{2,3},{3,2},{4,5},{5,4},{6,7},{7,6},{8,9},{9,8},{10,11... | collective-permute-start | bytes 1572872 | tf_op jit(solution)/shard_map/ppermute | solution.py:26
  197.8 1.5 copy-start.6
  200.8 2.3 %copy-start = (f32[1024,1024]{1,0:T(8,128)S(1)}, f32[1024,1024]{1,0:T(8,128)}, u32[]{:S(2)}) copy-start(f32[1024,1024]{1,0:T(8,128)} %fusion.63) | copy-start | bytes 12582916
Sparse Core Ops, SparseCore 0:
  10.4 82.7 all-gather.1

commit v12 on v9

--- a/solution.py
+++ b/solution.py
@@ -135,12 +135,14 @@
     band = width // seq_count
     share = row_count // sub_count
     my_rows = lax.dynamic_slice_in_dim(normed, sub_index * share, share, 0)
-    outgoing_rows = [
-        lax.dynamic_slice_in_dim(my_rows, ((seq_index + shift) % seq_count) * band, band, 1)
-        for shift in range(1, seq_count)
-    ]
+    arrived = []
+    for shift in range(1, seq_count):
+        target = (seq_index + shift) % seq_count
+        outgoing = lax.dynamic_slice_in_dim(my_rows, target * band, band, 1)
+        route = [(j, (j + shift) % seq_count) for j in range(seq_count)]
+        arrived.append(lax.ppermute((outgoing, row_scale), "seq", route))
     kv_pair = jnp.stack([keys, values]).swapaxes(0, 1)
-    outgoing_rows, kv_pair = lax.optimization_barrier((outgoing_rows, kv_pair))
+    arrived, kv_pair = lax.optimization_barrier((arrived, kv_pair))
     for section in range(1, seq_count.bit_length()):
         (far_pair,) = split_send((kv_pair,), "seq", section - 1)
         far_keys = far_pair[:, 0]
@@ -184,9 +186,7 @@
     mine = lax.dynamic_slice_in_dim(normed, seq_index * band, band, 1)
     gram_sum = jnp.einsum("tc,tr->cr", mine, owned, preferred_element_type=jnp.float32)
     for shift in range(1, seq_count):
-        outgoing = outgoing_rows[shift - 1]
-        route = [(j, (j + shift) % seq_count) for j in range(seq_count)]
-        incoming, their_scale = lax.ppermute((outgoing, row_scale), "seq", route)
+        incoming, their_scale = arrived[shift - 1]
         halves = swap_halves(incoming, sub_count, sub_index)
         source = (seq_index - shift) % seq_count
         their_raw = lax.dynamic_slice_in_dim(raw_columns, source * row_count, row_count, 0)

time: 196 us -> 202 us (1.031)
  starting transfers between devices: 14.2 us -> 30.7 us
  waiting for transfers between devices: 69.6 us -> 57.7 us
  matrix products: 40.3 us -> 46.4 us
  local copies, waits for them, and re-layouts: 31.1 us -> 29 us
    ppermute x2, starting transfers between devices: 1.14 us -> 16.2 us  [from_partner(): return lax.ppermute(block, axis, route)]
    ppermute x6, waiting for transfers between devices: 33.8 us -> 22.4 us  [body(): arrived.append(lax.ppermute((outgoing, row_scale), 'seq', route))]
    dot_general x1, matrix products: 3.31 us -> 7.47 us  [body(): jnp.einsum('tc,tr->cr', mine, owned, preferred_element_type=jnp.float32)]
    unnamed x32 -> x28, local copies, waits for them, and re-layouts: 11.3 us -> 9.1 us
  transfers between devices with their start and end apart: 18 -> 18, of which waited for: 3 -> 3; matrix products, arithmetic and copies ran while one was open for 45% -> 44% of each run, Pallas kernels for 0% -> 0%
where the time goes in v12:
time: 202 us
  waiting for transfers between devices  57.7 us (29%)
  matrix products  46.4 us (23%)
  starting transfers between devices  30.7 us (15%)
  local copies, waits for them, and re-layouts  29 us (14%)
  other arithmetic  23.4 us (12%)
  between operations  14.6 us (7%)
    ppermute x6, waiting for transfers between devices, body(): arrived.append(lax.ppermute((outgoing, row_scale), 'seq', route))  22.4 us
    ppermute x2, waiting for transfers between devices, from_partner(): return lax.ppermute(block, axis, route)  18.1 us
    ppermute x1, waiting for transfers between devices, body(): across.append(lax.ppermute(tokens, 'kvh', route))  17.1 us
    ppermute x2, starting transfers between devices, from_partner(): return lax.ppermute(block, axis, route)  16.2 us
    dot_general x6, matrix products, body(): jnp.einsum('tc,tr->cr', halves[lane_shift], their_rows, preferred_element...  10.7 us
    ppermute x6, starting transfers between devices, body(): arrived.append(lax.ppermute((outgoing, row_scale), 'seq', route))  9.73 us
    unnamed x28, local copies, waits for them, and re-layouts  9.1 us
    dot_general x1, matrix products, body(): jnp.einsum('td,dgc->tgc', normed, w_query, preferred_element_type=jnp.flo...  8.28 us
  transfers between devices with their start and end apart: 18, of which 3 were waited for; matrix products, arithmetic and copies ran while one was open for 44% of the time, Pallas kernels for 0%

profile of v12, /device:TPU:0, one launch (start us, length us, event | category | flops | bytes accessed | tf_op | source)
XLA Modules:
  0.0 201.7 jit_solution(6126694399080100362)
XLA Ops:
  7.2 3.0 %collective-permute-start.1 = (bf16[512,1024]{1,0:T(8,128)(2,1)}, bf16[512,1024]{1,0:T(8,128)(2,1)}, u32[]{:S(2)}, u32[]{:S(2)}) collective-permute-start(bf16[512,1024]{1,0:T(8,128)(2,1)} %param.6), channel_id=1, source_target_pairs={{0,2},{2,0},{1,3},{3,1},{4,6},{6,4},{5,7},{7,5},{8,10},{10,8},{9,1... | collective-permute-start | bytes 3145736 | tf_op jit(solution)/shard_map/ppermute | solution.py:70
  10.3 2.8 %copy_bitcast_fusion = (bf16[1,2048,4,128]{3,1,2,0:T(8,128)(2,1)S(1)}, bf16[1,2048,4,128]{3,1,2,0:T(8,128)(2,1)S(1)}) fusion(bf16[2048,4,128]{2,1,0:T(4,128)(2,1)} %param.9, bf16[2048,4,128]{2,1,0:T(4,128)(2,1)} %param.10), kind=kLoop, calls=%fused_computation.48 | loop fusion | bytes 8388608 | tf_op jit(solution)/shard_map/stack | solution.py:107
  13.1 2.4 %pad_maximum_fusion.1 = bf16[2,2048,4,128]{3,1,2,0:T(8,128)(2,1)} fusion(bf16[1,2048,4,128]{3,1,2,0:T(8,128)(2,1)S(1)} %get-tuple-element.71, bf16[1,2048,4,128]{3,1,2,0:T(8,128)(2,1)S(1)} %get-tuple-element.70), kind=kLoop, calls=%fused_computation.14 | loop fusion | flops 2097152 | bytes 8388608 | tf_op jit(solution)/shard_map/stack | solution.py:107
  16.6 17.1 %collective-permute-done.1 = bf16[512,1024]{1,0:T(8,128)(2,1)} collective-permute-done((bf16[512,1024]{1,0:T(8,128)(2,1)}, bf16[512,1024]{1,0:T(8,128)(2,1)}, u32[]{:S(2)}, u32[]{:S(2)}) %collective-permute-start.1) | collective-permute-done | bytes 1048608 | tf_op jit(solution)/shard_map/ppermute | solution.py:70
  33.9 2.7 %copy.53 = bf16[2048,4,128]{0,2,1:T(8,128)(2,1)} copy(bf16[2048,4,128]{2,1,0:T(4,128)(2,1)S(1)} %copy-done.3) | data formatting | bytes 4194304 | tf_op args[3]
  39.5 1.8 multiply_cosine_fusion
  41.3 2.5 %select_reduce_fusion.1 = (f32[512]{0:T(512)S(1)}, f32[512]{0:T(512)S(1)}) fusion(f32[]{:T(128)} %bitcast.45, f32[]{:T(128)} %bitcast.44, f32[]{:T(128)} %bitcast.32, f32[]{:T(128)} %bitcast.31), kind=kLoop, calls=%fused_computation.152 | loop fusion | flops 7168 | bytes 4112 | tf_op jit(solution)/shard_map/gather | solution.py:153
  43.9 2.1 %select_select_fusion.3 = (bf16[512,1024]{1,0:T(8,128)(2,1)S(1)}, bf16[512,1024]{1,0:T(8,128)(2,1)S(1)}, bf16[512,1024]{1,0:T(8,128)(2,1)S(1)}, bf16[512,1024]{1,0:T(8,128)(2,1)S(1)}) fusion(bf16[512,1024]{1,0:T(8,128)(2,1)} %collective-permute-done.1, bf16[512,1024]{1,0:T(8,128)(2,1)} %collective-permute-done.2, bf16[512,1024]{1,0:T(8,128)(2,1)S(1)} %copy-done.4, ...), kind=kLoop, calls=%fused_computation.84 | loop fusion | flops 6291456 | bytes 8388620 | tf_op jit(solution)/shard_map/select_n | solution.py:78
  47.1 1.9 collective-permute-start.5
  49.0 2.6 %collective-permute-start.7 = (f32[512]{0:T(512)S(1)}, f32[512]{0:T(512)S(1)}, u32[]{:S(2)}, u32[]{:S(2)}) collective-permute-start(f32[512]{0:T(512)S(1)} %add_rsqrt_fusion), channel_id=1, source_target_pairs={{0,8},{4,12},{8,0},{12,4},{1,9},{5,13},{9,1},{13,5},{2,10},{6,14},... | collective-permute-start | bytes 6152 | tf_op jit(solution)/shard_map/ppermute | solution.py:143
  52.9 2.6 %fusion.121 = (bf16[256,1024]{1,0:T(8,128)(2,1)}, bf16[256,1024]{1,0:T(8,128)(2,1)}, bf16[256,1024]{1,0:T(8,128)(2,1)}) fusion(bf16[512,4096]{1,0:T(8,128)(2,1)S(1)} %fusion.2, s32[]{:T(128)S(6)} %select_n.348, s32[]{:T(128)S(6)} %select_n.357, s32[]{:T(128)S(6)} %select_n.354, s32[]{:T(128)S(6)} %select_n.351), kind=kLoop, calls=%fused_computation.169 | loop fusion | bytes 3145744 | tf_op jit(solution)/shard_map/dynamic_slice | solution.py:141
  55.6 1.8 collective-permute-start.6
  59.0 8.3 %fusion.3 = f32[512,4,256]{0,2,1:T(8,128)S(1)} fusion(bf16[4096,4,256]{2,1,0:T(4,128)(2,1)} %param.8, bf16[512,4096]{1,0:T(8,128)(2,1)} %copy-done), kind=kOutput, calls=%fused_computation.6 | convolution fusion | flops 4294967296 | bytes 14680064 | tf_op jit(solution)/shard_map/td,dgc->tgc/dot_general | solution.py:93
  68.9 1.8 copy.91
  70.7 3.1 %copy.90 = f32[512,4,2,64]{3,0,2,1:T(8,128)} copy(f32[512,4,2,64]{0,3,2,1:T(8,128)} %get-tuple-element.44) | data formatting | bytes 2097152
  73.9 2.2 %collective-permute-start.8 = (bf16[256,1024]{1,0:T(8,128)(2,1)}, bf16[256,1024]{1,0:T(8,128)(2,1)}, u32[]{:S(2)}, u32[]{:S(2)}) collective-permute-start(bf16[256,1024]{1,0:T(8,128)(2,1)} %get-tuple-element.36), channel_id=1, source_target_pairs={{0,12},{4,0},{8,4},{12,8},{1,13},{5,1},{9,5},{13,9},{2,14},{6,2},{... | collective-permute-start | bytes 1572872 | tf_op jit(solution)/shard_map/ppermute | solution.py:143
  76.0 3.5 %fusion.21 = f32[512,4,128]{2,0,1:T(8,128)S(1)} fusion(bf16[2,2048,4,128]{3,1,2,0:T(8,128)(2,1)} %collective-permute-done.3, bf16[512,4096]{1,0:T(8,128)(2,1)} %copy-done, s32[]{:T(128)S(6)} %select_n.341), kind=kOutput, calls=%fused_computation.35 | convolution fusion | flops 1073741824 | bytes 5242884 | tf_op jit(solution)/shard_map/td,dgh->tgh/dot_general | solution.py:112
  79.5 2.1 %fusion.54 = bf16[512,4,128]{2,0,1:T(8,128)(2,1)} fusion(f32[512,4,128]{2,0,1:T(8,128)S(1)} %fusion.21, bf16[2048,4,128]{2,1,0:T(4,128)(2,1)S(1)} %copy-done.8, bf16[512,4096]{1,0:T(8,128)(2,1)S(1)} %copy-done.1, s32[]{:T(128)S(6)} %select_n.340), kind=kOutput, calls=%fused_computation.68 | convolution fusion | flops 1074266112 | bytes 5767172 | tf_op jit(solution)/shard_map/td,dgh->tgh/dot_general | solution.py:112
  81.6 3.0 %slice_bitcast_fusion = bf16[2048,4,128]{2,0,1:T(8,128)(2,1)} fusion(bf16[2,2048,4,128]{3,1,2,0:T(8,128)(2,1)} %collective-permute-done.3), kind=kLoop, calls=%fused_computation.33 | loop fusion | bytes 4194304 | tf_op jit(solution)/shard_map/squeeze | solution.py:108
  84.6 4.0 %copy.54 = bf16[2048,4,128]{0,2,1:T(8,128)(2,1)} copy(bf16[2048,4,128]{2,0,1:T(8,128)(2,1)} %slice_bitcast_fusion) | data formatting | bytes 4194304 | tf_op jit(solution)/shard_map/squeeze | solution.py:108
  88.6 4.5 %fusion.35 = f32[512,512]{0,1} fusion(bf16[2048,512]{0,1:T(8,128)(2,1)} %bitcast.182, bf16[512,4096]{1,0:T(8,128)(2,1)} %copy-done, s32[]{:T(128)S(6)} %select_n.341), kind=kOutput, calls=%fused_computation.57 | convolution fusion | flops 1073741824 | bytes 5242884
  93.1 2.5 %copy.56 = f32[512,4,128]{2,0,1:T(8,128)} copy(f32[512,4,128]{0,2,1:T(8,128)} %bitcast.188) | data formatting | bytes 2097152 | tf_op jit(solution)/shard_map/td,dgh->tgh/dot_general | solution.py:111
  100.3 22.4 %collective-permute-done.9 = f32[512]{0:T(512)S(1)} collective-permute-done((f32[512]{0:T(512)S(1)}, f32[512]{0:T(512)S(1)}, u32[]{:S(2)}, u32[]{:S(2)}) %collective-permute-start.9) | collective-permute-done | bytes 2080 | tf_op jit(solution)/shard_map/ppermute | solution.py:143
  122.7 14.6 %collective-permute-start.12 = (bf16[256,2,4,128]{3,0,2,1:T(8,128)(2,1)S(1)}, bf16[256,2,4,128]{3,0,2,1:T(8,128)(2,1)S(1)}, u32[]{:S(2)}, u32[]{:S(2)}) collective-permute-start(bf16[256,2,4,128]{3,0,2,1:T(8,128)(2,1)S(1)} %constant_dynamic-slice_fusion.2), channel_id=1, source_target_pairs={{0,8},{8,0},{4,12},{12,4},{1,9},{9,1},{5,13},{13,5},{2,10},{10,2},... | collective-permute-start | bytes 1572872 | tf_op jit(solution)/shard_map/ppermute | solution.py:18
  140.1 2.5 %fusion.7 = (f32[4,2,512]{2,1,0:T(2,128)S(1)}, f32[4,512,512,2]{2,1,3,0:T(8,128)S(1)}) fusion(pred[512,512]{0,1:T(8,128)(4,1)S(1)} %fusion.68, bf16[512,4,2,64]{3,0,2,1:T(8,128)(2,1)S(1)} %get-tuple-element.28, bf16[512,4,2,64]{3,0,2,1:T(8,128)(2,1)S(1)} %get-tuple-element.27, bf16[512,4,64]{2,0,1:T(8,128)(2,1)S(1)} %get-tuple-element.46, ...), kind=kOutput, calls=%fused_computation.11 | convolution fusion | flops 546304000 | bytes 10240000 | tf_op jit(solution)/shard_map/tgrh,ugh->grtu/dot_general | solution.py:120
  142.6 18.1 %collective-permute-done.12 = bf16[256,2,4,128]{3,0,2,1:T(8,128)(2,1)S(1)} collective-permute-done((bf16[256,2,4,128]{3,0,2,1:T(8,128)(2,1)S(1)}, bf16[256,2,4,128]{3,0,2,1:T(8,128)(2,1)S(1)}, u32[]{:S(2)}, u32[]{:S(2)}) %collective-permute-start.12) | collective-permute-done | bytes 524320 | tf_op jit(solution)/shard_map/ppermute | solution.py:18
  169.8 2.8 %fusion.33 = bf16[512,4,2,128]{0,3,2,1:T(8,128)(2,1)S(1)} fusion(f32[512,4,2,128]{0,3,2,1:T(8,128)S(1)} %bitcast.179, f32[512,4,2,128]{0,3,2,1:T(8,128)S(1)} %bitcast.180, f32[4,512,512,2]{2,1,3,0:T(8,128)S(1)} %get-tuple-element.65, f32[4,2,512]{2,1,0:T(2,128)S(1)} %get-tuple-element.64, pred[512,512]{0,1:T(8,128)(4,1)S(1)} %fusion.68, ...), kind=kOutput, calls=%fused_computation.54 | convolution fusion | flops 548405248 | bytes 14483456 | tf_op jit(solution)/shard_map/grtu,ugh->tgrh/dot_general | solution.py:130
  174.0 2.6 %multiply_convert_fusion.2 = (bf16[512,1024]{1,0:T(8,128)(2,1)S(1)}, bf16[512,1024]{1,0:T(8,128)(2,1)S(1)}, bf16[512,1024]{1,0:T(8,128)(2,1)S(1)}) fusion(f32[1024]{0:T(1024)S(1)} %dynamic-slice-done, f32[512]{0:T(512)S(1)} %collective-permute-done.5, bf16[2048,1024]{1,0:T(8,128)(2,1)} %all-gather.2.cloned.1.call-done, s32[]{:T(128)S(6)} %select_n.365, ...), kind=kLoop, calls=%fused_computation.51 | loop fusion | flops 6291456 | bytes 6301708 | tf_op jit(solution)/shard_map/convert_element_type | solution.py:195
  176.6 1.8 fusion.81
  182.8 1.8 fusion.83
  184.6 2.8 %fusion.87 = f32[1024,1024]{1,0:T(8,128)} fusion(bf16[256,1024]{1,0:T(8,128)(2,1)S(1)} %collective-permute-done.14, bf16[512,1024]{1,0:T(8,128)(2,1)S(1)} %get-tuple-element.33, s32[]{:T(128)S(6)} %select_n.359), kind=kOutput, calls=%fused_computation.105 | convolution fusion | flops 536870912 | bytes 5242884 | tf_op jit(solution)/shard_map/tc,tr->cr/dot_general | solution.py:199
  187.3 7.5 %add_multiply_fusion = f32[1024,1024]{1,0:T(8,128)} fusion(f32[1024,1024]{1,0:T(8,128)S(1)} %fusion.79, f32[1024,1024]{1,0:T(8,128)S(1)} %fusion.81, f32[1024,1024]{1,0:T(8,128)S(1)} %fusion.83, f32[1024,1024]{1,0:T(8,128)S(1)} %fusion.85, f32[1024,1024]{1,0:T(8,128)} %fusion.87, f32[1024,1024]{1,0:T(8,128)S(1)} %fusion.89, bf16[512,4096]{1,0:T(8,128)(2,1)} %copy-done, ...), kind=kOutput, calls=%fused_computation.22 | convolution fusion | flops 1081081856 | bytes 31457796 | tf_op jit(solution)/shard_map/tc,tr->cr/dot_general | solution.py:187
  (102 shorter events, 32.0 us)
Async XLA Ops:
  7.2 166.8 %all-gather.2.cloned.1.call-start = ((), (), s32[]{:S(2)}) async-start(), calls=%async_computation | async-start | bytes 5242880 | tf_op jit(solution)/shard_map/all_gather | solution.py:184
  7.2 26.5 %collective-permute-start.1 = (bf16[512,1024]{1,0:T(8,128)(2,1)}, bf16[512,1024]{1,0:T(8,128)(2,1)}, u32[]{:S(2)}, u32[]{:S(2)}) collective-permute-start(bf16[512,1024]{1,0:T(8,128)(2,1)} %param.6), channel_id=1, source_target_pairs={{0,2},{2,0},{1,3},{3,1},{4,6},{6,4},{5,7},{7,5},{8,10},{10,8},{9,1... | collective-permute-start | bytes 3145736 | tf_op jit(solution)/shard_map/ppermute | solution.py:70
  10.2 33.7 %collective-permute-start = (bf16[512,1024]{1,0:T(8,128)(2,1)}, bf16[512,1024]{1,0:T(8,128)(2,1)}, u32[]{:S(2)}, u32[]{:S(2)}) collective-permute-start(bf16[512,1024]{1,0:T(8,128)(2,1)} %param.6), channel_id=1, source_target_pairs={{0,1},{1,0},{2,3},{3,2},{4,5},{5,4},{6,7},{7,6},{8,9},{9,8},{10,11... | collective-permute-start | bytes 3145736 | tf_op jit(solution)/shard_map/ppermute | solution.py:26
  13.0 2.9 %copy-start.11 = (s32[3,8]{1,0:T(4,128)S(1)}, s32[3,8]{1,0:T(4,128)}, u32[]{:S(2)}) copy-start(s32[3,8]{1,0:T(4,128)} %param.11) | copy-start | bytes 292
  13.1 20.8 %copy-start.3 = (bf16[2048,4,128]{2,1,0:T(4,128)(2,1)S(1)}, bf16[2048,4,128]{2,1,0:T(4,128)(2,1)}, u32[]{:S(2)}) copy-start(bf16[2048,4,128]{2,1,0:T(4,128)(2,1)} %param.9) | copy-start | bytes 6291460
  15.4 28.5 %copy-start.4 = (bf16[512,1024]{1,0:T(8,128)(2,1)S(1)}, bf16[512,1024]{1,0:T(8,128)(2,1)}, u32[]{:S(2)}) copy-start(bf16[512,1024]{1,0:T(8,128)(2,1)} %param.6) | copy-start | bytes 3145732
  15.4 58.4 %collective-permute-start.3 = (bf16[2,2048,4,128]{3,1,2,0:T(8,128)(2,1)}, bf16[2,2048,4,128]{3,1,2,0:T(8,128)(2,1)}, u32[]{:S(2)}, u32[]{:S(2)}) collective-permute-start(bf16[2,2048,4,128]{3,1,2,0:T(8,128)(2,1)} %pad_maximum_fusion.1), channel_id=1, source_target_pairs={{0,1},{1,0},{2,3},{3,2},{4,5},{5,4},{6,7},{7,6},{8,9},{9,8},{10,11... | collective-permute-start | bytes 12582920 | tf_op jit(solution)/shard_map/ppermute | solution.py:107
  33.7 10.2 %collective-permute-start.2 = (bf16[512,1024]{1,0:T(8,128)(2,1)}, bf16[512,1024]{1,0:T(8,128)(2,1)}, u32[]{:S(2)}, u32[]{:S(2)}) collective-permute-start(bf16[512,1024]{1,0:T(8,128)(2,1)} %collective-permute-done.1), channel_id=1, source_target_pairs={{0,1},{1,0},{2,3},{3,2},{4,5},{5,4},{6,7},{7,6},{8,9},{9,8},{10,11... | collective-permute-start | bytes 3145736 | tf_op jit(solution)/shard_map/ppermute | solution.py:26
  46.1 5.5 %copy-start.10 = (f32[4096]{0:T(1024)S(1)}, f32[4096]{0:T(1024)}, u32[]{:S(2)}) copy-start(f32[4096]{0:T(1024)} %param.7) | copy-start | bytes 49156
  47.1 10.3 %copy-start.7 = (bf16[2048,4,128]{0,2,1:T(8,128)(2,1)S(1)}, bf16[2048,4,128]{0,2,1:T(8,128)(2,1)}, u32[]{:S(2)}) copy-start(bf16[2048,4,128]{0,2,1:T(8,128)(2,1)} %copy.53) | copy-start | bytes 6291460
  47.1 51.6 %collective-permute-start.5 = (f32[512]{0:T(512)S(1)}, f32[512]{0:T(512)S(1)}, u32[]{:S(2)}, u32[]{:S(2)}) collective-permute-start(f32[512]{0:T(512)S(1)} %add_rsqrt_fusion), channel_id=1, source_target_pairs={{0,4},{4,8},{8,12},{12,0},{1,5},{5,9},{9,13},{13,1},{2,6},{6,10},{... | collective-permute-start | bytes 6152 | tf_op jit(solution)/shard_map/ppermute | solution.py:143
  49.0 51.3 %collective-permute-start.7 = (f32[512]{0:T(512)S(1)}, f32[512]{0:T(512)S(1)}, u32[]{:S(2)}, u32[]{:S(2)}) collective-permute-start(f32[512]{0:T(512)S(1)} %add_rsqrt_fusion), channel_id=1, source_target_pairs={{0,8},{4,12},{8,0},{12,4},{1,9},{5,13},{9,1},{13,5},{2,10},{6,14},... | collective-permute-start | bytes 6152 | tf_op jit(solution)/shard_map/ppermute | solution.py:143
  52.9 5.8 %copy-start = (bf16[512,4096]{1,0:T(8,128)(2,1)}, bf16[512,4096]{1,0:T(8,128)(2,1)S(1)}, u32[]{:S(2)}) copy-start(bf16[512,4096]{1,0:T(8,128)(2,1)S(1)} %fusion.2) | copy-start | bytes 12582916
  55.5 67.2 %collective-permute-start.4 = (bf16[256,1024]{1,0:T(8,128)(2,1)}, bf16[256,1024]{1,0:T(8,128)(2,1)}, u32[]{:S(2)}, u32[]{:S(2)}) collective-permute-start(bf16[256,1024]{1,0:T(8,128)(2,1)} %get-tuple-element.38), channel_id=1, source_target_pairs={{0,4},{4,8},{8,12},{12,0},{1,5},{5,9},{9,13},{13,1},{2,6},{6,10},{... | collective-permute-start | bytes 1572872 | tf_op jit(solution)/shard_map/ppermute | solution.py:143
  55.6 67.1 %collective-permute-start.6 = (bf16[256,1024]{1,0:T(8,128)(2,1)}, bf16[256,1024]{1,0:T(8,128)(2,1)}, u32[]{:S(2)}, u32[]{:S(2)}) collective-permute-start(bf16[256,1024]{1,0:T(8,128)(2,1)} %get-tuple-element.37), channel_id=1, source_target_pairs={{0,8},{4,12},{8,0},{12,4},{1,9},{5,13},{9,1},{13,5},{2,10},{6,14},... | collective-permute-start | bytes 1572872 | tf_op jit(solution)/shard_map/ppermute | solution.py:143
  73.9 5.6 %copy-start.1 = (bf16[512,4096]{1,0:T(8,128)(2,1)S(1)}, bf16[512,4096]{1,0:T(8,128)(2,1)}, u32[]{:S(2)}) copy-start(bf16[512,4096]{1,0:T(8,128)(2,1)} %copy-done) | copy-start | bytes 12582916
  73.9 5.7 %copy-start.8 = (bf16[2048,4,128]{2,1,0:T(4,128)(2,1)S(1)}, bf16[2048,4,128]{2,1,0:T(4,128)(2,1)}, u32[]{:S(2)}) copy-start(bf16[2048,4,128]{2,1,0:T(4,128)(2,1)} %param.10) | copy-start | bytes 6291460
  73.9 48.8 %collective-permute-start.8 = (bf16[256,1024]{1,0:T(8,128)(2,1)}, bf16[256,1024]{1,0:T(8,128)(2,1)}, u32[]{:S(2)}, u32[]{:S(2)}) collective-permute-start(bf16[256,1024]{1,0:T(8,128)(2,1)} %get-tuple-element.36), channel_id=1, source_target_pairs={{0,12},{4,0},{8,4},{12,8},{1,13},{5,1},{9,5},{13,9},{2,14},{6,2},{... | collective-permute-start | bytes 1572872 | tf_op jit(solution)/shard_map/ppermute | solution.py:143
  95.6 4.3 %copy-start.9 = (bf16[512,4,128]{2,0,1:T(8,128)(2,1)S(1)}, bf16[512,4,128]{2,0,1:T(8,128)(2,1)}, u32[]{:S(2)}) copy-start(bf16[512,4,128]{2,0,1:T(8,128)(2,1)} %fusion.54) | copy-start | bytes 1572868
  97.0 41.9 %copy-start.2 = (f32[512,4,2,64]{3,0,2,1:T(8,128)S(1)}, f32[512,4,2,64]{3,0,2,1:T(8,128)}, u32[]{:S(2)}) copy-start(f32[512,4,2,64]{3,0,2,1:T(8,128)} %copy.90) | copy-start | bytes 3145732
  97.0 41.9 %copy-start.5 = (f32[512,64]{1,0:T(8,128)S(1)}, f32[512,64]{1,0:T(8,128)}, u32[]{:S(2)}) copy-start(f32[512,64]{1,0:T(8,128)} %get-tuple-element.51) | copy-start | bytes 393220
  97.1 41.9 %copy-start.6 = (f32[512,64]{1,0:T(8,128)S(1)}, f32[512,64]{1,0:T(8,128)}, u32[]{:S(2)}) copy-start(f32[512,64]{1,0:T(8,128)} %get-tuple-element.52) | copy-start | bytes 393220
  98.7 23.9 %collective-permute-start.9 = (f32[512]{0:T(512)S(1)}, f32[512]{0:T(512)S(1)}, u32[]{:S(2)}, u32[]{:S(2)}) collective-permute-start(f32[512]{0:T(512)S(1)} %add_rsqrt_fusion), channel_id=1, source_target_pairs={{0,12},{4,0},{8,4},{12,8},{1,13},{5,1},{9,5},{13,9},{2,14},{6,2},{... | collective-permute-start | bytes 6152 | tf_op jit(solution)/shard_map/ppermute | solution.py:143
  122.7 38.0 %collective-permute-start.12 = (bf16[256,2,4,128]{3,0,2,1:T(8,128)(2,1)S(1)}, bf16[256,2,4,128]{3,0,2,1:T(8,128)(2,1)S(1)}, u32[]{:S(2)}, u32[]{:S(2)}) collective-permute-start(bf16[256,2,4,128]{3,0,2,1:T(8,128)(2,1)S(1)} %constant_dynamic-slice_fusion.2), channel_id=1, source_target_pairs={{0,8},{8,0},{4,12},{12,4},{1,9},{9,1},{5,13},{13,5},{2,10},{10,2},... | collective-permute-start | bytes 1572872 | tf_op jit(solution)/shard_map/ppermute | solution.py:18
  137.3 23.4 %collective-permute-start.10 = (bf16[256,2,4,128]{3,0,2,1:T(8,128)(2,1)S(1)}, bf16[256,2,4,128]{3,0,2,1:T(8,128)(2,1)S(1)}, u32[]{:S(2)}, u32[]{:S(2)}) collective-permute-start(bf16[256,2,4,128]{3,0,2,1:T(8,128)(2,1)S(1)} %constant_dynamic-slice_fusion.2), channel_id=1, source_target_pairs={{0,4},{4,0},{8,12},{12,8},{1,5},{5,1},{9,13},{13,9},{2,6},{6,2},{1... | collective-permute-start | bytes 1572872 | tf_op jit(solution)/shard_map/ppermute | solution.py:18
  139.5 42.5 %collective-permute-start.16 = (bf16[256,1024]{1,0:T(8,128)(2,1)}, bf16[256,1024]{1,0:T(8,128)(2,1)S(1)}, u32[]{:S(2)}, u32[]{:S(2)}) collective-permute-start(bf16[256,1024]{1,0:T(8,128)(2,1)} %collective-permute-done.8), channel_id=1, source_target_pairs={{0,1},{1,0},{2,3},{3,2},{4,5},{5,4},{6,7},{7,6},{8,9},{9,8},{10,11... | collective-permute-start | bytes 1572872 | tf_op jit(solution)/shard_map/ppermute | solution.py:26
  139.5 43.2 %collective-permute-start.15 = (bf16[256,1024]{1,0:T(8,128)(2,1)}, bf16[256,1024]{1,0:T(8,128)(2,1)}, u32[]{:S(2)}, u32[]{:S(2)}) collective-permute-start(bf16[256,1024]{1,0:T(8,128)(2,1)} %collective-permute-done.6), channel_id=1, source_target_pairs={{0,1},{1,0},{2,3},{3,2},{4,5},{5,4},{6,7},{7,6},{8,9},{9,8},{10,11... | collective-permute-start | bytes 1572872 | tf_op jit(solution)/shard_map/ppermute | solution.py:26
  140.0 44.5 %collective-permute-start.14 = (bf16[256,1024]{1,0:T(8,128)(2,1)}, bf16[256,1024]{1,0:T(8,128)(2,1)S(1)}, u32[]{:S(2)}, u32[]{:S(2)}) collective-permute-start(bf16[256,1024]{1,0:T(8,128)(2,1)} %collective-permute-done.4), channel_id=1, source_target_pairs={{0,1},{1,0},{2,3},{3,2},{4,5},{5,4},{6,7},{7,6},{8,9},{9,8},{10,11... | collective-permute-start | bytes 1572872 | tf_op jit(solution)/shard_map/ppermute | solution.py:26
  160.7 2.7 %collective-permute-start.13 = (bf16[256,2,4,128]{3,0,2,1:T(8,128)(2,1)S(1)}, bf16[256,2,4,128]{3,0,2,1:T(8,128)(2,1)S(1)}, u32[]{:S(2)}, u32[]{:S(2)}) collective-permute-start(bf16[256,2,4,128]{3,0,2,1:T(8,128)(2,1)S(1)} %collective-permute-done.12), channel_id=1, source_target_pairs={{0,1},{1,0},{2,3},{3,2},{4,5},{5,4},{6,7},{7,6},{8,9},{9,8},{10,11... | collective-permute-start | bytes 1572872 | tf_op jit(solution)/shard_map/ppermute | solution.py:26
  160.7 2.8 %collective-permute-start.11 = (bf16[256,2,4,128]{3,0,2,1:T(8,128)(2,1)S(1)}, bf16[256,2,4,128]{3,0,2,1:T(8,128)(2,1)S(1)}, u32[]{:S(2)}, u32[]{:S(2)}) collective-permute-start(bf16[256,2,4,128]{3,0,2,1:T(8,128)(2,1)S(1)} %collective-permute-done.10), channel_id=1, source_target_pairs={{0,1},{1,0},{2,3},{3,2},{4,5},{5,4},{6,7},{7,6},{8,9},{9,8},{10,11... | collective-permute-start | bytes 1572872 | tf_op jit(solution)/shard_map/ppermute | solution.py:26
  169.8 4.2 %dynamic-slice-start = ((f32[4096]{0:T(1024)}, s32[]{:T(128)}), f32[1024]{0:T(1024)S(1)}, s32[]{:S(2)}) async-start(f32[4096]{0:T(1024)} %param.7, s32[]{:T(128)} %select_n.363), calls=%async_computation.1 | async-start | bytes 8704 | tf_op jit(solution)/shard_map/dynamic_slice | solution.py:185
Sparse Core Ops, SparseCore 0:
  10.4 121.9 all-gather.1

commit v13 on v7

--- a/solution.py
+++ b/solution.py
@@ -104,7 +104,8 @@
             key_part, value_part = w_key, w_value
         else:
             route = [(j, (j + shift) % sub_count) for j in range(sub_count)]
-            weight_pair = lax.ppermute(jnp.stack([w_key, w_value]), "sub", route)
+            weight_stack, normed = lax.optimization_barrier((jnp.stack([w_key, w_value]), normed))
+            weight_pair = lax.ppermute(weight_stack, "sub", route)
             key_part, value_part = weight_pair[0], weight_pair[1]
         source = (sub_index - shift) % sub_count
         rows = lax.dynamic_slice_in_dim(normed, source * row_share, row_share, 1)

time: 193 us -> 214 us (1.11)
  waiting for transfers between devices: 71 us -> 77.9 us
  local copies, waits for them, and re-layouts: 28.6 us -> 35.3 us
  matrix products: 41.9 us -> 46.6 us
    ppermute x6, waiting for transfers between devices: 33.9 us -> 40.5 us  [body(): incoming, their_scale = lax.ppermute((outgoing, row_scale), 'seq', route)]
    ppermute x1, waiting for transfers between devices: 17 us -> 23.4 us  [body(): across.append(lax.ppermute(tokens, 'kvh', route))]
    ppermute x2, waiting for transfers between devices: 20 us -> 14 us  [from_partner(): return lax.ppermute(block, axis, route)]
    dot_general x6, matrix products: 9.58 us -> 12.7 us  [body(): jnp.einsum('tc,tr->cr', halves[lane_shift], their_rows, preferred_element...]
    unnamed x36 -> x34, local copies, waits for them, and re-layouts: 10.5 us -> 13.5 us
    unnamed x2, matrix products: 5.75 us -> 7.99 us
  transfers between devices with their start and end apart: 18 -> 18, of which waited for: 3 -> 3; matrix products, arithmetic and copies ran while one was open for 44% -> 42% of each run, Pallas kernels for 0% -> 0%
where the time goes in v13:
time: 214 us; the launch traced here: 213 us
  waiting for transfers between devices  77.9 us (36%)
  matrix products  46.6 us (22%)
  local copies, waits for them, and re-layouts  35.3 us (16%)
  other arithmetic  23.5 us (11%)
  starting transfers between devices  14.9 us (7%)
  between operations  14.6 us (7%)
    ppermute x6, waiting for transfers between devices, body(): incoming, their_scale = lax.ppermute((outgoing, row_scale), 'seq', route)  40.5 us
    ppermute x1, waiting for transfers between devices, body(): across.append(lax.ppermute(tokens, 'kvh', route))  23.4 us
    ppermute x2, waiting for transfers between devices, from_partner(): return lax.ppermute(block, axis, route)  14 us
    unnamed x34, local copies, waits for them, and re-layouts  13.5 us
    dot_general x6, matrix products, body(): jnp.einsum('tc,tr->cr', halves[lane_shift], their_rows, preferred_element...  12.7 us
    ppermute x6, starting transfers between devices, body(): incoming, their_scale = lax.ppermute((outgoing, row_scale), 'seq', route)  10.2 us
    dot_general x1, matrix products, body(): jnp.einsum('td,dgc->tgc', normed, w_query, preferred_element_type=jnp.flo...  8.28 us
    unnamed x2, matrix products  7.99 us
  transfers between devices with their start and end apart: 18, of which 3 were waited for; matrix products, arithmetic and copies ran while one was open for 42% of the time, Pallas kernels for 0%

profile of v13, /device:TPU:0, one launch (start us, length us, event | category | flops | bytes accessed | tf_op | source)
XLA Modules:
  0.0 212.9 jit_solution(17178183674537317149)
XLA Ops:
  7.2 3.0 %collective-permute-start.1 = (bf16[512,1024]{1,0:T(8,128)(2,1)}, bf16[512,1024]{1,0:T(8,128)(2,1)S(1)}, u32[]{:S(2)}, u32[]{:S(2)}) collective-permute-start(bf16[512,1024]{1,0:T(8,128)(2,1)} %param.6), channel_id=1, source_target_pairs={{0,2},{2,0},{1,3},{3,1},{4,6},{6,4},{5,7},{7,5},{8,10},{10,8},{9,1... | collective-permute-start | bytes 3145736 | tf_op jit(solution)/shard_map/ppermute | solution.py:70
  10.2 23.4 %collective-permute-done.1 = bf16[512,1024]{1,0:T(8,128)(2,1)S(1)} collective-permute-done((bf16[512,1024]{1,0:T(8,128)(2,1)}, bf16[512,1024]{1,0:T(8,128)(2,1)S(1)}, u32[]{:S(2)}, u32[]{:S(2)}) %collective-permute-start.1) | collective-permute-done | bytes 1048608 | tf_op jit(solution)/shard_map/ppermute | solution.py:70
  33.7 2.8 %copy_bitcast_fusion = (bf16[1,2048,4,128]{3,1,2,0:T(8,128)(2,1)S(1)}, bf16[1,2048,4,128]{3,1,2,0:T(8,128)(2,1)S(1)}) fusion(bf16[2048,4,128]{2,1,0:T(4,128)(2,1)} %param.9, bf16[2048,4,128]{2,1,0:T(4,128)(2,1)} %param.10), kind=kLoop, calls=%fused_computation.48 | loop fusion | bytes 8388608 | tf_op jit(solution)/shard_map/stack | solution.py:107
  36.5 2.3 %pad_maximum_fusion.1 = bf16[2,2048,4,128]{3,1,2,0:T(8,128)(2,1)} fusion(bf16[1,2048,4,128]{3,1,2,0:T(8,128)(2,1)S(1)} %get-tuple-element.59, bf16[1,2048,4,128]{3,1,2,0:T(8,128)(2,1)S(1)} %get-tuple-element.58), kind=kLoop, calls=%fused_computation.14 | loop fusion | flops 2097152 | bytes 8388608 | tf_op jit(solution)/shard_map/stack | solution.py:107
  40.4 2.7 %fusion.2 = bf16[512,4096]{1,0:T(8,128)(2,1)} fusion(f32[4096]{0:T(1024)S(1)} %copy-done.11, f32[512]{0:T(512)S(1)} %add_rsqrt_fusion, bf16[512,1024]{1,0:T(8,128)(2,1)S(1)} %get-tuple-element.30, bf16[512,1024]{1,0:T(8,128)(2,1)S(1)} %get-tuple-element.31, bf16[512,1024]{1,0:T(8,128)(2,1)S(1)} %get-tuple-element.32, bf16[512,1024]{1,0:T(8,128)(2,1)S(1)} %get-tuple-element.29), kind=kLoop, calls=%fused_computation.4 | loop fusion | flops 23068672 | bytes 8407040 | tf_op jit(solution)/shard_map/convert_element_type | solution.py:83
  45.8 2.7 %copy.53 = bf16[2048,4,128]{0,2,1:T(8,128)(2,1)} copy(bf16[2048,4,128]{2,1,0:T(4,128)(2,1)S(1)} %copy-done.4) | data formatting | bytes 4194304 | tf_op args[3]
  48.4 2.5 %select_reduce_fusion.1 = (f32[512]{0:T(512)S(1)}, f32[512]{0:T(512)S(1)}) fusion(f32[]{:T(128)} %bitcast.45, f32[]{:T(128)} %bitcast.44, f32[]{:T(128)} %bitcast.32, f32[]{:T(128)} %bitcast.31), kind=kLoop, calls=%fused_computation.155 | loop fusion | flops 7168 | bytes 4112 | tf_op jit(solution)/shard_map/gather | solution.py:142
  52.6 1.8 multiply_cosine_fusion
  54.5 1.8 collective-permute-start.9
  56.3 2.6 %collective-permute-start.12 = (f32[512]{0:T(512)S(1)}, f32[512]{0:T(512)S(1)}, u32[]{:S(2)}, u32[]{:S(2)}) collective-permute-start(f32[512]{0:T(512)S(1)} %add_rsqrt_fusion), channel_id=1, source_target_pairs={{0,8},{4,12},{8,0},{12,4},{1,9},{5,13},{9,1},{13,5},{2,10},{6,14},... | collective-permute-start | bytes 6152 | tf_op jit(solution)/shard_map/ppermute | solution.py:182
  58.9 3.5 %fusion.38 = f32[512,512]{0,1:S(1)} fusion(bf16[2048,512]{0,1:T(8,128)(2,1)} %bitcast.180, bf16[512,4096]{1,0:T(8,128)(2,1)} %fusion.2, s32[]{:T(128)S(6)} %select_n.340), kind=kOutput, calls=%fused_computation.60 | convolution fusion | flops 1073741824 | bytes 5242884
  62.7 8.3 %fusion.3 = f32[512,4,256]{0,2,1:T(8,128)S(1)} fusion(bf16[4096,4,256]{2,1,0:T(4,128)(2,1)} %param.8, bf16[512,4096]{1,0:T(8,128)(2,1)} %fusion.2), kind=kOutput, calls=%fused_computation.6 | convolution fusion | flops 4294967296 | bytes 14680064 | tf_op jit(solution)/shard_map/td,dgc->tgc/dot_general | solution.py:93
  71.2 2.0 copy.91
  73.2 2.0 copy.90
  75.2 3.7 %fusion.121 = (bf16[256,1024]{1,0:T(8,128)(2,1)}, bf16[256,1024]{1,0:T(8,128)(2,1)}, bf16[256,1024]{1,0:T(8,128)(2,1)}) fusion(bf16[512,4096]{1,0:T(8,128)(2,1)} %fusion.2, s32[]{:T(128)S(6)} %select_n.354, s32[]{:T(128)S(6)} %select_n.357, s32[]{:T(128)S(6)} %select_n.367, s32[]{:T(128)S(6)} %select_n.362), kind=kLoop, calls=%fused_computation.172 | loop fusion | bytes 3145744 | tf_op jit(solution)/shard_map/dynamic_slice | solution.py:180
  80.6 5.1 %fusion.63 = f32[1024,1024]{1,0:T(8,128)} fusion(bf16[512,4096]{1,0:T(8,128)(2,1)} %fusion.2, s32[]{:T(128)} %select_n.353, s32[]{:T(128)S(6)} %select_n.352), kind=kOutput, calls=%fused_computation.77 | convolution fusion | flops 1073741824 | bytes 6291972 | tf_op jit(solution)/shard_map/tc,tr->cr/dot_general | solution.py:176
  86.8 3.1 %slice_bitcast_fusion = bf16[2048,4,128]{2,0,1:T(8,128)(2,1)} fusion(bf16[2,2048,4,128]{3,1,2,0:T(8,128)(2,1)} %collective-permute-done.3), kind=kLoop, calls=%fused_computation.33 | loop fusion | bytes 4194304 | tf_op jit(solution)/shard_map/squeeze | solution.py:109
  89.9 4.0 %copy.54 = bf16[2048,4,128]{0,2,1:T(8,128)(2,1)} copy(bf16[2048,4,128]{2,0,1:T(8,128)(2,1)} %slice_bitcast_fusion) | data formatting | bytes 4194304 | tf_op jit(solution)/shard_map/squeeze | solution.py:109
  93.9 4.5 %fusion.35 = f32[512,512]{0,1} fusion(bf16[2048,512]{0,1:T(8,128)(2,1)} %bitcast.184, bf16[512,4096]{1,0:T(8,128)(2,1)} %fusion.2, s32[]{:T(128)S(6)} %select_n.341), kind=kOutput, calls=%fused_computation.57 | convolution fusion | flops 1073741824 | bytes 5242884
  98.4 2.5 %copy.56 = f32[512,4,128]{2,0,1:T(8,128)} copy(f32[512,4,128]{0,2,1:T(8,128)} %bitcast.191) | data formatting | bytes 2097152 | tf_op jit(solution)/shard_map/td,dgh->tgh/dot_general | solution.py:112
  103.7 2.5 %fusion.7 = (f32[4,2,512]{2,1,0:T(2,128)S(1)}, f32[4,512,512,2]{2,1,3,0:T(8,128)S(1)}) fusion(pred[512,512]{0,1:T(8,128)(4,1)S(1)} %fusion.66, bf16[512,4,2,64]{3,0,2,1:T(8,128)(2,1)S(1)} %get-tuple-element.18, bf16[512,4,2,64]{3,0,2,1:T(8,128)(2,1)S(1)} %get-tuple-element.17, bf16[512,4,64]{2,0,1:T(8,128)(2,1)S(1)} %get-tuple-element.35, ...), kind=kOutput, calls=%fused_computation.11 | convolution fusion | flops 546304000 | bytes 10240000 | tf_op jit(solution)/shard_map/tgrh,ugh->grtu/dot_general | solution.py:121
  108.0 2.5 %copy-done = f32[4,512,512,2]{2,1,3,0:T(8,128)} copy-done((f32[4,512,512,2]{2,1,3,0:T(8,128)}, f32[4,512,512,2]{2,1,3,0:T(8,128)S(1)}, u32[]{:S(2)}) %copy-start) | copy-done | bytes 8388632
  111.5 3.0 %fusion.21 = f32[512,4,128]{2,0,1:T(8,128)S(1)} fusion(bf16[2,2048,4,128]{3,1,2,0:T(8,128)(2,1)} %collective-permute-done.3, bf16[512,4096]{1,0:T(8,128)(2,1)S(1)} %copy-done.1, s32[]{:T(128)S(6)} %select_n.341), kind=kOutput, calls=%fused_computation.35 | convolution fusion | flops 1073741824 | bytes 5242884 | tf_op jit(solution)/shard_map/td,dgh->tgh/dot_general | solution.py:113
  115.8 3.6 %collective-permute-start.15 = (f32[512]{0:T(512)S(1)}, f32[512]{0:T(512)S(1)}, u32[]{:S(2)}, u32[]{:S(2)}) collective-permute-start(f32[512]{0:T(512)S(1)} %add_rsqrt_fusion), channel_id=1, source_target_pairs={{0,12},{4,0},{8,4},{12,8},{1,13},{5,1},{9,5},{13,9},{2,14},{6,2},{... | collective-permute-start | bytes 6152 | tf_op jit(solution)/shard_map/ppermute | solution.py:182
  120.4 40.5 %collective-permute-done.11 = bf16[256,1024]{1,0:T(8,128)(2,1)} collective-permute-done((bf16[256,1024]{1,0:T(8,128)(2,1)}, bf16[256,1024]{1,0:T(8,128)(2,1)}, u32[]{:S(2)}, u32[]{:S(2)}) %collective-permute-start.11) | collective-permute-done | bytes 524320 | tf_op jit(solution)/shard_map/ppermute | solution.py:182
  161.6 2.6 %multiply_convert_fusion.2 = (bf16[512,1024]{1,0:T(8,128)(2,1)S(1)}, bf16[512,1024]{1,0:T(8,128)(2,1)S(1)}, bf16[512,1024]{1,0:T(8,128)(2,1)S(1)}) fusion(f32[1024]{0:T(1024)S(1)} %dynamic-slice-done, f32[512]{0:T(512)S(1)} %collective-permute-done.9, bf16[2048,1024]{1,0:T(8,128)(2,1)} %all-gather.2.cloned.1.call-done, s32[]{:T(128)S(6)} %select_n.359, ...), kind=kLoop, calls=%fused_computation.51 | loop fusion | flops 6291456 | bytes 6301708 | tf_op jit(solution)/shard_map/convert_element_type | solution.py:188
  164.2 1.8 fusion.81
  166.0 1.8 fusion.85
  167.8 1.8 fusion.89
  171.1 14.0 %collective-permute-done.6 = bf16[256,2,4,128]{3,0,2,1:T(8,128)(2,1)} collective-permute-done((bf16[256,2,4,128]{3,0,2,1:T(8,128)(2,1)}, bf16[256,2,4,128]{3,0,2,1:T(8,128)(2,1)}, u32[]{:S(2)}, u32[]{:S(2)}) %collective-permute-start.6) | collective-permute-done | bytes 524320 | tf_op jit(solution)/shard_map/ppermute | solution.py:18
  185.1 5.8 %add_multiply_fusion = f32[1024,1024]{1,0:T(8,128)} fusion(f32[1024,1024]{1,0:T(8,128)S(1)} %fusion.81, f32[1024,1024]{1,0:T(8,128)S(1)} %fusion.83, f32[1024,1024]{1,0:T(8,128)S(1)} %fusion.85, f32[1024,1024]{1,0:T(8,128)S(1)} %fusion.87, f32[1024,1024]{1,0:T(8,128)} %fusion.63, f32[1024,1024]{1,0:T(8,128)S(1)} %fusion.89, ...), kind=kOutput, calls=%fused_computation.22 | convolution fusion | flops 544210944 | bytes 30408708 | tf_op jit(solution)/shard_map/tc,tr->cr/dot_general | solution.py:192
  202.1 2.5 %fusion.33 = bf16[512,4,2,128]{0,3,2,1:T(8,128)(2,1)S(1)} fusion(f32[512,4,2,128]{0,3,2,1:T(8,128)S(1)} %bitcast.181, f32[512,4,2,128]{0,3,2,1:T(8,128)S(1)} %bitcast.182, f32[4,512,512,2]{2,1,3,0:T(8,128)S(1)} %bitcast.173, f32[4,2,512]{2,1,0:T(2,128)S(1)} %get-tuple-element.54, pred[512,512]{0,1:T(8,128)(4,1)S(1)} %fusion.66, ...), kind=kOutput, calls=%fused_computation.54 | convolution fusion | flops 548405248 | bytes 14483456 | tf_op jit(solution)/shard_map/grtu,ugh->tgrh/dot_general | solution.py:131
  (108 shorter events, 31.7 us)
Async XLA Ops:
  7.2 154.4 %all-gather.2.cloned.1.call-start = ((), (), s32[]{:S(2)}) async-start(), calls=%async_computation | async-start | bytes 5242880 | tf_op jit(solution)/shard_map/all_gather | solution.py:173
  7.2 26.4 %collective-permute-start.1 = (bf16[512,1024]{1,0:T(8,128)(2,1)}, bf16[512,1024]{1,0:T(8,128)(2,1)S(1)}, u32[]{:S(2)}, u32[]{:S(2)}) collective-permute-start(bf16[512,1024]{1,0:T(8,128)(2,1)} %param.6), channel_id=1, source_target_pairs={{0,2},{2,0},{1,3},{3,1},{4,6},{6,4},{5,7},{7,5},{8,10},{10,8},{9,1... | collective-permute-start | bytes 3145736 | tf_op jit(solution)/shard_map/ppermute | solution.py:70
  10.2 28.6 %collective-permute-start = (bf16[512,1024]{1,0:T(8,128)(2,1)}, bf16[512,1024]{1,0:T(8,128)(2,1)S(1)}, u32[]{:S(2)}, u32[]{:S(2)}) collective-permute-start(bf16[512,1024]{1,0:T(8,128)(2,1)} %param.6), channel_id=1, source_target_pairs={{0,1},{1,0},{2,3},{3,2},{4,5},{5,4},{6,7},{7,6},{8,9},{9,8},{10,11... | collective-permute-start | bytes 3145736 | tf_op jit(solution)/shard_map/ppermute | solution.py:26
  33.6 5.2 %collective-permute-start.2 = (bf16[512,1024]{1,0:T(8,128)(2,1)S(1)}, bf16[512,1024]{1,0:T(8,128)(2,1)S(1)}, u32[]{:S(2)}, u32[]{:S(2)}) collective-permute-start(bf16[512,1024]{1,0:T(8,128)(2,1)S(1)} %collective-permute-done.1), channel_id=1, source_target_pairs={{0,1},{1,0},{2,3},{3,2},{4,5},{5,4},{6,7},{7,6},{8,9},{9,8},{10,11... | collective-permute-start | bytes 3145736 | tf_op jit(solution)/shard_map/ppermute | solution.py:26
  36.5 2.4 %copy-start.5 = (bf16[512,1024]{1,0:T(8,128)(2,1)S(1)}, bf16[512,1024]{1,0:T(8,128)(2,1)}, u32[]{:S(2)}) copy-start(bf16[512,1024]{1,0:T(8,128)(2,1)} %param.6) | copy-start | bytes 3145732
  40.4 3.3 %copy-start.12 = (s32[3,8]{1,0:T(4,128)S(1)}, s32[3,8]{1,0:T(4,128)}, u32[]{:S(2)}) copy-start(s32[3,8]{1,0:T(4,128)} %param.11) | copy-start | bytes 292
  40.4 5.4 %copy-start.4 = (bf16[2048,4,128]{2,1,0:T(4,128)(2,1)S(1)}, bf16[2048,4,128]{2,1,0:T(4,128)(2,1)}, u32[]{:S(2)}) copy-start(bf16[2048,4,128]{2,1,0:T(4,128)(2,1)} %param.9) | copy-start | bytes 6291460
  43.2 43.1 %collective-permute-start.3 = (bf16[2,2048,4,128]{3,1,2,0:T(8,128)(2,1)}, bf16[2,2048,4,128]{3,1,2,0:T(8,128)(2,1)}, u32[]{:S(2)}, u32[]{:S(2)}) collective-permute-start(bf16[2,2048,4,128]{3,1,2,0:T(8,128)(2,1)} %pad_maximum_fusion.1), channel_id=1, source_target_pairs={{0,1},{1,0},{2,3},{3,2},{4,5},{5,4},{6,7},{7,6},{8,9},{9,8},{10,11... | collective-permute-start | bytes 12582920 | tf_op jit(solution)/shard_map/ppermute | solution.py:108
  54.5 61.3 %collective-permute-start.9 = (f32[512]{0:T(512)S(1)}, f32[512]{0:T(512)S(1)}, u32[]{:S(2)}, u32[]{:S(2)}) collective-permute-start(f32[512]{0:T(512)S(1)} %add_rsqrt_fusion), channel_id=1, source_target_pairs={{0,4},{4,8},{8,12},{12,0},{1,5},{5,9},{9,13},{13,1},{2,6},{6,10},{... | collective-permute-start | bytes 6152 | tf_op jit(solution)/shard_map/ppermute | solution.py:182
  56.3 105.1 %collective-permute-start.12 = (f32[512]{0:T(512)S(1)}, f32[512]{0:T(512)S(1)}, u32[]{:S(2)}, u32[]{:S(2)}) collective-permute-start(f32[512]{0:T(512)S(1)} %add_rsqrt_fusion), channel_id=1, source_target_pairs={{0,8},{4,12},{8,0},{12,4},{1,9},{5,13},{9,1},{13,5},{2,10},{6,14},... | collective-permute-start | bytes 6152 | tf_op jit(solution)/shard_map/ppermute | solution.py:182
  75.2 10.4 %copy-start.2 = (f32[512,4,2,64]{3,0,2,1:T(8,128)S(1)}, f32[512,4,2,64]{3,0,2,1:T(8,128)}, u32[]{:S(2)}) copy-start(f32[512,4,2,64]{3,0,2,1:T(8,128)} %copy.91) | copy-start | bytes 3145732
  75.2 10.4 %copy-start.3 = (f32[512,4,2,64]{3,0,2,1:T(8,128)S(1)}, f32[512,4,2,64]{3,0,2,1:T(8,128)}, u32[]{:S(2)}) copy-start(f32[512,4,2,64]{3,0,2,1:T(8,128)} %copy.90) | copy-start | bytes 3145732
  75.2 10.4 %copy-start.6 = (f32[512,64]{1,0:T(8,128)S(1)}, f32[512,64]{1,0:T(8,128)}, u32[]{:S(2)}) copy-start(f32[512,64]{1,0:T(8,128)} %get-tuple-element.41) | copy-start | bytes 393220
  75.2 10.4 %copy-start.7 = (f32[512,64]{1,0:T(8,128)S(1)}, f32[512,64]{1,0:T(8,128)}, u32[]{:S(2)}) copy-start(f32[512,64]{1,0:T(8,128)} %get-tuple-element.42) | copy-start | bytes 393220
  78.9 82.4 %collective-permute-start.14 = (bf16[256,1024]{1,0:T(8,128)(2,1)}, bf16[256,1024]{1,0:T(8,128)(2,1)}, u32[]{:S(2)}, u32[]{:S(2)}) collective-permute-start(bf16[256,1024]{1,0:T(8,128)(2,1)} %get-tuple-element.27), channel_id=1, source_target_pairs={{0,12},{4,0},{8,4},{12,8},{1,13},{5,1},{9,5},{13,9},{2,14},{6,2},{... | collective-permute-start | bytes 1572872 | tf_op jit(solution)/shard_map/ppermute | solution.py:182
  80.4 80.5 %collective-permute-start.11 = (bf16[256,1024]{1,0:T(8,128)(2,1)}, bf16[256,1024]{1,0:T(8,128)(2,1)}, u32[]{:S(2)}, u32[]{:S(2)}) collective-permute-start(bf16[256,1024]{1,0:T(8,128)(2,1)} %get-tuple-element.28), channel_id=1, source_target_pairs={{0,8},{4,12},{8,0},{12,4},{1,9},{5,13},{9,1},{13,5},{2,10},{6,14},... | collective-permute-start | bytes 1572872 | tf_op jit(solution)/shard_map/ppermute | solution.py:182
  86.3 74.5 %collective-permute-start.8 = (bf16[256,1024]{1,0:T(8,128)(2,1)}, bf16[256,1024]{1,0:T(8,128)(2,1)}, u32[]{:S(2)}, u32[]{:S(2)}) collective-permute-start(bf16[256,1024]{1,0:T(8,128)(2,1)} %get-tuple-element.26), channel_id=1, source_target_pairs={{0,4},{4,8},{8,12},{12,0},{1,5},{5,9},{9,13},{13,1},{2,6},{6,10},{... | collective-permute-start | bytes 1572872 | tf_op jit(solution)/shard_map/ppermute | solution.py:182
  106.2 4.3 %copy-start = (f32[4,512,512,2]{2,1,3,0:T(8,128)}, f32[4,512,512,2]{2,1,3,0:T(8,128)S(1)}, u32[]{:S(2)}) copy-start(f32[4,512,512,2]{2,1,3,0:T(8,128)S(1)} %get-tuple-element.55) | copy-start | bytes 25165828
  106.3 5.2 %copy-start.1 = (bf16[512,4096]{1,0:T(8,128)(2,1)S(1)}, bf16[512,4096]{1,0:T(8,128)(2,1)}, u32[]{:S(2)}) copy-start(bf16[512,4096]{1,0:T(8,128)(2,1)} %fusion.2) | copy-start | bytes 12582916
  111.5 3.0 %copy-start.8 = (bf16[2048,4,128]{2,1,0:T(4,128)(2,1)S(1)}, bf16[2048,4,128]{2,1,0:T(4,128)(2,1)}, u32[]{:S(2)}) copy-start(bf16[2048,4,128]{2,1,0:T(4,128)(2,1)} %param.10) | copy-start | bytes 6291460
  114.5 47.1 %dynamic-slice-start = ((f32[4096]{0:T(1024)}, s32[]{:T(128)}), f32[1024]{0:T(1024)S(1)}, s32[]{:S(2)}) async-start(f32[4096]{0:T(1024)} %param.7, s32[]{:T(128)} %select_n.353), calls=%async_computation.3 | async-start | bytes 8704 | tf_op jit(solution)/shard_map/dynamic_slice | solution.py:174
  115.8 45.1 %copy-start.9 = (bf16[512,4,128]{2,0,1:T(8,128)(2,1)}, bf16[512,4,128]{2,0,1:T(8,128)(2,1)S(1)}, u32[]{:S(2)}) copy-start(bf16[512,4,128]{2,0,1:T(8,128)(2,1)S(1)} %fusion.54) | copy-start | bytes 1572868
  115.8 45.6 %collective-permute-start.15 = (f32[512]{0:T(512)S(1)}, f32[512]{0:T(512)S(1)}, u32[]{:S(2)}, u32[]{:S(2)}) collective-permute-start(f32[512]{0:T(512)S(1)} %add_rsqrt_fusion), channel_id=1, source_target_pairs={{0,12},{4,0},{8,4},{12,8},{1,13},{5,1},{9,5},{13,9},{2,14},{6,2},{... | collective-permute-start | bytes 6152 | tf_op jit(solution)/shard_map/ppermute | solution.py:182
  160.8 8.8 %collective-permute-start.13 = (bf16[256,1024]{1,0:T(8,128)(2,1)}, bf16[256,1024]{1,0:T(8,128)(2,1)S(1)}, u32[]{:S(2)}, u32[]{:S(2)}) collective-permute-start(bf16[256,1024]{1,0:T(8,128)(2,1)} %collective-permute-done.11), channel_id=1, source_target_pairs={{0,1},{1,0},{2,3},{3,2},{4,5},{5,4},{6,7},{7,6},{8,9},{9,8},{10,11... | collective-permute-start | bytes 1572872 | tf_op jit(solution)/shard_map/ppermute | solution.py:26
  160.8 9.5 %collective-permute-start.10 = (bf16[256,1024]{1,0:T(8,128)(2,1)}, bf16[256,1024]{1,0:T(8,128)(2,1)S(1)}, u32[]{:S(2)}, u32[]{:S(2)}) collective-permute-start(bf16[256,1024]{1,0:T(8,128)(2,1)} %collective-permute-done.8), channel_id=1, source_target_pairs={{0,1},{1,0},{2,3},{3,2},{4,5},{5,4},{6,7},{7,6},{8,9},{9,8},{10,11... | collective-permute-start | bytes 1572872 | tf_op jit(solution)/shard_map/ppermute | solution.py:26
  161.3 23.7 %collective-permute-start.16 = (bf16[256,1024]{1,0:T(8,128)(2,1)}, bf16[256,1024]{1,0:T(8,128)(2,1)}, u32[]{:S(2)}, u32[]{:S(2)}) collective-permute-start(bf16[256,1024]{1,0:T(8,128)(2,1)} %collective-permute-done.14), channel_id=1, source_target_pairs={{0,1},{1,0},{2,3},{3,2},{4,5},{5,4},{6,7},{7,6},{8,9},{9,8},{10,11... | collective-permute-start | bytes 1572872 | tf_op jit(solution)/shard_map/ppermute | solution.py:26
  161.4 23.6 %collective-permute-start.6 = (bf16[256,2,4,128]{3,0,2,1:T(8,128)(2,1)}, bf16[256,2,4,128]{3,0,2,1:T(8,128)(2,1)}, u32[]{:S(2)}, u32[]{:S(2)}) collective-permute-start(bf16[256,2,4,128]{3,0,2,1:T(8,128)(2,1)} %fusion.74), channel_id=1, source_target_pairs={{0,8},{8,0},{4,12},{12,4},{1,9},{9,1},{5,13},{13,5},{2,10},{10,2},... | collective-permute-start | bytes 1572872 | tf_op jit(solution)/shard_map/ppermute | solution.py:18
  161.4 29.4 %collective-permute-start.4 = (bf16[256,2,4,128]{3,0,2,1:T(8,128)(2,1)}, bf16[256,2,4,128]{3,0,2,1:T(8,128)(2,1)}, u32[]{:S(2)}, u32[]{:S(2)}) collective-permute-start(bf16[256,2,4,128]{3,0,2,1:T(8,128)(2,1)} %fusion.74), channel_id=1, source_target_pairs={{0,4},{4,0},{8,12},{12,8},{1,5},{5,1},{9,13},{13,9},{2,6},{6,2},{1... | collective-permute-start | bytes 1572872 | tf_op jit(solution)/shard_map/ppermute | solution.py:18
  185.1 8.9 %collective-permute-start.7 = (bf16[256,2,4,128]{3,0,2,1:T(8,128)(2,1)}, bf16[256,2,4,128]{3,0,2,1:T(8,128)(2,1)S(1)}, u32[]{:S(2)}, u32[]{:S(2)}) collective-permute-start(bf16[256,2,4,128]{3,0,2,1:T(8,128)(2,1)} %collective-permute-done.6), channel_id=1, source_target_pairs={{0,1},{1,0},{2,3},{3,2},{4,5},{5,4},{6,7},{7,6},{8,9},{9,8},{10,11... | collective-permute-start | bytes 1572872 | tf_op jit(solution)/shard_map/ppermute | solution.py:26
  190.9 3.2 %collective-permute-start.5 = (bf16[256,2,4,128]{3,0,2,1:T(8,128)(2,1)}, bf16[256,2,4,128]{3,0,2,1:T(8,128)(2,1)S(1)}, u32[]{:S(2)}, u32[]{:S(2)}) collective-permute-start(bf16[256,2,4,128]{3,0,2,1:T(8,128)(2,1)} %collective-permute-done.4), channel_id=1, source_target_pairs={{0,1},{1,0},{2,3},{3,2},{4,5},{5,4},{6,7},{7,6},{8,9},{9,8},{10,11... | collective-permute-start | bytes 1572872 | tf_op jit(solution)/shard_map/ppermute | solution.py:26
  199.4 2.7 %slice-start.1 = ((s8[8388608]{0:T(1024)(128)(4,1)}), s8[4194304]{0:T(1024)(128)(4,1)S(1)}, s32[]{:S(2)}) async-start(s8[8388608]{0:T(1024)(128)(4,1)} %bitcast.172), calls=%async_computation.2 | async-start | bytes 8388608
  199.4 2.8 %copy-start.10 = (bf16[512,4,128]{2,0,1:T(8,128)(2,1)S(1)}, bf16[512,4,128]{2,0,1:T(8,128)(2,1)}, u32[]{:S(2)}) copy-start(bf16[512,4,128]{2,0,1:T(8,128)(2,1)} %copy-done.9) | copy-start | bytes 1572868
  (2 other events, 3.2 us)
Sparse Core Ops, SparseCore 0:
  33.8 122.4 all-gather.1

commit v14 on v7

--- a/solution.py
+++ b/solution.py
@@ -185,12 +185,15 @@
         their_owned = (
             their_raw.astype(jnp.float32) * their_scale[:, None] * column_gain
         ).astype(jnp.bfloat16)
-        for lane_shift in range(sub_count):
-            half_at = (sub_index - lane_shift) % sub_count
-            their_rows = lax.dynamic_slice_in_dim(their_owned, half_at * share, share, 0)
-            gram_sum = gram_sum + jnp.einsum(
-                "tc,tr->cr", halves[lane_shift], their_rows, preferred_element_type=jnp.float32
-            )
+        in_order = [
+            lax.select_n((sub_index - lane) % sub_count, *halves) for lane in range(sub_count)
+        ]
+        gram_sum = gram_sum + jnp.einsum(
+            "tc,tr->cr",
+            jnp.concatenate(in_order, axis=0),
+            their_owned,
+            preferred_element_type=jnp.float32,
+        )
     gram_sum = gram_sum * inverse_count
     gram_tile = gram_sum
     return (attended, gram_tile)

time: 193 us -> 227 us (1.18)
  waiting for transfers between devices: 71 us -> 87.9 us
  starting transfers between devices: 14.5 us -> 30.4 us
  other arithmetic: 21.9 us -> 27.6 us
  matrix products: 41.9 us -> 37.8 us
    ppermute x6, waiting for transfers between devices: 33.9 us -> 50.2 us  [body(): incoming, their_scale = lax.ppermute((outgoing, row_scale), 'seq', route)]
    ppermute x6, starting transfers between devices: 8.77 us -> 22 us  [body(): incoming, their_scale = lax.ppermute((outgoing, row_scale), 'seq', route)]
    select_n x0 -> x3, other arithmetic: none -> 5.75 us  [body(): lax.select_n((sub_index - lane) % sub_count, *halves)]
    dot_general x1, matrix products: 8.29 us -> 4.55 us  [body(): jnp.einsum('td,dgc->tgc', normed, w_query, preferred_element_type=jnp.flo...]
    ppermute x2, starting transfers between devices: 1.09 us -> 3.91 us  [from_partner(): return lax.ppermute(block, axis, route)]
    convert_element_type x1 -> x0, other arithmetic: 2.64 us -> none  [body(): their_owned = (their_raw.astype(jnp.float32) * their_scale[:, None] * col...]
    unnamed x36 -> x46, local copies, waits for them, and re-layouts: 10.5 us -> 8.9 us
    dot_general x6 -> x3, matrix products: 9.58 us -> 8.12 us  [body(): jnp.einsum('tc,tr->cr', jnp.concatenate(in_order, axis=0), their_owned, p...]
  transfers between devices with their start and end apart: 18 -> 18, of which waited for: 3 -> 4; matrix products, arithmetic and copies ran while one was open for 44% -> 39% of each run, Pallas kernels for 0% -> 0%
where the time goes in v14:
time: 227 us
  waiting for transfers between devices  87.9 us (39%)
  matrix products  37.8 us (17%)
  starting transfers between devices  30.4 us (13%)
  local copies, waits for them, and re-layouts  28.5 us (13%)
  other arithmetic  27.6 us (12%)
  between operations  14.6 us (6%)
    ppermute x6, waiting for transfers between devices, body(): incoming, their_scale = lax.ppermute((outgoing, row_scale), 'seq', route)  50.2 us
    ppermute x6, starting transfers between devices, body(): incoming, their_scale = lax.ppermute((outgoing, row_scale), 'seq', route)  22 us
    ppermute x2, waiting for transfers between devices, from_partner(): return lax.ppermute(block, axis, route)  20.6 us
    ppermute x1, waiting for transfers between devices, body(): across.append(lax.ppermute(tokens, 'kvh', route))  17 us
    unnamed x46, local copies, waits for them, and re-layouts  8.9 us
    dot_general x3, matrix products, body(): jnp.einsum('tc,tr->cr', jnp.concatenate(in_order, axis=0), their_owned, p...  8.12 us
    squeeze x2, local copies, waits for them, and re-layouts, body(): key_part, value_part = (weight_pair[0], weight_pair[1])  7.07 us
    unnamed x2, matrix products  6.73 us
  transfers between devices with their start and end apart: 18, of which 4 were waited for; matrix products, arithmetic and copies ran while one was open for 39% of the time, Pallas kernels for 0%

profile of v14, /device:TPU:0, one launch (start us, length us, event | category | flops | bytes accessed | tf_op | source)
XLA Modules:
  0.0 226.7 jit_solution(7333743461107684713)
XLA Ops:
  7.2 3.0 %collective-permute-start.1 = (bf16[512,1024]{1,0:T(8,128)(2,1)}, bf16[512,1024]{1,0:T(8,128)(2,1)}, u32[]{:S(2)}, u32[]{:S(2)}) collective-permute-start(bf16[512,1024]{1,0:T(8,128)(2,1)} %param.6), channel_id=1, source_target_pairs={{0,2},{2,0},{1,3},{3,1},{4,6},{6,4},{5,7},{7,5},{8,10},{10,8},{9,1... | collective-permute-start | bytes 3145736 | tf_op jit(solution)/shard_map/ppermute | solution.py:70
  10.3 2.8 %copy_bitcast_fusion = (bf16[1,2048,4,128]{3,1,2,0:T(8,128)(2,1)S(1)}, bf16[1,2048,4,128]{3,1,2,0:T(8,128)(2,1)S(1)}) fusion(bf16[2048,4,128]{2,1,0:T(4,128)(2,1)} %param.9, bf16[2048,4,128]{2,1,0:T(4,128)(2,1)} %param.10), kind=kLoop, calls=%fused_computation.48 | loop fusion | bytes 8388608 | tf_op jit(solution)/shard_map/stack | solution.py:107
  13.1 2.4 %pad_maximum_fusion.1 = bf16[2,2048,4,128]{3,1,2,0:T(8,128)(2,1)} fusion(bf16[1,2048,4,128]{3,1,2,0:T(8,128)(2,1)S(1)} %get-tuple-element.60, bf16[1,2048,4,128]{3,1,2,0:T(8,128)(2,1)S(1)} %get-tuple-element.59), kind=kLoop, calls=%fused_computation.14 | loop fusion | flops 2097152 | bytes 8388608 | tf_op jit(solution)/shard_map/stack | solution.py:107
  16.7 17.0 %collective-permute-done.1 = bf16[512,1024]{1,0:T(8,128)(2,1)} collective-permute-done((bf16[512,1024]{1,0:T(8,128)(2,1)}, bf16[512,1024]{1,0:T(8,128)(2,1)}, u32[]{:S(2)}, u32[]{:S(2)}) %collective-permute-start.1) | collective-permute-done | bytes 1048608 | tf_op jit(solution)/shard_map/ppermute | solution.py:70
  34.4 2.6 %copy.53 = bf16[2048,4,128]{0,2,1:T(8,128)(2,1)} copy(bf16[2048,4,128]{2,1,0:T(4,128)(2,1)S(1)} %copy-done.4) | data formatting | bytes 4194304 | tf_op args[3]
  37.0 2.6 %select_reduce_fusion.1 = (f32[512]{0:T(512)S(1)}, f32[512]{0:T(512)S(1)}) fusion(f32[]{:T(128)} %bitcast.45, f32[]{:T(128)} %bitcast.44, f32[]{:T(128)} %bitcast.32, f32[]{:T(128)} %bitcast.31), kind=kLoop, calls=%fused_computation.168 | loop fusion | flops 7168 | bytes 4112 | tf_op jit(solution)/shard_map/gather | solution.py:141
  42.1 1.8 multiply_cosine_fusion
  43.9 2.1 select_select_fusion.3
  47.1 2.9 %collective-permute-start.13 = (f32[512]{0:T(512)S(1)}, f32[512]{0:T(512)S(1)}, u32[]{:S(2)}, u32[]{:S(2)}) collective-permute-start(f32[512]{0:T(512)S(1)} %add_rsqrt_fusion), channel_id=1, source_target_pairs={{0,8},{4,12},{8,0},{12,4},{1,9},{5,13},{9,1},{13,5},{2,10},{6,14},... | collective-permute-start | bytes 6152 | tf_op jit(solution)/shard_map/ppermute | solution.py:181
  51.4 2.3 %fusion.131 = (bf16[256,1024]{1,0:T(8,128)(2,1)}, bf16[256,1024]{1,0:T(8,128)(2,1)}, bf16[256,1024]{1,0:T(8,128)(2,1)S(1)}) fusion(bf16[512,4096]{1,0:T(8,128)(2,1)S(1)} %fusion.2, s32[]{:T(128)S(6)} %select_n.388, s32[]{:T(128)S(6)} %select_n.407, s32[]{:T(128)S(6)} %select_n.400, s32[]{:T(128)S(6)} %select_n.391), kind=kLoop, calls=%fused_computation.188 | loop fusion | bytes 3145744 | tf_op jit(solution)/shard_map/dynamic_slice | solution.py:179
  55.6 4.5 %fusion.3 = f32[512,4,256]{0,2,1:T(8,128)S(1)} fusion(bf16[4096,4,256]{2,1,0:T(4,128)(2,1)S(1)} %bitcast.191, bf16[512,4096]{1,0:T(8,128)(2,1)S(1)} %fusion.2), kind=kOutput, calls=%fused_computation.6 | convolution fusion | flops 4294967296 | bytes 14680064 | tf_op jit(solution)/shard_map/td,dgc->tgc/dot_general | solution.py:93
  60.4 1.9 copy.91
  62.3 2.0 copy.90
  64.3 2.0 collective-permute-start.14
  66.3 2.8 %subtract_convert_fusion = (bf16[512,4,2,64]{3,0,2,1:T(8,128)(2,1)S(1)}, bf16[512,4,2,64]{3,0,2,1:T(8,128)(2,1)S(1)}) fusion(f32[512,4,2,64]{3,0,2,1:T(8,128)} %copy.91, f32[512,4,2,64]{3,0,2,1:T(8,128)} %copy.90, f32[512,64]{1,0:T(8,128)S(1)} %copy-done.8, f32[512,64]{1,0:T(8,128)S(1)} %copy-done.6), kind=kLoop, calls=%fused_computation.53 | loop fusion | flops 2097152 | bytes 3407872 | tf_op jit(solution)/shard_map/convert.8
  69.1 50.2 %collective-permute-done.11 = bf16[256,1024]{1,0:T(8,128)(2,1)} collective-permute-done((bf16[256,1024]{1,0:T(8,128)(2,1)}, bf16[256,1024]{1,0:T(8,128)(2,1)}, u32[]{:S(2)}, u32[]{:S(2)}) %collective-permute-start.11) | collective-permute-done | bytes 524320 | tf_op jit(solution)/shard_map/ppermute | solution.py:181
  119.8 2.3 fusion.38
  123.6 5.1 %fusion.84 = f32[1024,1024]{1,0:T(8,128)} fusion(bf16[512,4096]{1,0:T(8,128)(2,1)} %copy-done.1, s32[]{:T(128)S(6)} %select_n.385, s32[]{:T(128)S(6)} %select_n.384), kind=kOutput, calls=%fused_computation.98 | convolution fusion | flops 1073741824 | bytes 6291464 | tf_op jit(solution)/shard_map/tc,tr->cr/dot_general | solution.py:175
  128.7 15.2 %collective-permute-start.10 = (f32[512]{0:T(512)S(1)}, f32[512]{0:T(512)S(1)}, u32[]{:S(2)}, u32[]{:S(2)}) collective-permute-start(f32[512]{0:T(512)S(1)} %add_rsqrt_fusion), channel_id=1, source_target_pairs={{0,4},{4,8},{8,12},{12,0},{1,5},{5,9},{9,13},{13,1},{2,6},{6,10},{... | collective-permute-start | bytes 6152 | tf_op jit(solution)/shard_map/ppermute | solution.py:181
  143.9 2.2 broadcast_select_fusion.4
  146.5 2.2 broadcast_select_fusion.5
  148.8 3.1 %slice_bitcast_fusion = bf16[2048,4,128]{2,0,1:T(8,128)(2,1)} fusion(bf16[2,2048,4,128]{3,1,2,0:T(8,128)(2,1)} %collective-permute-done.3), kind=kLoop, calls=%fused_computation.33 | loop fusion | bytes 4194304 | tf_op jit(solution)/shard_map/squeeze | solution.py:108
  151.9 4.0 %copy.54 = bf16[2048,4,128]{0,2,1:T(8,128)(2,1)} copy(bf16[2048,4,128]{2,0,1:T(8,128)(2,1)} %slice_bitcast_fusion) | data formatting | bytes 4194304 | tf_op jit(solution)/shard_map/squeeze | solution.py:108
  155.9 4.5 %fusion.35 = f32[512,512]{0,1} fusion(bf16[2048,512]{0,1:T(8,128)(2,1)} %bitcast.176, bf16[512,4096]{1,0:T(8,128)(2,1)} %copy-done.1, s32[]{:T(128)S(6)} %select_n.373), kind=kOutput, calls=%fused_computation.57 | convolution fusion | flops 1073741824 | bytes 5242884
  160.3 2.6 %copy.56 = f32[512,4,128]{2,0,1:T(8,128)} copy(f32[512,4,128]{0,2,1:T(8,128)} %bitcast.183) | data formatting | bytes 2097152 | tf_op jit(solution)/shard_map/td,dgh->tgh/dot_general | solution.py:111
  164.3 3.6 %fusion.21 = f32[512,4,128]{2,0,1:T(8,128)S(1)} fusion(bf16[2,2048,4,128]{3,1,2,0:T(8,128)(2,1)} %collective-permute-done.3, bf16[512,4096]{1,0:T(8,128)(2,1)} %copy-done.1, s32[]{:T(128)S(6)} %select_n.373), kind=kOutput, calls=%fused_computation.35 | convolution fusion | flops 1073741824 | bytes 5242884 | tf_op jit(solution)/shard_map/td,dgh->tgh/dot_general | solution.py:112
  170.0 3.7 %collective-permute-start.6 = (bf16[256,2,4,128]{3,0,2,1:T(8,128)(2,1)S(1)}, bf16[256,2,4,128]{3,0,2,1:T(8,128)(2,1)S(1)}, u32[]{:S(2)}, u32[]{:S(2)}) collective-permute-start(bf16[256,2,4,128]{3,0,2,1:T(8,128)(2,1)S(1)} %fusion.95), channel_id=1, source_target_pairs={{0,8},{8,0},{4,12},{12,4},{1,9},{9,1},{5,13},{13,5},{2,10},{10,2},... | collective-permute-start | bytes 1572872 | tf_op jit(solution)/shard_map/ppermute | solution.py:18
  175.2 2.5 %fusion.7 = (f32[4,2,512]{2,1,0:T(2,128)S(1)}, f32[4,512,512,2]{2,1,3,0:T(8,128)S(1)}) fusion(pred[512,512]{0,1:T(8,128)(4,1)S(1)} %fusion.87, bf16[512,4,2,64]{3,0,2,1:T(8,128)(2,1)S(1)} %get-tuple-element.14, bf16[512,4,2,64]{3,0,2,1:T(8,128)(2,1)S(1)} %get-tuple-element.13, bf16[512,4,64]{2,0,1:T(8,128)(2,1)S(1)} %get-tuple-element.28, ...), kind=kOutput, calls=%fused_computation.11 | convolution fusion | flops 546304000 | bytes 10240000 | tf_op jit(solution)/shard_map/tgrh,ugh->grtu/dot_general | solution.py:120
  177.7 20.0 %collective-permute-done.6 = bf16[256,2,4,128]{3,0,2,1:T(8,128)(2,1)S(1)} collective-permute-done((bf16[256,2,4,128]{3,0,2,1:T(8,128)(2,1)S(1)}, bf16[256,2,4,128]{3,0,2,1:T(8,128)(2,1)S(1)}, u32[]{:S(2)}, u32[]{:S(2)}) %collective-permute-start.6) | collective-permute-done | bytes 524320 | tf_op jit(solution)/shard_map/ppermute | solution.py:18
  206.9 2.5 %fusion.33 = bf16[512,4,2,128]{0,3,2,1:T(8,128)(2,1)S(1)} fusion(f32[512,4,2,128]{0,3,2,1:T(8,128)S(1)} %bitcast.173, f32[512,4,2,128]{0,3,2,1:T(8,128)S(1)} %bitcast.174, f32[4,512,512,2]{2,1,3,0:T(8,128)S(1)} %get-tuple-element.54, f32[4,2,512]{2,1,0:T(2,128)S(1)} %get-tuple-element.53, pred[512,512]{0,1:T(8,128)(4,1)S(1)} %fusion.87, ...), kind=kOutput, calls=%fused_computation.54 | convolution fusion | flops 548405248 | bytes 14483456 | tf_op jit(solution)/shard_map/grtu,ugh->tgrh/dot_general | solution.py:130
  211.0 2.8 %fusion.60 = f32[1024,1024]{1,0:T(8,128)S(1)} fusion(bf16[256,1024]{1,0:T(8,128)(2,1)S(1)} %copy-done.13, bf16[256,1024]{1,0:T(8,128)(2,1)S(1)} %copy-done.12, f32[512]{0:T(512)S(1)} %collective-permute-done.13, bf16[2048,1024]{1,0:T(8,128)(2,1)} %all-gather.2.cloned.1.call-done, s32[]{:T(128)S(6)} %select_n.404, f32[1024]{0:T(1024)S(1)} %dynamic_slice.66), kind=kOutput, calls=%fused_computation.70 | convolution fusion | flops 1077936128 | bytes 6297604 | tf_op jit(solution)/shard_map/tc,tr->cr/dot_general | solution.py:191
  216.0 3.9 %add_multiply_fusion = f32[1024,1024]{1,0:T(8,128)} fusion(f32[1024,1024]{1,0:T(8,128)S(1)} %fusion.60, f32[1024,1024]{1,0:T(8,128)S(1)} %copy-done, f32[1024,1024]{1,0:T(8,128)S(1)} %fusion.59, bf16[256,1024]{1,0:T(8,128)(2,1)S(1)} %get-tuple-element.31, bf16[256,1024]{1,0:T(8,128)(2,1)S(1)} %get-tuple-element.30, f32[512]{0:T(512)S(1)} %collective-permute-done.16, ...), kind=kOutput, calls=%fused_computation.22 | convolution fusion | flops 1082130432 | bytes 18880516 | tf_op jit(solution)/shard_map/tc,tr->cr/dot_general | solution.py:191
  (118 shorter events, 29.0 us)
Async XLA Ops:
  7.2 203.8 %all-gather.2.cloned.1.call-start = ((), (), s32[]{:S(2)}) async-start(), calls=%async_computation | async-start | bytes 5242880 | tf_op jit(solution)/shard_map/all_gather | solution.py:172
  7.2 26.5 %collective-permute-start.1 = (bf16[512,1024]{1,0:T(8,128)(2,1)}, bf16[512,1024]{1,0:T(8,128)(2,1)}, u32[]{:S(2)}, u32[]{:S(2)}) collective-permute-start(bf16[512,1024]{1,0:T(8,128)(2,1)} %param.6), channel_id=1, source_target_pairs={{0,2},{2,0},{1,3},{3,1},{4,6},{6,4},{5,7},{7,5},{8,10},{10,8},{9,1... | collective-permute-start | bytes 3145736 | tf_op jit(solution)/shard_map/ppermute | solution.py:70
  10.2 33.7 %collective-permute-start = (bf16[512,1024]{1,0:T(8,128)(2,1)}, bf16[512,1024]{1,0:T(8,128)(2,1)}, u32[]{:S(2)}, u32[]{:S(2)}) collective-permute-start(bf16[512,1024]{1,0:T(8,128)(2,1)} %param.6), channel_id=1, source_target_pairs={{0,1},{1,0},{2,3},{3,2},{4,5},{5,4},{6,7},{7,6},{8,9},{9,8},{10,11... | collective-permute-start | bytes 3145736 | tf_op jit(solution)/shard_map/ppermute | solution.py:26
  13.1 21.3 %copy-start.4 = (bf16[2048,4,128]{2,1,0:T(4,128)(2,1)S(1)}, bf16[2048,4,128]{2,1,0:T(4,128)(2,1)}, u32[]{:S(2)}) copy-start(bf16[2048,4,128]{2,1,0:T(4,128)(2,1)} %param.9) | copy-start | bytes 6291460
  15.4 24.3 %copy-start.17 = (f32[4096]{0:T(1024)S(1)}, f32[4096]{0:T(1024)}, u32[]{:S(2)}) copy-start(f32[4096]{0:T(1024)} %param.7) | copy-start | bytes 49156
  15.4 28.5 %copy-start.5 = (bf16[512,1024]{1,0:T(8,128)(2,1)S(1)}, bf16[512,1024]{1,0:T(8,128)(2,1)}, u32[]{:S(2)}) copy-start(bf16[512,1024]{1,0:T(8,128)(2,1)} %param.6) | copy-start | bytes 3145732
  15.4 133.4 %collective-permute-start.3 = (bf16[2,2048,4,128]{3,1,2,0:T(8,128)(2,1)}, bf16[2,2048,4,128]{3,1,2,0:T(8,128)(2,1)}, u32[]{:S(2)}, u32[]{:S(2)}) collective-permute-start(bf16[2,2048,4,128]{3,1,2,0:T(8,128)(2,1)} %pad_maximum_fusion.1), channel_id=1, source_target_pairs={{0,1},{1,0},{2,3},{3,2},{4,5},{5,4},{6,7},{7,6},{8,9},{9,8},{10,11... | collective-permute-start | bytes 12582920 | tf_op jit(solution)/shard_map/ppermute | solution.py:107
  33.7 10.2 %collective-permute-start.2 = (bf16[512,1024]{1,0:T(8,128)(2,1)}, bf16[512,1024]{1,0:T(8,128)(2,1)}, u32[]{:S(2)}, u32[]{:S(2)}) collective-permute-start(bf16[512,1024]{1,0:T(8,128)(2,1)} %collective-permute-done.1), channel_id=1, source_target_pairs={{0,1},{1,0},{2,3},{3,2},{4,5},{5,4},{6,7},{7,6},{8,9},{9,8},{10,11... | collective-permute-start | bytes 3145736 | tf_op jit(solution)/shard_map/ppermute | solution.py:26
  46.1 9.5 %slice-start = ((s8[8388608]{0:T(1024)(128)(4,1)}), s8[4194304]{0:T(1024)(128)(4,1)S(1)}, s32[]{:S(2)}) async-start(s8[8388608]{0:T(1024)(128)(4,1)} %bitcast.190), calls=%async_computation.1 | async-start | bytes 8388608
  47.1 8.5 %slice-start.1 = ((s8[8388608]{0:T(1024)(128)(4,1)}), s8[4194304]{0:T(1024)(128)(4,1)S(1)}, s32[]{:S(2)}) async-start(s8[8388608]{0:T(1024)(128)(4,1)} %bitcast.190), calls=%async_computation.2 | async-start | bytes 8388608
  47.1 163.8 %collective-permute-start.13 = (f32[512]{0:T(512)S(1)}, f32[512]{0:T(512)S(1)}, u32[]{:S(2)}, u32[]{:S(2)}) collective-permute-start(f32[512]{0:T(512)S(1)} %add_rsqrt_fusion), channel_id=1, source_target_pairs={{0,8},{4,12},{8,0},{12,4},{1,9},{5,13},{9,1},{13,5},{2,10},{6,14},... | collective-permute-start | bytes 6152 | tf_op jit(solution)/shard_map/ppermute | solution.py:181
  51.3 8.8 %copy-start.1 = (bf16[512,4096]{1,0:T(8,128)(2,1)}, bf16[512,4096]{1,0:T(8,128)(2,1)S(1)}, u32[]{:S(2)}) copy-start(bf16[512,4096]{1,0:T(8,128)(2,1)S(1)} %fusion.2) | copy-start | bytes 12582916
  53.7 65.6 %collective-permute-start.11 = (bf16[256,1024]{1,0:T(8,128)(2,1)}, bf16[256,1024]{1,0:T(8,128)(2,1)}, u32[]{:S(2)}, u32[]{:S(2)}) collective-permute-start(bf16[256,1024]{1,0:T(8,128)(2,1)} %get-tuple-element.20), channel_id=1, source_target_pairs={{0,8},{4,12},{8,0},{12,4},{1,9},{5,13},{9,1},{13,5},{2,10},{6,14},... | collective-permute-start | bytes 1572872 | tf_op jit(solution)/shard_map/ppermute | solution.py:181
  53.8 65.5 %collective-permute-start.8 = (bf16[256,1024]{1,0:T(8,128)(2,1)S(1)}, bf16[256,1024]{1,0:T(8,128)(2,1)}, u32[]{:S(2)}, u32[]{:S(2)}) collective-permute-start(bf16[256,1024]{1,0:T(8,128)(2,1)S(1)} %get-tuple-element.21), channel_id=1, source_target_pairs={{0,4},{4,8},{8,12},{12,0},{1,5},{5,9},{9,13},{13,1},{2,6},{6,10},{... | collective-permute-start | bytes 1572872 | tf_op jit(solution)/shard_map/ppermute | solution.py:181
  60.4 5.9 %copy-start.6 = (f32[512,64]{1,0:T(8,128)S(1)}, f32[512,64]{1,0:T(8,128)}, u32[]{:S(2)}) copy-start(f32[512,64]{1,0:T(8,128)} %get-tuple-element.40) | copy-start | bytes 393220
  60.4 5.9 %copy-start.8 = (f32[512,64]{1,0:T(8,128)S(1)}, f32[512,64]{1,0:T(8,128)}, u32[]{:S(2)}) copy-start(f32[512,64]{1,0:T(8,128)} %get-tuple-element.41) | copy-start | bytes 393220
  64.3 55.5 %copy-start.2 = (bf16[512,4096]{1,0:T(8,128)(2,1)S(1)}, bf16[512,4096]{1,0:T(8,128)(2,1)}, u32[]{:S(2)}) copy-start(bf16[512,4096]{1,0:T(8,128)(2,1)} %copy-done.1) | copy-start | bytes 12582916
  64.3 55.5 %copy-start.10 = (bf16[2048,4,128]{0,2,1:T(8,128)(2,1)S(1)}, bf16[2048,4,128]{0,2,1:T(8,128)(2,1)}, u32[]{:S(2)}) copy-start(bf16[2048,4,128]{0,2,1:T(8,128)(2,1)} %copy.53) | copy-start | bytes 6291460
  64.3 81.9 %collective-permute-start.14 = (bf16[256,1024]{1,0:T(8,128)(2,1)}, bf16[256,1024]{1,0:T(8,128)(2,1)}, u32[]{:S(2)}, u32[]{:S(2)}) collective-permute-start(bf16[256,1024]{1,0:T(8,128)(2,1)} %get-tuple-element.19), channel_id=1, source_target_pairs={{0,12},{4,0},{8,4},{12,8},{1,13},{5,1},{9,5},{13,9},{2,14},{6,2},{... | collective-permute-start | bytes 1572872 | tf_op jit(solution)/shard_map/ppermute | solution.py:181
  119.3 9.4 %collective-permute-start.12 = (bf16[256,1024]{1,0:T(8,128)(2,1)}, bf16[256,1024]{1,0:T(8,128)(2,1)}, u32[]{:S(2)}, u32[]{:S(2)}) collective-permute-start(bf16[256,1024]{1,0:T(8,128)(2,1)} %collective-permute-done.11), channel_id=1, source_target_pairs={{0,1},{1,0},{2,3},{3,2},{4,5},{5,4},{6,7},{7,6},{8,9},{9,8},{10,11... | collective-permute-start | bytes 1572872 | tf_op jit(solution)/shard_map/ppermute | solution.py:26
  119.3 26.8 %collective-permute-start.9 = (bf16[256,1024]{1,0:T(8,128)(2,1)}, bf16[256,1024]{1,0:T(8,128)(2,1)}, u32[]{:S(2)}, u32[]{:S(2)}) collective-permute-start(bf16[256,1024]{1,0:T(8,128)(2,1)} %collective-permute-done.8), channel_id=1, source_target_pairs={{0,1},{1,0},{2,3},{3,2},{4,5},{5,4},{6,7},{7,6},{8,9},{9,8},{10,11... | collective-permute-start | bytes 1572872 | tf_op jit(solution)/shard_map/ppermute | solution.py:26
  128.7 85.0 %collective-permute-start.10 = (f32[512]{0:T(512)S(1)}, f32[512]{0:T(512)S(1)}, u32[]{:S(2)}, u32[]{:S(2)}) collective-permute-start(f32[512]{0:T(512)S(1)} %add_rsqrt_fusion), channel_id=1, source_target_pairs={{0,4},{4,8},{8,12},{12,0},{1,5},{5,9},{9,13},{13,1},{2,6},{6,10},{... | collective-permute-start | bytes 6152 | tf_op jit(solution)/shard_map/ppermute | solution.py:181
  146.1 69.1 %collective-permute-start.16 = (f32[512]{0:T(512)S(1)}, f32[512]{0:T(512)S(1)}, u32[]{:S(2)}, u32[]{:S(2)}) collective-permute-start(f32[512]{0:T(512)S(1)} %add_rsqrt_fusion), channel_id=1, source_target_pairs={{0,12},{4,0},{8,4},{12,8},{1,13},{5,1},{9,5},{13,9},{2,14},{6,2},{... | collective-permute-start | bytes 6152 | tf_op jit(solution)/shard_map/ppermute | solution.py:181
  146.2 27.6 %collective-permute-start.15 = (bf16[256,1024]{1,0:T(8,128)(2,1)}, bf16[256,1024]{1,0:T(8,128)(2,1)}, u32[]{:S(2)}, u32[]{:S(2)}) collective-permute-start(bf16[256,1024]{1,0:T(8,128)(2,1)} %collective-permute-done.14), channel_id=1, source_target_pairs={{0,1},{1,0},{2,3},{3,2},{4,5},{5,4},{6,7},{7,6},{8,9},{9,8},{10,11... | collective-permute-start | bytes 1572872 | tf_op jit(solution)/shard_map/ppermute | solution.py:26
  164.3 4.1 %copy-start.3 = (bf16[512,4096]{1,0:T(8,128)(2,1)S(1)}, bf16[512,4096]{1,0:T(8,128)(2,1)}, u32[]{:S(2)}) copy-start(bf16[512,4096]{1,0:T(8,128)(2,1)} %copy-done.1) | copy-start | bytes 12582916
  164.3 4.3 %copy-start.11 = (bf16[2048,4,128]{2,1,0:T(4,128)(2,1)S(1)}, bf16[2048,4,128]{2,1,0:T(4,128)(2,1)}, u32[]{:S(2)}) copy-start(bf16[2048,4,128]{2,1,0:T(4,128)(2,1)} %param.10) | copy-start | bytes 6291460
  170.0 27.7 %collective-permute-start.6 = (bf16[256,2,4,128]{3,0,2,1:T(8,128)(2,1)S(1)}, bf16[256,2,4,128]{3,0,2,1:T(8,128)(2,1)S(1)}, u32[]{:S(2)}, u32[]{:S(2)}) collective-permute-start(bf16[256,2,4,128]{3,0,2,1:T(8,128)(2,1)S(1)} %fusion.95), channel_id=1, source_target_pairs={{0,8},{8,0},{4,12},{12,4},{1,9},{9,1},{5,13},{13,5},{2,10},{10,2},... | collective-permute-start | bytes 1572872 | tf_op jit(solution)/shard_map/ppermute | solution.py:18
  173.7 24.5 %collective-permute-start.4 = (bf16[256,2,4,128]{3,0,2,1:T(8,128)(2,1)S(1)}, bf16[256,2,4,128]{3,0,2,1:T(8,128)(2,1)S(1)}, u32[]{:S(2)}, u32[]{:S(2)}) collective-permute-start(bf16[256,2,4,128]{3,0,2,1:T(8,128)(2,1)S(1)} %fusion.95), channel_id=1, source_target_pairs={{0,4},{4,0},{8,12},{12,8},{1,5},{5,1},{9,13},{13,9},{2,6},{6,2},{1... | collective-permute-start | bytes 1572872 | tf_op jit(solution)/shard_map/ppermute | solution.py:18
  197.7 2.8 %collective-permute-start.7 = (bf16[256,2,4,128]{3,0,2,1:T(8,128)(2,1)S(1)}, bf16[256,2,4,128]{3,0,2,1:T(8,128)(2,1)S(1)}, u32[]{:S(2)}, u32[]{:S(2)}) collective-permute-start(bf16[256,2,4,128]{3,0,2,1:T(8,128)(2,1)S(1)} %collective-permute-done.6), channel_id=1, source_target_pairs={{0,1},{1,0},{2,3},{3,2},{4,5},{5,4},{6,7},{7,6},{8,9},{9,8},{10,11... | collective-permute-start | bytes 1572872 | tf_op jit(solution)/shard_map/ppermute | solution.py:26
  198.2 2.3 %collective-permute-start.5 = (bf16[256,2,4,128]{3,0,2,1:T(8,128)(2,1)S(1)}, bf16[256,2,4,128]{3,0,2,1:T(8,128)(2,1)S(1)}, u32[]{:S(2)}, u32[]{:S(2)}) collective-permute-start(bf16[256,2,4,128]{3,0,2,1:T(8,128)(2,1)S(1)} %collective-permute-done.4), channel_id=1, source_target_pairs={{0,1},{1,0},{2,3},{3,2},{4,5},{5,4},{6,7},{7,6},{8,9},{9,8},{10,11... | collective-permute-start | bytes 1572872 | tf_op jit(solution)/shard_map/ppermute | solution.py:26
  206.9 4.0 %copy-start.12 = (bf16[256,1024]{1,0:T(8,128)(2,1)S(1)}, bf16[256,1024]{1,0:T(8,128)(2,1)}, u32[]{:S(2)}) copy-start(bf16[256,1024]{1,0:T(8,128)(2,1)} %get-tuple-element.34) | copy-start | bytes 1572868
  206.9 4.0 %copy-start.13 = (bf16[256,1024]{1,0:T(8,128)(2,1)S(1)}, bf16[256,1024]{1,0:T(8,128)(2,1)}, u32[]{:S(2)}) copy-start(bf16[256,1024]{1,0:T(8,128)(2,1)} %get-tuple-element.35) | copy-start | bytes 1572868
  (7 other events, 21.0 us)
Sparse Core Ops, SparseCore 0:
  10.4 123.0 all-gather.1

commit v15 on v7

--- a/solution.py
+++ b/solution.py
@@ -170,6 +170,7 @@
     inverse_count = 1.0 / (row_count * seq_count)
     share = row_count // sub_count
     raw_columns = lax.all_gather(tokens, "seq", axis=0, tiled=True)
+    all_scales = lax.all_gather(row_scale, "seq", axis=0, tiled=True)
     column_gain = lax.dynamic_slice_in_dim(norm_gain, owner_index * tile_cols, tile_cols, 0)
     mine = lax.dynamic_slice_in_dim(normed, seq_index * band, band, 1)
     gram_sum = jnp.einsum("tc,tr->cr", mine, owned, preferred_element_type=jnp.float32)
@@ -178,10 +179,11 @@
         target = (seq_index + shift) % seq_count
         outgoing = lax.dynamic_slice_in_dim(my_rows, target * band, band, 1)
         route = [(j, (j + shift) % seq_count) for j in range(seq_count)]
-        incoming, their_scale = lax.ppermute((outgoing, row_scale), "seq", route)
+        incoming = lax.ppermute(outgoing, "seq", route)
         halves = swap_halves(incoming, sub_count, sub_index)
         source = (seq_index - shift) % seq_count
         their_raw = lax.dynamic_slice_in_dim(raw_columns, source * row_count, row_count, 0)
+        their_scale = lax.dynamic_slice_in_dim(all_scales, source * row_count, row_count, 0)
         their_owned = (
             their_raw.astype(jnp.float32) * their_scale[:, None] * column_gain
         ).astype(jnp.bfloat16)

time: 193 us -> 229 us (1.19)
  blocking collectives: 0 us -> 69.1 us
  waiting for transfers between devices: 71 us -> 35.8 us
  starting transfers between devices: 14.5 us -> 11.1 us
  local copies, waits for them, and re-layouts: 28.6 us -> 31.6 us
  matrix products: 41.9 us -> 44.2 us
    all_gather x0 -> x1, blocking collectives: none -> 69.1 us  [body(): all_scales = lax.all_gather(row_scale, 'seq', axis=0, tiled=True)]
    ppermute x6 -> x3, waiting for transfers between devices: 33.9 us -> 0.01 us  [body(): incoming = lax.ppermute(outgoing, 'seq', route)]
    ppermute x6 -> x3, starting transfers between devices: 8.77 us -> 4.88 us  [body(): incoming = lax.ppermute(outgoing, 'seq', route)]
    dot_general x6, matrix products: 9.58 us -> 11.9 us  [body(): jnp.einsum('tc,tr->cr', halves[lane_shift], their_rows, preferred_element...]
  transfers between devices with their start and end apart: 18 -> 15, of which waited for: 3 -> 2; matrix products, arithmetic and copies ran while one was open for 44% -> 39% of each run, Pallas kernels for 0% -> 0%
where the time goes in v15:
time: 229 us
  blocking collectives  69.1 us (30%)
  matrix products  44.2 us (19%)
  waiting for transfers between devices  35.8 us (16%)
  local copies, waits for them, and re-layouts  31.6 us (14%)
  other arithmetic  22.3 us (10%)
  between operations  14.6 us (6%)
  starting transfers between devices  11.1 us (5%)
    all_gather x1, blocking collectives, body(): all_scales = lax.all_gather(row_scale, 'seq', axis=0, tiled=True)  69.1 us
    ppermute x2, waiting for transfers between devices, from_partner(): return lax.ppermute(block, axis, route)  18.7 us
    ppermute x1, waiting for transfers between devices, body(): across.append(lax.ppermute(tokens, 'kvh', route))  17 us
    dot_general x6, matrix products, body(): jnp.einsum('tc,tr->cr', halves[lane_shift], their_rows, preferred_element...  11.9 us
    unnamed x36, local copies, waits for them, and re-layouts  11.9 us
    dot_general x1, matrix products, body(): jnp.einsum('td,dgc->tgc', normed, w_query, preferred_element_type=jnp.flo...  8.29 us
    squeeze x2, local copies, waits for them, and re-layouts, body(): key_part, value_part = (weight_pair[0], weight_pair[1])  7.05 us
    unnamed x2, matrix products  5.75 us
  transfers between devices with their start and end apart: 15, of which 2 were waited for; matrix products, arithmetic and copies ran while one was open for 39% of the time, Pallas kernels for 0%

profile of v15, /device:TPU:0, one launch (start us, length us, event | category | flops | bytes accessed | tf_op | source)
XLA Modules:
  0.0 228.6 jit_solution(15292897427230092055)
XLA Ops:
  7.2 3.0 %collective-permute-start.1 = (bf16[512,1024]{1,0:T(8,128)(2,1)}, bf16[512,1024]{1,0:T(8,128)(2,1)}, u32[]{:S(2)}, u32[]{:S(2)}) collective-permute-start(bf16[512,1024]{1,0:T(8,128)(2,1)} %param.6), channel_id=1, source_target_pairs={{0,2},{2,0},{1,3},{3,1},{4,6},{6,4},{5,7},{7,5},{8,10},{10,8},{9,1... | collective-permute-start | bytes 3145736 | tf_op jit(solution)/shard_map/ppermute | solution.py:70
  10.3 2.8 %copy_bitcast_fusion = (bf16[1,2048,4,128]{3,1,2,0:T(8,128)(2,1)S(1)}, bf16[1,2048,4,128]{3,1,2,0:T(8,128)(2,1)S(1)}) fusion(bf16[2048,4,128]{2,1,0:T(4,128)(2,1)} %param.9, bf16[2048,4,128]{2,1,0:T(4,128)(2,1)} %param.10), kind=kLoop, calls=%fused_computation.48 | loop fusion | bytes 8388608 | tf_op jit(solution)/shard_map/stack | solution.py:107
  13.1 2.4 %pad_maximum_fusion.1 = bf16[2,2048,4,128]{3,1,2,0:T(8,128)(2,1)} fusion(bf16[1,2048,4,128]{3,1,2,0:T(8,128)(2,1)S(1)} %get-tuple-element.60, bf16[1,2048,4,128]{3,1,2,0:T(8,128)(2,1)S(1)} %get-tuple-element.59), kind=kLoop, calls=%fused_computation.14 | loop fusion | flops 2097152 | bytes 8388608 | tf_op jit(solution)/shard_map/stack | solution.py:107
  16.7 17.0 %collective-permute-done.1 = bf16[512,1024]{1,0:T(8,128)(2,1)} collective-permute-done((bf16[512,1024]{1,0:T(8,128)(2,1)}, bf16[512,1024]{1,0:T(8,128)(2,1)}, u32[]{:S(2)}, u32[]{:S(2)}) %collective-permute-start.1) | collective-permute-done | bytes 1048608 | tf_op jit(solution)/shard_map/ppermute | solution.py:70
  34.4 2.7 %copy.53 = bf16[2048,4,128]{0,2,1:T(8,128)(2,1)} copy(bf16[2048,4,128]{2,1,0:T(4,128)(2,1)S(1)} %copy-done.5) | data formatting | bytes 4194304 | tf_op args[3]
  37.1 2.5 %select_reduce_fusion.1 = (f32[512]{0:T(512)S(1)}, f32[512]{0:T(512)S(1)}) fusion(f32[]{:T(128)} %bitcast.45, f32[]{:T(128)} %bitcast.44, f32[]{:T(128)} %bitcast.32, f32[]{:T(128)} %bitcast.31), kind=kLoop, calls=%fused_computation.155 | loop fusion | flops 7168 | bytes 4112 | tf_op jit(solution)/shard_map/gather | solution.py:141
  42.0 1.8 multiply_cosine_fusion
  43.9 2.1 select_select_fusion.3
  48.5 1.9 copy-done.1
  52.0 8.3 %fusion.3 = f32[512,4,256]{0,2,1:T(8,128)S(1)} fusion(bf16[4096,4,256]{2,1,0:T(4,128)(2,1)} %param.8, bf16[512,4096]{1,0:T(8,128)(2,1)} %copy-done.1), kind=kOutput, calls=%fused_computation.6 | convolution fusion | flops 4294967296 | bytes 14680064 | tf_op jit(solution)/shard_map/td,dgc->tgc/dot_general | solution.py:93
  60.5 2.0 copy.91
  62.5 1.9 copy.90
  64.4 3.7 %fusion.121 = (bf16[256,1024]{1,0:T(8,128)(2,1)}, bf16[256,1024]{1,0:T(8,128)(2,1)}, bf16[256,1024]{1,0:T(8,128)(2,1)}) fusion(bf16[512,4096]{1,0:T(8,128)(2,1)} %copy-done.1, s32[]{:T(128)S(6)} %select_n.357, s32[]{:T(128)S(6)} %select_n.360, s32[]{:T(128)S(6)} %select_n.370, s32[]{:T(128)S(6)} %select_n.365), kind=kLoop, calls=%fused_computation.172 | loop fusion | bytes 3145744 | tf_op jit(solution)/shard_map/dynamic_slice | solution.py:180
  68.1 3.8 %collective-permute-start.12 = (bf16[256,1024]{1,0:T(8,128)(2,1)}, bf16[256,1024]{1,0:T(8,128)(2,1)}, u32[]{:S(2)}, u32[]{:S(2)}) collective-permute-start(bf16[256,1024]{1,0:T(8,128)(2,1)} %get-tuple-element.23), channel_id=1, source_target_pairs={{0,12},{4,0},{8,4},{12,8},{1,13},{5,1},{9,5},{13,9},{2,14},{6,2},{... | collective-permute-start | bytes 1572872 | tf_op jit(solution)/shard_map/ppermute | solution.py:182
  73.0 69.1 %all-gather = f32[4,1,512]{2,1,0:T(1,128)S(1)} all-gather(f32[1,1,512]{2,1,0:T(1,128)S(1)} %bitcast.199), channel_id=1, replica_groups=mesh['grp'=2,'seq'=4,'kvh'=2,'sub'=2] {'seq'}, dimensions={0}, use_global_device_ids=true | all-gather | bytes 10240 | tf_op jit(solution)/shard_map/all_gather | solution.py:173
  142.1 5.0 %fusion.63 = f32[1024,1024]{1,0:T(8,128)} fusion(bf16[512,4096]{1,0:T(8,128)(2,1)} %copy-done.1, s32[]{:T(128)} %select_n.356, s32[]{:T(128)S(6)} %select_n.355), kind=kOutput, calls=%fused_computation.77 | convolution fusion | flops 1073741824 | bytes 6291972 | tf_op jit(solution)/shard_map/tc,tr->cr/dot_general | solution.py:176
  147.7 3.0 %slice_bitcast_fusion = bf16[2048,4,128]{2,0,1:T(8,128)(2,1)} fusion(bf16[2,2048,4,128]{3,1,2,0:T(8,128)(2,1)} %collective-permute-done.3), kind=kLoop, calls=%fused_computation.33 | loop fusion | bytes 4194304 | tf_op jit(solution)/shard_map/squeeze | solution.py:108
  150.7 4.0 %copy.54 = bf16[2048,4,128]{0,2,1:T(8,128)(2,1)} copy(bf16[2048,4,128]{2,0,1:T(8,128)(2,1)} %slice_bitcast_fusion) | data formatting | bytes 4194304 | tf_op jit(solution)/shard_map/squeeze | solution.py:108
  154.7 4.5 %fusion.35 = f32[512,512]{0,1} fusion(bf16[2048,512]{0,1:T(8,128)(2,1)} %bitcast.184, bf16[512,4096]{1,0:T(8,128)(2,1)} %copy-done.1, s32[]{:T(128)S(6)} %select_n.344), kind=kOutput, calls=%fused_computation.57 | convolution fusion | flops 1073741824 | bytes 5242884
  159.2 2.5 %copy.56 = f32[512,4,128]{2,0,1:T(8,128)} copy(f32[512,4,128]{0,2,1:T(8,128)} %bitcast.191) | data formatting | bytes 2097152 | tf_op jit(solution)/shard_map/td,dgh->tgh/dot_general | solution.py:111
  163.1 3.6 %fusion.21 = f32[512,4,128]{2,0,1:T(8,128)S(1)} fusion(bf16[2,2048,4,128]{3,1,2,0:T(8,128)(2,1)} %collective-permute-done.3, bf16[512,4096]{1,0:T(8,128)(2,1)} %copy-done.1, s32[]{:T(128)S(6)} %select_n.344), kind=kOutput, calls=%fused_computation.35 | convolution fusion | flops 1073741824 | bytes 5242884 | tf_op jit(solution)/shard_map/td,dgh->tgh/dot_general | solution.py:112
  169.2 1.5 collective-permute-start.4
  171.4 2.5 %fusion.7 = (f32[4,2,512]{2,1,0:T(2,128)S(1)}, f32[4,512,512,2]{2,1,3,0:T(8,128)S(1)}) fusion(pred[512,512]{0,1:T(8,128)(4,1)S(1)} %fusion.66, bf16[512,4,2,64]{3,0,2,1:T(8,128)(2,1)S(1)} %get-tuple-element.14, bf16[512,4,2,64]{3,0,2,1:T(8,128)(2,1)S(1)} %get-tuple-element.13, bf16[512,4,64]{2,0,1:T(8,128)(2,1)S(1)} %get-tuple-element.31, ...), kind=kOutput, calls=%fused_computation.11 | convolution fusion | flops 546304000 | bytes 10240000 | tf_op jit(solution)/shard_map/tgrh,ugh->grtu/dot_general | solution.py:120
  173.9 18.7 %collective-permute-done.6 = bf16[256,2,4,128]{3,0,2,1:T(8,128)(2,1)S(1)} collective-permute-done((bf16[256,2,4,128]{3,0,2,1:T(8,128)(2,1)S(1)}, bf16[256,2,4,128]{3,0,2,1:T(8,128)(2,1)S(1)}, u32[]{:S(2)}, u32[]{:S(2)}) %collective-permute-start.6) | collective-permute-done | bytes 524320 | tf_op jit(solution)/shard_map/ppermute | solution.py:18
  193.1 1.8 fusion.5
  201.8 2.5 %fusion.33 = bf16[512,4,2,128]{0,3,2,1:T(8,128)(2,1)S(1)} fusion(f32[512,4,2,128]{0,3,2,1:T(8,128)S(1)} %bitcast.181, f32[512,4,2,128]{0,3,2,1:T(8,128)S(1)} %bitcast.182, f32[4,512,512,2]{2,1,3,0:T(8,128)S(1)} %get-tuple-element.54, f32[4,2,512]{2,1,0:T(2,128)S(1)} %get-tuple-element.53, pred[512,512]{0,1:T(8,128)(4,1)S(1)} %fusion.66, ...), kind=kOutput, calls=%fused_computation.54 | convolution fusion | flops 548405248 | bytes 14483456 | tf_op jit(solution)/shard_map/grtu,ugh->tgrh/dot_general | solution.py:130
  204.3 1.4 copy.71
  205.8 2.6 %multiply_convert_fusion.2 = (bf16[512,1024]{1,0:T(8,128)(2,1)S(1)}, bf16[512,1024]{1,0:T(8,128)(2,1)S(1)}, bf16[512,1024]{1,0:T(8,128)(2,1)S(1)}) fusion(f32[1024]{0:T(1024)S(1)} %dynamic-slice-done, f32[512]{0:T(512)S(1)} %get-tuple-element.37, bf16[2048,1024]{1,0:T(8,128)(2,1)} %all-gather.3.cloned.1.call-done, s32[]{:T(128)S(6)} %select_n.362, ...), kind=kLoop, calls=%fused_computation.51 | loop fusion | flops 6291456 | bytes 6301708 | tf_op jit(solution)/shard_map/convert_element_type | solution.py:189
  208.4 2.2 fusion.81
  210.6 1.8 fusion.85
  213.2 1.8 fusion.89
  217.1 4.7 %add_multiply_fusion = f32[1024,1024]{1,0:T(8,128)} fusion(f32[1024,1024]{1,0:T(8,128)S(1)} %fusion.81, f32[1024,1024]{1,0:T(8,128)S(1)} %fusion.83, f32[1024,1024]{1,0:T(8,128)S(1)} %fusion.85, f32[1024,1024]{1,0:T(8,128)S(1)} %fusion.87, f32[1024,1024]{1,0:T(8,128)S(1)} %copy-done, f32[1024,1024]{1,0:T(8,128)S(1)} %fusion.89, ...), kind=kOutput, calls=%fused_computation.22 | convolution fusion | flops 544210944 | bytes 30408708 | tf_op jit(solution)/shard_map/tc,tr->cr/dot_general | solution.py:193
  (105 shorter events, 24.9 us)
Async XLA Ops:
  7.2 198.6 %all-gather.3.cloned.1.call-start = ((), (), s32[]{:S(2)}) async-start(), calls=%async_computation | async-start | bytes 5242880 | tf_op jit(solution)/shard_map/all_gather | solution.py:172
  7.2 26.5 %collective-permute-start.1 = (bf16[512,1024]{1,0:T(8,128)(2,1)}, bf16[512,1024]{1,0:T(8,128)(2,1)}, u32[]{:S(2)}, u32[]{:S(2)}) collective-permute-start(bf16[512,1024]{1,0:T(8,128)(2,1)} %param.6), channel_id=1, source_target_pairs={{0,2},{2,0},{1,3},{3,1},{4,6},{6,4},{5,7},{7,5},{8,10},{10,8},{9,1... | collective-permute-start | bytes 3145736 | tf_op jit(solution)/shard_map/ppermute | solution.py:70
  10.2 33.6 %collective-permute-start = (bf16[512,1024]{1,0:T(8,128)(2,1)}, bf16[512,1024]{1,0:T(8,128)(2,1)}, u32[]{:S(2)}, u32[]{:S(2)}) collective-permute-start(bf16[512,1024]{1,0:T(8,128)(2,1)} %param.6), channel_id=1, source_target_pairs={{0,1},{1,0},{2,3},{3,2},{4,5},{5,4},{6,7},{7,6},{8,9},{9,8},{10,11... | collective-permute-start | bytes 3145736 | tf_op jit(solution)/shard_map/ppermute | solution.py:26
  13.0 2.9 %copy-start.15 = (s32[3,8]{1,0:T(4,128)S(1)}, s32[3,8]{1,0:T(4,128)}, u32[]{:S(2)}) copy-start(s32[3,8]{1,0:T(4,128)} %param.11) | copy-start | bytes 292
  13.1 21.3 %copy-start.5 = (bf16[2048,4,128]{2,1,0:T(4,128)(2,1)S(1)}, bf16[2048,4,128]{2,1,0:T(4,128)(2,1)}, u32[]{:S(2)}) copy-start(bf16[2048,4,128]{2,1,0:T(4,128)(2,1)} %param.9) | copy-start | bytes 6291460
  15.4 28.5 %copy-start.7 = (bf16[512,1024]{1,0:T(8,128)(2,1)S(1)}, bf16[512,1024]{1,0:T(8,128)(2,1)}, u32[]{:S(2)}) copy-start(bf16[512,1024]{1,0:T(8,128)(2,1)} %param.6) | copy-start | bytes 3145732
  15.4 132.2 %collective-permute-start.3 = (bf16[2,2048,4,128]{3,1,2,0:T(8,128)(2,1)}, bf16[2,2048,4,128]{3,1,2,0:T(8,128)(2,1)}, u32[]{:S(2)}, u32[]{:S(2)}) collective-permute-start(bf16[2,2048,4,128]{3,1,2,0:T(8,128)(2,1)} %pad_maximum_fusion.1), channel_id=1, source_target_pairs={{0,1},{1,0},{2,3},{3,2},{4,5},{5,4},{6,7},{7,6},{8,9},{9,8},{10,11... | collective-permute-start | bytes 12582920 | tf_op jit(solution)/shard_map/ppermute | solution.py:107
  33.7 10.2 %collective-permute-start.2 = (bf16[512,1024]{1,0:T(8,128)(2,1)}, bf16[512,1024]{1,0:T(8,128)(2,1)}, u32[]{:S(2)}, u32[]{:S(2)}) collective-permute-start(bf16[512,1024]{1,0:T(8,128)(2,1)} %collective-permute-done.1), channel_id=1, source_target_pairs={{0,1},{1,0},{2,3},{3,2},{4,5},{5,4},{6,7},{7,6},{8,9},{9,8},{10,11... | collective-permute-start | bytes 3145736 | tf_op jit(solution)/shard_map/ppermute | solution.py:26
  46.0 1.0 copy-start.14
  47.1 3.4 %copy-start.12 = (bf16[2048,4,128]{0,2,1:T(8,128)(2,1)S(1)}, bf16[2048,4,128]{0,2,1:T(8,128)(2,1)}, u32[]{:S(2)}) copy-start(bf16[2048,4,128]{0,2,1:T(8,128)(2,1)} %copy.53) | copy-start | bytes 6291460
  48.5 1.9 copy-start.1
  64.4 82.6 %copy-start.3 = (f32[512,4,2,64]{3,0,2,1:T(8,128)S(1)}, f32[512,4,2,64]{3,0,2,1:T(8,128)}, u32[]{:S(2)}) copy-start(f32[512,4,2,64]{3,0,2,1:T(8,128)} %copy.91) | copy-start | bytes 3145732
  64.4 82.6 %copy-start.4 = (f32[512,4,2,64]{3,0,2,1:T(8,128)S(1)}, f32[512,4,2,64]{3,0,2,1:T(8,128)}, u32[]{:S(2)}) copy-start(f32[512,4,2,64]{3,0,2,1:T(8,128)} %copy.90) | copy-start | bytes 3145732
  64.4 82.6 %copy-start.8 = (f32[512,64]{1,0:T(8,128)S(1)}, f32[512,64]{1,0:T(8,128)}, u32[]{:S(2)}) copy-start(f32[512,64]{1,0:T(8,128)} %get-tuple-element.40) | copy-start | bytes 393220
  64.4 82.7 %copy-start.10 = (f32[512,64]{1,0:T(8,128)S(1)}, f32[512,64]{1,0:T(8,128)}, u32[]{:S(2)}) copy-start(f32[512,64]{1,0:T(8,128)} %get-tuple-element.41) | copy-start | bytes 393220
  68.1 103.2 %collective-permute-start.12 = (bf16[256,1024]{1,0:T(8,128)(2,1)}, bf16[256,1024]{1,0:T(8,128)(2,1)}, u32[]{:S(2)}, u32[]{:S(2)}) collective-permute-start(bf16[256,1024]{1,0:T(8,128)(2,1)} %get-tuple-element.23), channel_id=1, source_target_pairs={{0,12},{4,0},{8,4},{12,8},{1,13},{5,1},{9,5},{13,9},{2,14},{6,2},{... | collective-permute-start | bytes 1572872 | tf_op jit(solution)/shard_map/ppermute | solution.py:182
  71.9 98.8 %collective-permute-start.10 = (bf16[256,1024]{1,0:T(8,128)(2,1)}, bf16[256,1024]{1,0:T(8,128)(2,1)}, u32[]{:S(2)}, u32[]{:S(2)}) collective-permute-start(bf16[256,1024]{1,0:T(8,128)(2,1)} %get-tuple-element.24), channel_id=1, source_target_pairs={{0,8},{4,12},{8,0},{12,4},{1,9},{5,13},{9,1},{13,5},{2,10},{6,14},... | collective-permute-start | bytes 1572872 | tf_op jit(solution)/shard_map/ppermute | solution.py:182
  71.9 98.9 %collective-permute-start.8 = (bf16[256,1024]{1,0:T(8,128)(2,1)}, bf16[256,1024]{1,0:T(8,128)(2,1)}, u32[]{:S(2)}, u32[]{:S(2)}) collective-permute-start(bf16[256,1024]{1,0:T(8,128)(2,1)} %get-tuple-element.22), channel_id=1, source_target_pairs={{0,4},{4,8},{8,12},{12,0},{1,5},{5,9},{9,13},{13,1},{2,6},{6,10},{... | collective-permute-start | bytes 1572872 | tf_op jit(solution)/shard_map/ppermute | solution.py:182
  163.1 3.7 %copy-start.2 = (bf16[512,4096]{1,0:T(8,128)(2,1)S(1)}, bf16[512,4096]{1,0:T(8,128)(2,1)}, u32[]{:S(2)}) copy-start(bf16[512,4096]{1,0:T(8,128)(2,1)} %copy-done.1) | copy-start | bytes 12582916
  163.1 4.1 %copy-start.13 = (bf16[2048,4,128]{2,1,0:T(4,128)(2,1)S(1)}, bf16[2048,4,128]{2,1,0:T(4,128)(2,1)}, u32[]{:S(2)}) copy-start(bf16[2048,4,128]{2,1,0:T(4,128)(2,1)} %param.10) | copy-start | bytes 6291460
  167.2 1.3 copy-start.9
  167.2 1.3 copy-start.11
  169.1 23.4 %collective-permute-start.6 = (bf16[256,2,4,128]{3,0,2,1:T(8,128)(2,1)S(1)}, bf16[256,2,4,128]{3,0,2,1:T(8,128)(2,1)S(1)}, u32[]{:S(2)}, u32[]{:S(2)}) collective-permute-start(bf16[256,2,4,128]{3,0,2,1:T(8,128)(2,1)S(1)} %fusion.74), channel_id=1, source_target_pairs={{0,8},{8,0},{4,12},{12,4},{1,9},{9,1},{5,13},{13,5},{2,10},{10,2},... | collective-permute-start | bytes 1572872 | tf_op jit(solution)/shard_map/ppermute | solution.py:18
  169.2 23.4 %collective-permute-start.4 = (bf16[256,2,4,128]{3,0,2,1:T(8,128)(2,1)S(1)}, bf16[256,2,4,128]{3,0,2,1:T(8,128)(2,1)S(1)}, u32[]{:S(2)}, u32[]{:S(2)}) collective-permute-start(bf16[256,2,4,128]{3,0,2,1:T(8,128)(2,1)S(1)} %fusion.74), channel_id=1, source_target_pairs={{0,4},{4,0},{8,12},{12,8},{1,5},{5,1},{9,13},{13,9},{2,6},{6,2},{1... | collective-permute-start | bytes 1572872 | tf_op jit(solution)/shard_map/ppermute | solution.py:18
  170.8 41.6 %collective-permute-start.11 = (bf16[256,1024]{1,0:T(8,128)(2,1)}, bf16[256,1024]{1,0:T(8,128)(2,1)S(1)}, u32[]{:S(2)}, u32[]{:S(2)}) collective-permute-start(bf16[256,1024]{1,0:T(8,128)(2,1)} %collective-permute-done.10), channel_id=1, source_target_pairs={{0,1},{1,0},{2,3},{3,2},{4,5},{5,4},{6,7},{7,6},{8,9},{9,8},{10,11... | collective-permute-start | bytes 1572872 | tf_op jit(solution)/shard_map/ppermute | solution.py:26
  170.8 44.2 %collective-permute-start.9 = (bf16[256,1024]{1,0:T(8,128)(2,1)}, bf16[256,1024]{1,0:T(8,128)(2,1)S(1)}, u32[]{:S(2)}, u32[]{:S(2)}) collective-permute-start(bf16[256,1024]{1,0:T(8,128)(2,1)} %collective-permute-done.8), channel_id=1, source_target_pairs={{0,1},{1,0},{2,3},{3,2},{4,5},{5,4},{6,7},{7,6},{8,9},{9,8},{10,11... | collective-permute-start | bytes 1572872 | tf_op jit(solution)/shard_map/ppermute | solution.py:26
  171.3 44.4 %collective-permute-start.13 = (bf16[256,1024]{1,0:T(8,128)(2,1)}, bf16[256,1024]{1,0:T(8,128)(2,1)}, u32[]{:S(2)}, u32[]{:S(2)}) collective-permute-start(bf16[256,1024]{1,0:T(8,128)(2,1)} %collective-permute-done.12), channel_id=1, source_target_pairs={{0,1},{1,0},{2,3},{3,2},{4,5},{5,4},{6,7},{7,6},{8,9},{9,8},{10,11... | collective-permute-start | bytes 1572872 | tf_op jit(solution)/shard_map/ppermute | solution.py:26
  192.6 2.7 %collective-permute-start.7 = (bf16[256,2,4,128]{3,0,2,1:T(8,128)(2,1)S(1)}, bf16[256,2,4,128]{3,0,2,1:T(8,128)(2,1)S(1)}, u32[]{:S(2)}, u32[]{:S(2)}) collective-permute-start(bf16[256,2,4,128]{3,0,2,1:T(8,128)(2,1)S(1)} %collective-permute-done.6), channel_id=1, source_target_pairs={{0,1},{1,0},{2,3},{3,2},{4,5},{5,4},{6,7},{7,6},{8,9},{9,8},{10,11... | collective-permute-start | bytes 1572872 | tf_op jit(solution)/shard_map/ppermute | solution.py:26
  192.6 2.8 %collective-permute-start.5 = (bf16[256,2,4,128]{3,0,2,1:T(8,128)(2,1)S(1)}, bf16[256,2,4,128]{3,0,2,1:T(8,128)(2,1)S(1)}, u32[]{:S(2)}, u32[]{:S(2)}) collective-permute-start(bf16[256,2,4,128]{3,0,2,1:T(8,128)(2,1)S(1)} %collective-permute-done.4), channel_id=1, source_target_pairs={{0,1},{1,0},{2,3},{3,2},{4,5},{5,4},{6,7},{7,6},{8,9},{9,8},{10,11... | collective-permute-start | bytes 1572872 | tf_op jit(solution)/shard_map/ppermute | solution.py:26
  201.8 4.0 %dynamic-slice-start = ((f32[4096]{0:T(1024)}, s32[]{:T(128)}), f32[1024]{0:T(1024)S(1)}, s32[]{:S(2)}) async-start(f32[4096]{0:T(1024)} %param.7, s32[]{:T(128)} %select_n.356), calls=%async_computation.1 | async-start | bytes 8704 | tf_op jit(solution)/shard_map/dynamic_slice | solution.py:174
  208.4 4.0 %copy-start.6 = (bf16[512,1024]{1,0:T(8,128)(2,1)}, bf16[512,1024]{1,0:T(8,128)(2,1)S(1)}, u32[]{:S(2)}) copy-start(bf16[512,1024]{1,0:T(8,128)(2,1)S(1)} %get-tuple-element.21) | copy-start | bytes 3145732
  215.0 2.2 copy-start
Sparse Core Ops, SparseCore 0:
  10.4 100.6 all-gather.2
